TPU v7x, 32 devices: a whole 2x2x4 slice. The times are simulated.
32 devices in a mesh: fsdp: 4 (over y, x), seq: 8 (over z, core).
Axes of the slice: x: 2, y: 2, z: 4, core: 2. Of those that a mesh axis runs over, the one named last changes fastest.
Arguments:
- events: bfloat16 [4, 1024, 2048], P('fsdp', 'seq'), may hold values from -6 to 6
- type_ids: int32 [4, 1024], P('fsdp', 'seq'), may hold values from 0 to 255
- type_table: bfloat16 [256, 2048], P('fsdp'), may hold values from -6 to 6
- norm_gain: float32 [2048], replicated, may hold values from 0.25 to 1.75
- kernel: bfloat16 [2048, 1152], P('fsdp'), may hold values from -0.1875 to 0.1875
- upstream: bfloat16 [4, 1024, 2048], P('fsdp', 'seq'), may hold values from -6 to 6
Outputs:
- input_grad: bfloat16 [4, 1024, 2048], P('fsdp', 'seq')
- table_grad: float32 [256, 2048], P(('fsdp', 'seq'))
- gain_grad: float32 [2048], P(('fsdp', 'seq'))
- kernel_grad: float32 [2048, 1152], P('seq')
All inputs are finite; a program needn't handle non-finite values.
Results may differ from a plain program's by a relative error of at most 0.0053.
Values may be sent and summed in bfloat16 or wider, within the bound.
No kernel may reach another device: no remote copies, remote signals or barrier semaphores. Data moves between devices by JAX's collectives and lax.ppermute only.
A program may use at most 128 MiB of HBM per device.

v0:
```python
import jax
import jax.numpy as jnp
from jax import lax
from jax.sharding import PartitionSpec as P

GROUPS = 16
KERNEL = 9


def with_halo(cells, sides, width):
    for axis, dim in sides:
        count = lax.axis_size(axis)
        ends = count - 1
        head = lax.slice_in_dim(cells, 0, width, axis=dim)
        tail = lax.slice_in_dim(cells, cells.shape[dim] - width, cells.shape[dim], axis=dim)
        cells = jnp.concatenate(
            [
                lax.ppermute(tail, axis, [(i, (i + 1) % count) for i in range(ends)]),
                cells,
                lax.ppermute(head, axis, [((i + 1) % count, i) for i in range(ends)]),
            ],
            axis=dim,
        )
    return cells


def from_partner(value, axis, apart):
    mask = 2**apart
    pairs = [(source, source ^ mask) for source in range(lax.axis_size(axis))]
    return lax.ppermute(value, axis, pairs)


def body(events, type_ids, type_table, norm_gain, kernel, upstream):
    length = events.shape[1]
    width = events.shape[2]
    chans = width // GROUPS
    half = KERNEL // 2
    seq_count = lax.axis_size("seq")
    total = length * seq_count * lax.axis_size("fsdp")
    scale = 1.0 / jnp.sqrt(jnp.float32(total))
    table = lax.all_gather(type_table, "fsdp", axis=0, tiled=True)
    onehot = (type_ids[0][:, None] == jnp.arange(table.shape[0], dtype=jnp.int32)[None, :]).astype(
        jnp.bfloat16
    )
    mixed = events[0].astype(jnp.float32) + jnp.dot(
        onehot, table, preferred_element_type=jnp.float32
    )
    inv = lax.rsqrt(jnp.mean(mixed * mixed, axis=-1, keepdims=True) + 1e-06)
    normed = (mixed * inv * norm_gain).astype(jnp.bfloat16)
    padded = with_halo(normed, (("seq", 0),), half)
    padded = padded.reshape(length + 2 * half, GROUPS, chans)
    weights = lax.all_gather(kernel, "fsdp", axis=0, tiled=True).reshape(
        GROUPS, chans, KERNEL, chans
    )
    conv = jnp.zeros((length, GROUPS, chans), jnp.float32)
    for k in range(KERNEL):
        conv = conv + jnp.einsum(
            "tgc,goc->tgo",
            padded[k : k + length],
            weights[:, :, k, :],
            preferred_element_type=jnp.float32,
        )
    up_float = upstream[0].astype(jnp.float32)
    sig = jax.nn.sigmoid(conv)
    dconv = (up_float.reshape(length, GROUPS, chans) * sig * (1.0 + conv * (1.0 - sig))).astype(
        jnp.bfloat16
    )
    dflat = dconv.reshape(length, width)
    dpad = with_halo(dflat, (("seq", 0),), half)
    dpad = dpad.reshape(length + 2 * half, GROUPS, chans)
    dnormed = jnp.zeros((length, GROUPS, chans), jnp.float32)
    for k in range(KERNEL):
        dnormed = dnormed + jnp.einsum(
            "tgo,goc->tgc",
            dpad[2 * half - k : 2 * half - k + length],
            weights[:, :, k, :],
            preferred_element_type=jnp.float32,
        )
    slice_width = width // seq_count
    normed_slice, dconv_slice = (
        lax.all_to_all(normed, "seq", split_axis=1, concat_axis=0, tiled=True),
        lax.all_to_all(dflat, "seq", split_axis=1, concat_axis=0, tiled=True),
    )
    whole = normed_slice.shape[0]
    if slice_width < chans:
        spread = chans // slice_width
        position = lax.axis_index("seq")
        group_rows = normed_slice
        for bit in range(spread.bit_length() - 1):
            partner = from_partner(group_rows, "seq", bit)
            lower = position >> bit & 1 == 0
            group_rows = jnp.where(
                lower,
                jnp.concatenate([group_rows, partner], axis=1),
                jnp.concatenate([partner, group_rows], axis=1),
            )
        group_in = group_rows.reshape(whole, 1, chans)
        group_out = dconv_slice.reshape(whole, 1, slice_width)
    else:
        local_groups = slice_width // chans
        group_in = normed_slice.reshape(whole, local_groups, chans)
        group_out = dconv_slice.reshape(whole, local_groups, chans)
    group_pad = jnp.pad(group_in, ((half, half), (0, 0), (0, 0)))
    kterms = []
    for k in range(KERNEL):
        kterms.append(
            jnp.einsum(
                "tgo,tgc->goc",
                group_out,
                group_pad[k : k + whole],
                preferred_element_type=jnp.float32,
            )
        )
    kernel_part = jnp.stack(kterms, axis=2).reshape(slice_width, KERNEL * chans) * scale
    kernel_grad = lax.psum(kernel_part, "fsdp")
    dnormed = dnormed.reshape(length, width)
    gain_term = jnp.sum(dnormed * mixed * inv, axis=0) * scale
    scaled = norm_gain * dnormed
    dmixed = inv * scaled - mixed * inv * inv * inv * jnp.mean(
        scaled * mixed, axis=-1, keepdims=True
    )
    input_grad = (up_float + dmixed).astype(jnp.bfloat16)
    table_term = (
        lax.dot_general(
            onehot, input_grad, (((0,), (0,)), ((), ())), preferred_element_type=jnp.float32
        )
        * scale
    )
    table_grad, gain_grad = (
        lax.psum_scatter(table_term, ("fsdp", "seq"), scatter_dimension=0, tiled=True),
        lax.psum_scatter(gain_term, ("fsdp", "seq"), scatter_dimension=0, tiled=True),
    )
    return (input_grad[None], table_grad, gain_grad, kernel_grad)


def solution(mesh):
    return jax.shard_map(
        body,
        mesh=mesh,
        in_specs=(
            P("fsdp", "seq", None),
            P("fsdp", "seq"),
            P("fsdp", None),
            P(),
            P("fsdp", None),
            P("fsdp", "seq", None),
        ),
        out_specs=(
            P("fsdp", "seq", None),
            P(("fsdp", "seq"), None),
            P(("fsdp", "seq")),
            P("seq", None),
        ),
        check_vma=False,
    )
```

profile of v0, /device:TPU:0, one launch (start us, length us, event | category | flops | bytes accessed | tf_op | source)
XLA Modules:
  0.0 384.2 jit_solution(598750002941307094)
XLA Ops:
  7.2 0.7 all-gather.3.cloned.1.call-update
  8.0 0.7 all-gather.5.cloned.1.call-update
  8.7 30.6 %all-gather.3.cloned.1.call-done = bf16[256,2048]{1,0:T(8,128)(2,1)} async-done(((bf16[64,2048]{1,0:T(8,128)(2,1)}), bf16[256,2048]{1,0:T(8,128)(2,1)}) %all-gather.3.cloned.1.call-update) | async-done | bytes 1048592 | tf_op jit(solution)/shard_map/all_gather | solution.py:41
  39.2 1.7 multiply_reduce_fusion.2
  41.1 1.0 copy.192
  42.1 4.6 %all-to-all-start.1 = ((bf16[128,8,256]{0,2,1:T(8,128)(2,1)}), bf16[128,8,256]{0,2,1:T(8,128)(2,1)S(1)}, u32[]{:S(2)}, u32[]{:S(2)}) async-start(bf16[128,8,256]{0,2,1:T(8,128)(2,1)} %bitcast.30), calls=%async_computation.2 | async-start | bytes 1048576 | tf_op jit(solution)/shard_map/all_to_all | solution.py:81
  46.7 2.4 collective-permute-start
  49.1 1.3 collective-permute-start.1
  50.6 1.2 copy.213
  51.7 1.6 collective-permute-done.1
  53.4 2.7 fusion.52
  56.0 6.0 %all-to-all-done.1 = bf16[128,8,256]{0,2,1:T(8,128)(2,1)S(1)} async-done(((bf16[128,8,256]{0,2,1:T(8,128)(2,1)}), bf16[128,8,256]{0,2,1:T(8,128)(2,1)S(1)}, u32[]{:S(2)}, u32[]{:S(2)}) %all-to-all-start.1) | async-done | bytes 524320 | tf_op jit(solution)/shard_map/all_to_all | solution.py:81
  62.6 1.0 copy.169
  63.7 34.5 %all-gather.5.cloned.1.call-done = bf16[2048,1152]{1,0:T(8,128)(2,1)} async-done(((bf16[512,1152]{1,0:T(8,128)(2,1)}), bf16[2048,1152]{1,0:T(8,128)(2,1)}) %all-gather.5.cloned.1.call-update) | async-done | bytes 4718608 | tf_op jit(solution)/shard_map/all_gather | solution.py:52
  98.2 10.5 %reshape.88 = bf16[16,128,9,128]{3,2,1,0:T(8,128)(2,1)} reshape(bf16[2048,1152]{1,0:T(8,128)(2,1)} %all-gather.5.cloned.1.call-done) | data formatting | bytes 9437184 | tf_op jit(solution)/shard_map/reshape | solution.py:52
  108.6 19.8 %fusion.82 = (bf16[16,128,1,128]{3,2,1,0:T(2,128)(2,1)S(1)}, bf16[16,128,1,128]{3,2,1,0:T(2,128)(2,1)S(1)}, bf16[16,128,1,128]{3,2,1,0:T(2,128)(2,1)S(1)}, bf16[...) fusion(bf16[16,128,9,128]{3,2,1,0:T(8,128)(2,1)} %reshape.88), kind=kLoop, calls=%fused_computation.154 | loop fusion | bytes 9437184 | tf_op jit(solution)/shard_map/slice | solution.py:60
  128.5 0.5 fusion.49
  129.0 0.9 copy-done.22
  129.9 0.5 convolution_add_fusion.15
  130.5 0.9 copy-done.21
  131.3 0.5 convolution_add_fusion.14
  131.8 0.7 copy-done.20
  132.5 0.5 convolution_add_fusion.13
  133.0 0.5 convolution_add_fusion.12
  133.6 0.5 copy-done.19
  134.1 0.5 convolution_add_fusion.11
  134.6 0.5 copy-done.18
  135.1 0.5 convolution_add_fusion.10
  135.6 0.5 convolution_add_fusion.9
  136.1 0.7 copy-done.25
  137.0 0.8 fusion.14
  137.9 1.1 copy.145
  138.9 1.3 collective-permute-start.2
  140.2 1.1 copy.155
  141.3 3.8 collective-permute-start.3
  145.1 2.7 fusion.63
  147.8 1.0 copy.144
  148.8 4.7 %all-to-all-start = ((bf16[128,8,256]{0,2,1:T(8,128)(2,1)}), bf16[128,8,256]{0,2,1:T(8,128)(2,1)S(1)}, u32[]{:S(2)}, u32[]{:S(2)}) async-start(bf16[128,8,256]{0,2,1:T(8,128)(2,1)} %bitcast.28), calls=%async_computation.1 | async-start | bytes 1048576 | tf_op jit(solution)/shard_map/all_to_all | solution.py:82
  153.7 6.9 %pad_maximum_fusion = (bf16[128,2048]{0,1:T(8,128)(2,1)S(1)}, bf16[128,2048]{0,1:T(8,128)(2,1)S(1)}, bf16[128,2048]{0,1:T(8,128)(2,1)S(1)}, bf16[128,2048]{0,1:T...) fusion(bf16[128,2048]{0,1:T(8,128)(2,1)} %bitcast.13, ...), kind=kLoop, calls=%fused_computation.105 | loop fusion | flops 8388608 | bytes 4751360 | tf_op jit(solution)/shard_map/concatenate | solution.py:16
  161.0 0.8 copy-done.7
  161.8 0.4 convolution_add_fusion.7
  162.2 0.9 copy-done.5
  163.1 0.4 convolution_add_fusion.6
  163.4 0.9 copy-done.12
  165.0 0.9 copy-done.3
  165.8 0.4 convolution_add_fusion.4
  166.2 0.9 copy-done.1
  167.4 0.4 convolution_add_fusion.2
  167.8 0.8 copy-done.15
  168.6 1.3 convolution_add_fusion.1
  170.0 1.6 copy.191
  171.5 1.1 copy.166
  172.7 1.3 reshape.83
  174.0 1.4 fusion.10
  178.0 1.9 copy.171
  180.0 2.4 copy.284
  182.7 0.7 copy-done.17
  183.4 0.4 fusion.12
  183.8 1.9 convolution_multiply_fusion
  185.7 39.9 %all-reduce.1 = f32[2048]{0:T(1024)S(1)} all-reduce(f32[2048]{0:T(1024)S(1)} %broadcast_multiply_fusion.1), channel_id=3, replica_groups=mesh['fsdp'=4,'seq'=8] {'fsdp','seq'}, use_global_device_ids=true, to_apply=%region_4.5.clone | all-reduce | flops 2048 | bytes 16384
  225.6 0.6 dynamic-slice
  226.2 11.7 %all-reduce.4.cloned.1.call-done = f32[256,1152]{0,1:T(8,128)} async-done(((f32[256,1152]{0,1:T(8,128)}), f32[256,1152]{0,1:T(8,128)}) %all-reduce.4.cloned.1.call-update) | async-done | bytes 1179664 | tf_op jit(solution)/shard_map/psum | solution.py:115
  237.9 2.7 copy.172
  240.6 137.1 %reduce-scatter.2.cloned.1.call-done = f32[8,2048]{1,0:T(8,128)} async-done(((f32[256,2048]{1,0:T(8,128)}), f32[8,2048]{1,0:T(8,128)}) %reduce-scatter.2.cloned.1.call-update) | async-done | bytes 65552 | tf_op jit(solution)/shard_map/reduce_scatter | solution.py:130
  (81 shorter events, 5.7 us)
Async XLA Ops:
  7.2 32.1 %copy-start.30 = (s32[1,128]{1,0:T(1,128)S(1)}, s32[1,128]{1,0:T(1,128)}, u32[]{:S(2)}) copy-start(s32[1,128]{1,0:T(1,128)} %param.7) | copy-start | bytes 1540
  7.2 32.1 %copy-start.26 = (bf16[1,128,2048]{2,1,0:T(8,128)(2,1)S(1)}, bf16[1,128,2048]{2,1,0:T(8,128)(2,1)}, u32[]{:S(2)}) copy-start(bf16[1,128,2048]{2,1,0:T(8,128)(2,1)} %param.6) | copy-start | bytes 1572868
  7.2 32.0 %all-gather.3.cloned.1.call-start = ((), (), s32[]{:S(2)}) async-start(), calls=%async_computation.3 | async-start | bytes 1310720 | tf_op jit(solution)/shard_map/all_gather | solution.py:41
  7.9 90.2 %all-gather.5.cloned.1.call-start = ((), (), s32[]{:S(2)}) async-start(), calls=%async_computation.4 | async-start | bytes 5898240 | tf_op jit(solution)/shard_map/all_gather | solution.py:52
  39.2 1.7 copy-start.29
  41.1 9.4 %copy-start.16 = (bf16[1,128,2048]{2,1,0:T(8,128)(2,1)S(1)}, bf16[1,128,2048]{2,1,0:T(8,128)(2,1)}, u32[]{:S(2)}) copy-start(bf16[1,128,2048]{2,1,0:T(8,128)(2,1)} %param.11) | copy-start | bytes 1572868
  42.1 20.0 %all-to-all-start.1 = ((bf16[128,8,256]{0,2,1:T(8,128)(2,1)}), bf16[128,8,256]{0,2,1:T(8,128)(2,1)S(1)}, u32[]{:S(2)}, u32[]{:S(2)}) async-start(bf16[128,8,256]{0,2,1:T(8,128)(2,1)} %bitcast.30), calls=%async_computation.2 | async-start | bytes 1048576 | tf_op jit(solution)/shard_map/all_to_all | solution.py:81
  46.7 5.0 %collective-permute-start = (bf16[4,2048]{1,0:T(4,128)(2,1)S(1)}, bf16[4,2048]{1,0:T(4,128)(2,1)S(1)}, u32[]{:S(2)}, u32[]{:S(2)}) collective-permute-start(bf16[4,2048]{1,0:T(4,128)(2,1)S(1)} %get-tuple-element.54), channel_id=1, source_target_pairs={{0,1},{1,2},{2,3},{3,4},{4,5},{5,6},{6,7},{8,9},{9,10},{10,11},{11... | collective-permute-start | bytes 49160 | tf_op jit(solution)/shard_map/ppermute | solution.py:18
  49.1 4.2 %collective-permute-start.1 = (bf16[4,2048]{1,0:T(4,128)(2,1)S(1)}, bf16[4,2048]{1,0:T(4,128)(2,1)S(1)}, u32[]{:S(2)}, u32[]{:S(2)}) collective-permute-start(bf16[4,2048]{1,0:T(4,128)(2,1)S(1)} %get-tuple-element.53), channel_id=1, source_target_pairs={{1,0},{2,1},{3,2},{4,3},{5,4},{6,5},{7,6},{9,8},{10,9},{11,10},{12... | collective-permute-start | bytes 49160 | tf_op jit(solution)/shard_map/ppermute | solution.py:20
  108.6 19.9 %copy-start.23 = (bf16[16,16,8,128]{3,2,1,0:T(8,128)(2,1)S(1)}, bf16[16,16,8,128]{3,2,1,0:T(8,128)(2,1)}, u32[]{:S(2)}) copy-start(bf16[16,16,8,128]{3,2,1,0:T(8,128)(2,1)} %get-tuple-element.51) | copy-start | bytes 1572868
  128.4 2.0 copy-start.6
  128.4 2.0 copy-start.8
  128.5 2.0 copy-start.4
  128.5 3.4 copy-start.11
  128.5 4.6 %copy-start.10 = (bf16[16,128,1,128]{3,2,1,0:T(2,128)(2,1)}, bf16[16,128,1,128]{3,2,1,0:T(2,128)(2,1)S(1)}, u32[]{:S(2)}) copy-start(bf16[16,128,1,128]{3,2,1,0:T(2,128)(2,1)S(1)} %get-tuple-element.22) | copy-start | bytes 1572868
  128.5 5.1 %copy-start.2 = (bf16[16,128,1,128]{3,2,1,0:T(2,128)(2,1)}, bf16[16,128,1,128]{3,2,1,0:T(2,128)(2,1)S(1)}, u32[]{:S(2)}) copy-start(bf16[16,128,1,128]{3,2,1,0:T(2,128)(2,1)S(1)} %get-tuple-element.21) | copy-start | bytes 1572868
  128.5 6.1 %copy-start = (bf16[16,128,1,128]{3,2,1,0:T(2,128)(2,1)}, bf16[16,128,1,128]{3,2,1,0:T(2,128)(2,1)S(1)}, u32[]{:S(2)}) copy-start(bf16[16,128,1,128]{3,2,1,0:T(2,128)(2,1)S(1)} %get-tuple-element.20) | copy-start | bytes 1572868
  128.5 7.6 %copy-start.14 = (bf16[16,128,1,128]{3,2,1,0:T(2,128)(2,1)}, bf16[16,128,1,128]{3,2,1,0:T(2,128)(2,1)S(1)}, u32[]{:S(2)}) copy-start(bf16[16,128,1,128]{3,2,1,0:T(2,128)(2,1)S(1)} %get-tuple-element.18) | copy-start | bytes 1572868
  128.5 1.4 copy-start.22
  129.9 1.4 copy-start.21
  131.3 1.2 copy-start.20
  133.0 1.0 copy-start.19
  134.1 1.0 copy-start.18
  135.6 1.2 copy-start.25
  135.6 1.3 copy-start.27
  138.9 14.8 %collective-permute-start.2 = (bf16[4,2048]{0,1:T(8,128)(2,1)}, bf16[4,2048]{0,1:T(8,128)(2,1)}, u32[]{:S(2)}, u32[]{:S(2)}) collective-permute-start(bf16[4,2048]{0,1:T(8,128)(2,1)} %copy.145), channel_id=1, source_target_pairs={{1,0},{2,1},{3,2},{4,3},{5,4},{6,5},{7,6},{9,8},{10,9},{11,10},{12... | collective-permute-start | bytes 49160 | tf_op jit(solution)/shard_map/ppermute | solution.py:20
  141.3 12.4 %collective-permute-start.3 = (bf16[4,2048]{0,1:T(8,128)(2,1)}, bf16[4,2048]{0,1:T(8,128)(2,1)}, u32[]{:S(2)}, u32[]{:S(2)}) collective-permute-start(bf16[4,2048]{0,1:T(8,128)(2,1)} %copy.155), channel_id=1, source_target_pairs={{0,1},{1,2},{2,3},{3,4},{4,5},{5,6},{6,7},{8,9},{9,10},{10,11},{11... | collective-permute-start | bytes 49160 | tf_op jit(solution)/shard_map/ppermute | solution.py:18
  148.8 22.7 %all-to-all-start = ((bf16[128,8,256]{0,2,1:T(8,128)(2,1)}), bf16[128,8,256]{0,2,1:T(8,128)(2,1)S(1)}, u32[]{:S(2)}, u32[]{:S(2)}) async-start(bf16[128,8,256]{0,2,1:T(8,128)(2,1)} %bitcast.28), calls=%async_computation.1 | async-start | bytes 1048576 | tf_op jit(solution)/shard_map/all_to_all | solution.py:82
  153.5 84.4 %all-reduce.4.cloned.1.call-start = ((), (), s32[]{:S(2)}) async-start(), calls=%async_computation.6 | async-start | bytes 2359296 | tf_op jit(solution)/shard_map/psum | solution.py:115
  153.7 6.9 %copy-start.9 = (bf16[16,128,1,128]{3,2,1,0:T(2,128)(2,1)S(1)}, bf16[16,128,1,128]{3,2,1,0:T(2,128)(2,1)}, u32[]{:S(2)}) copy-start(bf16[16,128,1,128]{3,2,1,0:T(2,128)(2,1)} %copy-done.8) | copy-start | bytes 1572868
  160.6 1.2 copy-start.7
  161.8 1.2 copy-start.5
  163.1 1.2 copy-start.12
  163.1 1.5 copy-start.13
  164.6 1.2 copy-start.3
  165.8 1.2 copy-start.1
  167.4 1.2 copy-start.15
  173.9 1.4 copy-start.28
  182.3 1.0 copy-start.17
  182.4 195.3 %reduce-scatter.2.cloned.1.call-start = ((), (), s32[]{:S(2)}) async-start(), calls=%async_computation.5 | async-start | bytes 2162688 | tf_op jit(solution)/shard_map/reduce_scatter | solution.py:130
  183.8 1.9 copy-start.24
Sparse Core Ops, SparseCore 0:
  9.9 29.3 all-gather.2
  41.1 57.0 all-gather.4
  182.5 55.3 all-reduce.3
  240.7 136.9 reduce-scatter.1
where the time goes:
time: 386 us; the launch traced here: 384 us
  waiting for transfers between devices  223 us (58%)
  local copies, waits for them, and re-layouts  59.2 us (15%)
  blocking collectives  39.9 us (10%)
  matrix products  18.8 us (5%)
  starting transfers between devices  18.4 us (5%)
  between operations  14.4 us (4%)
  other arithmetic  10.6 us (3%)
    reduce_scatter x1, waiting for transfers between devices, body(): lax.psum_scatter(table_term, ('fsdp', 'seq'), scatter_dimension=0, tiled=...  137 us
    unnamed x1, blocking collectives  39.9 us
    all_gather x1, waiting for transfers between devices, body(): lax.all_gather(kernel, 'fsdp', axis=0, tiled=True)  34.5 us
    all_gather x1, waiting for transfers between devices, body(): table = lax.all_gather(type_table, 'fsdp', axis=0, tiled=True)  30.6 us
    slice x1, local copies, waits for them, and re-layouts, body(): weights[:, :, k, :]  19.8 us
    unnamed x66, local copies, waits for them, and re-layouts  17.4 us
    psum x1, waiting for transfers between devices, body(): kernel_grad = lax.psum(kernel_part, 'fsdp')  11.7 us
    reshape x1, local copies, waits for them, and re-layouts, body(): lax.all_gather(kernel, 'fsdp', axis=0, tiled=True)  10.5 us
  transfers between devices with their start and end apart: 10, of which 6 were waited for; matrix products, arithmetic and copies ran while one was open for 8% of the time, Pallas kernels for 0%

commit v1 on v0

--- a/solution.py
+++ b/solution.py
@@ -30,6 +30,37 @@
     return lax.ppermute(value, axis, pairs)
 
 
+def gather_rows(block, axis):
+    count = lax.axis_size(axis)
+    return lax.all_to_all(jnp.tile(block, (count, 1)), axis, 0, 0, tiled=True)
+
+
+def sum_rows(block, axis):
+    count = lax.axis_size(axis)
+    parts = block.reshape(count, block.shape[0] // count, *block.shape[1:])
+    return lax.all_to_all(parts, axis, 0, 0, tiled=True).sum(axis=0)
+
+
+def psum_rows(block, axis):
+    return gather_rows(sum_rows(block, axis), axis)
+
+
+def scatter_terms(table_term, gain_term):
+    fsdp = lax.axis_size("fsdp")
+    seq = lax.axis_size("seq")
+    types, width = table_term.shape
+    wide = width // fsdp
+    gain_rows = jnp.zeros((fsdp, 1, width), jnp.float32).at[:, 0, :wide].set(gain_term.reshape(fsdp, wide))
+    first = jnp.concatenate([table_term.reshape(fsdp, types // fsdp, width), gain_rows], axis=1)
+    first = lax.all_to_all(first, "fsdp", 0, 0, tiled=True).sum(axis=0)
+    rows = types // fsdp
+    narrow = wide // seq
+    gain_rows = jnp.zeros((seq, 1, width), jnp.float32).at[:, 0, :narrow].set(first[rows, :wide].reshape(seq, narrow))
+    second = jnp.concatenate([first[:rows].reshape(seq, rows // seq, width), gain_rows], axis=1)
+    second = lax.all_to_all(second, "seq", 0, 0, tiled=True).sum(axis=0)
+    return second[: rows // seq], second[rows // seq, :narrow]
+
+
 def body(events, type_ids, type_table, norm_gain, kernel, upstream):
     length = events.shape[1]
     width = events.shape[2]
@@ -38,7 +69,7 @@
     seq_count = lax.axis_size("seq")
     total = length * seq_count * lax.axis_size("fsdp")
     scale = 1.0 / jnp.sqrt(jnp.float32(total))
-    table = lax.all_gather(type_table, "fsdp", axis=0, tiled=True)
+    table = gather_rows(type_table, "fsdp")
     onehot = (type_ids[0][:, None] == jnp.arange(table.shape[0], dtype=jnp.int32)[None, :]).astype(
         jnp.bfloat16
     )
@@ -112,7 +143,7 @@
             )
         )
     kernel_part = jnp.stack(kterms, axis=2).reshape(slice_width, KERNEL * chans) * scale
-    kernel_grad = lax.psum(kernel_part, "fsdp")
+    kernel_grad = psum_rows(kernel_part, "fsdp")
     dnormed = dnormed.reshape(length, width)
     gain_term = jnp.sum(dnormed * mixed * inv, axis=0) * scale
     scaled = norm_gain * dnormed
@@ -126,10 +157,7 @@
         )
         * scale
     )
-    table_grad, gain_grad = (
-        lax.psum_scatter(table_term, ("fsdp", "seq"), scatter_dimension=0, tiled=True),
-        lax.psum_scatter(gain_term, ("fsdp", "seq"), scatter_dimension=0, tiled=True),
-    )
+    table_grad, gain_grad = scatter_terms(table_term, gain_term)
     return (input_grad[None], table_grad, gain_grad, kernel_grad)
 
 

time: 386 us -> 259 us (0.67)
  waiting for transfers between devices: 223 us -> 96.4 us
  blocking collectives: 39.9 us -> 23.8 us
  starting transfers between devices: 18.4 us -> 34.4 us
  other arithmetic: 10.6 us -> 14.6 us
    reduce_scatter x1 -> x0, waiting for transfers between devices: 137 us -> none  [body(): lax.psum_scatter(table_term, ('fsdp', 'seq'), scatter_dimension=0, tiled=...]
    all_to_all x0 -> x4, waiting for transfers between devices: none -> 70.8 us  [the longest x1 25.2 us: scatter_terms(): second = lax.all_to_all(second, 'seq', 0, 0, tiled=True).sum(axis=0)]
    unnamed x1 -> x0, blocking collectives: 39.9 us -> none
    all_gather x1 -> x0, waiting for transfers between devices: 30.6 us -> none  [body(): table = lax.all_gather(type_table, 'fsdp', axis=0, tiled=True)]
    all_to_all x0 -> x1, blocking collectives: none -> 23.8 us  [gather_rows(): return lax.all_to_all(jnp.tile(block, (count, 1)), axis, 0, 0, tiled=True)]
    all_gather x1, waiting for transfers between devices: 34.5 us -> 17.2 us  [body(): lax.all_gather(kernel, 'fsdp', axis=0, tiled=True)]
    all_to_all x0 -> x4, starting transfers between devices: none -> 15.8 us  [the longest x1 4.35 us: scatter_terms(): second = lax.all_to_all(second, 'seq', 0, 0, tiled=True).sum(axis=0)]
    psum x1 -> x0, waiting for transfers between devices: 11.7 us -> none  [body(): kernel_grad = lax.psum(kernel_part, 'fsdp')]
  transfers between devices with their start and end apart: 10 -> 11, of which waited for: 6 -> 7; matrix products, arithmetic and copies ran while one was open for 8% -> 15% of each run, Pallas kernels for 0% -> 0%
where the time goes in v1:
time: 259 us; the launch traced here: 257 us
  waiting for transfers between devices  96.4 us (37%)
  local copies, waits for them, and re-layouts  58.1 us (22%)
  starting transfers between devices  34.4 us (13%)
  blocking collectives  23.8 us (9%)
  matrix products  15.2 us (6%)
  between operations  14.7 us (6%)
  other arithmetic  14.6 us (6%)
    all_to_all x1, waiting for transfers between devices, scatter_terms(): second = lax.all_to_all(second, 'seq', 0, 0, tiled=True).sum(axis=0)  25.2 us
    all_to_all x1, blocking collectives, gather_rows(): return lax.all_to_all(jnp.tile(block, (count, 1)), axis, 0, 0, tiled=True)  23.8 us
    slice x1, local copies, waits for them, and re-layouts, body(): weights[:, :, k, :]  19.7 us
    all_to_all x1, waiting for transfers between devices, scatter_terms(): first = lax.all_to_all(first, 'fsdp', 0, 0, tiled=True).sum(axis=0)  17.9 us
    all_gather x1, waiting for transfers between devices, body(): lax.all_gather(kernel, 'fsdp', axis=0, tiled=True)  17.2 us
    unnamed x70, local copies, waits for them, and re-layouts  13.9 us
    all_to_all x1, waiting for transfers between devices, gather_rows(): return lax.all_to_all(jnp.tile(block, (count, 1)), axis, 0, 0, tiled=True)  13.9 us
    all_to_all x1, waiting for transfers between devices, sum_rows(): return lax.all_to_all(parts, axis, 0, 0, tiled=True).sum(axis=0)  13.9 us
  transfers between devices with their start and end apart: 11, of which 7 were waited for; matrix products, arithmetic and copies ran while one was open for 15% of the time, Pallas kernels for 0%

profile of v1, /device:TPU:0, one launch (start us, length us, event | category | flops | bytes accessed | tf_op | source)
XLA Modules:
  0.0 257.1 jit_solution(17122217566961818963)
XLA Ops:
  7.2 0.7 all-gather.2.cloned.1.call-update
  8.3 23.8 %all_to_all.65 = bf16[4,64,2048]{2,1,0:T(8,128)(2,1)S(1)} all-to-all(bf16[4,64,2048]{2,1,0:T(8,128)(2,1)S(1)} %tile.4), channel_id=1, replica_groups=mesh['fsdp'=4,'seq'=8] {'fsdp'}, dimensions={0} | all-to-all | bytes 2097152 | tf_op jit(solution)/shard_map/all_to_all | solution.py:35
  32.0 0.4 multiply_reduce_fusion.2
  32.9 1.0 copy.290
  33.9 5.2 %all-to-all-start.4 = ((bf16[128,8,256]{0,2,1:T(8,128)(2,1)}), bf16[128,8,256]{0,2,1:T(8,128)(2,1)S(1)}, u32[]{:S(2)}, u32[]{:S(2)}) async-start(bf16[128,8,256]{0,2,1:T(8,128)(2,1)} %bitcast.35), calls=%async_computation.4 | async-start | bytes 1048576 | tf_op jit(solution)/shard_map/all_to_all | solution.py:112
  39.1 2.4 collective-permute-start
  41.5 1.3 collective-permute-start.1
  42.9 1.2 copy.314
  44.0 1.6 collective-permute-done.1
  45.7 2.7 %fusion.52 = (bf16[16,16,8,128]{3,2,1,0:T(8,128)(2,1)}, bf16[16,16,8,128]{3,2,1,0:T(8,128)(2,1)}, bf16[16,16,8,128]{3,2,1,0:T(8,128)(2,1)}, bf16[16,16,8,128]{3,...) fusion(bf16[4,2048]{1,0:T(4,128)(2,1)S(1)} %collective-permute-, ...), kind=kLoop, calls=%fused_computation.112 | loop fusion | flops 8388608 | bytes 4751360
  48.3 6.1 %all-to-all-done.4 = bf16[128,8,256]{0,2,1:T(8,128)(2,1)S(1)} async-done(((bf16[128,8,256]{0,2,1:T(8,128)(2,1)}), bf16[128,8,256]{0,2,1:T(8,128)(2,1)S(1)}, u32[]{:S(2)}, u32[]{:S(2)}) %all-to-all-start.4) | async-done | bytes 524320 | tf_op jit(solution)/shard_map/all_to_all | solution.py:112
  55.0 1.0 copy.268
  56.0 17.2 %all-gather.2.cloned.1.call-done = bf16[2048,1152]{1,0:T(8,128)(2,1)} async-done(((bf16[512,1152]{1,0:T(8,128)(2,1)}), bf16[2048,1152]{1,0:T(8,128)(2,1)}) %all-gather.2.cloned.1.call-update) | async-done | bytes 4718608 | tf_op jit(solution)/shard_map/all_gather | solution.py:83
  73.1 10.5 %reshape.199 = bf16[16,128,9,128]{3,2,1,0:T(8,128)(2,1)} reshape(bf16[2048,1152]{1,0:T(8,128)(2,1)} %all-gather.2.cloned.1.call-done) | data formatting | bytes 9437184 | tf_op jit(solution)/shard_map/reshape | solution.py:83
  83.6 19.7 %fusion.82 = (bf16[16,128,1,128]{3,2,1,0:T(2,128)(2,1)S(1)}, bf16[16,128,1,128]{3,2,1,0:T(2,128)(2,1)S(1)}, bf16[16,128,1,128]{3,2,1,0:T(2,128)(2,1)S(1)}, bf16[...) fusion(bf16[16,128,9,128]{3,2,1,0:T(8,128)(2,1)} %reshape.199), kind=kLoop, calls=%fused_computation.160 | loop fusion | bytes 9437184 | tf_op jit(solution)/shard_map/slice | solution.py:91
  103.5 0.5 fusion.49
  103.9 0.9 copy-done.24
  104.9 0.5 convolution_add_fusion.15
  105.4 0.9 copy-done.23
  106.3 0.5 convolution_add_fusion.14
  106.8 0.7 copy-done.22
  107.5 0.5 convolution_add_fusion.13
  108.0 0.5 convolution_add_fusion.12
  108.5 0.5 copy-done.21
  109.0 0.5 convolution_add_fusion.11
  109.5 0.5 copy-done.20
  110.1 0.5 convolution_add_fusion.10
  110.6 0.5 convolution_add_fusion.9
  111.1 0.7 copy-done.27
  111.9 0.8 fusion.14
  113.1 1.3 collective-permute-start.2
  114.4 1.1 copy.253
  115.5 3.9 %collective-permute-start.3 = (bf16[4,2048]{0,1:T(8,128)(2,1)}, bf16[4,2048]{0,1:T(8,128)(2,1)}, u32[]{:S(2)}, u32[]{:S(2)}) collective-permute-start(bf16[4,2048]{0,1:T(8,128)(2,1)} %copy.253), channel_id=1, source_target_pairs={{0,1},{1,2},{2,3},{3,4},{4,5},{5,6},{6,7},{8,9},{9,10},{10,11},{11... | collective-permute-start | bytes 49160 | tf_op jit(solution)/shard_map/ppermute | solution.py:18
  119.3 2.7 %fusion.63 = f32[16,128,128]{1,2,0:T(8,128)} fusion(bf16[128,16,128]{2,0,1:T(8,128)(2,1)S(1)} %fusion.14, bf16[16,128,1,128]{3,2,1,0:T(2,128)(2,1)} %copy-done.12), kind=kOutput, calls=%fused_computation.133 | convolution fusion | flops 67108864 | bytes 2097152 | tf_op jit(solution)/shard_map/tgo,goc->tgc/dot_general | solution.py:104
  122.0 1.1 copy.242
  123.1 4.6 %all-to-all-start.3 = ((bf16[128,8,256]{0,2,1:T(8,128)(2,1)}), bf16[128,8,256]{0,2,1:T(8,128)(2,1)}, u32[]{:S(2)}, u32[]{:S(2)}) async-start(bf16[128,8,256]{0,2,1:T(8,128)(2,1)} %bitcast.33), calls=%async_computation.3 | async-start | bytes 1048576 | tf_op jit(solution)/shard_map/all_to_all | solution.py:113
  127.7 6.5 %pad_maximum_fusion = (bf16[128,2048]{0,1:T(8,128)(2,1)S(1)}, bf16[128,2048]{0,1:T(8,128)(2,1)S(1)}, bf16[128,2048]{0,1:T(8,128)(2,1)S(1)}, bf16[128,2048]{0,1:T...) fusion(bf16[128,2048]{0,1:T(8,128)(2,1)} %bitcast.14, ...), kind=kLoop, calls=%fused_computation.109 | loop fusion | flops 8388608 | bytes 4751360 | tf_op jit(solution)/shard_map/concatenate | solution.py:16
  134.6 0.8 copy-done.9
  135.8 0.9 copy-done.7
  137.0 0.9 copy-done.14
  138.5 0.9 copy-done.5
  139.8 0.9 copy-done.3
  141.4 0.9 copy-done.17
  143.2 0.7 copy-done.19
  144.4 0.5 convolution_multiply_fusion
  145.2 1.7 select_maximum_fusion
  146.8 3.6 %all-to-all-start.1 = ((f32[4,65,2048]{2,1,0:T(8,128)}), f32[4,65,2048]{2,1,0:T(8,128)S(1)}, u32[]{:S(2)}, u32[]{:S(2)}) async-start(f32[4,65,2048]{2,1,0:T(8,128)} %select_maximum_fusion), calls=%async_computation.1 | async-start | bytes 4718592 | tf_op jit(solution)/shard_map/all_to_all | solution.py:55
  150.5 1.4 copy.265
  152.1 1.4 fusion.10
  156.6 2.1 copy.270
  158.7 2.5 mul.133
  161.2 17.9 %all-to-all-done.1 = f32[4,65,2048]{2,1,0:T(8,128)S(1)} async-done(((f32[4,65,2048]{2,1,0:T(8,128)}), f32[4,65,2048]{2,1,0:T(8,128)S(1)}, u32[]{:S(2)}, u32[]{:S(2)}) %all-to-all-start.1) | async-done | bytes 2129952 | tf_op jit(solution)/shard_map/all_to_all | solution.py:55
  179.1 4.3 %all-to-all-start.5 = ((f32[4,64,1152]{2,1,0:T(8,128)}), f32[4,64,1152]{2,1,0:T(8,128)}, u32[]{:S(2)}, u32[]{:S(2)}) async-start(f32[4,64,1152]{2,1,0:T(8,128)} %mul.133), calls=%async_computation.5 | async-start | bytes 2359296 | tf_op jit(solution)/shard_map/all_to_all | solution.py:41
  183.7 1.1 select_maximum_fusion.1
  184.8 13.9 %all-to-all-done.5 = f32[4,64,1152]{2,1,0:T(8,128)} async-done(((f32[4,64,1152]{2,1,0:T(8,128)}), f32[4,64,1152]{2,1,0:T(8,128)}, u32[]{:S(2)}, u32[]{:S(2)}) %all-to-all-start.5) | async-done | bytes 1179680 | tf_op jit(solution)/shard_map/all_to_all | solution.py:41
  198.6 4.3 %all-to-all-start.2 = ((f32[8,9,2048]{2,1,0:T(8,128)}), f32[8,9,2048]{2,1,0:T(8,128)S(1)}, u32[]{:S(2)}, u32[]{:S(2)}) async-start(f32[8,9,2048]{2,1,0:T(8,128)} %select_maximum_fusion.1), calls=%async_computation.2 | async-start | bytes 2097152 | tf_op jit(solution)/shard_map/all_to_all | solution.py:60
  203.0 1.4 reduce_sum.59
  204.3 25.2 %all-to-all-done.2 = f32[8,9,2048]{2,1,0:T(8,128)S(1)} async-done(((f32[8,9,2048]{2,1,0:T(8,128)}), f32[8,9,2048]{2,1,0:T(8,128)S(1)}, u32[]{:S(2)}, u32[]{:S(2)}) %all-to-all-start.2) | async-done | bytes 589856 | tf_op jit(solution)/shard_map/all_to_all | solution.py:60
  229.6 1.1 tile.5
  230.6 3.5 %all-to-all-start.6 = ((f32[4,64,1152]{2,1,0:T(8,128)}), f32[4,64,1152]{2,1,0:T(8,128)S(1)}, u32[]{:S(2)}, u32[]{:S(2)}) async-start(f32[4,64,1152]{2,1,0:T(8,128)} %tile.5), calls=%async_computation.6 | async-start | bytes 2359296 | tf_op jit(solution)/shard_map/all_to_all | solution.py:35
  234.3 0.6 slice.354
  234.9 0.5 slice_bitcast_fusion.3
  235.4 13.9 %all-to-all-done.6 = f32[4,64,1152]{2,1,0:T(8,128)S(1)} async-done(((f32[4,64,1152]{2,1,0:T(8,128)}), f32[4,64,1152]{2,1,0:T(8,128)S(1)}, u32[]{:S(2)}, u32[]{:S(2)}) %all-to-all-start.6) | async-done | bytes 1179680 | tf_op jit(solution)/shard_map/all_to_all | solution.py:35
  249.3 1.0 copy.392
  (97 shorter events, 10.0 us)
Async XLA Ops:
  7.2 1.0 copy-start.31
  7.2 66.0 %all-gather.2.cloned.1.call-start = ((), (), s32[]{:S(2)}) async-start(), calls=%async_computation.7 | async-start | bytes 5898240 | tf_op jit(solution)/shard_map/all_gather | solution.py:83
  8.2 23.8 %copy-start.28 = (bf16[1,128,2048]{2,1,0:T(8,128)(2,1)S(1)}, bf16[1,128,2048]{2,1,0:T(8,128)(2,1)}, u32[]{:S(2)}) copy-start(bf16[1,128,2048]{2,1,0:T(8,128)(2,1)} %param.10) | copy-start | bytes 1572868
  8.2 23.8 %copy-start.33 = (s32[1,128]{1,0:T(1,128)S(1)}, s32[1,128]{1,0:T(1,128)}, u32[]{:S(2)}) copy-start(s32[1,128]{1,0:T(1,128)} %param.11) | copy-start | bytes 1540
  32.0 0.7 copy-start.32
  32.9 9.9 %copy-start.18 = (bf16[1,128,2048]{2,1,0:T(8,128)(2,1)S(1)}, bf16[1,128,2048]{2,1,0:T(8,128)(2,1)}, u32[]{:S(2)}) copy-start(bf16[1,128,2048]{2,1,0:T(8,128)(2,1)} %param.15) | copy-start | bytes 1572868
  33.9 20.5 %all-to-all-start.4 = ((bf16[128,8,256]{0,2,1:T(8,128)(2,1)}), bf16[128,8,256]{0,2,1:T(8,128)(2,1)S(1)}, u32[]{:S(2)}, u32[]{:S(2)}) async-start(bf16[128,8,256]{0,2,1:T(8,128)(2,1)} %bitcast.35), calls=%async_computation.4 | async-start | bytes 1048576 | tf_op jit(solution)/shard_map/all_to_all | solution.py:112
  39.1 5.0 %collective-permute-start = (bf16[4,2048]{1,0:T(4,128)(2,1)S(1)}, bf16[4,2048]{1,0:T(4,128)(2,1)S(1)}, u32[]{:S(2)}, u32[]{:S(2)}) collective-permute-start(bf16[4,2048]{1,0:T(4,128)(2,1)S(1)} %get-tuple-element.66), channel_id=1, source_target_pairs={{0,1},{1,2},{2,3},{3,4},{4,5},{5,6},{6,7},{8,9},{9,10},{10,11},{11... | collective-permute-start | bytes 49160 | tf_op jit(solution)/shard_map/ppermute | solution.py:18
  41.5 4.2 %collective-permute-start.1 = (bf16[4,2048]{1,0:T(4,128)(2,1)S(1)}, bf16[4,2048]{1,0:T(4,128)(2,1)S(1)}, u32[]{:S(2)}, u32[]{:S(2)}) collective-permute-start(bf16[4,2048]{1,0:T(4,128)(2,1)S(1)} %get-tuple-element.65), channel_id=1, source_target_pairs={{1,0},{2,1},{3,2},{4,3},{5,4},{6,5},{7,6},{9,8},{10,9},{11,10},{12... | collective-permute-start | bytes 49160 | tf_op jit(solution)/shard_map/ppermute | solution.py:20
  55.0 28.6 %copy-start = (bf16[1024,2,128]{0,2,1:T(8,128)(2,1)}, bf16[1024,2,128]{0,2,1:T(8,128)(2,1)S(1)}, u32[]{:S(2)}) copy-start(bf16[1024,2,128]{0,2,1:T(8,128)(2,1)S(1)} %reshape.195) | copy-start | bytes 1572868
  83.6 19.8 %copy-start.25 = (bf16[16,16,8,128]{3,2,1,0:T(8,128)(2,1)S(1)}, bf16[16,16,8,128]{3,2,1,0:T(8,128)(2,1)}, u32[]{:S(2)}) copy-start(bf16[16,16,8,128]{3,2,1,0:T(8,128)(2,1)} %get-tuple-element.63) | copy-start | bytes 1572868
  103.4 2.0 copy-start.8
  103.4 2.0 copy-start.10
  103.4 2.0 copy-start.6
  103.4 3.4 %copy-start.13 = (bf16[16,128,1,128]{3,2,1,0:T(2,128)(2,1)}, bf16[16,128,1,128]{3,2,1,0:T(2,128)(2,1)S(1)}, u32[]{:S(2)}) copy-start(bf16[16,128,1,128]{3,2,1,0:T(2,128)(2,1)S(1)} %get-tuple-element.35) | copy-start | bytes 1572868
  103.4 4.6 %copy-start.12 = (bf16[16,128,1,128]{3,2,1,0:T(2,128)(2,1)}, bf16[16,128,1,128]{3,2,1,0:T(2,128)(2,1)S(1)}, u32[]{:S(2)}) copy-start(bf16[16,128,1,128]{3,2,1,0:T(2,128)(2,1)S(1)} %get-tuple-element.34) | copy-start | bytes 1572868
  103.4 5.1 %copy-start.4 = (bf16[16,128,1,128]{3,2,1,0:T(2,128)(2,1)}, bf16[16,128,1,128]{3,2,1,0:T(2,128)(2,1)S(1)}, u32[]{:S(2)}) copy-start(bf16[16,128,1,128]{3,2,1,0:T(2,128)(2,1)S(1)} %get-tuple-element.33) | copy-start | bytes 1572868
  103.4 6.1 %copy-start.2 = (bf16[16,128,1,128]{3,2,1,0:T(2,128)(2,1)}, bf16[16,128,1,128]{3,2,1,0:T(2,128)(2,1)S(1)}, u32[]{:S(2)}) copy-start(bf16[16,128,1,128]{3,2,1,0:T(2,128)(2,1)S(1)} %get-tuple-element.32) | copy-start | bytes 1572868
  103.4 7.6 %copy-start.16 = (bf16[16,128,1,128]{3,2,1,0:T(2,128)(2,1)}, bf16[16,128,1,128]{3,2,1,0:T(2,128)(2,1)S(1)}, u32[]{:S(2)}) copy-start(bf16[16,128,1,128]{3,2,1,0:T(2,128)(2,1)S(1)} %get-tuple-element.30) | copy-start | bytes 1572868
  103.4 1.4 copy-start.24
  104.9 1.4 copy-start.23
  106.3 1.2 copy-start.22
  108.0 1.0 copy-start.21
  109.0 1.0 copy-start.20
  110.5 1.2 copy-start.27
  110.6 1.3 copy-start.29
  113.1 14.5 %collective-permute-start.2 = (bf16[4,2048]{0,1:T(8,128)(2,1)S(1)}, bf16[4,2048]{0,1:T(8,128)(2,1)}, u32[]{:S(2)}, u32[]{:S(2)}) collective-permute-start(bf16[4,2048]{0,1:T(8,128)(2,1)S(1)} %copy.243), channel_id=1, source_target_pairs={{1,0},{2,1},{3,2},{4,3},{5,4},{6,5},{7,6},{9,8},{10,9},{11,10},{12... | collective-permute-start | bytes 49160 | tf_op jit(solution)/shard_map/ppermute | solution.py:20
  115.5 12.2 %collective-permute-start.3 = (bf16[4,2048]{0,1:T(8,128)(2,1)}, bf16[4,2048]{0,1:T(8,128)(2,1)}, u32[]{:S(2)}, u32[]{:S(2)}) collective-permute-start(bf16[4,2048]{0,1:T(8,128)(2,1)} %copy.253), channel_id=1, source_target_pairs={{0,1},{1,2},{2,3},{3,4},{4,5},{5,6},{6,7},{8,9},{9,10},{10,11},{11... | collective-permute-start | bytes 49160 | tf_op jit(solution)/shard_map/ppermute | solution.py:18
  123.1 23.8 %all-to-all-start.3 = ((bf16[128,8,256]{0,2,1:T(8,128)(2,1)}), bf16[128,8,256]{0,2,1:T(8,128)(2,1)}, u32[]{:S(2)}, u32[]{:S(2)}) async-start(bf16[128,8,256]{0,2,1:T(8,128)(2,1)} %bitcast.33), calls=%async_computation.3 | async-start | bytes 1048576 | tf_op jit(solution)/shard_map/all_to_all | solution.py:113
  127.7 6.5 %copy-start.11 = (bf16[16,128,1,128]{3,2,1,0:T(2,128)(2,1)S(1)}, bf16[16,128,1,128]{3,2,1,0:T(2,128)(2,1)}, u32[]{:S(2)}) copy-start(bf16[16,128,1,128]{3,2,1,0:T(2,128)(2,1)} %copy-done.10) | copy-start | bytes 1572868
  134.2 1.2 copy-start.9
  135.4 1.2 copy-start.7
  136.6 1.2 copy-start.14
  136.6 1.5 copy-start.15
  138.2 1.2 copy-start.5
  139.4 1.2 copy-start.3
  141.0 1.2 copy-start.17
  142.9 1.0 copy-start.19
  144.4 0.8 copy-start.26
  146.8 32.2 %all-to-all-start.1 = ((f32[4,65,2048]{2,1,0:T(8,128)}), f32[4,65,2048]{2,1,0:T(8,128)S(1)}, u32[]{:S(2)}, u32[]{:S(2)}) async-start(f32[4,65,2048]{2,1,0:T(8,128)} %select_maximum_fusion), calls=%async_computation.1 | async-start | bytes 4718592 | tf_op jit(solution)/shard_map/all_to_all | solution.py:55
  152.1 1.4 copy-start.30
  153.9 1.0 copy-start.1
  179.1 19.5 %all-to-all-start.5 = ((f32[4,64,1152]{2,1,0:T(8,128)}), f32[4,64,1152]{2,1,0:T(8,128)}, u32[]{:S(2)}, u32[]{:S(2)}) async-start(f32[4,64,1152]{2,1,0:T(8,128)} %mul.133), calls=%async_computation.5 | async-start | bytes 2359296 | tf_op jit(solution)/shard_map/all_to_all | solution.py:41
  198.6 30.9 %all-to-all-start.2 = ((f32[8,9,2048]{2,1,0:T(8,128)}), f32[8,9,2048]{2,1,0:T(8,128)S(1)}, u32[]{:S(2)}, u32[]{:S(2)}) async-start(f32[8,9,2048]{2,1,0:T(8,128)} %select_maximum_fusion.1), calls=%async_computation.2 | async-start | bytes 2097152 | tf_op jit(solution)/shard_map/all_to_all | solution.py:60
  230.6 18.6 %all-to-all-start.6 = ((f32[4,64,1152]{2,1,0:T(8,128)}), f32[4,64,1152]{2,1,0:T(8,128)S(1)}, u32[]{:S(2)}, u32[]{:S(2)}) async-start(f32[4,64,1152]{2,1,0:T(8,128)} %tile.5), calls=%async_computation.6 | async-start | bytes 2359296 | tf_op jit(solution)/shard_map/all_to_all | solution.py:35
Sparse Core Ops, SparseCore 0:
  9.8 63.2 all-gather.1

commit v2 on v0

v2 whole, which is shorter than its diff:
```python
import jax
import jax.numpy as jnp
from jax import lax
from jax.sharding import PartitionSpec as P

GROUPS = 16
KERNEL = 9


def with_halo(cells, axis, dim, width):
    count = lax.axis_size(axis)
    ends = count - 1
    head = lax.slice_in_dim(cells, 0, width, axis=dim)
    tail = lax.slice_in_dim(cells, cells.shape[dim] - width, cells.shape[dim], axis=dim)
    return jnp.concatenate(
        [
            lax.ppermute(tail, axis, [(i, (i + 1) % count) for i in range(ends)]),
            cells,
            lax.ppermute(head, axis, [((i + 1) % count, i) for i in range(ends)]),
        ],
        axis=dim,
    )


def from_partner(value, axis, apart):
    mask = 2**apart
    pairs = [(source, source ^ mask) for source in range(lax.axis_size(axis))]
    return lax.ppermute(value, axis, pairs)


def gather_rows(block, axis):
    count = lax.axis_size(axis)
    return lax.all_to_all(jnp.tile(block, (count,) + (1,) * (block.ndim - 1)), axis, 0, 0, tiled=True)


def conv_forward(padded, weights, length):
    chans = padded.shape[-1]
    total = None
    for k in range(KERNEL):
        term = jnp.einsum(
            "gtc,goc->gto",
            padded[:, k : k + length],
            weights[:, :, k * chans : (k + 1) * chans],
            preferred_element_type=jnp.float32,
        )
        total = term if total is None else total + term
    return total


def conv_backward(dpad, weights, length):
    chans = weights.shape[-1] // KERNEL
    half = KERNEL // 2
    total = None
    for k in range(KERNEL):
        term = jnp.einsum(
            "gto,goc->gtc",
            dpad[:, 2 * half - k : 2 * half - k + length],
            weights[:, :, k * chans : (k + 1) * chans],
            preferred_element_type=jnp.float32,
        )
        total = term if total is None else total + term
    return total


def spread_groups(normed, dflat, chans):
    normed_slice = lax.all_to_all(normed, "seq", 1, 0, tiled=True)
    dconv_slice = lax.all_to_all(dflat, "seq", 1, 0, tiled=True)
    whole, slice_width = normed_slice.shape
    spread = chans // slice_width
    position = lax.axis_index("seq")
    group_rows = normed_slice
    for bit in range(spread.bit_length() - 1):
        partner = from_partner(group_rows, "seq", bit)
        lower = position >> bit & 1 == 0
        group_rows = jnp.where(
            lower,
            jnp.concatenate([group_rows, partner], axis=1),
            jnp.concatenate([partner, group_rows], axis=1),
        )
    return group_rows.reshape(1, whole, chans), dconv_slice.reshape(1, whole, slice_width)


def body(events, type_ids, type_table, norm_gain, kernel, upstream):
    length = events.shape[1]
    width = events.shape[2]
    chans = width // GROUPS
    half = KERNEL // 2
    fsdp = lax.axis_size("fsdp")
    seq_count = lax.axis_size("seq")
    total = length * seq_count * fsdp
    scale = 1.0 / jnp.sqrt(jnp.float32(total))
    table = gather_rows(type_table, "fsdp")
    types = table.shape[0]
    onehot = (type_ids[0][:, None] == jnp.arange(types, dtype=jnp.int32)[None, :]).astype(jnp.bfloat16)
    mixed = events[0].astype(jnp.float32) + jnp.dot(onehot, table, preferred_element_type=jnp.float32)
    inv = lax.rsqrt(jnp.mean(mixed * mixed, axis=-1, keepdims=True) + 1e-06)
    normed = (mixed * inv * norm_gain).astype(jnp.bfloat16)
    normed_g = normed.reshape(length, GROUPS, chans).transpose(1, 0, 2)
    padded = with_halo(normed_g, "seq", 1, half)
    weights = lax.all_gather(kernel, "fsdp", axis=0, tiled=True).reshape(GROUPS, chans, KERNEL * chans)
    conv = conv_forward(padded, weights, length)
    up_float = upstream[0].astype(jnp.float32)
    up_g = up_float.reshape(length, GROUPS, chans).transpose(1, 0, 2)
    sig = jax.nn.sigmoid(conv)
    dconv = (up_g * sig * (1.0 + conv * (1.0 - sig))).astype(jnp.bfloat16)
    dpad = with_halo(dconv, "seq", 1, half)
    dnormed = conv_backward(dpad, weights, length)
    if seq_count <= GROUPS:
        group_in = lax.all_to_all(normed_g, "seq", 0, 1, tiled=True)
        group_out = lax.all_to_all(dconv, "seq", 0, 1, tiled=True)
    else:
        group_in, group_out = spread_groups(normed, dconv.transpose(1, 0, 2).reshape(length, width), chans)
    local_groups = group_in.shape[0]
    whole = group_in.shape[1]
    group_pad = jnp.pad(group_in, ((0, 0), (half, half), (0, 0)))
    kterms = [
        jnp.einsum("gto,gtc->goc", group_out, group_pad[:, k : k + whole], preferred_element_type=jnp.float32)
        for k in range(KERNEL)
    ]
    kernel_part = jnp.concatenate(kterms, axis=-1).reshape(-1, KERNEL * chans) * scale
    dnormed = dnormed.transpose(1, 0, 2).reshape(length, width)
    gain_term = jnp.sum(dnormed * mixed * inv, axis=0) * scale
    scaled = norm_gain * dnormed
    dmixed = inv * scaled - mixed * inv * inv * inv * jnp.mean(scaled * mixed, axis=-1, keepdims=True)
    input_grad = (up_float + dmixed).astype(jnp.bfloat16)
    table_term = (
        lax.dot_general(onehot, input_grad, (((0,), (0,)), ((), ())), preferred_element_type=jnp.float32)
        * scale
    )
    wide = width // fsdp
    rows = types // fsdp
    kg_rows = kernel_part.shape[0] // fsdp
    gain_rows = jnp.zeros((fsdp, 1, width), jnp.float32).at[:, 0, :wide].set(gain_term.reshape(fsdp, wide))
    first_table = jnp.concatenate([table_term.reshape(fsdp, rows, width), gain_rows], axis=1)
    first_kg = jnp.zeros((fsdp, rows + 1, kernel_part.shape[1]), jnp.float32)
    first_kg = first_kg.at[:, :kg_rows].set(kernel_part.reshape(fsdp, kg_rows, kernel_part.shape[1]))
    first = jnp.concatenate([first_table, first_kg], axis=2)
    first = lax.all_to_all(first, "fsdp", 0, 0, tiled=True).sum(axis=0)
    kg_sum = first[:kg_rows, width:]
    kernel_grad = gather_rows(kg_sum, "fsdp")
    narrow = wide // seq_count
    gain_rows = jnp.zeros((seq_count, 1, width), jnp.float32).at[:, 0, :narrow].set(
        first[rows, :wide].reshape(seq_count, narrow)
    )
    second = jnp.concatenate([first[:rows, :width].reshape(seq_count, rows // seq_count, width), gain_rows], axis=1)
    second = lax.all_to_all(second, "seq", 0, 0, tiled=True).sum(axis=0)
    table_grad = second[: rows // seq_count]
    gain_grad = second[rows // seq_count, :narrow]
    return (input_grad[None], table_grad, gain_grad, kernel_grad)


def solution(mesh):
    return jax.shard_map(
        body,
        mesh=mesh,
        in_specs=(
            P("fsdp", "seq", None),
            P("fsdp", "seq"),
            P("fsdp", None),
            P(),
            P("fsdp", None),
            P("fsdp", "seq", None),
        ),
        out_specs=(
            P("fsdp", "seq", None),
            P(("fsdp", "seq"), None),
            P(("fsdp", "seq")),
            P("seq", None),
        ),
        check_vma=False,
    )
```

time: 386 us -> 239 us (0.62)
  waiting for transfers between devices: 223 us -> 69.8 us
  local copies, waits for them, and re-layouts: 59.2 us -> 11.2 us
  blocking collectives: 39.9 us -> 71.2 us
  matrix products: 18.8 us -> 35.1 us
  starting transfers between devices: 18.4 us -> 27.6 us
    reduce_scatter x1 -> x0, waiting for transfers between devices: 137 us -> none  [body(): lax.psum_scatter(table_term, ('fsdp', 'seq'), scatter_dimension=0, tiled=...]
    all_to_all x0 -> x2, blocking collectives: none -> 71.2 us  [the longest x1 46.7 us: body(): first = lax.all_to_all(first, 'fsdp', 0, 0, tiled=True).sum(axis=0)]
    all_to_all x2 -> x4, waiting for transfers between devices: 6.03 us -> 52 us  [the longest x1 26.6 us: body(): second = lax.all_to_all(second, 'seq', 0, 0, tiled=True).sum(axis=0)]
    unnamed x1 -> x0, blocking collectives: 39.9 us -> none
    all_gather x1 -> x0, waiting for transfers between devices: 30.6 us -> none  [body(): table = lax.all_gather(type_table, 'fsdp', axis=0, tiled=True)]
    slice x1 -> x3, local copies, waits for them, and re-layouts: 19.8 us -> 0.68 us  [the longest x1 0.63 us: body(): table_grad = second[:rows // seq_count]]
    dot_general x27, matrix products: 15.2 us -> 34.1 us  [the longest x9 15.5 us: conv_backward(): jnp.einsum('gto,goc->gtc', dpad[:, 2 * half - k:2 * half - k + length], w...]
    all_gather x1, waiting for transfers between devices: 34.5 us -> 17.1 us  [body(): lax.all_gather(kernel, 'fsdp', axis=0, tiled=True)]
  transfers between devices with their start and end apart: 10 -> 9, of which waited for: 6 -> 4; matrix products, arithmetic and copies ran while one was open for 8% -> 13% of each run, Pallas kernels for 0% -> 0%
where the time goes in v2:
time: 239 us; the launch traced here: 237 us
  blocking collectives  71.2 us (30%)
  waiting for transfers between devices  69.8 us (29%)
  matrix products  35.1 us (15%)
  starting transfers between devices  27.6 us (12%)
  between operations  14.4 us (6%)
  local copies, waits for them, and re-layouts  11.2 us (5%)
  other arithmetic  7.95 us (3%)
    all_to_all x1, blocking collectives, body(): first = lax.all_to_all(first, 'fsdp', 0, 0, tiled=True).sum(axis=0)  46.7 us
    all_to_all x1, waiting for transfers between devices, body(): second = lax.all_to_all(second, 'seq', 0, 0, tiled=True).sum(axis=0)  26.6 us
    all_to_all x1, blocking collectives, gather_rows(): lax.all_to_all(jnp.tile(block, (count,) + (1,) * (block.ndim - 1)), axis,...  24.5 us
    all_gather x1, waiting for transfers between devices, body(): lax.all_gather(kernel, 'fsdp', axis=0, tiled=True)  17.1 us
    dot_general x9, matrix products, conv_backward(): jnp.einsum('gto,goc->gtc', dpad[:, 2 * half - k:2 * half - k + length], w...  15.5 us
    dot_general x9, matrix products, conv_forward(): jnp.einsum('gtc,goc->gto', padded[:, k:k + length], weights[:, :, k * cha...  15.4 us
    all_to_all x1, waiting for transfers between devices, gather_rows(): lax.all_to_all(jnp.tile(block, (count,) + (1,) * (block.ndim - 1)), axis,...  14.9 us
    all_to_all x1, waiting for transfers between devices, body(): group_in = lax.all_to_all(normed_g, 'seq', 0, 1, tiled=True)  10.5 us
  transfers between devices with their start and end apart: 9, of which 4 were waited for; matrix products, arithmetic and copies ran while one was open for 13% of the time, Pallas kernels for 0%

profile of v2, /device:TPU:0, one launch (start us, length us, event | category | flops | bytes accessed | tf_op | source)
XLA Modules:
  0.0 237.2 jit_solution(3273193479734358696)
XLA Ops:
  7.2 0.7 all-gather.2.cloned.1.call-update
  7.9 1.1 tile.4
  9.0 24.5 %all_to_all.64 = bf16[4,64,2048]{2,1,0:T(8,128)(2,1)S(1)} all-to-all(bf16[4,64,2048]{2,1,0:T(8,128)(2,1)S(1)} %tile.4), channel_id=1, replica_groups=mesh['fsdp'=4,'seq'=8] {'fsdp'}, dimensions={0} | all-to-all | bytes 2097152 | tf_op jit(solution)/shard_map/all_to_all | solution.py:33
  33.5 0.4 multiply_reduce_fusion.2
  34.0 1.0 bitcast_bitcast_fusion
  35.0 5.2 %all-to-all-start.2 = ((bf16[16,128,128]{2,1,0:T(8,128)(2,1)}), bf16[16,128,128]{2,1,0:T(8,128)(2,1)S(1)}, u32[]{:S(2)}, u32[]{:S(2)}) async-start(bf16[16,128,128]{2,1,0:T(8,128)(2,1)} %bitcast_bitcast_fusion), calls=%async_computation.2 | async-start | bytes 1048576 | tf_op jit(solution)/shard_map/all_to_all | solution.py:109
  40.2 0.2 copy.53
  40.4 0.8 fusion.145
  41.2 2.4 %collective-permute-start = (bf16[16,4,128]{2,1,0:T(4,128)(2,1)S(1)}, bf16[16,4,128]{2,1,0:T(4,128)(2,1)S(1)}, u32[]{:S(2)}, u32[]{:S(2)}) collective-permute-start(bf16[16,4,128]{2,1,0:T(4,128)(2,1)S(1)} %get-tuple-element.44), channel_id=1, source_target_pairs={{0,1},{1,2},{2,3},{3,4},{4,5},{5,6},{6,7},{8,9},{9,10},{10,11},{11... | collective-permute-start | bytes 49160 | tf_op jit(solution)/shard_map/ppermute | solution.py:17
  43.6 1.3 collective-permute-start.1
  44.9 10.5 %all-to-all-done.2 = bf16[16,128,128]{2,1,0:T(8,128)(2,1)S(1)} async-done(((bf16[16,128,128]{2,1,0:T(8,128)(2,1)}), bf16[16,128,128]{2,1,0:T(8,128)(2,1)S(1)}, u32[]{:S(2)}, u32[]{:S(2)}) %all-to-all-start.2) | async-done | bytes 524320 | tf_op jit(solution)/shard_map/all_to_all | solution.py:109
  55.5 0.3 copy.38
  55.8 1.0 all_to_all.53
  56.8 17.1 %all-gather.2.cloned.1.call-done = bf16[2048,1152]{1,0:T(8,128)(2,1)} async-done(((bf16[512,1152]{1,0:T(8,128)(2,1)}), bf16[2048,1152]{1,0:T(8,128)(2,1)}) %all-gather.2.cloned.1.call-update) | async-done | bytes 4718608 | tf_op jit(solution)/shard_map/all_gather | solution.py:100
  73.9 1.7 fusion.88
  75.6 1.7 fusion.42
  77.3 1.5 fusion.47
  78.8 1.5 fusion.65
  80.4 1.5 fusion.39
  81.9 1.5 fusion.34
  83.4 1.5 fusion.60
  85.0 1.6 fusion.12
  86.6 2.8 %fusion.16 = bf16[16,128,128]{2,1,0:T(8,128)(2,1)} fusion(f32[128,16,128]{2,1,0:T(8,128)S(1)} %bitcast.104, f32[16,128,128]{2,1,0:T(8,128)S(1)} %fusion.60, f32[16,128,128]{2,1,0:T(8,128)S(1)} %fusion.34, f32[16,128,128]{2,1,0:T(8,128)S(1)} %fusion.39, f32[16,128,128]{2,1,0:T(8,128)S(1)} %fusion.12, bf16[16,4,128]{2,1,0:T(4,128)(2,1)S(1)} %collective-permute-done.1, ...), kind=kOutput, calls=%fused_computation.41 | convolution fusion | flops 71565312 | bytes 6832128 | tf_op jit(solution)/shard_map/gtc,goc->gto/dot_general | solution.py:40
  89.4 4.6 %all-to-all-start.1 = ((bf16[16,128,128]{2,1,0:T(8,128)(2,1)}), bf16[16,128,128]{2,1,0:T(8,128)(2,1)}, u32[]{:S(2)}, u32[]{:S(2)}) async-start(bf16[16,128,128]{2,1,0:T(8,128)(2,1)} %fusion.16), calls=%async_computation.1 | async-start | bytes 1048576 | tf_op jit(solution)/shard_map/all_to_all | solution.py:110
  94.0 0.8 fusion.144
  94.8 1.3 collective-permute-start.2
  96.1 1.7 fusion.86
  97.8 3.2 %collective-permute-start.3 = (bf16[16,4,128]{2,1,0:T(4,128)(2,1)S(1)}, bf16[16,4,128]{2,1,0:T(4,128)(2,1)S(1)}, u32[]{:S(2)}, u32[]{:S(2)}) collective-permute-start(bf16[16,4,128]{2,1,0:T(4,128)(2,1)S(1)} %get-tuple-element.43), channel_id=1, source_target_pairs={{0,1},{1,2},{2,3},{3,4},{4,5},{5,6},{6,7},{8,9},{9,10},{10,11},{11... | collective-permute-start | bytes 49160 | tf_op jit(solution)/shard_map/ppermute | solution.py:17
  101.1 1.7 fusion.31
  102.8 1.7 fusion.26
  104.5 1.7 fusion.55
  106.2 1.7 fusion.23
  107.9 1.7 fusion.18
  109.7 1.7 fusion.50
  111.4 1.7 fusion.6
  113.1 1.8 fusion.3
  114.9 0.3 copy.50
  115.2 0.3 multiply_reduce_fusion
  115.6 1.5 fusion.14
  117.0 0.8 copy-done.3
  117.8 0.5 convolution_multiply_fusion
  118.4 1.1 copy.37
  119.5 0.4 convolution_dynamic-update-slice_fusion.8
  119.8 0.4 convolution_dynamic-update-slice_fusion.7
  120.2 0.4 convolution_dynamic-update-slice_fusion.6
  120.6 0.4 convolution_dynamic-update-slice_fusion.5
  120.9 0.3 convolution_dynamic-update-slice_fusion.4
  121.2 0.4 convolution_dynamic-update-slice_fusion.3
  121.6 0.4 convolution_dynamic-update-slice_fusion.2
  122.0 0.4 convolution_dynamic-update-slice_fusion.1
  122.3 0.4 convolution_dynamic-update-slice_fusion
  122.8 1.4 copy.39
  124.2 1.5 select_maximum_fusion
  125.7 46.7 %all_to_all.65 = f32[4,65,3200]{2,1,0:T(8,128)} all-to-all(f32[4,65,3200]{2,1,0:T(8,128)S(1)} %select_maximum_fusion), channel_id=1, replica_groups=mesh['fsdp'=4,'seq'=8] {'fsdp'}, dimensions={0} | all-to-all | bytes 6656000 | tf_op jit(solution)/shard_map/all_to_all | solution.py:138
  172.4 2.3 reduce_sum.48
  174.8 1.1 tile.5
  175.9 3.5 %all-to-all-start.5 = ((f32[4,64,1152]{2,1,0:T(8,128)}), f32[4,64,1152]{2,1,0:T(8,128)S(1)}, u32[]{:S(2)}, u32[]{:S(2)}) async-start(f32[4,64,1152]{2,1,0:T(8,128)} %tile.5), calls=%async_computation.5 | async-start | bytes 2359296 | tf_op jit(solution)/shard_map/all_to_all | solution.py:33
  179.6 1.0 select_maximum_fusion.2
  180.6 14.9 %all-to-all-done.5 = f32[4,64,1152]{2,1,0:T(8,128)S(1)} async-done(((f32[4,64,1152]{2,1,0:T(8,128)}), f32[4,64,1152]{2,1,0:T(8,128)S(1)}, u32[]{:S(2)}, u32[]{:S(2)}) %all-to-all-start.5) | async-done | bytes 1179680 | tf_op jit(solution)/shard_map/all_to_all | solution.py:33
  195.5 6.1 %all-to-all-start.4 = ((f32[8,9,2048]{2,1,0:T(8,128)}), f32[8,9,2048]{2,1,0:T(8,128)S(1)}, u32[]{:S(2)}, u32[]{:S(2)}) async-start(f32[8,9,2048]{2,1,0:T(8,128)} %select_maximum_fusion.2), calls=%async_computation.4 | async-start | bytes 2097152 | tf_op jit(solution)/shard_map/all_to_all | solution.py:146
  201.6 26.6 %all-to-all-done.4 = f32[8,9,2048]{2,1,0:T(8,128)S(1)} async-done(((f32[8,9,2048]{2,1,0:T(8,128)}), f32[8,9,2048]{2,1,0:T(8,128)S(1)}, u32[]{:S(2)}, u32[]{:S(2)}) %all-to-all-start.4) | async-done | bytes 589856 | tf_op jit(solution)/shard_map/all_to_all | solution.py:146
  228.2 0.6 slice.300
  228.9 0.5 slice_bitcast_fusion.1
  229.4 1.0 copy.66
  (29 shorter events, 0.5 us)
Async XLA Ops:
  7.2 26.3 %copy-start.6 = (s32[1,128]{1,0:T(1,128)S(1)}, s32[1,128]{1,0:T(1,128)}, u32[]{:S(2)}) copy-start(s32[1,128]{1,0:T(1,128)} %param.13) | copy-start | bytes 1540
  7.2 26.3 %copy-start.4 = (bf16[1,128,2048]{2,1,0:T(8,128)(2,1)S(1)}, bf16[1,128,2048]{2,1,0:T(8,128)(2,1)}, u32[]{:S(2)}) copy-start(bf16[1,128,2048]{2,1,0:T(8,128)(2,1)} %param.12) | copy-start | bytes 1572868
  7.2 26.8 %copy-start.5 = (f32[2048]{0:T(1024)S(1)}, f32[2048]{0:T(1024)}, u32[]{:S(2)}) copy-start(f32[2048]{0:T(1024)} %param.15) | copy-start | bytes 24580
  7.2 66.7 %all-gather.2.cloned.1.call-start = ((), (), s32[]{:S(2)}) async-start(), calls=%async_computation.6 | async-start | bytes 5898240 | tf_op jit(solution)/shard_map/all_gather | solution.py:100
  9.0 31.1 %copy-start.1 = (bf16[1,128,2048]{2,1,0:T(8,128)(2,1)S(1)}, bf16[1,128,2048]{2,1,0:T(8,128)(2,1)}, u32[]{:S(2)}) copy-start(bf16[1,128,2048]{2,1,0:T(8,128)(2,1)} %param.17) | copy-start | bytes 1572868
  35.0 20.5 %all-to-all-start.2 = ((bf16[16,128,128]{2,1,0:T(8,128)(2,1)}), bf16[16,128,128]{2,1,0:T(8,128)(2,1)S(1)}, u32[]{:S(2)}, u32[]{:S(2)}) async-start(bf16[16,128,128]{2,1,0:T(8,128)(2,1)} %bitcast_bitcast_fusion), calls=%async_computation.2 | async-start | bytes 1048576 | tf_op jit(solution)/shard_map/all_to_all | solution.py:109
  41.2 34.4 %collective-permute-start = (bf16[16,4,128]{2,1,0:T(4,128)(2,1)S(1)}, bf16[16,4,128]{2,1,0:T(4,128)(2,1)S(1)}, u32[]{:S(2)}, u32[]{:S(2)}) collective-permute-start(bf16[16,4,128]{2,1,0:T(4,128)(2,1)S(1)} %get-tuple-element.44), channel_id=1, source_target_pairs={{0,1},{1,2},{2,3},{3,4},{4,5},{5,6},{6,7},{8,9},{9,10},{10,11},{11... | collective-permute-start | bytes 49160 | tf_op jit(solution)/shard_map/ppermute | solution.py:17
  43.6 36.7 %collective-permute-start.1 = (bf16[16,4,128]{2,1,0:T(4,128)(2,1)S(1)}, bf16[16,4,128]{2,1,0:T(4,128)(2,1)S(1)}, u32[]{:S(2)}, u32[]{:S(2)}) collective-permute-start(bf16[16,4,128]{2,1,0:T(4,128)(2,1)S(1)} %get-tuple-element.45), channel_id=1, source_target_pairs={{1,0},{2,1},{3,2},{4,3},{5,4},{6,5},{7,6},{9,8},{10,9},{11,10},{12... | collective-permute-start | bytes 49160 | tf_op jit(solution)/shard_map/ppermute | solution.py:19
  73.9 3.4 %copy-start = (bf16[2048,1152]{1,0:T(8,128)(2,1)S(1)}, bf16[2048,1152]{1,0:T(8,128)(2,1)}, u32[]{:S(2)}) copy-start(bf16[2048,1152]{1,0:T(8,128)(2,1)} %all-gather.2.cloned.1.call-done) | copy-start | bytes 14155780
  89.4 29.0 %all-to-all-start.1 = ((bf16[16,128,128]{2,1,0:T(8,128)(2,1)}), bf16[16,128,128]{2,1,0:T(8,128)(2,1)}, u32[]{:S(2)}, u32[]{:S(2)}) async-start(bf16[16,128,128]{2,1,0:T(8,128)(2,1)} %fusion.16), calls=%async_computation.1 | async-start | bytes 1048576 | tf_op jit(solution)/shard_map/all_to_all | solution.py:110
  94.8 6.2 %collective-permute-start.2 = (bf16[16,4,128]{2,1,0:T(4,128)(2,1)S(1)}, bf16[16,4,128]{2,1,0:T(4,128)(2,1)S(1)}, u32[]{:S(2)}, u32[]{:S(2)}) collective-permute-start(bf16[16,4,128]{2,1,0:T(4,128)(2,1)S(1)} %get-tuple-element.42), channel_id=1, source_target_pairs={{1,0},{2,1},{3,2},{4,3},{5,4},{6,5},{7,6},{9,8},{10,9},{11,10},{12... | collective-permute-start | bytes 49160 | tf_op jit(solution)/shard_map/ppermute | solution.py:19
  97.8 8.4 %collective-permute-start.3 = (bf16[16,4,128]{2,1,0:T(4,128)(2,1)S(1)}, bf16[16,4,128]{2,1,0:T(4,128)(2,1)S(1)}, u32[]{:S(2)}, u32[]{:S(2)}) collective-permute-start(bf16[16,4,128]{2,1,0:T(4,128)(2,1)S(1)} %get-tuple-element.43), channel_id=1, source_target_pairs={{0,1},{1,2},{2,3},{3,4},{4,5},{5,6},{6,7},{8,9},{9,10},{10,11},{11... | collective-permute-start | bytes 49160 | tf_op jit(solution)/shard_map/ppermute | solution.py:17
  115.5 4.0 %copy-start.2 = (bf16[2,1024,128]{1,2,0:T(8,128)(2,1)S(1)}, bf16[2,1024,128]{1,2,0:T(8,128)(2,1)}, u32[]{:S(2)}) copy-start(bf16[2,1024,128]{1,2,0:T(8,128)(2,1)} %all_to_all.53) | copy-start | bytes 1572868
  117.0 0.8 copy-start.3
  175.9 19.6 %all-to-all-start.5 = ((f32[4,64,1152]{2,1,0:T(8,128)}), f32[4,64,1152]{2,1,0:T(8,128)S(1)}, u32[]{:S(2)}, u32[]{:S(2)}) async-start(f32[4,64,1152]{2,1,0:T(8,128)} %tile.5), calls=%async_computation.5 | async-start | bytes 2359296 | tf_op jit(solution)/shard_map/all_to_all | solution.py:33
  195.5 32.7 %all-to-all-start.4 = ((f32[8,9,2048]{2,1,0:T(8,128)}), f32[8,9,2048]{2,1,0:T(8,128)S(1)}, u32[]{:S(2)}, u32[]{:S(2)}) async-start(f32[8,9,2048]{2,1,0:T(8,128)} %select_maximum_fusion.2), calls=%async_computation.4 | async-start | bytes 2097152 | tf_op jit(solution)/shard_map/all_to_all | solution.py:146
Sparse Core Ops, SparseCore 0:
  9.9 63.9 all-gather.1

commit v3 on v2

--- a/solution.py
+++ b/solution.py
@@ -80,6 +80,46 @@
     return group_rows.reshape(1, whole, chans), dconv_slice.reshape(1, whole, slice_width)
 
 
+def sum_rows(block, axis):
+    count = lax.axis_size(axis)
+    parts = block.reshape(count, block.shape[0] // count, *block.shape[1:])
+    return lax.all_to_all(parts, axis, 0, 0, tiled=True).sum(axis=0)
+
+
+def psum_rows(block, axis):
+    return gather_rows(sum_rows(block, axis), axis)
+
+
+def table_and_gain(input_grad, ids, gain_term, types, scale):
+    every = ("fsdp", "seq")
+    count = lax.axis_size("fsdp") * lax.axis_size("seq")
+    length, width = input_grad.shape
+    narrow = width // count
+    id_rows = -(-length // narrow)
+    ids_wide = jnp.zeros((id_rows * narrow,), jnp.bfloat16).at[:length].set(ids.astype(jnp.bfloat16))
+    send = jnp.concatenate(
+        [
+            input_grad.reshape(length, count, narrow).transpose(1, 0, 2),
+            jnp.broadcast_to(ids_wide.reshape(1, id_rows, narrow), (count, id_rows, narrow)),
+        ],
+        axis=1,
+    )
+    got = lax.all_to_all(send, every, 0, 0, tiled=True)
+    rows_all = got[:, :length].reshape(count * length, narrow)
+    ids_all = got[:, length:].reshape(count, id_rows * narrow)[:, :length].reshape(-1).astype(jnp.int32)
+    onehot = (ids_all[:, None] == jnp.arange(types, dtype=jnp.int32)[None, :]).astype(jnp.bfloat16)
+    columns = lax.dot_general(onehot, rows_all, (((0,), (0,)), ((), ())), preferred_element_type=jnp.float32)
+    columns = columns * scale
+    per = types // count
+    back = jnp.concatenate(
+        [columns.reshape(count, per, narrow), gain_term.reshape(count, 1, narrow)], axis=1
+    )
+    back = lax.all_to_all(back, every, 0, 0, tiled=True)
+    table_grad = back[:, :per].transpose(1, 0, 2).reshape(per, width)
+    gain_grad = back[:, per].sum(axis=0)
+    return table_grad, gain_grad
+
+
 def body(events, type_ids, type_table, norm_gain, kernel, upstream):
     length = events.shape[1]
     width = events.shape[2]
@@ -123,29 +163,8 @@
     scaled = norm_gain * dnormed
     dmixed = inv * scaled - mixed * inv * inv * inv * jnp.mean(scaled * mixed, axis=-1, keepdims=True)
     input_grad = (up_float + dmixed).astype(jnp.bfloat16)
-    table_term = (
-        lax.dot_general(onehot, input_grad, (((0,), (0,)), ((), ())), preferred_element_type=jnp.float32)
-        * scale
-    )
-    wide = width // fsdp
-    rows = types // fsdp
-    kg_rows = kernel_part.shape[0] // fsdp
-    gain_rows = jnp.zeros((fsdp, 1, width), jnp.float32).at[:, 0, :wide].set(gain_term.reshape(fsdp, wide))
-    first_table = jnp.concatenate([table_term.reshape(fsdp, rows, width), gain_rows], axis=1)
-    first_kg = jnp.zeros((fsdp, rows + 1, kernel_part.shape[1]), jnp.float32)
-    first_kg = first_kg.at[:, :kg_rows].set(kernel_part.reshape(fsdp, kg_rows, kernel_part.shape[1]))
-    first = jnp.concatenate([first_table, first_kg], axis=2)
-    first = lax.all_to_all(first, "fsdp", 0, 0, tiled=True).sum(axis=0)
-    kg_sum = first[:kg_rows, width:]
-    kernel_grad = gather_rows(kg_sum, "fsdp")
-    narrow = wide // seq_count
-    gain_rows = jnp.zeros((seq_count, 1, width), jnp.float32).at[:, 0, :narrow].set(
-        first[rows, :wide].reshape(seq_count, narrow)
-    )
-    second = jnp.concatenate([first[:rows, :width].reshape(seq_count, rows // seq_count, width), gain_rows], axis=1)
-    second = lax.all_to_all(second, "seq", 0, 0, tiled=True).sum(axis=0)
-    table_grad = second[: rows // seq_count]
-    gain_grad = second[rows // seq_count, :narrow]
+    kernel_grad = psum_rows(kernel_part, "fsdp")
+    table_grad, gain_grad = table_and_gain(input_grad, type_ids[0], gain_term, types, scale)
     return (input_grad[None], table_grad, gain_grad, kernel_grad)
 
 

time: 239 us -> 214 us (0.90)
  blocking collectives: 71.2 us -> 24.2 us
  waiting for transfers between devices: 69.8 us -> 82.9 us
  starting transfers between devices: 27.6 us -> 37.5 us
  other arithmetic: 7.95 us -> 4.66 us
    all_to_all x1 -> x0, blocking collectives: 46.7 us -> none  [body(): first = lax.all_to_all(first, 'fsdp', 0, 0, tiled=True).sum(axis=0)]
    all_to_all x1 -> x3, waiting for transfers between devices: 26.6 us -> 41.8 us  [the longest x1 21.6 us: table_and_gain(): got = lax.all_to_all(send, every, 0, 0, tiled=True)]
    all_to_all x1 -> x3, starting transfers between devices: 6.06 us -> 16.2 us  [the longest x1 10.1 us: table_and_gain(): got = lax.all_to_all(send, every, 0, 0, tiled=True)]
  transfers between devices with their start and end apart: 9 -> 11, of which waited for: 4 -> 6; matrix products, arithmetic and copies ran while one was open for 13% -> 19% of each run, Pallas kernels for 0% -> 0%
where the time goes in v3:
time: 214 us; the launch traced here: 212 us
  waiting for transfers between devices  82.9 us (39%)
  starting transfers between devices  37.5 us (18%)
  matrix products  35.4 us (17%)
  blocking collectives  24.2 us (11%)
  between operations  14.5 us (7%)
  local copies, waits for them, and re-layouts  13.2 us (6%)
  other arithmetic  4.66 us (2%)
    all_to_all x1, blocking collectives, gather_rows(): lax.all_to_all(jnp.tile(block, (count,) + (1,) * (block.ndim - 1)), axis,...  24.2 us
    all_to_all x1, waiting for transfers between devices, table_and_gain(): got = lax.all_to_all(send, every, 0, 0, tiled=True)  21.6 us
    all_gather x1, waiting for transfers between devices, body(): lax.all_gather(kernel, 'fsdp', axis=0, tiled=True)  17.2 us
    dot_general x9, matrix products, conv_backward(): jnp.einsum('gto,goc->gtc', dpad[:, 2 * half - k:2 * half - k + length], w...  15.5 us
    dot_general x9, matrix products, conv_forward(): jnp.einsum('gtc,goc->gto', padded[:, k:k + length], weights[:, :, k * cha...  15.4 us
    all_to_all x1, waiting for transfers between devices, gather_rows(): lax.all_to_all(jnp.tile(block, (count,) + (1,) * (block.ndim - 1)), axis,...  12.8 us
    all_to_all x1, waiting for transfers between devices, sum_rows(): return lax.all_to_all(parts, axis, 0, 0, tiled=True).sum(axis=0)  12.7 us
    all_to_all x1, waiting for transfers between devices, body(): group_in = lax.all_to_all(normed_g, 'seq', 0, 1, tiled=True)  10.3 us
  transfers between devices with their start and end apart: 11, of which 6 were waited for; matrix products, arithmetic and copies ran while one was open for 19% of the time, Pallas kernels for 0%

profile of v3, /device:TPU:0, one launch (start us, length us, event | category | flops | bytes accessed | tf_op | source)
XLA Modules:
  0.0 212.4 jit_solution(8196837961377310453)
XLA Ops:
  7.2 0.7 all-gather.2.cloned.1.call-update
  7.9 1.1 tile.4
  9.0 24.2 %all_to_all.69 = bf16[4,64,2048]{2,1,0:T(8,128)(2,1)S(1)} all-to-all(bf16[4,64,2048]{2,1,0:T(8,128)(2,1)S(1)} %tile.4), channel_id=1, replica_groups=mesh['fsdp'=4,'seq'=8] {'fsdp'}, dimensions={0} | all-to-all | bytes 2097152 | tf_op jit(solution)/shard_map/all_to_all | solution.py:33
  33.2 0.4 multiply_reduce_fusion.2
  33.7 1.0 bitcast_bitcast_fusion
  34.7 5.2 %all-to-all-start.4 = ((bf16[16,128,128]{2,1,0:T(8,128)(2,1)}), bf16[16,128,128]{2,1,0:T(8,128)(2,1)S(1)}, u32[]{:S(2)}, u32[]{:S(2)}) async-start(bf16[16,128,128]{2,1,0:T(8,128)(2,1)} %bitcast_bitcast_fusion), calls=%async_computation.4 | async-start | bytes 1048576 | tf_op jit(solution)/shard_map/all_to_all | solution.py:149
  40.4 0.8 fusion.148
  41.2 2.4 %collective-permute-start = (bf16[16,4,128]{2,1,0:T(4,128)(2,1)S(1)}, bf16[16,4,128]{2,1,0:T(4,128)(2,1)S(1)}, u32[]{:S(2)}, u32[]{:S(2)}) collective-permute-start(bf16[16,4,128]{2,1,0:T(4,128)(2,1)S(1)} %get-tuple-element.28), channel_id=1, source_target_pairs={{0,1},{1,2},{2,3},{3,4},{4,5},{5,6},{6,7},{8,9},{9,10},{10,11},{11... | collective-permute-start | bytes 49160 | tf_op jit(solution)/shard_map/ppermute | solution.py:17
  43.6 1.3 collective-permute-start.1
  44.9 10.3 %all-to-all-done.4 = bf16[16,128,128]{2,1,0:T(8,128)(2,1)S(1)} async-done(((bf16[16,128,128]{2,1,0:T(8,128)(2,1)}), bf16[16,128,128]{2,1,0:T(8,128)(2,1)S(1)}, u32[]{:S(2)}, u32[]{:S(2)}) %all-to-all-start.4) | async-done | bytes 524320 | tf_op jit(solution)/shard_map/all_to_all | solution.py:149
  55.5 1.0 all_to_all.58
  56.5 17.2 %all-gather.2.cloned.1.call-done = bf16[2048,1152]{1,0:T(8,128)(2,1)} async-done(((bf16[512,1152]{1,0:T(8,128)(2,1)}), bf16[2048,1152]{1,0:T(8,128)(2,1)}) %all-gather.2.cloned.1.call-update) | async-done | bytes 4718608 | tf_op jit(solution)/shard_map/all_gather | solution.py:140
  73.8 1.7 fusion.92
  75.5 1.7 fusion.44
  77.2 1.5 fusion.49
  78.7 1.5 fusion.69
  80.2 1.5 fusion.41
  81.8 1.5 fusion.36
  83.3 1.5 fusion.64
  84.8 1.6 fusion.13
  86.4 2.8 %fusion.18 = bf16[16,128,128]{2,1,0:T(8,128)(2,1)} fusion(f32[128,16,128]{2,1,0:T(8,128)S(1)} %bitcast.109, f32[16,128,128]{2,1,0:T(8,128)S(1)} %fusion.64, f32[16,128,128]{2,1,0:T(8,128)S(1)} %fusion.36, f32[16,128,128]{2,1,0:T(8,128)S(1)} %fusion.41, f32[16,128,128]{2,1,0:T(8,128)S(1)} %fusion.13, bf16[16,4,128]{2,1,0:T(4,128)(2,1)S(1)} %collective-permute-done.1, ...), kind=kOutput, calls=%fused_computation.37 | convolution fusion | flops 71565312 | bytes 6832128 | tf_op jit(solution)/shard_map/gtc,goc->gto/dot_general | solution.py:40
  89.3 4.6 %all-to-all-start.3 = ((bf16[16,128,128]{2,1,0:T(8,128)(2,1)}), bf16[16,128,128]{2,1,0:T(8,128)(2,1)}, u32[]{:S(2)}, u32[]{:S(2)}) async-start(bf16[16,128,128]{2,1,0:T(8,128)(2,1)} %fusion.18), calls=%async_computation.3 | async-start | bytes 1048576 | tf_op jit(solution)/shard_map/all_to_all | solution.py:150
  93.9 0.8 fusion.147
  94.7 1.3 collective-permute-start.2
  96.0 1.7 fusion.90
  97.7 3.0 %collective-permute-start.3 = (bf16[16,4,128]{2,1,0:T(4,128)(2,1)S(1)}, bf16[16,4,128]{2,1,0:T(4,128)(2,1)S(1)}, u32[]{:S(2)}, u32[]{:S(2)}) collective-permute-start(bf16[16,4,128]{2,1,0:T(4,128)(2,1)S(1)} %get-tuple-element.27), channel_id=1, source_target_pairs={{0,1},{1,2},{2,3},{3,4},{4,5},{5,6},{6,7},{8,9},{9,10},{10,11},{11... | collective-permute-start | bytes 49160 | tf_op jit(solution)/shard_map/ppermute | solution.py:17
  100.7 1.7 fusion.33
  102.5 1.7 fusion.28
  104.2 1.7 fusion.59
  105.9 1.7 fusion.25
  107.6 1.7 fusion.20
  109.3 1.7 fusion.54
  111.1 1.7 fusion.7
  112.8 1.8 fusion.4
  114.6 0.3 copy.122
  115.2 0.7 copy-done.2
  116.0 0.4 fusion.16
  116.8 1.2 pad_maximum_fusion
  118.0 10.1 %all-to-all-start.1 = ((bf16[32,130,64]{1,2,0:T(8,128)(2,1)}), bf16[32,130,64]{1,2,0:T(8,128)(2,1)S(1)}, u32[]{:S(2)}, u32[]{:S(2)}) async-start(bf16[32,130,64]{1,2,0:T(8,128)(2,1)} %pad_maximum_fusion), calls=%async_computation.1 | async-start | bytes 2097152 | tf_op jit(solution)/shard_map/all_to_all | solution.py:107
  128.1 1.1 copy.110
  129.2 0.4 convolution_dynamic-update-slice_fusion.8
  129.6 0.4 convolution_dynamic-update-slice_fusion.7
  129.9 0.4 convolution_dynamic-update-slice_fusion.6
  130.3 0.4 convolution_dynamic-update-slice_fusion.5
  131.0 0.4 convolution_dynamic-update-slice_fusion.3
  131.3 0.4 convolution_dynamic-update-slice_fusion.2
  131.7 0.4 convolution_dynamic-update-slice_fusion.1
  132.1 0.4 convolution_dynamic-update-slice_fusion
  132.5 1.4 copy.112
  133.9 21.6 %all-to-all-done.1 = bf16[32,130,64]{1,2,0:T(8,128)(2,1)S(1)} async-done(((bf16[32,130,64]{1,2,0:T(8,128)(2,1)}), bf16[32,130,64]{1,2,0:T(8,128)(2,1)S(1)}, u32[]{:S(2)}, u32[]{:S(2)}) %all-to-all-start.1) | async-done | bytes 532512 | tf_op jit(solution)/shard_map/all_to_all | solution.py:107
  155.5 3.5 %all-to-all-start.5 = ((f32[4,64,1152]{2,1,0:T(8,128)}), f32[4,64,1152]{2,1,0:T(8,128)S(1)}, u32[]{:S(2)}, u32[]{:S(2)}) async-start(f32[4,64,1152]{2,1,0:T(8,128)} %bitcast.21), calls=%async_computation.5 | async-start | bytes 2359296 | tf_op jit(solution)/shard_map/all_to_all | solution.py:86
  159.7 0.9 fusion.14
  160.7 0.8 reshape.134
  161.5 12.7 %all-to-all-done.5 = f32[4,64,1152]{2,1,0:T(8,128)S(1)} async-done(((f32[4,64,1152]{2,1,0:T(8,128)}), f32[4,64,1152]{2,1,0:T(8,128)S(1)}, u32[]{:S(2)}, u32[]{:S(2)}) %all-to-all-start.5) | async-done | bytes 1179680 | tf_op jit(solution)/shard_map/all_to_all | solution.py:86
  174.2 2.6 %all-to-all-start.2 = ((f32[32,1,576]{2,1,0:T(1,128)}), f32[32,1,576]{2,1,0:T(1,128)S(1)}, u32[]{:S(2)}, u32[]{:S(2)}) async-start(f32[32,1,576]{2,1,0:T(1,128)} %reshape.134), calls=%async_computation.2 | async-start | bytes 163840 | tf_op jit(solution)/shard_map/all_to_all | solution.py:117
  176.8 7.5 %all-to-all-done.2 = f32[32,1,576]{2,1,0:T(1,128)S(1)} async-done(((f32[32,1,576]{2,1,0:T(1,128)}), f32[32,1,576]{2,1,0:T(1,128)S(1)}, u32[]{:S(2)}, u32[]{:S(2)}) %all-to-all-start.2) | async-done | bytes 73760 | tf_op jit(solution)/shard_map/all_to_all | solution.py:117
  184.3 1.1 tile.5
  185.4 3.5 %all-to-all-start.6 = ((f32[4,64,1152]{2,1,0:T(8,128)}), f32[4,64,1152]{2,1,0:T(8,128)S(1)}, u32[]{:S(2)}, u32[]{:S(2)}) async-start(f32[4,64,1152]{2,1,0:T(8,128)} %tile.5), calls=%async_computation.6 | async-start | bytes 2359296 | tf_op jit(solution)/shard_map/all_to_all | solution.py:33
  189.0 0.5 broadcast.67
  189.5 0.8 reduce.7
  190.5 0.7 reshape.122
  191.2 0.6 slice_reduce_fusion
  191.7 12.8 %all-to-all-done.6 = f32[4,64,1152]{2,1,0:T(8,128)S(1)} async-done(((f32[4,64,1152]{2,1,0:T(8,128)}), f32[4,64,1152]{2,1,0:T(8,128)S(1)}, u32[]{:S(2)}, u32[]{:S(2)}) %all-to-all-start.6) | async-done | bytes 1179680 | tf_op jit(solution)/shard_map/all_to_all | solution.py:33
  204.5 1.0 copy.143
  (47 shorter events, 2.9 us)
Async XLA Ops:
  7.2 26.1 %copy-start.7 = (s32[1,128]{1,0:T(1,128)S(1)}, s32[1,128]{1,0:T(1,128)}, u32[]{:S(2)}) copy-start(s32[1,128]{1,0:T(1,128)} %param.11) | copy-start | bytes 1540
  7.2 26.1 %copy-start.5 = (bf16[1,128,2048]{2,1,0:T(8,128)(2,1)S(1)}, bf16[1,128,2048]{2,1,0:T(8,128)(2,1)}, u32[]{:S(2)}) copy-start(bf16[1,128,2048]{2,1,0:T(8,128)(2,1)} %param.10) | copy-start | bytes 1572868
  7.2 66.6 %all-gather.2.cloned.1.call-start = ((), (), s32[]{:S(2)}) async-start(), calls=%async_computation.7 | async-start | bytes 5898240 | tf_op jit(solution)/shard_map/all_gather | solution.py:140
  9.0 24.7 %copy-start.6 = (f32[2048]{0:T(1024)S(1)}, f32[2048]{0:T(1024)}, u32[]{:S(2)}) copy-start(f32[2048]{0:T(1024)} %param.13) | copy-start | bytes 24580
  33.2 6.6 %copy-start.1 = (bf16[1,128,2048]{2,1,0:T(8,128)(2,1)S(1)}, bf16[1,128,2048]{2,1,0:T(8,128)(2,1)}, u32[]{:S(2)}) copy-start(bf16[1,128,2048]{2,1,0:T(8,128)(2,1)} %param.15) | copy-start | bytes 1572868
  34.7 20.5 %all-to-all-start.4 = ((bf16[16,128,128]{2,1,0:T(8,128)(2,1)}), bf16[16,128,128]{2,1,0:T(8,128)(2,1)S(1)}, u32[]{:S(2)}, u32[]{:S(2)}) async-start(bf16[16,128,128]{2,1,0:T(8,128)(2,1)} %bitcast_bitcast_fusion), calls=%async_computation.4 | async-start | bytes 1048576 | tf_op jit(solution)/shard_map/all_to_all | solution.py:149
  41.2 34.3 %collective-permute-start = (bf16[16,4,128]{2,1,0:T(4,128)(2,1)S(1)}, bf16[16,4,128]{2,1,0:T(4,128)(2,1)S(1)}, u32[]{:S(2)}, u32[]{:S(2)}) collective-permute-start(bf16[16,4,128]{2,1,0:T(4,128)(2,1)S(1)} %get-tuple-element.28), channel_id=1, source_target_pairs={{0,1},{1,2},{2,3},{3,4},{4,5},{5,6},{6,7},{8,9},{9,10},{10,11},{11... | collective-permute-start | bytes 49160 | tf_op jit(solution)/shard_map/ppermute | solution.py:17
  43.6 36.6 %collective-permute-start.1 = (bf16[16,4,128]{2,1,0:T(4,128)(2,1)S(1)}, bf16[16,4,128]{2,1,0:T(4,128)(2,1)S(1)}, u32[]{:S(2)}, u32[]{:S(2)}) collective-permute-start(bf16[16,4,128]{2,1,0:T(4,128)(2,1)S(1)} %get-tuple-element.29), channel_id=1, source_target_pairs={{1,0},{2,1},{3,2},{4,3},{5,4},{6,5},{7,6},{9,8},{10,9},{11,10},{12... | collective-permute-start | bytes 49160 | tf_op jit(solution)/shard_map/ppermute | solution.py:19
  73.8 3.4 %copy-start = (bf16[2048,1152]{1,0:T(8,128)(2,1)S(1)}, bf16[2048,1152]{1,0:T(8,128)(2,1)}, u32[]{:S(2)}) copy-start(bf16[2048,1152]{1,0:T(8,128)(2,1)} %all-gather.2.cloned.1.call-done) | copy-start | bytes 14155780
  89.3 28.7 %all-to-all-start.3 = ((bf16[16,128,128]{2,1,0:T(8,128)(2,1)}), bf16[16,128,128]{2,1,0:T(8,128)(2,1)}, u32[]{:S(2)}, u32[]{:S(2)}) async-start(bf16[16,128,128]{2,1,0:T(8,128)(2,1)} %fusion.18), calls=%async_computation.3 | async-start | bytes 1048576 | tf_op jit(solution)/shard_map/all_to_all | solution.py:150
  94.7 6.1 %collective-permute-start.2 = (bf16[16,4,128]{2,1,0:T(4,128)(2,1)S(1)}, bf16[16,4,128]{2,1,0:T(4,128)(2,1)S(1)}, u32[]{:S(2)}, u32[]{:S(2)}) collective-permute-start(bf16[16,4,128]{2,1,0:T(4,128)(2,1)S(1)} %get-tuple-element.26), channel_id=1, source_target_pairs={{1,0},{2,1},{3,2},{4,3},{5,4},{6,5},{7,6},{9,8},{10,9},{11,10},{12... | collective-permute-start | bytes 49160 | tf_op jit(solution)/shard_map/ppermute | solution.py:19
  97.7 8.2 %collective-permute-start.3 = (bf16[16,4,128]{2,1,0:T(4,128)(2,1)S(1)}, bf16[16,4,128]{2,1,0:T(4,128)(2,1)S(1)}, u32[]{:S(2)}, u32[]{:S(2)}) collective-permute-start(bf16[16,4,128]{2,1,0:T(4,128)(2,1)S(1)} %get-tuple-element.27), channel_id=1, source_target_pairs={{0,1},{1,2},{2,3},{3,4},{4,5},{5,6},{6,7},{8,9},{9,10},{10,11},{11... | collective-permute-start | bytes 49160 | tf_op jit(solution)/shard_map/ppermute | solution.py:17
  114.9 1.0 copy-start.2
  116.4 1.7 copy-start.4
  118.0 11.2 %copy-start.3 = (bf16[2,1024,128]{1,2,0:T(8,128)(2,1)S(1)}, bf16[2,1024,128]{1,2,0:T(8,128)(2,1)}, u32[]{:S(2)}) copy-start(bf16[2,1024,128]{1,2,0:T(8,128)(2,1)} %all_to_all.58) | copy-start | bytes 1572868
  118.0 37.5 %all-to-all-start.1 = ((bf16[32,130,64]{1,2,0:T(8,128)(2,1)}), bf16[32,130,64]{1,2,0:T(8,128)(2,1)S(1)}, u32[]{:S(2)}, u32[]{:S(2)}) async-start(bf16[32,130,64]{1,2,0:T(8,128)(2,1)} %pad_maximum_fusion), calls=%async_computation.1 | async-start | bytes 2097152 | tf_op jit(solution)/shard_map/all_to_all | solution.py:107
  155.5 18.7 %all-to-all-start.5 = ((f32[4,64,1152]{2,1,0:T(8,128)}), f32[4,64,1152]{2,1,0:T(8,128)S(1)}, u32[]{:S(2)}, u32[]{:S(2)}) async-start(f32[4,64,1152]{2,1,0:T(8,128)} %bitcast.21), calls=%async_computation.5 | async-start | bytes 2359296 | tf_op jit(solution)/shard_map/all_to_all | solution.py:86
  174.2 10.2 %all-to-all-start.2 = ((f32[32,1,576]{2,1,0:T(1,128)}), f32[32,1,576]{2,1,0:T(1,128)S(1)}, u32[]{:S(2)}, u32[]{:S(2)}) async-start(f32[32,1,576]{2,1,0:T(1,128)} %reshape.134), calls=%async_computation.2 | async-start | bytes 163840 | tf_op jit(solution)/shard_map/all_to_all | solution.py:117
  185.4 19.1 %all-to-all-start.6 = ((f32[4,64,1152]{2,1,0:T(8,128)}), f32[4,64,1152]{2,1,0:T(8,128)S(1)}, u32[]{:S(2)}, u32[]{:S(2)}) async-start(f32[4,64,1152]{2,1,0:T(8,128)} %tile.5), calls=%async_computation.6 | async-start | bytes 2359296 | tf_op jit(solution)/shard_map/all_to_all | solution.py:33
Sparse Core Ops, SparseCore 0:
  9.9 63.8 all-gather.1

commit v4 on v3

--- a/solution.py
+++ b/solution.py
@@ -163,7 +163,7 @@
     scaled = norm_gain * dnormed
     dmixed = inv * scaled - mixed * inv * inv * inv * jnp.mean(scaled * mixed, axis=-1, keepdims=True)
     input_grad = (up_float + dmixed).astype(jnp.bfloat16)
-    kernel_grad = psum_rows(kernel_part, "fsdp")
+    kernel_grad = lax.psum(kernel_part, "fsdp")
     table_grad, gain_grad = table_and_gain(input_grad, type_ids[0], gain_term, types, scale)
     return (input_grad[None], table_grad, gain_grad, kernel_grad)
 

time: 214 us -> 204 us (0.953)
  blocking collectives: 24.2 us -> 33.9 us
  waiting for transfers between devices: 82.9 us -> 73.3 us
  starting transfers between devices: 37.5 us -> 28 us
    all_to_all x3 -> x0, waiting for transfers between devices: 33 us -> none  [the longest x1 12.8 us: gather_rows(): lax.all_to_all(jnp.tile(block, (count,) + (1,) * (block.ndim - 1)), axis,...]
    psum x0 -> x1, waiting for transfers between devices: none -> 23.7 us  [body(): kernel_grad = lax.psum(kernel_part, 'fsdp')]
    all_to_all x3 -> x0, starting transfers between devices: 9.63 us -> none  [the longest x1 3.53 us: sum_rows(): return lax.all_to_all(parts, axis, 0, 0, tiled=True).sum(axis=0)]
    all_to_all x0 -> x1, blocking collectives: none -> 9.6 us  [table_and_gain(): back = lax.all_to_all(back, every, 0, 0, tiled=True)]
  transfers between devices with their start and end apart: 11 -> 9, of which waited for: 6 -> 4; matrix products, arithmetic and copies ran while one was open for 19% -> 20% of each run, Pallas kernels for 0% -> 0%
where the time goes in v4:
time: 204 us; the launch traced here: 203 us
  waiting for transfers between devices  73.3 us (36%)
  matrix products  35.4 us (17%)
  blocking collectives  33.9 us (17%)
  starting transfers between devices  28 us (14%)
  between operations  14.5 us (7%)
  local copies, waits for them, and re-layouts  12.2 us (6%)
  other arithmetic  5.63 us (3%)
    all_to_all x1, blocking collectives, gather_rows(): lax.all_to_all(jnp.tile(block, (count,) + (1,) * (block.ndim - 1)), axis,...  24.3 us
    psum x1, waiting for transfers between devices, body(): kernel_grad = lax.psum(kernel_part, 'fsdp')  23.7 us
    all_to_all x1, waiting for transfers between devices, table_and_gain(): got = lax.all_to_all(send, every, 0, 0, tiled=True)  21.5 us
    all_gather x1, waiting for transfers between devices, body(): lax.all_gather(kernel, 'fsdp', axis=0, tiled=True)  17.2 us
    dot_general x9, matrix products, conv_backward(): jnp.einsum('gto,goc->gtc', dpad[:, 2 * half - k:2 * half - k + length], w...  15.5 us
    dot_general x9, matrix products, conv_forward(): jnp.einsum('gtc,goc->gto', padded[:, k:k + length], weights[:, :, k * cha...  15.4 us
    all_to_all x1, waiting for transfers between devices, body(): group_in = lax.all_to_all(normed_g, 'seq', 0, 1, tiled=True)  10.3 us
    all_to_all x1, starting transfers between devices, table_and_gain(): got = lax.all_to_all(send, every, 0, 0, tiled=True)  9.92 us
  transfers between devices with their start and end apart: 9, of which 4 were waited for; matrix products, arithmetic and copies ran while one was open for 20% of the time, Pallas kernels for 0%

profile of v4, /device:TPU:0, one launch (start us, length us, event | category | flops | bytes accessed | tf_op | source)
XLA Modules:
  0.0 202.8 jit_solution(586247132597513163)
XLA Ops:
  7.2 0.7 all-gather.2.cloned.1.call-update
  7.9 1.1 tile.2
  9.1 24.3 %all_to_all.55 = bf16[4,64,2048]{2,1,0:T(8,128)(2,1)S(1)} all-to-all(bf16[4,64,2048]{2,1,0:T(8,128)(2,1)S(1)} %tile.2), channel_id=1, replica_groups=mesh['fsdp'=4,'seq'=8] {'fsdp'}, dimensions={0} | all-to-all | bytes 2097152 | tf_op jit(solution)/shard_map/all_to_all | solution.py:33
  33.4 0.4 multiply_reduce_fusion.2
  33.8 1.0 bitcast_bitcast_fusion
  34.8 5.2 %all-to-all-start.4 = ((bf16[16,128,128]{2,1,0:T(8,128)(2,1)}), bf16[16,128,128]{2,1,0:T(8,128)(2,1)S(1)}, u32[]{:S(2)}, u32[]{:S(2)}) async-start(bf16[16,128,128]{2,1,0:T(8,128)(2,1)} %bitcast_bitcast_fusion), calls=%async_computation.4 | async-start | bytes 1048576 | tf_op jit(solution)/shard_map/all_to_all | solution.py:149
  40.1 0.2 copy.126
  40.5 0.8 fusion.148
  41.3 2.4 %collective-permute-start = (bf16[16,4,128]{2,1,0:T(4,128)(2,1)S(1)}, bf16[16,4,128]{2,1,0:T(4,128)(2,1)S(1)}, u32[]{:S(2)}, u32[]{:S(2)}) collective-permute-start(bf16[16,4,128]{2,1,0:T(4,128)(2,1)S(1)} %get-tuple-element.28), channel_id=1, source_target_pairs={{0,1},{1,2},{2,3},{3,4},{4,5},{5,6},{6,7},{8,9},{9,10},{10,11},{11... | collective-permute-start | bytes 49160 | tf_op jit(solution)/shard_map/ppermute | solution.py:17
  43.7 1.3 collective-permute-start.1
  45.0 10.3 %all-to-all-done.4 = bf16[16,128,128]{2,1,0:T(8,128)(2,1)S(1)} async-done(((bf16[16,128,128]{2,1,0:T(8,128)(2,1)}), bf16[16,128,128]{2,1,0:T(8,128)(2,1)S(1)}, u32[]{:S(2)}, u32[]{:S(2)}) %all-to-all-start.4) | async-done | bytes 524320 | tf_op jit(solution)/shard_map/all_to_all | solution.py:149
  55.3 0.3 copy.111
  55.6 1.0 all_to_all.49
  56.7 17.2 %all-gather.2.cloned.1.call-done = bf16[2048,1152]{1,0:T(8,128)(2,1)} async-done(((bf16[512,1152]{1,0:T(8,128)(2,1)}), bf16[2048,1152]{1,0:T(8,128)(2,1)}) %all-gather.2.cloned.1.call-update) | async-done | bytes 4718608 | tf_op jit(solution)/shard_map/all_gather | solution.py:140
  73.8 1.7 fusion.92
  75.6 1.7 fusion.44
  77.2 1.5 fusion.49
  78.8 1.5 fusion.69
  80.3 1.5 fusion.41
  81.8 1.5 fusion.36
  83.4 1.5 fusion.64
  84.9 1.6 fusion.13
  86.5 2.8 %fusion.18 = bf16[16,128,128]{2,1,0:T(8,128)(2,1)} fusion(f32[128,16,128]{2,1,0:T(8,128)S(1)} %bitcast.108, f32[16,128,128]{2,1,0:T(8,128)S(1)} %fusion.64, f32[16,128,128]{2,1,0:T(8,128)S(1)} %fusion.36, f32[16,128,128]{2,1,0:T(8,128)S(1)} %fusion.41, f32[16,128,128]{2,1,0:T(8,128)S(1)} %fusion.13, bf16[16,4,128]{2,1,0:T(4,128)(2,1)S(1)} %collective-permute-done.1, ...), kind=kOutput, calls=%fused_computation.37 | convolution fusion | flops 71565312 | bytes 6832128 | tf_op jit(solution)/shard_map/gtc,goc->gto/dot_general | solution.py:40
  89.3 4.6 %all-to-all-start.3 = ((bf16[16,128,128]{2,1,0:T(8,128)(2,1)}), bf16[16,128,128]{2,1,0:T(8,128)(2,1)}, u32[]{:S(2)}, u32[]{:S(2)}) async-start(bf16[16,128,128]{2,1,0:T(8,128)(2,1)} %fusion.18), calls=%async_computation.3 | async-start | bytes 1048576 | tf_op jit(solution)/shard_map/all_to_all | solution.py:150
  93.9 0.8 fusion.147
  94.8 1.3 collective-permute-start.2
  96.1 1.7 fusion.90
  97.8 3.0 %collective-permute-start.3 = (bf16[16,4,128]{2,1,0:T(4,128)(2,1)S(1)}, bf16[16,4,128]{2,1,0:T(4,128)(2,1)S(1)}, u32[]{:S(2)}, u32[]{:S(2)}) collective-permute-start(bf16[16,4,128]{2,1,0:T(4,128)(2,1)S(1)} %get-tuple-element.27), channel_id=1, source_target_pairs={{0,1},{1,2},{2,3},{3,4},{4,5},{5,6},{6,7},{8,9},{9,10},{10,11},{11... | collective-permute-start | bytes 49160 | tf_op jit(solution)/shard_map/ppermute | solution.py:17
  100.8 1.7 fusion.33
  102.5 1.7 fusion.28
  104.3 1.7 fusion.59
  106.0 1.7 fusion.25
  107.7 1.7 fusion.20
  109.4 1.7 fusion.54
  111.1 1.7 fusion.7
  112.9 1.8 fusion.4
  114.6 0.3 copy.122
  115.0 0.3 multiply_reduce_fusion
  115.3 1.4 fusion.16
  116.7 0.3 copy.102
  117.1 1.3 pad_maximum_fusion
  118.4 9.9 %all-to-all-start.1 = ((bf16[32,130,64]{1,2,0:T(8,128)(2,1)}), bf16[32,130,64]{1,2,0:T(8,128)(2,1)S(1)}, u32[]{:S(2)}, u32[]{:S(2)}) async-start(bf16[32,130,64]{1,2,0:T(8,128)(2,1)} %pad_maximum_fusion), calls=%async_computation.1 | async-start | bytes 2097152 | tf_op jit(solution)/shard_map/all_to_all | solution.py:107
  128.3 0.2 all-reduce.3.cloned.1.call-start
  128.6 1.1 copy.110
  129.6 0.4 convolution_dynamic-update-slice_fusion.8
  130.0 0.4 convolution_dynamic-update-slice_fusion.7
  130.4 0.4 convolution_dynamic-update-slice_fusion.6
  130.7 0.4 convolution_dynamic-update-slice_fusion.5
  131.1 0.3 convolution_dynamic-update-slice_fusion.4
  131.4 0.4 convolution_dynamic-update-slice_fusion.3
  131.8 0.4 convolution_dynamic-update-slice_fusion.2
  132.1 0.4 convolution_dynamic-update-slice_fusion.1
  132.5 0.4 convolution_dynamic-update-slice_fusion
  133.0 1.4 copy.112
  134.5 21.5 %all-to-all-done.1 = bf16[32,130,64]{1,2,0:T(8,128)(2,1)S(1)} async-done(((bf16[32,130,64]{1,2,0:T(8,128)(2,1)}), bf16[32,130,64]{1,2,0:T(8,128)(2,1)S(1)}, u32[]{:S(2)}, u32[]{:S(2)}) %all-to-all-start.1) | async-done | bytes 532512 | tf_op jit(solution)/shard_map/all_to_all | solution.py:107
  156.0 0.3 copy.123
  156.4 0.9 fusion.14
  157.6 9.6 %all_to_all.56 = f32[32,1,576]{2,1,0:T(1,128)S(1)} all-to-all(f32[32,1,576]{2,1,0:T(1,128)S(1)} %reshape.125), channel_id=1, replica_groups=mesh['fsdp'=4,'seq'=8] {'fsdp','seq'}, dimensions={0} | all-to-all | bytes 147456 | tf_op jit(solution)/shard_map/all_to_all | solution.py:117
  167.2 0.5 broadcast.63
  167.7 0.8 reduce.7
  168.7 0.7 reshape.113
  169.4 0.6 slice_reduce_fusion
  170.0 23.7 %all-reduce.3.cloned.1.call-done = f32[256,1152]{1,0:T(8,128)} async-done(((f32[256,1152]{1,0:T(8,128)}), f32[256,1152]{1,0:T(8,128)}) %all-reduce.3.cloned.1.call-update) | async-done | bytes 1179664 | tf_op jit(solution)/shard_map/psum | solution.py:166
  193.6 2.4 %copy.143 = f32[256,1152]{1,0:T(8,128)} copy(f32[256,1152]{1,0:T(8,128)} %all-reduce.3.cloned.1.call-done) | data formatting | bytes 2359296
  (41 shorter events, 1.3 us)
Async XLA Ops:
  7.2 26.2 %copy-start.6 = (s32[1,128]{1,0:T(1,128)S(1)}, s32[1,128]{1,0:T(1,128)}, u32[]{:S(2)}) copy-start(s32[1,128]{1,0:T(1,128)} %param.11) | copy-start | bytes 1540
  7.2 26.2 %copy-start.4 = (bf16[1,128,2048]{2,1,0:T(8,128)(2,1)S(1)}, bf16[1,128,2048]{2,1,0:T(8,128)(2,1)}, u32[]{:S(2)}) copy-start(bf16[1,128,2048]{2,1,0:T(8,128)(2,1)} %param.10) | copy-start | bytes 1572868
  7.2 26.6 %copy-start.5 = (f32[2048]{0:T(1024)S(1)}, f32[2048]{0:T(1024)}, u32[]{:S(2)}) copy-start(f32[2048]{0:T(1024)} %param.13) | copy-start | bytes 24580
  7.2 66.6 %all-gather.2.cloned.1.call-start = ((), (), s32[]{:S(2)}) async-start(), calls=%async_computation.5 | async-start | bytes 5898240 | tf_op jit(solution)/shard_map/all_gather | solution.py:140
  7.9 32.0 %copy-start.1 = (bf16[1,128,2048]{2,1,0:T(8,128)(2,1)S(1)}, bf16[1,128,2048]{2,1,0:T(8,128)(2,1)}, u32[]{:S(2)}) copy-start(bf16[1,128,2048]{2,1,0:T(8,128)(2,1)} %param.15) | copy-start | bytes 1572868
  34.8 20.5 %all-to-all-start.4 = ((bf16[16,128,128]{2,1,0:T(8,128)(2,1)}), bf16[16,128,128]{2,1,0:T(8,128)(2,1)S(1)}, u32[]{:S(2)}, u32[]{:S(2)}) async-start(bf16[16,128,128]{2,1,0:T(8,128)(2,1)} %bitcast_bitcast_fusion), calls=%async_computation.4 | async-start | bytes 1048576 | tf_op jit(solution)/shard_map/all_to_all | solution.py:149
  41.3 34.3 %collective-permute-start = (bf16[16,4,128]{2,1,0:T(4,128)(2,1)S(1)}, bf16[16,4,128]{2,1,0:T(4,128)(2,1)S(1)}, u32[]{:S(2)}, u32[]{:S(2)}) collective-permute-start(bf16[16,4,128]{2,1,0:T(4,128)(2,1)S(1)} %get-tuple-element.28), channel_id=1, source_target_pairs={{0,1},{1,2},{2,3},{3,4},{4,5},{5,6},{6,7},{8,9},{9,10},{10,11},{11... | collective-permute-start | bytes 49160 | tf_op jit(solution)/shard_map/ppermute | solution.py:17
  43.7 36.6 %collective-permute-start.1 = (bf16[16,4,128]{2,1,0:T(4,128)(2,1)S(1)}, bf16[16,4,128]{2,1,0:T(4,128)(2,1)S(1)}, u32[]{:S(2)}, u32[]{:S(2)}) collective-permute-start(bf16[16,4,128]{2,1,0:T(4,128)(2,1)S(1)} %get-tuple-element.29), channel_id=1, source_target_pairs={{1,0},{2,1},{3,2},{4,3},{5,4},{6,5},{7,6},{9,8},{10,9},{11,10},{12... | collective-permute-start | bytes 49160 | tf_op jit(solution)/shard_map/ppermute | solution.py:19
  73.8 3.4 %copy-start = (bf16[2048,1152]{1,0:T(8,128)(2,1)S(1)}, bf16[2048,1152]{1,0:T(8,128)(2,1)}, u32[]{:S(2)}) copy-start(bf16[2048,1152]{1,0:T(8,128)(2,1)} %all-gather.2.cloned.1.call-done) | copy-start | bytes 14155780
  89.3 29.1 %all-to-all-start.3 = ((bf16[16,128,128]{2,1,0:T(8,128)(2,1)}), bf16[16,128,128]{2,1,0:T(8,128)(2,1)}, u32[]{:S(2)}, u32[]{:S(2)}) async-start(bf16[16,128,128]{2,1,0:T(8,128)(2,1)} %fusion.18), calls=%async_computation.3 | async-start | bytes 1048576 | tf_op jit(solution)/shard_map/all_to_all | solution.py:150
  94.8 6.1 %collective-permute-start.2 = (bf16[16,4,128]{2,1,0:T(4,128)(2,1)S(1)}, bf16[16,4,128]{2,1,0:T(4,128)(2,1)S(1)}, u32[]{:S(2)}, u32[]{:S(2)}) collective-permute-start(bf16[16,4,128]{2,1,0:T(4,128)(2,1)S(1)} %get-tuple-element.26), channel_id=1, source_target_pairs={{1,0},{2,1},{3,2},{4,3},{5,4},{6,5},{7,6},{9,8},{10,9},{11,10},{12... | collective-permute-start | bytes 49160 | tf_op jit(solution)/shard_map/ppermute | solution.py:19
  97.8 8.2 %collective-permute-start.3 = (bf16[16,4,128]{2,1,0:T(4,128)(2,1)S(1)}, bf16[16,4,128]{2,1,0:T(4,128)(2,1)S(1)}, u32[]{:S(2)}, u32[]{:S(2)}) collective-permute-start(bf16[16,4,128]{2,1,0:T(4,128)(2,1)S(1)} %get-tuple-element.27), channel_id=1, source_target_pairs={{0,1},{1,2},{2,3},{3,4},{4,5},{5,6},{6,7},{8,9},{9,10},{10,11},{11... | collective-permute-start | bytes 49160 | tf_op jit(solution)/shard_map/ppermute | solution.py:17
  116.7 13.7 %copy-start.3 = (bf16[128,2048]{1,0:T(8,128)(2,1)}, bf16[128,2048]{1,0:T(8,128)(2,1)S(1)}, u32[]{:S(2)}) copy-start(bf16[128,2048]{1,0:T(8,128)(2,1)S(1)} %fusion.16) | copy-start | bytes 1572868
  116.7 12.9 %copy-start.2 = (bf16[2,1024,128]{1,2,0:T(8,128)(2,1)S(1)}, bf16[2,1024,128]{1,2,0:T(8,128)(2,1)}, u32[]{:S(2)}) copy-start(bf16[2,1024,128]{1,2,0:T(8,128)(2,1)} %all_to_all.49) | copy-start | bytes 1572868
  118.4 37.5 %all-to-all-start.1 = ((bf16[32,130,64]{1,2,0:T(8,128)(2,1)}), bf16[32,130,64]{1,2,0:T(8,128)(2,1)S(1)}, u32[]{:S(2)}, u32[]{:S(2)}) async-start(bf16[32,130,64]{1,2,0:T(8,128)(2,1)} %pad_maximum_fusion), calls=%async_computation.1 | async-start | bytes 2097152 | tf_op jit(solution)/shard_map/all_to_all | solution.py:107
  128.3 65.3 %all-reduce.3.cloned.1.call-start = ((), (), s32[]{:S(2)}) async-start(), calls=%async_computation.6 | async-start | bytes 2359296 | tf_op jit(solution)/shard_map/psum | solution.py:166
Sparse Core Ops, SparseCore 0:
  9.9 63.9 all-gather.1
  134.5 59.0 all-reduce.2

commit v5 on v4

--- a/solution.py
+++ b/solution.py
@@ -1,6 +1,8 @@
 import jax
 import jax.numpy as jnp
 from jax import lax
+from jax.experimental import pallas as pl
+from jax.experimental.pallas import tpu as pltpu
 from jax.sharding import PartitionSpec as P
 
 GROUPS = 16
@@ -33,33 +35,79 @@
     return lax.all_to_all(jnp.tile(block, (count,) + (1,) * (block.ndim - 1)), axis, 0, 0, tiled=True)
 
 
-def conv_forward(padded, weights, length):
-    chans = padded.shape[-1]
-    total = None
-    for k in range(KERNEL):
-        term = jnp.einsum(
-            "gtc,goc->gto",
-            padded[:, k : k + length],
-            weights[:, :, k * chans : (k + 1) * chans],
-            preferred_element_type=jnp.float32,
-        )
-        total = term if total is None else total + term
-    return total
-
-
-def conv_backward(dpad, weights, length):
-    chans = weights.shape[-1] // KERNEL
+STEP_GROUPS = 4
+
+
+def forward_kernel(pad_ref, w_ref, up_ref, out_ref):
+    length = out_ref.shape[1]
+    chans = pad_ref.shape[2]
+    for g in range(out_ref.shape[0]):
+        acc = None
+        for k in range(KERNEL):
+            x = pad_ref[g, k : k + length, :].astype(jnp.bfloat16)
+            w = w_ref[g, :, k * chans : (k + 1) * chans]
+            term = lax.dot_general(x, w, (((1,), (1,)), ((), ())), preferred_element_type=jnp.float32)
+            acc = term if acc is None else acc + term
+        sig = 1.0 / (1.0 + jnp.exp(-acc))
+        out_ref[g] = (up_ref[g] * sig * (1.0 + acc * (1.0 - sig))).astype(out_ref.dtype)
+
+
+def backward_kernel(pad_ref, w_ref, out_ref):
+    length = out_ref.shape[1]
+    chans = out_ref.shape[2]
     half = KERNEL // 2
-    total = None
-    for k in range(KERNEL):
-        term = jnp.einsum(
-            "gto,goc->gtc",
-            dpad[:, 2 * half - k : 2 * half - k + length],
-            weights[:, :, k * chans : (k + 1) * chans],
-            preferred_element_type=jnp.float32,
-        )
-        total = term if total is None else total + term
-    return total
+    for g in range(out_ref.shape[0]):
+        acc = None
+        for k in range(KERNEL):
+            x = pad_ref[g, 2 * half - k : 2 * half - k + length, :].astype(jnp.bfloat16)
+            w = w_ref[g, :, k * chans : (k + 1) * chans]
+            term = jnp.dot(x, w, preferred_element_type=jnp.float32)
+            acc = term if acc is None else acc + term
+        out_ref[g] = acc
+
+
+def conv_dconv(padded, weights, up):
+    groups, rows, chans = padded.shape
+    length = up.shape[1]
+    step = STEP_GROUPS if groups % STEP_GROUPS == 0 else 1
+    flops = 2 * groups * length * chans * weights.shape[1] * KERNEL
+    return pl.pallas_call(
+        forward_kernel,
+        grid=(groups // step,),
+        in_specs=[
+            pl.BlockSpec((step, rows, chans), lambda i: (i, 0, 0)),
+            pl.BlockSpec((step, weights.shape[1], weights.shape[2]), lambda i: (i, 0, 0)),
+            pl.BlockSpec((step, length, up.shape[2]), lambda i: (i, 0, 0)),
+        ],
+        out_specs=pl.BlockSpec((step, length, up.shape[2]), lambda i: (i, 0, 0)),
+        out_shape=jax.ShapeDtypeStruct(up.shape, jnp.bfloat16),
+        cost_estimate=pl.CostEstimate(
+            flops=flops,
+            transcendentals=up.size,
+            bytes_accessed=padded.size * 4 + weights.size * 2 + up.size * 6,
+        ),
+    )(padded, weights, up)
+
+
+def conv_transpose(dpad, weights, length):
+    groups, rows, outs = dpad.shape
+    chans = weights.shape[2] // KERNEL
+    step = STEP_GROUPS if groups % STEP_GROUPS == 0 else 1
+    return pl.pallas_call(
+        backward_kernel,
+        grid=(groups // step,),
+        in_specs=[
+            pl.BlockSpec((step, rows, outs), lambda i: (i, 0, 0)),
+            pl.BlockSpec((step, weights.shape[1], weights.shape[2]), lambda i: (i, 0, 0)),
+        ],
+        out_specs=pl.BlockSpec((step, length, chans), lambda i: (i, 0, 0)),
+        out_shape=jax.ShapeDtypeStruct((groups, length, chans), jnp.float32),
+        cost_estimate=pl.CostEstimate(
+            flops=2 * groups * length * chans * outs * KERNEL,
+            transcendentals=0,
+            bytes_accessed=dpad.size * 4 + weights.size * 2 + groups * length * chans * 4,
+        ),
+    )(dpad, weights)
 
 
 def spread_groups(normed, dflat, chans):
@@ -138,13 +186,11 @@
     normed_g = normed.reshape(length, GROUPS, chans).transpose(1, 0, 2)
     padded = with_halo(normed_g, "seq", 1, half)
     weights = lax.all_gather(kernel, "fsdp", axis=0, tiled=True).reshape(GROUPS, chans, KERNEL * chans)
-    conv = conv_forward(padded, weights, length)
     up_float = upstream[0].astype(jnp.float32)
     up_g = up_float.reshape(length, GROUPS, chans).transpose(1, 0, 2)
-    sig = jax.nn.sigmoid(conv)
-    dconv = (up_g * sig * (1.0 + conv * (1.0 - sig))).astype(jnp.bfloat16)
+    dconv = conv_dconv(padded.astype(jnp.float32), weights, up_g)
     dpad = with_halo(dconv, "seq", 1, half)
-    dnormed = conv_backward(dpad, weights, length)
+    dnormed = conv_transpose(dpad.astype(jnp.float32), weights, length)
     if seq_count <= GROUPS:
         group_in = lax.all_to_all(normed_g, "seq", 0, 1, tiled=True)
         group_out = lax.all_to_all(dconv, "seq", 0, 1, tiled=True)

time: 204 us -> 185 us (0.907)
  matrix products: 35.4 us -> 4.46 us
  Pallas kernels: 0 us -> 11.7 us
  starting transfers between devices: 28 us -> 21.1 us
  local copies, waits for them, and re-layouts: 12.2 us -> 16.6 us
    dot_general x18 -> x0, matrix products: 31 us -> none  [the longest x9 15.5 us: conv_backward(): jnp.einsum('gto,goc->gtc', dpad[:, 2 * half - k:2 * half - k + length], w...]
    pallas_call x0 -> x2, Pallas kernels: none -> 11.7 us  [the longest x1 6.55 us: conv_dconv(): pl.pallas_call(forward_kernel, grid=(groups // step,), in_specs=[pl.Block...]
    all_to_all x1, waiting for transfers between devices: 10.3 us -> 0.01 us  [body(): group_in = lax.all_to_all(normed_g, 'seq', 0, 1, tiled=True)]
    all_gather x1, waiting for transfers between devices: 17.2 us -> 24.8 us  [body(): lax.all_gather(kernel, 'fsdp', axis=0, tiled=True)]
    all_to_all x1, starting transfers between devices: 9.92 us -> 2.64 us  [table_and_gain(): got = lax.all_to_all(send, every, 0, 0, tiled=True)]
    all_to_all x1, waiting for transfers between devices: 0.01 us -> 4.12 us  [body(): group_out = lax.all_to_all(dconv, 'seq', 0, 1, tiled=True)]
    convert_element_type x0 -> x3, other arithmetic: none -> 3.54 us  [the longest x1 2.27 us: body(): dconv = conv_dconv(padded.astype(jnp.float32), weights, up_g)]
    transpose x0 -> x2, local copies, waits for them, and re-layouts: none -> 2.9 us  [the longest x1 1.55 us: body(): dnormed = dnormed.transpose(1, 0, 2).reshape(length, width)]
  transfers between devices with their start and end apart: 9 -> 9, of which waited for: 4 -> 4; matrix products, arithmetic and copies ran while one was open for 20% -> 13% of each run, Pallas kernels for 0% -> 6%
where the time goes in v5:
time: 185 us; the launch traced here: 184 us
  waiting for transfers between devices  74.9 us (40%)
  blocking collectives  33.3 us (18%)
  starting transfers between devices  21.1 us (11%)
  local copies, waits for them, and re-layouts  16.6 us (9%)
  between operations  14.4 us (8%)
  Pallas kernels  11.7 us (6%)
  other arithmetic  7.03 us (4%)
  matrix products  4.46 us (2%)
    all_gather x1, waiting for transfers between devices, body(): lax.all_gather(kernel, 'fsdp', axis=0, tiled=True)  24.8 us
    all_to_all x1, blocking collectives, gather_rows(): lax.all_to_all(jnp.tile(block, (count,) + (1,) * (block.ndim - 1)), axis,...  23.8 us
    psum x1, waiting for transfers between devices, body(): kernel_grad = lax.psum(kernel_part, 'fsdp')  23.6 us
    all_to_all x1, waiting for transfers between devices, table_and_gain(): got = lax.all_to_all(send, every, 0, 0, tiled=True)  21.7 us
    all_to_all x1, blocking collectives, table_and_gain(): back = lax.all_to_all(back, every, 0, 0, tiled=True)  9.53 us
    pallas_call x1, Pallas kernels, conv_dconv(): pl.pallas_call(forward_kernel, grid=(groups // step,), in_specs=[pl.Block...  6.55 us
    ppermute x2, starting transfers between devices, with_halo(): lax.ppermute(tail, axis, [(i, (i + 1) % count) for i in range(ends)])  6.07 us
    pallas_call x1, Pallas kernels, conv_transpose(): pl.pallas_call(backward_kernel, grid=(groups // step,), in_specs=[pl.Bloc...  5.18 us
  transfers between devices with their start and end apart: 9, of which 4 were waited for; matrix products, arithmetic and copies ran while one was open for 13% of the time, Pallas kernels for 6%

profile of v5, /device:TPU:0, one launch (start us, length us, event | category | flops | bytes accessed | tf_op | source)
XLA Modules:
  0.0 183.5 jit_solution(15111240756138462109)
XLA Ops:
  7.2 0.7 all-gather.2.cloned.1.call-update
  7.9 0.2 copy-done.6
  8.1 0.1 tile.2
  8.3 23.8 %all_to_all.55 = bf16[4,64,2048]{2,1,0:T(8,128)(2,1)S(1)} all-to-all(bf16[4,64,2048]{2,1,0:T(8,128)(2,1)S(1)} %tile.2), channel_id=1, replica_groups=mesh['fsdp'=4,'seq'=8] {'fsdp'}, dimensions={0} | all-to-all | bytes 2097152 | tf_op jit(solution)/shard_map/all_to_all | solution.py:35
  32.0 0.4 multiply_reduce_fusion.2
  32.5 0.3 copy-done.7
  32.7 0.2 multiply_convert_fusion
  32.9 0.3 copy.63
  33.2 1.0 copy.64
  34.2 5.2 %all-to-all-start.4 = ((bf16[16,128,128]{2,1,0:T(8,128)(2,1)}), bf16[16,128,128]{2,1,0:T(8,128)(2,1)S(1)}, u32[]{:S(2)}, u32[]{:S(2)}) async-start(bf16[16,128,128]{2,1,0:T(8,128)(2,1)} %bitcast.5), calls=%async_computation.4 | async-start | bytes 1048576 | tf_op jit(solution)/shard_map/all_to_all | solution.py:195
  39.3 0.8 fusion.32
  40.1 1.3 collective-permute-start.1
  41.4 3.0 %collective-permute-start = (bf16[16,4,128]{2,1,0:T(4,128)(2,1)S(1)}, bf16[16,4,128]{2,1,0:T(4,128)(2,1)S(1)}, u32[]{:S(2)}, u32[]{:S(2)}) collective-permute-start(bf16[16,4,128]{2,1,0:T(4,128)(2,1)S(1)} %get-tuple-element.28), channel_id=1, source_target_pairs={{0,1},{1,2},{2,3},{3,4},{4,5},{5,6},{6,7},{8,9},{9,10},{10,11},{11... | collective-permute-start | bytes 49160 | tf_op jit(solution)/shard_map/ppermute | solution.py:19
  44.5 0.2 copy.65
  44.7 1.4 copy.66
  46.1 2.3 %maximum_convert_fusion.pad_ref = f32[16,136,128]{2,1,0:T(8,128)} fusion(bf16[16,4,128]{2,1,0:T(4,128)(2,1)S(1)} %collective-permute-done.1, bf16[16,128,128]{2,1,0:T(8,128)(2,1)} %bitcast.5, bf16[16,4,128]{2,1,0:T(4,128)(2,1)S(1)} %collective-permute-done), kind=kLoop, calls=%fused_computation.22 | loop fusion | flops 1671168 | bytes 1671168 | tf_op jit(solution)/shard_map/convert_element_type | solution.py:191
  48.3 24.8 %all-gather.2.cloned.1.call-done = bf16[2048,1152]{1,0:T(8,128)(2,1)} async-done(((bf16[512,1152]{1,0:T(8,128)(2,1)}), bf16[2048,1152]{1,0:T(8,128)(2,1)}) %all-gather.2.cloned.1.call-update) | async-done | bytes 4718608 | tf_op jit(solution)/shard_map/all_gather | solution.py:188
  73.1 6.6 %shard_map.98 = bf16[16,128,128]{2,1,0:T(8,128)(2,1)} custom-call(f32[16,136,128]{2,1,0:T(8,128)} %maximum_convert_fusion.pad_ref, bf16[16,128,1152]{2,1,0:T(8,128)(2,1)} %bitcast.54, f32[16,128,128]{2,1,0:T(8,128)} %bitcast.57), custom_call_target="tpu_custom_call" | custom-call | flops 603979776 | bytes 7405568 | tf_op jit(solution)/shard_map/pallas_call | solution.py:74
  79.7 0.8 fusion.31
  80.5 1.3 collective-permute-start.3
  81.8 3.0 %collective-permute-start.2 = (bf16[16,4,128]{2,1,0:T(4,128)(2,1)S(1)}, bf16[16,4,128]{2,1,0:T(4,128)(2,1)S(1)}, u32[]{:S(2)}, u32[]{:S(2)}) collective-permute-start(bf16[16,4,128]{2,1,0:T(4,128)(2,1)S(1)} %get-tuple-element.26), channel_id=1, source_target_pairs={{0,1},{1,2},{2,3},{3,4},{4,5},{5,6},{6,7},{8,9},{9,10},{10,11},{11... | collective-permute-start | bytes 49160 | tf_op jit(solution)/shard_map/ppermute | solution.py:19
  84.8 0.1 broadcast_in_dim.7
  84.9 0.1 copy.70
  85.1 0.3 copy.79
  85.4 1.0 all_to_all.49
  86.4 4.6 %all-to-all-start.3 = ((bf16[16,128,128]{2,1,0:T(8,128)(2,1)}), bf16[16,128,128]{2,1,0:T(8,128)(2,1)}, u32[]{:S(2)}, u32[]{:S(2)}) async-start(bf16[16,128,128]{2,1,0:T(8,128)(2,1)} %shard_map.98), calls=%async_computation.3 | async-start | bytes 1048576 | tf_op jit(solution)/shard_map/all_to_all | solution.py:196
  91.0 1.1 maximum_convert_fusion.1.pad_ref
  92.2 5.2 %shard_map.99 = f32[16,128,128]{2,1,0:T(8,128)} custom-call(f32[16,136,128]{2,1,0:T(8,128)} %maximum_convert_fusion.1.pad_ref, bf16[16,128,1152]{2,1,0:T(8,128)(2,1)} %bitcast.55), custom_call_target="tpu_custom_call" | custom-call | flops 603979776 | bytes 6881280 | tf_op jit(solution)/shard_map/pallas_call | solution.py:96
  97.3 1.6 copy.67
  98.9 0.3 copy.68
  99.3 0.3 multiply_reduce_fusion
  99.6 0.7 copy-done.2
  100.3 0.4 fusion.3
  100.7 0.3 copy.69
  101.0 0.1 broadcast_in_dim.8
  101.1 1.3 pad_maximum_fusion
  102.4 4.1 %all-to-all-done.3 = bf16[16,128,128]{2,1,0:T(8,128)(2,1)} async-done(((bf16[16,128,128]{2,1,0:T(8,128)(2,1)}), bf16[16,128,128]{2,1,0:T(8,128)(2,1)}, u32[]{:S(2)}, u32[]{:S(2)}) %all-to-all-start.3) | async-done | bytes 524320 | tf_op jit(solution)/shard_map/all_to_all | solution.py:196
  106.5 2.6 %all-to-all-start.1 = ((bf16[32,130,64]{1,2,0:T(8,128)(2,1)}), bf16[32,130,64]{1,2,0:T(8,128)(2,1)S(1)}, u32[]{:S(2)}, u32[]{:S(2)}) async-start(bf16[32,130,64]{1,2,0:T(8,128)(2,1)} %pad_maximum_fusion), calls=%async_computation.1 | async-start | bytes 2097152 | tf_op jit(solution)/shard_map/all_to_all | solution.py:155
  109.2 1.1 copy.78
  110.3 0.4 convolution_dynamic-update-slice_fusion.8
  110.6 0.4 convolution_dynamic-update-slice_fusion.7
  111.0 0.4 convolution_dynamic-update-slice_fusion.6
  111.4 0.4 convolution_dynamic-update-slice_fusion.5
  111.7 0.3 convolution_dynamic-update-slice_fusion.4
  112.0 0.4 convolution_dynamic-update-slice_fusion.3
  112.4 0.4 convolution_dynamic-update-slice_fusion.2
  112.8 0.4 convolution_dynamic-update-slice_fusion.1
  113.1 0.4 convolution_dynamic-update-slice_fusion
  113.6 1.4 copy.80
  115.1 21.7 %all-to-all-done.1 = bf16[32,130,64]{1,2,0:T(8,128)(2,1)S(1)} async-done(((bf16[32,130,64]{1,2,0:T(8,128)(2,1)}), bf16[32,130,64]{1,2,0:T(8,128)(2,1)S(1)}, u32[]{:S(2)}, u32[]{:S(2)}) %all-to-all-start.1) | async-done | bytes 532512 | tf_op jit(solution)/shard_map/all_to_all | solution.py:155
  136.7 0.1 slice.78
  136.8 0.3 copy.81
  137.2 0.1 reshape.116
  137.3 0.9 fusion.2
  138.1 0.1 copy.74
  138.3 0.1 reshape.125
  138.4 9.5 %all_to_all.56 = f32[32,1,576]{2,1,0:T(1,128)S(1)} all-to-all(f32[32,1,576]{2,1,0:T(1,128)S(1)} %reshape.125), channel_id=1, replica_groups=mesh['fsdp'=4,'seq'=8] {'fsdp','seq'}, dimensions={0} | all-to-all | bytes 147456 | tf_op jit(solution)/shard_map/all_to_all | solution.py:165
  147.9 0.5 broadcast.58
  148.4 0.8 reduce.7
  149.3 0.1 reshape.126
  149.4 0.7 reshape.113
  150.1 0.6 slice_reduce_fusion
  150.7 23.6 %all-reduce.3.cloned.1.call-done = f32[256,1152]{1,0:T(8,128)} async-done(((f32[256,1152]{1,0:T(8,128)}), f32[256,1152]{1,0:T(8,128)}) %all-reduce.3.cloned.1.call-update) | async-done | bytes 1179664 | tf_op jit(solution)/shard_map/psum | solution.py:212
  174.3 2.4 %copy.96 = f32[256,1152]{1,0:T(8,128)} copy(f32[256,1152]{1,0:T(8,128)} %all-reduce.3.cloned.1.call-done) | data formatting | bytes 2359296
  (34 shorter events, 0.4 us)
Async XLA Ops:
  7.2 1.0 copy-start.6
  7.2 66.0 %all-gather.2.cloned.1.call-start = ((), (), s32[]{:S(2)}) async-start(), calls=%async_computation.5 | async-start | bytes 5898240 | tf_op jit(solution)/shard_map/all_gather | solution.py:188
  8.2 23.8 %copy-start.5 = (bf16[1,128,2048]{2,1,0:T(8,128)(2,1)S(1)}, bf16[1,128,2048]{2,1,0:T(8,128)(2,1)}, u32[]{:S(2)}) copy-start(bf16[1,128,2048]{2,1,0:T(8,128)(2,1)} %param.10) | copy-start | bytes 1572868
  8.2 23.8 %copy-start.8 = (s32[1,128]{1,0:T(1,128)S(1)}, s32[1,128]{1,0:T(1,128)}, u32[]{:S(2)}) copy-start(s32[1,128]{1,0:T(1,128)} %param.11) | copy-start | bytes 1540
  32.0 0.7 copy-start.7
  33.2 11.3 %copy-start.1 = (bf16[1,128,2048]{2,1,0:T(8,128)(2,1)S(1)}, bf16[1,128,2048]{2,1,0:T(8,128)(2,1)}, u32[]{:S(2)}) copy-start(bf16[1,128,2048]{2,1,0:T(8,128)(2,1)} %param.15) | copy-start | bytes 1572868
  34.2 50.9 %all-to-all-start.4 = ((bf16[16,128,128]{2,1,0:T(8,128)(2,1)}), bf16[16,128,128]{2,1,0:T(8,128)(2,1)S(1)}, u32[]{:S(2)}, u32[]{:S(2)}) async-start(bf16[16,128,128]{2,1,0:T(8,128)(2,1)} %bitcast.5), calls=%async_computation.4 | async-start | bytes 1048576 | tf_op jit(solution)/shard_map/all_to_all | solution.py:195
  40.1 5.9 %collective-permute-start.1 = (bf16[16,4,128]{2,1,0:T(4,128)(2,1)S(1)}, bf16[16,4,128]{2,1,0:T(4,128)(2,1)S(1)}, u32[]{:S(2)}, u32[]{:S(2)}) collective-permute-start(bf16[16,4,128]{2,1,0:T(4,128)(2,1)S(1)} %get-tuple-element.29), channel_id=1, source_target_pairs={{1,0},{2,1},{3,2},{4,3},{5,4},{6,5},{7,6},{9,8},{10,9},{11,10},{12... | collective-permute-start | bytes 49160 | tf_op jit(solution)/shard_map/ppermute | solution.py:21
  41.4 4.6 %collective-permute-start = (bf16[16,4,128]{2,1,0:T(4,128)(2,1)S(1)}, bf16[16,4,128]{2,1,0:T(4,128)(2,1)S(1)}, u32[]{:S(2)}, u32[]{:S(2)}) collective-permute-start(bf16[16,4,128]{2,1,0:T(4,128)(2,1)S(1)} %get-tuple-element.28), channel_id=1, source_target_pairs={{0,1},{1,2},{2,3},{3,4},{4,5},{5,6},{6,7},{8,9},{9,10},{10,11},{11... | collective-permute-start | bytes 49160 | tf_op jit(solution)/shard_map/ppermute | solution.py:19
  80.5 10.5 %collective-permute-start.3 = (bf16[16,4,128]{2,1,0:T(4,128)(2,1)S(1)}, bf16[16,4,128]{2,1,0:T(4,128)(2,1)S(1)}, u32[]{:S(2)}, u32[]{:S(2)}) collective-permute-start(bf16[16,4,128]{2,1,0:T(4,128)(2,1)S(1)} %get-tuple-element.27), channel_id=1, source_target_pairs={{1,0},{2,1},{3,2},{4,3},{5,4},{6,5},{7,6},{9,8},{10,9},{11,10},{12... | collective-permute-start | bytes 49160 | tf_op jit(solution)/shard_map/ppermute | solution.py:21
  81.8 9.2 %collective-permute-start.2 = (bf16[16,4,128]{2,1,0:T(4,128)(2,1)S(1)}, bf16[16,4,128]{2,1,0:T(4,128)(2,1)S(1)}, u32[]{:S(2)}, u32[]{:S(2)}) collective-permute-start(bf16[16,4,128]{2,1,0:T(4,128)(2,1)S(1)} %get-tuple-element.26), channel_id=1, source_target_pairs={{0,1},{1,2},{2,3},{3,4},{4,5},{5,6},{6,7},{8,9},{9,10},{10,11},{11... | collective-permute-start | bytes 49160 | tf_op jit(solution)/shard_map/ppermute | solution.py:19
  85.4 5.7 %copy-start = (bf16[16,128,128]{2,1,0:T(8,128)(2,1)S(1)}, bf16[16,128,128]{2,1,0:T(8,128)(2,1)}, u32[]{:S(2)}) copy-start(bf16[16,128,128]{2,1,0:T(8,128)(2,1)} %shard_map.98) | copy-start | bytes 1572868
  86.4 20.1 %all-to-all-start.3 = ((bf16[16,128,128]{2,1,0:T(8,128)(2,1)}), bf16[16,128,128]{2,1,0:T(8,128)(2,1)}, u32[]{:S(2)}, u32[]{:S(2)}) async-start(bf16[16,128,128]{2,1,0:T(8,128)(2,1)} %shard_map.98), calls=%async_computation.3 | async-start | bytes 1048576 | tf_op jit(solution)/shard_map/all_to_all | solution.py:196
  99.2 1.0 copy-start.2
  100.7 1.7 copy-start.4
  102.4 7.9 %copy-start.3 = (bf16[2,1024,128]{1,2,0:T(8,128)(2,1)S(1)}, bf16[2,1024,128]{1,2,0:T(8,128)(2,1)}, u32[]{:S(2)}) copy-start(bf16[2,1024,128]{1,2,0:T(8,128)(2,1)} %all_to_all.49) | copy-start | bytes 1572868
  106.5 30.2 %all-to-all-start.1 = ((bf16[32,130,64]{1,2,0:T(8,128)(2,1)}), bf16[32,130,64]{1,2,0:T(8,128)(2,1)S(1)}, u32[]{:S(2)}, u32[]{:S(2)}) async-start(bf16[32,130,64]{1,2,0:T(8,128)(2,1)} %pad_maximum_fusion), calls=%async_computation.1 | async-start | bytes 2097152 | tf_op jit(solution)/shard_map/all_to_all | solution.py:155
  109.1 65.2 %all-reduce.3.cloned.1.call-start = ((), (), s32[]{:S(2)}) async-start(), calls=%async_computation.6 | async-start | bytes 2359296 | tf_op jit(solution)/shard_map/psum | solution.py:212
Sparse Core Ops, SparseCore 0:
  9.8 63.2 all-gather.1
  115.1 59.1 all-reduce.2

commit v6 on v5

--- a/solution.py
+++ b/solution.py
@@ -184,12 +184,13 @@
     inv = lax.rsqrt(jnp.mean(mixed * mixed, axis=-1, keepdims=True) + 1e-06)
     normed = (mixed * inv * norm_gain).astype(jnp.bfloat16)
     normed_g = normed.reshape(length, GROUPS, chans).transpose(1, 0, 2)
-    padded = with_halo(normed_g, "seq", 1, half)
+    padded = with_halo(normed_g, "seq", 1, 2 * half)
+    up_g = upstream[0].reshape(length, GROUPS, chans).transpose(1, 0, 2)
+    up_pad = with_halo(up_g, "seq", 1, half)
     weights = lax.all_gather(kernel, "fsdp", axis=0, tiled=True).reshape(GROUPS, chans, KERNEL * chans)
     up_float = upstream[0].astype(jnp.float32)
-    up_g = up_float.reshape(length, GROUPS, chans).transpose(1, 0, 2)
-    dconv = conv_dconv(padded.astype(jnp.float32), weights, up_g)
-    dpad = with_halo(dconv, "seq", 1, half)
+    dpad = conv_dconv(padded.astype(jnp.float32), weights, up_pad.astype(jnp.float32))
+    dconv = dpad[:, half : half + length]
     dnormed = conv_transpose(dpad.astype(jnp.float32), weights, length)
     if seq_count <= GROUPS:
         group_in = lax.all_to_all(normed_g, "seq", 0, 1, tiled=True)

time: 185 us -> 186 us (level)
  other arithmetic: 7.03 us -> 9.11 us
    all_to_all x1, waiting for transfers between devices: 4.12 us -> 11.9 us  [body(): group_out = lax.all_to_all(dconv, 'seq', 0, 1, tiled=True)]
    all_gather x1, waiting for transfers between devices: 24.8 us -> 17.2 us  [body(): lax.all_gather(kernel, 'fsdp', axis=0, tiled=True)]
    unnamed x22 -> x23, local copies, waits for them, and re-layouts: 4.11 us -> 4.76 us
  transfers between devices with their start and end apart: 9 -> 9, of which waited for: 4 -> 5; matrix products, arithmetic and copies ran while one was open for 13% -> 10% of each run, Pallas kernels for 6% -> 0%
where the time goes in v6:
time: 186 us; the launch traced here: 185 us
  waiting for transfers between devices  74.7 us (40%)
  blocking collectives  33.3 us (18%)
  starting transfers between devices  22.4 us (12%)
  local copies, waits for them, and re-layouts  15.1 us (8%)
  between operations  14.4 us (8%)
  Pallas kernels  11.5 us (6%)
  other arithmetic  9.11 us (5%)
  matrix products  4.47 us (2%)
    all_to_all x1, blocking collectives, gather_rows(): lax.all_to_all(jnp.tile(block, (count,) + (1,) * (block.ndim - 1)), axis,...  23.8 us
    all_to_all x1, waiting for transfers between devices, table_and_gain(): got = lax.all_to_all(send, every, 0, 0, tiled=True)  22.7 us
    psum x1, waiting for transfers between devices, body(): kernel_grad = lax.psum(kernel_part, 'fsdp')  21.8 us
    all_gather x1, waiting for transfers between devices, body(): lax.all_gather(kernel, 'fsdp', axis=0, tiled=True)  17.2 us
    all_to_all x1, waiting for transfers between devices, body(): group_out = lax.all_to_all(dconv, 'seq', 0, 1, tiled=True)  11.9 us
    all_to_all x1, blocking collectives, table_and_gain(): back = lax.all_to_all(back, every, 0, 0, tiled=True)  9.5 us
    ppermute x2, starting transfers between devices, with_halo(): lax.ppermute(tail, axis, [(i, (i + 1) % count) for i in range(ends)])  7.33 us
    pallas_call x1, Pallas kernels, conv_dconv(): pl.pallas_call(forward_kernel, grid=(groups // step,), in_specs=[pl.Block...  6.32 us
  transfers between devices with their start and end apart: 9, of which 5 were waited for; matrix products, arithmetic and copies ran while one was open for 10% of the time, Pallas kernels for 0%

profile of v6, /device:TPU:0, one launch (start us, length us, event | category | flops | bytes accessed | tf_op | source)
XLA Modules:
  0.0 184.9 jit_solution(2290641564131563985)
XLA Ops:
  7.2 0.7 all-gather.2.cloned.1.call-update
  7.9 0.2 copy-done.6
  8.1 0.1 tile.2
  8.3 23.8 %all_to_all.55 = bf16[4,64,2048]{2,1,0:T(8,128)(2,1)S(1)} all-to-all(bf16[4,64,2048]{2,1,0:T(8,128)(2,1)S(1)} %tile.2), channel_id=1, replica_groups=mesh['fsdp'=4,'seq'=8] {'fsdp'}, dimensions={0} | all-to-all | bytes 2097152 | tf_op jit(solution)/shard_map/all_to_all | solution.py:35
  32.0 0.4 multiply_reduce_fusion.2
  32.5 0.3 copy-done.7
  32.7 0.2 multiply_convert_fusion
  32.9 0.3 copy.63
  33.2 1.0 copy.64
  34.2 5.2 %all-to-all-start.4 = ((bf16[16,128,128]{2,1,0:T(8,128)(2,1)}), bf16[16,128,128]{2,1,0:T(8,128)(2,1)S(1)}, u32[]{:S(2)}, u32[]{:S(2)}) async-start(bf16[16,128,128]{2,1,0:T(8,128)(2,1)} %bitcast.5), calls=%async_computation.4 | async-start | bytes 1048576 | tf_op jit(solution)/shard_map/all_to_all | solution.py:196
  39.3 0.3 copy.65
  39.6 0.3 copy.66
  39.9 1.3 collective-permute-start.3
  41.2 3.0 %collective-permute-start.2 = (bf16[16,4,128]{2,1,0:T(4,128)(2,1)S(1)}, bf16[16,4,128]{2,1,0:T(4,128)(2,1)S(1)}, u32[]{:S(2)}, u32[]{:S(2)}) collective-permute-start(bf16[16,4,128]{2,1,0:T(4,128)(2,1)S(1)} %get-tuple-element.26), channel_id=1, source_target_pairs={{0,1},{1,2},{2,3},{3,4},{4,5},{5,6},{6,7},{8,9},{9,10},{10,11},{11... | collective-permute-start | bytes 49160 | tf_op jit(solution)/shard_map/ppermute | solution.py:19
  44.4 0.1 copy.70
  44.5 0.8 fusion.32
  45.3 1.3 collective-permute-start.1
  46.6 4.3 %collective-permute-start = (bf16[16,8,128]{2,1,0:T(8,128)(2,1)S(1)}, bf16[16,8,128]{2,1,0:T(8,128)(2,1)S(1)}, u32[]{:S(2)}, u32[]{:S(2)}) collective-permute-start(bf16[16,8,128]{2,1,0:T(8,128)(2,1)S(1)} %get-tuple-element.28), channel_id=1, source_target_pairs={{0,1},{1,2},{2,3},{3,4},{4,5},{5,6},{6,7},{8,9},{9,10},{10,11},{11... | collective-permute-start | bytes 98312 | tf_op jit(solution)/shard_map/ppermute | solution.py:19
  50.9 1.2 maximum_convert_fusion.1.up_ref
  52.1 2.1 %maximum_convert_fusion.pad_ref = f32[16,144,128]{2,1,0:T(8,128)} fusion(bf16[16,8,128]{2,1,0:T(8,128)(2,1)S(1)} %collective-permute-done.1, bf16[16,128,128]{2,1,0:T(8,128)(2,1)} %bitcast.5, bf16[16,8,128]{2,1,0:T(8,128)(2,1)S(1)} %collective-permute-done), kind=kLoop, calls=%fused_computation.21 | loop fusion | flops 1769472 | bytes 1769472 | tf_op jit(solution)/shard_map/convert_element_type | solution.py:192
  54.2 0.5 all-to-all-done.4
  54.7 0.3 copy.79
  55.0 1.0 all_to_all.49
  56.0 17.2 %all-gather.2.cloned.1.call-done = bf16[2048,1152]{1,0:T(8,128)(2,1)} async-done(((bf16[512,1152]{1,0:T(8,128)(2,1)}), bf16[2048,1152]{1,0:T(8,128)(2,1)}) %all-gather.2.cloned.1.call-update) | async-done | bytes 4718608 | tf_op jit(solution)/shard_map/all_gather | solution.py:190
  73.2 6.3 %shard_map.98 = bf16[16,136,128]{2,1,0:T(8,128)(2,1)} custom-call(f32[16,144,128]{2,1,0:T(8,128)} %maximum_convert_fusion.pad_ref, bf16[16,128,1152]{2,1,0:T(8,128)(2,1)} %bitcast.53, f32[16,136,128]{2,1,0:T(8,128)} %maximum_convert_fusion.1.up_ref), custom_call_target="tpu_custom_call" | custom-call | flops 641728512 | bytes 7569408 | tf_op jit(solution)/shard_map/pallas_call | solution.py:74
  79.5 2.2 %convert_element_type.52.pad_ref = f32[16,136,128]{2,1,0:T(8,128)} convert(bf16[16,136,128]{2,1,0:T(8,128)(2,1)} %shard_map.98) | non-fusion elementwise | flops 278528 | bytes 1671168 | tf_op jit(solution)/shard_map/convert_element_type | solution.py:194
  81.7 0.9 slice.86
  82.6 5.2 %shard_map.99 = f32[16,128,128]{2,1,0:T(8,128)} custom-call(f32[16,136,128]{2,1,0:T(8,128)} %convert_element_type.52.pad_ref, bf16[16,128,1152]{2,1,0:T(8,128)(2,1)} %bitcast.54), custom_call_target="tpu_custom_call" | custom-call | flops 603979776 | bytes 6881280 | tf_op jit(solution)/shard_map/pallas_call | solution.py:96
  87.8 1.6 copy.67
  89.4 0.3 copy.68
  89.7 4.6 %all-to-all-start.3 = ((bf16[16,128,128]{2,1,0:T(8,128)(2,1)}), bf16[16,128,128]{2,1,0:T(8,128)(2,1)S(1)}, u32[]{:S(2)}, u32[]{:S(2)}) async-start(bf16[16,128,128]{2,1,0:T(8,128)(2,1)} %slice.86), calls=%async_computation.3 | async-start | bytes 1048576 | tf_op jit(solution)/shard_map/all_to_all | solution.py:197
  94.3 0.3 multiply_reduce_fusion
  94.6 0.7 copy-done.3
  95.4 0.4 fusion.3
  95.8 0.3 copy.69
  96.1 0.1 broadcast_in_dim.8
  96.2 0.4 copy-done.4
  96.6 1.2 pad_maximum_fusion
  97.8 11.9 %all-to-all-done.3 = bf16[16,128,128]{2,1,0:T(8,128)(2,1)S(1)} async-done(((bf16[16,128,128]{2,1,0:T(8,128)(2,1)}), bf16[16,128,128]{2,1,0:T(8,128)(2,1)S(1)}, u32[]{:S(2)}, u32[]{:S(2)}) %all-to-all-start.3) | async-done | bytes 524320 | tf_op jit(solution)/shard_map/all_to_all | solution.py:197
  109.7 2.6 %all-to-all-start.1 = ((bf16[32,130,64]{1,2,0:T(8,128)(2,1)}), bf16[32,130,64]{1,2,0:T(8,128)(2,1)S(1)}, u32[]{:S(2)}, u32[]{:S(2)}) async-start(bf16[32,130,64]{1,2,0:T(8,128)(2,1)} %pad_maximum_fusion), calls=%async_computation.1 | async-start | bytes 2097152 | tf_op jit(solution)/shard_map/all_to_all | solution.py:155
  112.4 0.4 convolution_dynamic-update-slice_fusion.8
  112.8 0.4 convolution_dynamic-update-slice_fusion.7
  113.2 0.4 convolution_dynamic-update-slice_fusion.6
  113.5 0.4 convolution_dynamic-update-slice_fusion.5
  113.9 0.3 convolution_dynamic-update-slice_fusion.4
  114.2 0.4 convolution_dynamic-update-slice_fusion.3
  114.6 0.4 convolution_dynamic-update-slice_fusion.2
  114.9 0.4 convolution_dynamic-update-slice_fusion.1
  115.3 0.4 convolution_dynamic-update-slice_fusion
  115.8 1.4 copy.80
  117.3 22.7 %all-to-all-done.1 = bf16[32,130,64]{1,2,0:T(8,128)(2,1)S(1)} async-done(((bf16[32,130,64]{1,2,0:T(8,128)(2,1)}), bf16[32,130,64]{1,2,0:T(8,128)(2,1)S(1)}, u32[]{:S(2)}, u32[]{:S(2)}) %all-to-all-start.1) | async-done | bytes 532512 | tf_op jit(solution)/shard_map/all_to_all | solution.py:155
  139.9 0.1 slice.82
  140.0 0.3 copy.81
  140.4 0.1 reshape.112
  140.5 0.9 fusion.2
  141.3 0.1 copy.74
  141.5 0.1 reshape.120
  141.6 9.5 %all_to_all.56 = f32[32,1,576]{2,1,0:T(1,128)S(1)} all-to-all(f32[32,1,576]{2,1,0:T(1,128)S(1)} %reshape.120), channel_id=1, replica_groups=mesh['fsdp'=4,'seq'=8] {'fsdp','seq'}, dimensions={0} | all-to-all | bytes 147456 | tf_op jit(solution)/shard_map/all_to_all | solution.py:165
  151.1 0.5 broadcast.58
  151.6 0.8 reduce.7
  152.6 0.7 reshape.109
  153.3 0.6 slice_reduce_fusion
  153.9 21.8 %all-reduce.3.cloned.1.call-done = f32[256,1152]{1,0:T(8,128)} async-done(((f32[256,1152]{1,0:T(8,128)}), f32[256,1152]{1,0:T(8,128)}) %all-reduce.3.cloned.1.call-update) | async-done | bytes 1179664 | tf_op jit(solution)/shard_map/psum | solution.py:213
  175.7 2.4 %copy.96 = f32[256,1152]{1,0:T(8,128)} copy(f32[256,1152]{1,0:T(8,128)} %all-reduce.3.cloned.1.call-done) | data formatting | bytes 2359296
  (36 shorter events, 0.7 us)
Async XLA Ops:
  7.2 1.0 copy-start.6
  7.2 66.0 %all-gather.2.cloned.1.call-start = ((), (), s32[]{:S(2)}) async-start(), calls=%async_computation.5 | async-start | bytes 5898240 | tf_op jit(solution)/shard_map/all_gather | solution.py:190
  8.2 23.8 %copy-start.5 = (bf16[1,128,2048]{2,1,0:T(8,128)(2,1)S(1)}, bf16[1,128,2048]{2,1,0:T(8,128)(2,1)}, u32[]{:S(2)}) copy-start(bf16[1,128,2048]{2,1,0:T(8,128)(2,1)} %param.10) | copy-start | bytes 1572868
  8.2 23.8 %copy-start.8 = (s32[1,128]{1,0:T(1,128)S(1)}, s32[1,128]{1,0:T(1,128)}, u32[]{:S(2)}) copy-start(s32[1,128]{1,0:T(1,128)} %param.11) | copy-start | bytes 1540
  32.0 0.7 copy-start.7
  33.2 6.2 %copy-start.2 = (bf16[1,128,2048]{2,1,0:T(8,128)(2,1)S(1)}, bf16[1,128,2048]{2,1,0:T(8,128)(2,1)}, u32[]{:S(2)}) copy-start(bf16[1,128,2048]{2,1,0:T(8,128)(2,1)} %param.15) | copy-start | bytes 1572868
  34.2 20.5 %all-to-all-start.4 = ((bf16[16,128,128]{2,1,0:T(8,128)(2,1)}), bf16[16,128,128]{2,1,0:T(8,128)(2,1)S(1)}, u32[]{:S(2)}, u32[]{:S(2)}) async-start(bf16[16,128,128]{2,1,0:T(8,128)(2,1)} %bitcast.5), calls=%async_computation.4 | async-start | bytes 1048576 | tf_op jit(solution)/shard_map/all_to_all | solution.py:196
  39.9 10.9 %collective-permute-start.3 = (bf16[16,4,128]{2,1,0:T(4,128)(2,1)S(1)}, bf16[16,4,128]{2,1,0:T(4,128)(2,1)S(1)}, u32[]{:S(2)}, u32[]{:S(2)}) collective-permute-start(bf16[16,4,128]{2,1,0:T(4,128)(2,1)S(1)} %get-tuple-element.27), channel_id=1, source_target_pairs={{1,0},{2,1},{3,2},{4,3},{5,4},{6,5},{7,6},{9,8},{10,9},{11,10},{12... | collective-permute-start | bytes 49160 | tf_op jit(solution)/shard_map/ppermute | solution.py:21
  41.2 9.7 %collective-permute-start.2 = (bf16[16,4,128]{2,1,0:T(4,128)(2,1)S(1)}, bf16[16,4,128]{2,1,0:T(4,128)(2,1)S(1)}, u32[]{:S(2)}, u32[]{:S(2)}) collective-permute-start(bf16[16,4,128]{2,1,0:T(4,128)(2,1)S(1)} %get-tuple-element.26), channel_id=1, source_target_pairs={{0,1},{1,2},{2,3},{3,4},{4,5},{5,6},{6,7},{8,9},{9,10},{10,11},{11... | collective-permute-start | bytes 49160 | tf_op jit(solution)/shard_map/ppermute | solution.py:19
  45.3 6.8 %collective-permute-start.1 = (bf16[16,8,128]{2,1,0:T(8,128)(2,1)S(1)}, bf16[16,8,128]{2,1,0:T(8,128)(2,1)S(1)}, u32[]{:S(2)}, u32[]{:S(2)}) collective-permute-start(bf16[16,8,128]{2,1,0:T(8,128)(2,1)S(1)} %get-tuple-element.29), channel_id=1, source_target_pairs={{1,0},{2,1},{3,2},{4,3},{5,4},{6,5},{7,6},{9,8},{10,9},{11,10},{12... | collective-permute-start | bytes 98312 | tf_op jit(solution)/shard_map/ppermute | solution.py:21
  46.6 5.5 %collective-permute-start = (bf16[16,8,128]{2,1,0:T(8,128)(2,1)S(1)}, bf16[16,8,128]{2,1,0:T(8,128)(2,1)S(1)}, u32[]{:S(2)}, u32[]{:S(2)}) collective-permute-start(bf16[16,8,128]{2,1,0:T(8,128)(2,1)S(1)} %get-tuple-element.28), channel_id=1, source_target_pairs={{0,1},{1,2},{2,3},{3,4},{4,5},{5,6},{6,7},{8,9},{9,10},{10,11},{11... | collective-permute-start | bytes 98312 | tf_op jit(solution)/shard_map/ppermute | solution.py:19
  79.5 2.2 %copy-start = (bf16[16,136,128]{2,1,0:T(8,128)(2,1)S(1)}, bf16[16,136,128]{2,1,0:T(8,128)(2,1)}, u32[]{:S(2)}) copy-start(bf16[16,136,128]{2,1,0:T(8,128)(2,1)} %shard_map.98) | copy-start | bytes 1671172
  89.7 20.0 %all-to-all-start.3 = ((bf16[16,128,128]{2,1,0:T(8,128)(2,1)}), bf16[16,128,128]{2,1,0:T(8,128)(2,1)S(1)}, u32[]{:S(2)}, u32[]{:S(2)}) async-start(bf16[16,128,128]{2,1,0:T(8,128)(2,1)} %slice.86), calls=%async_computation.3 | async-start | bytes 1048576 | tf_op jit(solution)/shard_map/all_to_all | solution.py:197
  94.3 1.0 copy-start.3
  95.8 0.8 copy-start.4
  97.8 14.6 %copy-start.1 = (bf16[2,1024,128]{1,2,0:T(8,128)(2,1)S(1)}, bf16[2,1024,128]{1,2,0:T(8,128)(2,1)}, u32[]{:S(2)}) copy-start(bf16[2,1024,128]{1,2,0:T(8,128)(2,1)} %all_to_all.49) | copy-start | bytes 1572868
  109.7 30.2 %all-to-all-start.1 = ((bf16[32,130,64]{1,2,0:T(8,128)(2,1)}), bf16[32,130,64]{1,2,0:T(8,128)(2,1)S(1)}, u32[]{:S(2)}, u32[]{:S(2)}) async-start(bf16[32,130,64]{1,2,0:T(8,128)(2,1)} %pad_maximum_fusion), calls=%async_computation.1 | async-start | bytes 2097152 | tf_op jit(solution)/shard_map/all_to_all | solution.py:155
  112.3 63.4 %all-reduce.3.cloned.1.call-start = ((), (), s32[]{:S(2)}) async-start(), calls=%async_computation.6 | async-start | bytes 2359296 | tf_op jit(solution)/shard_map/psum | solution.py:213
Sparse Core Ops, SparseCore 0:
  9.8 63.2 all-gather.1
  117.3 58.3 all-reduce.2

commit v7 on v6

--- a/solution.py
+++ b/solution.py
@@ -191,7 +191,6 @@
     up_float = upstream[0].astype(jnp.float32)
     dpad = conv_dconv(padded.astype(jnp.float32), weights, up_pad.astype(jnp.float32))
     dconv = dpad[:, half : half + length]
-    dnormed = conv_transpose(dpad.astype(jnp.float32), weights, length)
     if seq_count <= GROUPS:
         group_in = lax.all_to_all(normed_g, "seq", 0, 1, tiled=True)
         group_out = lax.all_to_all(dconv, "seq", 0, 1, tiled=True)
@@ -205,6 +204,8 @@
         for k in range(KERNEL)
     ]
     kernel_part = jnp.concatenate(kterms, axis=-1).reshape(-1, KERNEL * chans) * scale
+    kernel_part, dpad = lax.optimization_barrier((kernel_part, dpad))
+    dnormed = conv_transpose(dpad.astype(jnp.float32), weights, length)
     dnormed = dnormed.transpose(1, 0, 2).reshape(length, width)
     gain_term = jnp.sum(dnormed * mixed * inv, axis=0) * scale
     scaled = norm_gain * dnormed

time: 186 us -> 193 us (1.038)
  waiting for transfers between devices: 74.7 us -> 83.8 us
    all_to_all x1, waiting for transfers between devices: 22.7 us -> 26.8 us  [table_and_gain(): got = lax.all_to_all(send, every, 0, 0, tiled=True)]
    all_to_all x1, waiting for transfers between devices: 11.9 us -> 14.6 us  [body(): group_out = lax.all_to_all(dconv, 'seq', 0, 1, tiled=True)]
    unnamed x23 -> x21, local copies, waits for them, and re-layouts: 4.76 us -> 4.37 us
  transfers between devices with their start and end apart: 9 -> 9, of which waited for: 5 -> 5; matrix products, arithmetic and copies ran while one was open for 10% -> 7% of each run, Pallas kernels for 0% -> 3%
where the time goes in v7:
time: 193 us; the launch traced here: 192 us
  waiting for transfers between devices  83.8 us (43%)
  blocking collectives  33.3 us (17%)
  starting transfers between devices  21.7 us (11%)
  local copies, waits for them, and re-layouts  14.9 us (8%)
  between operations  14.4 us (7%)
  Pallas kernels  11.5 us (6%)
  other arithmetic  8.04 us (4%)
  matrix products  4.45 us (2%)
    all_to_all x1, waiting for transfers between devices, table_and_gain(): got = lax.all_to_all(send, every, 0, 0, tiled=True)  26.8 us
    all_to_all x1, blocking collectives, gather_rows(): lax.all_to_all(jnp.tile(block, (count,) + (1,) * (block.ndim - 1)), axis,...  23.8 us
    psum x1, waiting for transfers between devices, body(): kernel_grad = lax.psum(kernel_part, 'fsdp')  21.1 us
    all_gather x1, waiting for transfers between devices, body(): lax.all_gather(kernel, 'fsdp', axis=0, tiled=True)  18.1 us
    all_to_all x1, waiting for transfers between devices, body(): group_out = lax.all_to_all(dconv, 'seq', 0, 1, tiled=True)  14.6 us
    all_to_all x1, blocking collectives, table_and_gain(): back = lax.all_to_all(back, every, 0, 0, tiled=True)  9.5 us
    ppermute x2, starting transfers between devices, with_halo(): lax.ppermute(tail, axis, [(i, (i + 1) % count) for i in range(ends)])  6.59 us
    pallas_call x1, Pallas kernels, conv_dconv(): pl.pallas_call(forward_kernel, grid=(groups // step,), in_specs=[pl.Block...  6.32 us
  transfers between devices with their start and end apart: 9, of which 5 were waited for; matrix products, arithmetic and copies ran while one was open for 7% of the time, Pallas kernels for 3%

profile of v7, /device:TPU:0, one launch (start us, length us, event | category | flops | bytes accessed | tf_op | source)
XLA Modules:
  0.0 192.0 jit_solution(1926767253375580099)
XLA Ops:
  7.2 0.7 all-gather.2.cloned.1.call-update
  7.9 0.2 copy-done.5
  8.1 0.1 tile.2
  8.3 23.8 %all_to_all.55 = bf16[4,64,2048]{2,1,0:T(8,128)(2,1)S(1)} all-to-all(bf16[4,64,2048]{2,1,0:T(8,128)(2,1)S(1)} %tile.2), channel_id=1, replica_groups=mesh['fsdp'=4,'seq'=8] {'fsdp'}, dimensions={0} | all-to-all | bytes 2097152 | tf_op jit(solution)/shard_map/all_to_all | solution.py:35
  32.0 0.4 multiply_reduce_fusion.2
  32.5 0.3 copy-done.6
  32.7 0.2 multiply_convert_fusion
  32.9 0.3 copy.63
  33.2 1.0 copy.64
  34.2 5.2 %all-to-all-start.2 = ((bf16[16,128,128]{2,1,0:T(8,128)(2,1)}), bf16[16,128,128]{2,1,0:T(8,128)(2,1)S(1)}, u32[]{:S(2)}, u32[]{:S(2)}) async-start(bf16[16,128,128]{2,1,0:T(8,128)(2,1)} %bitcast.5), calls=%async_computation.2 | async-start | bytes 1048576 | tf_op jit(solution)/shard_map/all_to_all | solution.py:195
  39.3 0.3 copy.65
  39.6 0.3 copy.66
  39.9 2.4 %collective-permute-start.2 = (bf16[16,4,128]{2,1,0:T(4,128)(2,1)S(1)}, bf16[16,4,128]{2,1,0:T(4,128)(2,1)S(1)}, u32[]{:S(2)}, u32[]{:S(2)}) collective-permute-start(bf16[16,4,128]{2,1,0:T(4,128)(2,1)S(1)} %get-tuple-element.30), channel_id=1, source_target_pairs={{0,1},{1,2},{2,3},{3,4},{4,5},{5,6},{6,7},{8,9},{9,10},{10,11},{11... | collective-permute-start | bytes 49160 | tf_op jit(solution)/shard_map/ppermute | solution.py:19
  42.3 1.3 collective-permute-start.3
  43.6 0.8 fusion.32
  44.4 4.2 %collective-permute-start = (bf16[16,8,128]{2,1,0:T(8,128)(2,1)S(1)}, bf16[16,8,128]{2,1,0:T(8,128)(2,1)S(1)}, u32[]{:S(2)}, u32[]{:S(2)}) collective-permute-start(bf16[16,8,128]{2,1,0:T(8,128)(2,1)S(1)} %get-tuple-element.32), channel_id=1, source_target_pairs={{0,1},{1,2},{2,3},{3,4},{4,5},{5,6},{6,7},{8,9},{9,10},{10,11},{11... | collective-permute-start | bytes 98312 | tf_op jit(solution)/shard_map/ppermute | solution.py:19
  48.6 1.3 collective-permute-start.1
  49.9 1.2 maximum_convert_fusion.1.up_ref
  51.1 1.9 collective-permute-done.1
  53.0 2.1 %maximum_convert_fusion.pad_ref = f32[16,144,128]{2,1,0:T(8,128)} fusion(bf16[16,8,128]{2,1,0:T(8,128)(2,1)S(1)} %collective-permute-done.1, bf16[16,128,128]{2,1,0:T(8,128)(2,1)} %bitcast.5, bf16[16,8,128]{2,1,0:T(8,128)(2,1)S(1)} %collective-permute-done), kind=kLoop, calls=%fused_computation.21 | loop fusion | flops 1769472 | bytes 1769472 | tf_op jit(solution)/shard_map/convert_element_type | solution.py:192
  55.1 18.1 %all-gather.2.cloned.1.call-done = bf16[2048,1152]{1,0:T(8,128)(2,1)} async-done(((bf16[512,1152]{1,0:T(8,128)(2,1)}), bf16[2048,1152]{1,0:T(8,128)(2,1)}) %all-gather.2.cloned.1.call-update) | async-done | bytes 4718608 | tf_op jit(solution)/shard_map/all_gather | solution.py:190
  73.1 6.3 %shard_map.98 = bf16[16,136,128]{2,1,0:T(8,128)(2,1)} custom-call(f32[16,144,128]{2,1,0:T(8,128)} %maximum_convert_fusion.pad_ref, bf16[16,128,1152]{2,1,0:T(8,128)(2,1)} %bitcast.53, f32[16,136,128]{2,1,0:T(8,128)} %maximum_convert_fusion.1.up_ref), custom_call_target="tpu_custom_call" | custom-call | flops 641728512 | bytes 7569408 | tf_op jit(solution)/shard_map/pallas_call | solution.py:74
  79.5 2.0 %slice.82 = bf16[16,128,128]{2,1,0:T(8,128)(2,1)} slice(bf16[16,136,128]{2,1,0:T(8,128)(2,1)} %shard_map.98), slice={[0:16], [4:132], [0:128]} | slice | bytes 1048576 | tf_op jit(solution)/shard_map/slice | solution.py:193
  81.5 4.6 %all-to-all-start.1 = ((bf16[16,128,128]{2,1,0:T(8,128)(2,1)}), bf16[16,128,128]{2,1,0:T(8,128)(2,1)S(1)}, u32[]{:S(2)}, u32[]{:S(2)}) async-start(bf16[16,128,128]{2,1,0:T(8,128)(2,1)} %slice.82), calls=%async_computation.1 | async-start | bytes 1048576 | tf_op jit(solution)/shard_map/all_to_all | solution.py:196
  86.2 0.1 copy.73
  86.3 0.3 copy.68
  86.6 0.2 all_to_all.47
  86.8 14.6 %all-to-all-done.1 = bf16[16,128,128]{2,1,0:T(8,128)(2,1)S(1)} async-done(((bf16[16,128,128]{2,1,0:T(8,128)(2,1)}), bf16[16,128,128]{2,1,0:T(8,128)(2,1)S(1)}, u32[]{:S(2)}, u32[]{:S(2)}) %all-to-all-start.1) | async-done | bytes 524320 | tf_op jit(solution)/shard_map/all_to_all | solution.py:196
  101.5 0.4 convolution_dynamic-update-slice_fusion.8
  101.8 0.4 convolution_dynamic-update-slice_fusion.7
  102.2 0.4 convolution_dynamic-update-slice_fusion.6
  102.6 0.4 convolution_dynamic-update-slice_fusion.5
  102.9 0.3 convolution_dynamic-update-slice_fusion.4
  103.2 0.4 convolution_dynamic-update-slice_fusion.3
  103.6 0.4 convolution_dynamic-update-slice_fusion.2
  104.0 0.4 convolution_dynamic-update-slice_fusion.1
  104.3 0.4 convolution_dynamic-update-slice_fusion
  104.8 1.4 copy.69
  106.2 1.1 convert_element_type.52.pad_ref
  107.3 5.2 %shard_map.99 = f32[16,128,128]{2,1,0:T(8,128)} custom-call(f32[16,136,128]{2,1,0:T(8,128)} %convert_element_type.52.pad_ref, bf16[16,128,1152]{2,1,0:T(8,128)(2,1)} %bitcast.54), custom_call_target="tpu_custom_call" | custom-call | flops 603979776 | bytes 6881280 | tf_op jit(solution)/shard_map/pallas_call | solution.py:96
  112.5 1.6 copy.70
  114.0 0.3 copy.71
  114.4 0.3 multiply_reduce_fusion
  114.7 0.7 copy-done.2
  115.4 0.4 fusion.3
  115.8 0.3 copy.72
  116.1 0.1 broadcast_in_dim.8
  116.2 1.3 pad_maximum_fusion
  117.5 2.6 %all-to-all-start.3 = ((bf16[32,130,64]{1,2,0:T(8,128)(2,1)}), bf16[32,130,64]{1,2,0:T(8,128)(2,1)S(1)}, u32[]{:S(2)}, u32[]{:S(2)}) async-start(bf16[32,130,64]{1,2,0:T(8,128)(2,1)} %pad_maximum_fusion), calls=%async_computation.3 | async-start | bytes 2097152 | tf_op jit(solution)/shard_map/all_to_all | solution.py:155
  120.2 0.7 all-reduce.3.cloned.1.call-update
  121.0 26.8 %all-to-all-done.3 = bf16[32,130,64]{1,2,0:T(8,128)(2,1)S(1)} async-done(((bf16[32,130,64]{1,2,0:T(8,128)(2,1)}), bf16[32,130,64]{1,2,0:T(8,128)(2,1)S(1)}, u32[]{:S(2)}, u32[]{:S(2)}) %all-to-all-start.3) | async-done | bytes 532512 | tf_op jit(solution)/shard_map/all_to_all | solution.py:155
  147.7 0.1 slice.83
  147.8 0.3 copy.81
  148.2 0.1 reshape.112
  148.2 0.9 fusion.2
  149.1 0.1 copy.77
  149.2 0.1 reshape.120
  149.4 9.5 %all_to_all.56 = f32[32,1,576]{2,1,0:T(1,128)S(1)} all-to-all(f32[32,1,576]{2,1,0:T(1,128)S(1)} %reshape.120), channel_id=1, replica_groups=mesh['fsdp'=4,'seq'=8] {'fsdp','seq'}, dimensions={0} | all-to-all | bytes 147456 | tf_op jit(solution)/shard_map/all_to_all | solution.py:165
  158.9 0.5 broadcast.58
  159.4 0.8 reduce.7
  160.4 0.7 reshape.109
  161.1 0.6 slice_reduce_fusion
  161.7 21.1 %all-reduce.3.cloned.1.call-done = f32[256,1152]{1,0:T(8,128)} async-done(((f32[256,1152]{1,0:T(8,128)}), f32[256,1152]{1,0:T(8,128)}) %all-reduce.3.cloned.1.call-update) | async-done | bytes 1179664 | tf_op jit(solution)/shard_map/psum | solution.py:214
  182.8 2.4 %copy.96 = f32[256,1152]{1,0:T(8,128)} copy(f32[256,1152]{1,0:T(8,128)} %all-reduce.3.cloned.1.call-done) | data formatting | bytes 2359296
  (34 shorter events, 0.7 us)
Async XLA Ops:
  7.2 1.0 copy-start.5
  7.2 66.0 %all-gather.2.cloned.1.call-start = ((), (), s32[]{:S(2)}) async-start(), calls=%async_computation.5 | async-start | bytes 5898240 | tf_op jit(solution)/shard_map/all_gather | solution.py:190
  8.2 23.8 %copy-start.4 = (bf16[1,128,2048]{2,1,0:T(8,128)(2,1)S(1)}, bf16[1,128,2048]{2,1,0:T(8,128)(2,1)}, u32[]{:S(2)}) copy-start(bf16[1,128,2048]{2,1,0:T(8,128)(2,1)} %param.10) | copy-start | bytes 1572868
  8.2 23.8 %copy-start.7 = (s32[1,128]{1,0:T(1,128)S(1)}, s32[1,128]{1,0:T(1,128)}, u32[]{:S(2)}) copy-start(s32[1,128]{1,0:T(1,128)} %param.11) | copy-start | bytes 1540
  32.0 0.7 copy-start.6
  33.2 6.2 %copy-start.1 = (bf16[1,128,2048]{2,1,0:T(8,128)(2,1)S(1)}, bf16[1,128,2048]{2,1,0:T(8,128)(2,1)}, u32[]{:S(2)}) copy-start(bf16[1,128,2048]{2,1,0:T(8,128)(2,1)} %param.15) | copy-start | bytes 1572868
  34.2 47.3 %all-to-all-start.2 = ((bf16[16,128,128]{2,1,0:T(8,128)(2,1)}), bf16[16,128,128]{2,1,0:T(8,128)(2,1)S(1)}, u32[]{:S(2)}, u32[]{:S(2)}) async-start(bf16[16,128,128]{2,1,0:T(8,128)(2,1)} %bitcast.5), calls=%async_computation.2 | async-start | bytes 1048576 | tf_op jit(solution)/shard_map/all_to_all | solution.py:195
  39.9 10.0 %collective-permute-start.2 = (bf16[16,4,128]{2,1,0:T(4,128)(2,1)S(1)}, bf16[16,4,128]{2,1,0:T(4,128)(2,1)S(1)}, u32[]{:S(2)}, u32[]{:S(2)}) collective-permute-start(bf16[16,4,128]{2,1,0:T(4,128)(2,1)S(1)} %get-tuple-element.30), channel_id=1, source_target_pairs={{0,1},{1,2},{2,3},{3,4},{4,5},{5,6},{6,7},{8,9},{9,10},{10,11},{11... | collective-permute-start | bytes 49160 | tf_op jit(solution)/shard_map/ppermute | solution.py:19
  42.3 7.6 %collective-permute-start.3 = (bf16[16,4,128]{2,1,0:T(4,128)(2,1)S(1)}, bf16[16,4,128]{2,1,0:T(4,128)(2,1)S(1)}, u32[]{:S(2)}, u32[]{:S(2)}) collective-permute-start(bf16[16,4,128]{2,1,0:T(4,128)(2,1)S(1)} %get-tuple-element.31), channel_id=1, source_target_pairs={{1,0},{2,1},{3,2},{4,3},{5,4},{6,5},{7,6},{9,8},{10,9},{11,10},{12... | collective-permute-start | bytes 49160 | tf_op jit(solution)/shard_map/ppermute | solution.py:21
  44.4 6.7 %collective-permute-start = (bf16[16,8,128]{2,1,0:T(8,128)(2,1)S(1)}, bf16[16,8,128]{2,1,0:T(8,128)(2,1)S(1)}, u32[]{:S(2)}, u32[]{:S(2)}) collective-permute-start(bf16[16,8,128]{2,1,0:T(8,128)(2,1)S(1)} %get-tuple-element.32), channel_id=1, source_target_pairs={{0,1},{1,2},{2,3},{3,4},{4,5},{5,6},{6,7},{8,9},{9,10},{10,11},{11... | collective-permute-start | bytes 98312 | tf_op jit(solution)/shard_map/ppermute | solution.py:19
  48.6 4.3 %collective-permute-start.1 = (bf16[16,8,128]{2,1,0:T(8,128)(2,1)S(1)}, bf16[16,8,128]{2,1,0:T(8,128)(2,1)S(1)}, u32[]{:S(2)}, u32[]{:S(2)}) collective-permute-start(bf16[16,8,128]{2,1,0:T(8,128)(2,1)S(1)} %get-tuple-element.33), channel_id=1, source_target_pairs={{1,0},{2,1},{3,2},{4,3},{5,4},{6,5},{7,6},{9,8},{10,9},{11,10},{12... | collective-permute-start | bytes 98312 | tf_op jit(solution)/shard_map/ppermute | solution.py:21
  81.5 20.0 %all-to-all-start.1 = ((bf16[16,128,128]{2,1,0:T(8,128)(2,1)}), bf16[16,128,128]{2,1,0:T(8,128)(2,1)S(1)}, u32[]{:S(2)}, u32[]{:S(2)}) async-start(bf16[16,128,128]{2,1,0:T(8,128)(2,1)} %slice.82), calls=%async_computation.1 | async-start | bytes 1048576 | tf_op jit(solution)/shard_map/all_to_all | solution.py:196
  104.8 1.4 copy-start
  114.4 1.0 copy-start.2
  115.8 1.7 copy-start.3
  117.5 30.2 %all-to-all-start.3 = ((bf16[32,130,64]{1,2,0:T(8,128)(2,1)}), bf16[32,130,64]{1,2,0:T(8,128)(2,1)S(1)}, u32[]{:S(2)}, u32[]{:S(2)}) async-start(bf16[32,130,64]{1,2,0:T(8,128)(2,1)} %pad_maximum_fusion), calls=%async_computation.3 | async-start | bytes 2097152 | tf_op jit(solution)/shard_map/all_to_all | solution.py:155
  120.1 62.7 %all-reduce.3.cloned.1.call-start = ((), (), s32[]{:S(2)}) async-start(), calls=%async_computation.6 | async-start | bytes 2359296 | tf_op jit(solution)/shard_map/psum | solution.py:214
Sparse Core Ops, SparseCore 0:
  9.8 63.2 all-gather.1
  124.6 58.1 all-reduce.2

commit v8 on v5

--- a/solution.py
+++ b/solution.py
@@ -168,6 +168,16 @@
     return table_grad, gain_grad
 
 
+def gather_by_halves(block, gather):
+    core = lax.axis_index("seq") % 2
+    half_rows = block.shape[0] // 2
+    mine = gather(lax.dynamic_slice_in_dim(block, core * half_rows, half_rows, axis=0))
+    other = from_partner(mine, "seq", 0)
+    lower = jnp.where(core == 0, mine, other)
+    upper = jnp.where(core == 0, other, mine)
+    return jnp.stack([lower, upper], axis=1).reshape(-1, block.shape[1])
+
+
 def body(events, type_ids, type_table, norm_gain, kernel, upstream):
     length = events.shape[1]
     width = events.shape[2]
@@ -177,7 +187,8 @@
     seq_count = lax.axis_size("seq")
     total = length * seq_count * fsdp
     scale = 1.0 / jnp.sqrt(jnp.float32(total))
-    table = gather_rows(type_table, "fsdp")
+    fsdp_parts = lambda part: gather_rows(part, "fsdp").reshape(fsdp, *part.shape)
+    table = gather_by_halves(type_table, fsdp_parts)
     types = table.shape[0]
     onehot = (type_ids[0][:, None] == jnp.arange(types, dtype=jnp.int32)[None, :]).astype(jnp.bfloat16)
     mixed = events[0].astype(jnp.float32) + jnp.dot(onehot, table, preferred_element_type=jnp.float32)
@@ -185,7 +196,8 @@
     normed = (mixed * inv * norm_gain).astype(jnp.bfloat16)
     normed_g = normed.reshape(length, GROUPS, chans).transpose(1, 0, 2)
     padded = with_halo(normed_g, "seq", 1, half)
-    weights = lax.all_gather(kernel, "fsdp", axis=0, tiled=True).reshape(GROUPS, chans, KERNEL * chans)
+    weights = gather_by_halves(kernel, lambda part: lax.all_gather(part, "fsdp", axis=0))
+    weights = weights.reshape(GROUPS, chans, KERNEL * chans)
     up_float = upstream[0].astype(jnp.float32)
     up_g = up_float.reshape(length, GROUPS, chans).transpose(1, 0, 2)
     dconv = conv_dconv(padded.astype(jnp.float32), weights, up_g)

time: 185 us -> 191 us (1.032)
  blocking collectives: 33.3 us -> 23.1 us
  local copies, waits for them, and re-layouts: 16.6 us -> 23.5 us
  other arithmetic: 7.03 us -> 13.3 us
  starting transfers between devices: 21.1 us -> 26 us
    all_to_all x1, blocking collectives: 23.8 us -> 13.5 us  [gather_rows(): lax.all_to_all(jnp.tile(block, (count,) + (1,) * (block.ndim - 1)), axis,...]
    another operation x0 -> x4, other arithmetic: none -> 5.59 us  [gather_by_halves(): return jnp.stack([lower, upper], axis=1).reshape(-1, block.shape[1])]
    all_to_all x1, waiting for transfers between devices: 4.12 us -> 0.13 us  [body(): group_out = lax.all_to_all(dconv, 'seq', 0, 1, tiled=True)]
    all_gather x1, waiting for transfers between devices: 24.8 us -> 27.7 us  [body(): lax.all_gather(part, 'fsdp', axis=0)]
    all_to_all x1, starting transfers between devices: 4.6 us -> 6.96 us  [body(): group_out = lax.all_to_all(dconv, 'seq', 0, 1, tiled=True)]
    all_to_all x1, starting transfers between devices: 2.64 us -> 4.96 us  [table_and_gain(): got = lax.all_to_all(send, every, 0, 0, tiled=True)]
    unnamed x22 -> x20, local copies, waits for them, and re-layouts: 4.11 us -> 6 us
  transfers between devices with their start and end apart: 9 -> 11, of which waited for: 4 -> 4; matrix products, arithmetic and copies ran while one was open for 13% -> 18% of each run, Pallas kernels for 6% -> 6%
where the time goes in v8:
time: 191 us; the launch traced here: 190 us
  waiting for transfers between devices  73.1 us (38%)
  starting transfers between devices  26 us (14%)
  local copies, waits for them, and re-layouts  23.5 us (12%)
  blocking collectives  23.1 us (12%)
  between operations  14.4 us (8%)
  other arithmetic  13.3 us (7%)
  Pallas kernels  11.7 us (6%)
  matrix products  4.46 us (2%)
    all_gather x1, waiting for transfers between devices, body(): lax.all_gather(part, 'fsdp', axis=0)  27.7 us
    psum x1, waiting for transfers between devices, body(): kernel_grad = lax.psum(kernel_part, 'fsdp')  23.7 us
    all_to_all x1, waiting for transfers between devices, table_and_gain(): got = lax.all_to_all(send, every, 0, 0, tiled=True)  21.5 us
    all_to_all x1, blocking collectives, gather_rows(): lax.all_to_all(jnp.tile(block, (count,) + (1,) * (block.ndim - 1)), axis,...  13.5 us
    all_to_all x1, blocking collectives, table_and_gain(): back = lax.all_to_all(back, every, 0, 0, tiled=True)  9.6 us
    all_to_all x1, starting transfers between devices, body(): group_out = lax.all_to_all(dconv, 'seq', 0, 1, tiled=True)  6.96 us
    pallas_call x1, Pallas kernels, conv_dconv(): pl.pallas_call(forward_kernel, grid=(groups // step,), in_specs=[pl.Block...  6.56 us
    all_to_all x1, starting transfers between devices, body(): group_in = lax.all_to_all(normed_g, 'seq', 0, 1, tiled=True)  6.46 us
  transfers between devices with their start and end apart: 11, of which 4 were waited for; matrix products, arithmetic and copies ran while one was open for 18% of the time, Pallas kernels for 6%

profile of v8, /device:TPU:0, one launch (start us, length us, event | category | flops | bytes accessed | tf_op | source)
XLA Modules:
  0.0 189.7 jit_solution(16379731959902863108)
XLA Ops:
  7.3 1.2 copy-done
  8.4 0.9 constant_dynamic-slice_fusion
  9.4 13.5 %all_to_all.52 = bf16[4,32,2048]{2,1,0:T(8,128)(2,1)S(1)} all-to-all(bf16[4,32,2048]{2,1,0:T(8,128)(2,1)S(1)} %tile.2), channel_id=1, replica_groups=mesh['fsdp'=4,'seq'=8] {'fsdp'}, dimensions={0} | all-to-all | bytes 1048576 | tf_op jit(solution)/shard_map/all_to_all | solution.py:35
  22.9 27.7 %all-gather.3.cloned.1.call-done = bf16[1024,1152]{1,0:T(8,128)(2,1)} async-done(((bf16[256,1152]{1,0:T(8,128)(2,1)}), bf16[1024,1152]{1,0:T(8,128)(2,1)}) %all-gather.3.cloned.1.call-update) | async-done | bytes 2359312 | tf_op jit(solution)/shard_map/all_gather | solution.py:199
  50.8 0.1 pad_maximum_fusion.1
  50.9 0.9 copy-done.4
  51.8 0.4 multiply_reduce_fusion.2
  52.2 0.3 copy-done.5
  52.5 0.2 multiply_convert_fusion
  52.6 0.3 copy.71
  52.9 1.0 copy.72
  53.9 0.8 fusion.32
  54.7 2.4 %collective-permute-start.1 = (bf16[16,4,128]{2,1,0:T(4,128)(2,1)S(1)}, bf16[16,4,128]{2,1,0:T(4,128)(2,1)S(1)}, u32[]{:S(2)}, u32[]{:S(2)}) collective-permute-start(bf16[16,4,128]{2,1,0:T(4,128)(2,1)S(1)} %get-tuple-element.32), channel_id=1, source_target_pairs={{0,1},{1,2},{2,3},{3,4},{4,5},{5,6},{6,7},{8,9},{9,10},{10,11},{11... | collective-permute-start | bytes 49160 | tf_op jit(solution)/shard_map/ppermute | solution.py:19
  57.1 1.3 collective-permute-start.2
  58.4 1.2 copy.74
  59.7 1.3 copy.75
  61.0 6.5 %all-to-all-start.4 = ((bf16[16,128,128]{2,1,0:T(8,128)(2,1)}), bf16[16,128,128]{2,1,0:T(8,128)(2,1)S(1)}, u32[]{:S(2)}, u32[]{:S(2)}) async-start(bf16[16,128,128]{2,1,0:T(8,128)(2,1)} %bitcast.8), calls=%async_computation.4 | async-start | bytes 1048576 | tf_op jit(solution)/shard_map/all_to_all | solution.py:207
  67.5 2.2 %maximum_convert_fusion.pad_ref = f32[16,136,128]{2,1,0:T(8,128)} fusion(bf16[16,4,128]{2,1,0:T(4,128)(2,1)S(1)} %collective-permute-done.2, bf16[16,128,128]{2,1,0:T(8,128)(2,1)} %bitcast.8, bf16[16,4,128]{2,1,0:T(4,128)(2,1)S(1)} %collective-permute-done.1), kind=kLoop, calls=%fused_computation.26 | loop fusion | flops 1671168 | bytes 1671168 | tf_op jit(solution)/shard_map/convert_element_type | solution.py:203
  69.7 2.8 %select_bitcast_fusion.1 = (bf16[4,1,256,1152]{3,2,1,0:T(8,128)(2,1)S(1)}, bf16[4,1,256,1152]{3,2,1,0:T(8,128)(2,1)S(1)}) fusion(bf16[4,256,1152]{2,1,0:T(8,128)(2,1)} %bitcast.76, bf16[4,256,1152]{2,1,0:T(8,128)(2,1)} %collective-permute-done.3, pred[]{:T(512)S(6)} %eq.41), kind=kLoop, calls=%fused_computation.5 | loop fusion | flops 2359296 | bytes 9437185 | tf_op jit(solution)/shard_map/stack | solution.py:178
  72.5 2.6 %pad_maximum_fusion = bf16[4,2,256,1152]{3,2,1,0:T(8,128)(2,1)} fusion(bf16[4,1,256,1152]{3,2,1,0:T(8,128)(2,1)S(1)} %get-tuple-element.27, bf16[4,1,256,1152]{3,2,1,0:T(8,128)(2,1)S(1)} %get-tuple-element.26), kind=kLoop, calls=%fused_computation | loop fusion | flops 2359296 | bytes 9437184 | tf_op jit(solution)/shard_map/stack | solution.py:178
  75.1 6.6 %shard_map.98 = bf16[16,128,128]{2,1,0:T(8,128)(2,1)} custom-call(f32[16,136,128]{2,1,0:T(8,128)} %maximum_convert_fusion.pad_ref, bf16[16,128,1152]{2,1,0:T(8,128)(2,1)} %bitcast.67, f32[16,128,128]{2,1,0:T(8,128)} %bitcast.70), custom_call_target="tpu_custom_call" | custom-call | flops 603979776 | bytes 7405568 | tf_op jit(solution)/shard_map/pallas_call | solution.py:74
  81.7 0.8 fusion.31
  82.5 2.4 %collective-permute-start.4 = (bf16[16,4,128]{2,1,0:T(4,128)(2,1)S(1)}, bf16[16,4,128]{2,1,0:T(4,128)(2,1)S(1)}, u32[]{:S(2)}, u32[]{:S(2)}) collective-permute-start(bf16[16,4,128]{2,1,0:T(4,128)(2,1)S(1)} %get-tuple-element.30), channel_id=1, source_target_pairs={{0,1},{1,2},{2,3},{3,4},{4,5},{5,6},{6,7},{8,9},{9,10},{10,11},{11... | collective-permute-start | bytes 49160 | tf_op jit(solution)/shard_map/ppermute | solution.py:19
  84.9 1.3 collective-permute-start.5
  86.3 0.1 copy.79
  86.4 0.3 copy.88
  86.7 1.0 all_to_all.46
  87.8 7.0 %all-to-all-start.3 = ((bf16[16,128,128]{2,1,0:T(8,128)(2,1)}), bf16[16,128,128]{2,1,0:T(8,128)(2,1)}, u32[]{:S(2)}, u32[]{:S(2)}) async-start(bf16[16,128,128]{2,1,0:T(8,128)(2,1)} %shard_map.98), calls=%async_computation.3 | async-start | bytes 1048576 | tf_op jit(solution)/shard_map/all_to_all | solution.py:208
  94.7 1.1 maximum_convert_fusion.1.pad_ref
  95.9 5.2 %shard_map.99 = f32[16,128,128]{2,1,0:T(8,128)} custom-call(f32[16,136,128]{2,1,0:T(8,128)} %maximum_convert_fusion.1.pad_ref, bf16[16,128,1152]{2,1,0:T(8,128)(2,1)} %bitcast.68), custom_call_target="tpu_custom_call" | custom-call | flops 603979776 | bytes 6881280 | tf_op jit(solution)/shard_map/pallas_call | solution.py:96
  101.0 2.5 %copy.76 = f32[128,16,128]{0,2,1:T(8,128)} copy(f32[128,16,128]{2,0,1:T(8,128)} %bitcast.74) | data formatting | bytes 2097152 | tf_op jit(solution)/shard_map/transpose | solution.py:219
  103.6 1.6 copy.77
  105.1 0.3 multiply_reduce_fusion
  105.4 0.7 copy-done.2
  106.2 1.2 fusion.3
  107.4 1.3 copy.78
  108.7 0.1 broadcast_in_dim.8
  108.8 1.3 pad_maximum_fusion.2
  110.1 0.1 all-to-all-done.3
  110.2 5.0 %all-to-all-start.1 = ((bf16[32,130,64]{1,2,0:T(8,128)(2,1)}), bf16[32,130,64]{1,2,0:T(8,128)(2,1)S(1)}, u32[]{:S(2)}, u32[]{:S(2)}) async-start(bf16[32,130,64]{1,2,0:T(8,128)(2,1)} %pad_maximum_fusion.2), calls=%async_computation.1 | async-start | bytes 2097152 | tf_op jit(solution)/shard_map/all_to_all | solution.py:155
  115.2 0.2 all-reduce.3.cloned.1.call-start
  115.4 1.1 copy.87
  116.5 0.4 convolution_dynamic-update-slice_fusion.8
  116.8 0.4 convolution_dynamic-update-slice_fusion.7
  117.2 0.4 convolution_dynamic-update-slice_fusion.6
  117.6 0.4 convolution_dynamic-update-slice_fusion.5
  117.9 0.3 convolution_dynamic-update-slice_fusion.4
  118.2 0.4 convolution_dynamic-update-slice_fusion.3
  118.6 0.4 convolution_dynamic-update-slice_fusion.2
  119.0 0.4 convolution_dynamic-update-slice_fusion.1
  119.3 0.4 convolution_dynamic-update-slice_fusion
  119.8 1.4 copy.89
  121.3 21.5 %all-to-all-done.1 = bf16[32,130,64]{1,2,0:T(8,128)(2,1)S(1)} async-done(((bf16[32,130,64]{1,2,0:T(8,128)(2,1)}), bf16[32,130,64]{1,2,0:T(8,128)(2,1)S(1)}, u32[]{:S(2)}, u32[]{:S(2)}) %all-to-all-start.1) | async-done | bytes 532512 | tf_op jit(solution)/shard_map/all_to_all | solution.py:155
  142.7 0.1 slice.78
  142.8 0.3 copy.90
  143.3 0.9 fusion.2
  144.3 0.1 reshape.128
  144.4 9.6 %all_to_all.53 = f32[32,1,576]{2,1,0:T(1,128)S(1)} all-to-all(f32[32,1,576]{2,1,0:T(1,128)S(1)} %reshape.128), channel_id=1, replica_groups=mesh['fsdp'=4,'seq'=8] {'fsdp','seq'}, dimensions={0} | all-to-all | bytes 147456 | tf_op jit(solution)/shard_map/all_to_all | solution.py:165
  154.0 0.5 broadcast.59
  154.5 0.8 reduce.7
  155.5 0.7 reshape.115
  156.2 0.6 slice_reduce_fusion
  156.8 23.7 %all-reduce.3.cloned.1.call-done = f32[256,1152]{1,0:T(8,128)} async-done(((f32[256,1152]{1,0:T(8,128)}), f32[256,1152]{1,0:T(8,128)}) %all-reduce.3.cloned.1.call-update) | async-done | bytes 1179664 | tf_op jit(solution)/shard_map/psum | solution.py:224
  180.5 2.4 %copy.105 = f32[256,1152]{1,0:T(8,128)} copy(f32[256,1152]{1,0:T(8,128)} %all-reduce.3.cloned.1.call-done) | data formatting | bytes 2359296
  (42 shorter events, 0.9 us)
Async XLA Ops:
  7.2 1.3 copy-start
  7.2 2.2 %copy-start.6 = (bf16[64,2048]{1,0:T(8,128)(2,1)S(1)}, bf16[64,2048]{1,0:T(8,128)(2,1)}, u32[]{:S(2)}) copy-start(bf16[64,2048]{1,0:T(8,128)(2,1)} %param.12) | copy-start | bytes 786436
  7.2 43.5 %all-gather.3.cloned.1.call-start = ((), (), s32[]{:S(2)}) async-start(), calls=%async_computation.6 | async-start | bytes 2949120 | tf_op jit(solution)/shard_map/all_gather | solution.py:199
  22.9 27.8 %collective-permute-start = (bf16[4,32,2048]{2,1,0:T(8,128)(2,1)S(1)}, bf16[4,32,2048]{2,1,0:T(8,128)(2,1)S(1)}, u32[]{:S(2)}, u32[]{:S(2)}) collective-permute-start(bf16[4,32,2048]{2,1,0:T(8,128)(2,1)S(1)} %all_to_all.52), channel_id=1, source_target_pairs={{0,1},{1,0},{2,3},{3,2},{4,5},{5,4},{6,7},{7,6},{8,9},{9,8},{10,11... | collective-permute-start | bytes 1572872 | tf_op jit(solution)/shard_map/ppermute | solution.py:30
  50.7 19.0 %collective-permute-start.3 = (bf16[4,256,1152]{2,1,0:T(8,128)(2,1)}, bf16[4,256,1152]{2,1,0:T(8,128)(2,1)}, u32[]{:S(2)}, u32[]{:S(2)}) collective-permute-start(bf16[4,256,1152]{2,1,0:T(8,128)(2,1)} %bitcast.75), channel_id=1, source_target_pairs={{0,1},{1,0},{2,3},{3,2},{4,5},{5,4},{6,7},{7,6},{8,9},{9,8},{10,11... | collective-permute-start | bytes 7077896 | tf_op jit(solution)/shard_map/ppermute | solution.py:30
  50.7 1.0 copy-start.4
  50.7 1.0 copy-start.7
  51.8 0.7 copy-start.5
  54.7 12.8 %collective-permute-start.1 = (bf16[16,4,128]{2,1,0:T(4,128)(2,1)S(1)}, bf16[16,4,128]{2,1,0:T(4,128)(2,1)S(1)}, u32[]{:S(2)}, u32[]{:S(2)}) collective-permute-start(bf16[16,4,128]{2,1,0:T(4,128)(2,1)S(1)} %get-tuple-element.32), channel_id=1, source_target_pairs={{0,1},{1,2},{2,3},{3,4},{4,5},{5,6},{6,7},{8,9},{9,10},{10,11},{11... | collective-permute-start | bytes 49160 | tf_op jit(solution)/shard_map/ppermute | solution.py:19
  57.1 10.4 %collective-permute-start.2 = (bf16[16,4,128]{2,1,0:T(4,128)(2,1)S(1)}, bf16[16,4,128]{2,1,0:T(4,128)(2,1)S(1)}, u32[]{:S(2)}, u32[]{:S(2)}) collective-permute-start(bf16[16,4,128]{2,1,0:T(4,128)(2,1)S(1)} %get-tuple-element.33), channel_id=1, source_target_pairs={{1,0},{2,1},{3,2},{4,3},{5,4},{6,5},{7,6},{9,8},{10,9},{11,10},{12... | collective-permute-start | bytes 49160 | tf_op jit(solution)/shard_map/ppermute | solution.py:21
  61.0 25.4 %all-to-all-start.4 = ((bf16[16,128,128]{2,1,0:T(8,128)(2,1)}), bf16[16,128,128]{2,1,0:T(8,128)(2,1)S(1)}, u32[]{:S(2)}, u32[]{:S(2)}) async-start(bf16[16,128,128]{2,1,0:T(8,128)(2,1)} %bitcast.8), calls=%async_computation.4 | async-start | bytes 1048576 | tf_op jit(solution)/shard_map/all_to_all | solution.py:207
  82.5 12.3 %collective-permute-start.4 = (bf16[16,4,128]{2,1,0:T(4,128)(2,1)S(1)}, bf16[16,4,128]{2,1,0:T(4,128)(2,1)S(1)}, u32[]{:S(2)}, u32[]{:S(2)}) collective-permute-start(bf16[16,4,128]{2,1,0:T(4,128)(2,1)S(1)} %get-tuple-element.30), channel_id=1, source_target_pairs={{0,1},{1,2},{2,3},{3,4},{4,5},{5,6},{6,7},{8,9},{9,10},{10,11},{11... | collective-permute-start | bytes 49160 | tf_op jit(solution)/shard_map/ppermute | solution.py:19
  84.9 9.9 %collective-permute-start.5 = (bf16[16,4,128]{2,1,0:T(4,128)(2,1)S(1)}, bf16[16,4,128]{2,1,0:T(4,128)(2,1)S(1)}, u32[]{:S(2)}, u32[]{:S(2)}) collective-permute-start(bf16[16,4,128]{2,1,0:T(4,128)(2,1)S(1)} %get-tuple-element.31), channel_id=1, source_target_pairs={{1,0},{2,1},{3,2},{4,3},{5,4},{6,5},{7,6},{9,8},{10,9},{11,10},{12... | collective-permute-start | bytes 49160 | tf_op jit(solution)/shard_map/ppermute | solution.py:21
  86.7 8.0 %copy-start.1 = (bf16[16,128,128]{2,1,0:T(8,128)(2,1)S(1)}, bf16[16,128,128]{2,1,0:T(8,128)(2,1)}, u32[]{:S(2)}) copy-start(bf16[16,128,128]{2,1,0:T(8,128)(2,1)} %shard_map.98) | copy-start | bytes 1572868
  87.8 22.4 %all-to-all-start.3 = ((bf16[16,128,128]{2,1,0:T(8,128)(2,1)}), bf16[16,128,128]{2,1,0:T(8,128)(2,1)}, u32[]{:S(2)}, u32[]{:S(2)}) async-start(bf16[16,128,128]{2,1,0:T(8,128)(2,1)} %shard_map.98), calls=%async_computation.3 | async-start | bytes 1048576 | tf_op jit(solution)/shard_map/all_to_all | solution.py:208
  105.1 1.0 copy-start.2
  110.1 6.4 %copy-start.3 = (bf16[2,1024,128]{1,2,0:T(8,128)(2,1)S(1)}, bf16[2,1024,128]{1,2,0:T(8,128)(2,1)}, u32[]{:S(2)}) copy-start(bf16[2,1024,128]{1,2,0:T(8,128)(2,1)} %all_to_all.46) | copy-start | bytes 1572868
  110.2 32.6 %all-to-all-start.1 = ((bf16[32,130,64]{1,2,0:T(8,128)(2,1)}), bf16[32,130,64]{1,2,0:T(8,128)(2,1)S(1)}, u32[]{:S(2)}, u32[]{:S(2)}) async-start(bf16[32,130,64]{1,2,0:T(8,128)(2,1)} %pad_maximum_fusion.2), calls=%async_computation.1 | async-start | bytes 2097152 | tf_op jit(solution)/shard_map/all_to_all | solution.py:155
  115.2 65.3 %all-reduce.3.cloned.1.call-start = ((), (), s32[]{:S(2)}) async-start(), calls=%async_computation.5 | async-start | bytes 2359296 | tf_op jit(solution)/shard_map/psum | solution.py:224
Sparse Core Ops, SparseCore 0:
  10.4 40.1 all-gather.2
  121.3 59.1 all-reduce.2

commit v9 on v5

--- a/solution.py
+++ b/solution.py
@@ -196,20 +196,25 @@
         group_out = lax.all_to_all(dconv, "seq", 0, 1, tiled=True)
     else:
         group_in, group_out = spread_groups(normed, dconv.transpose(1, 0, 2).reshape(length, width), chans)
-    local_groups = group_in.shape[0]
-    whole = group_in.shape[1]
-    group_pad = jnp.pad(group_in, ((0, 0), (half, half), (0, 0)))
+    local_groups, whole, outs = group_out.shape
+    splits = fsdp // local_groups
+    share = outs // splits
+    send_out = group_out.reshape(local_groups, whole, splits, share).transpose(0, 2, 1, 3).reshape(fsdp, whole, share)
+    send_in = jnp.stack([group_in[part // splits] for part in range(fsdp)])
+    streams_out = lax.all_to_all(send_out, "fsdp", 0, 0, tiled=True)
+    streams_in = lax.all_to_all(send_in, "fsdp", 0, 0, tiled=True)
+    streams_pad = jnp.pad(streams_in, ((0, 0), (half, half), (0, 0)))
     kterms = [
-        jnp.einsum("gto,gtc->goc", group_out, group_pad[:, k : k + whole], preferred_element_type=jnp.float32)
+        jnp.einsum("sto,stc->oc", streams_out, streams_pad[:, k : k + whole], preferred_element_type=jnp.float32)
         for k in range(KERNEL)
     ]
-    kernel_part = jnp.concatenate(kterms, axis=-1).reshape(-1, KERNEL * chans) * scale
+    kernel_rows = jnp.concatenate(kterms, axis=-1) * scale
+    kernel_grad = lax.all_gather(kernel_rows, "fsdp", axis=0, tiled=True)
     dnormed = dnormed.transpose(1, 0, 2).reshape(length, width)
     gain_term = jnp.sum(dnormed * mixed * inv, axis=0) * scale
     scaled = norm_gain * dnormed
     dmixed = inv * scaled - mixed * inv * inv * inv * jnp.mean(scaled * mixed, axis=-1, keepdims=True)
     input_grad = (up_float + dmixed).astype(jnp.bfloat16)
-    kernel_grad = lax.psum(kernel_part, "fsdp")
     table_grad, gain_grad = table_and_gain(input_grad, type_ids[0], gain_term, types, scale)
     return (input_grad[None], table_grad, gain_grad, kernel_grad)
 

time: 185 us -> 194 us (1.049)
  waiting for transfers between devices: 74.9 us -> 60.5 us
  matrix products: 4.46 us -> 14.2 us
  starting transfers between devices: 21.1 us -> 28.3 us
  other arithmetic: 7.03 us -> 10.5 us
  local copies, waits for them, and re-layouts: 16.6 us -> 19.5 us
    psum x1 -> x0, waiting for transfers between devices: 23.6 us -> none  [body(): kernel_grad = lax.psum(kernel_part, 'fsdp')]
    all_to_all x1, waiting for transfers between devices: 4.12 us -> 14.2 us  [body(): group_out = lax.all_to_all(dconv, 'seq', 0, 1, tiled=True)]
    dot_general x9, matrix products: 3.16 us -> 12.9 us  [body(): jnp.einsum('sto,stc->oc', streams_out, streams_pad[:, k:k + whole], prefe...]
    all_to_all x1, waiting for transfers between devices: 21.7 us -> 13.7 us  [table_and_gain(): got = lax.all_to_all(send, every, 0, 0, tiled=True)]
    all_to_all x0 -> x2, starting transfers between devices: none -> 7.65 us  [the longest x1 4.14 us: body(): streams_out = lax.all_to_all(send_out, 'fsdp', 0, 0, tiled=True)]
    all_to_all x0 -> x2, waiting for transfers between devices: none -> 3.19 us  [the longest x1 3.19 us: body(): streams_out = lax.all_to_all(send_out, 'fsdp', 0, 0, tiled=True)]
    ppermute x2, waiting for transfers between devices: 0.01 us -> 2.9 us  [with_halo(): lax.ppermute(head, axis, [((i + 1) % count, i) for i in range(ends)])]
    ppermute x2, starting transfers between devices: 6.07 us -> 3.95 us  [with_halo(): lax.ppermute(tail, axis, [(i, (i + 1) % count) for i in range(ends)])]
  transfers between devices with their start and end apart: 9 -> 11, of which waited for: 4 -> 7; matrix products, arithmetic and copies ran while one was open for 13% -> 21% of each run, Pallas kernels for 6% -> 6%
where the time goes in v9:
time: 194 us; the launch traced here: 193 us
  waiting for transfers between devices  60.5 us (31%)
  blocking collectives  33.5 us (17%)
  starting transfers between devices  28.3 us (15%)
  local copies, waits for them, and re-layouts  19.5 us (10%)
  between operations  14.4 us (7%)
  matrix products  14.2 us (7%)
  Pallas kernels  11.7 us (6%)
  other arithmetic  10.5 us (5%)
    all_gather x1, waiting for transfers between devices, body(): lax.all_gather(kernel, 'fsdp', axis=0, tiled=True)  24.2 us
    all_to_all x1, blocking collectives, gather_rows(): lax.all_to_all(jnp.tile(block, (count,) + (1,) * (block.ndim - 1)), axis,...  23.8 us
    all_to_all x1, waiting for transfers between devices, body(): group_out = lax.all_to_all(dconv, 'seq', 0, 1, tiled=True)  14.2 us
    all_to_all x1, waiting for transfers between devices, table_and_gain(): got = lax.all_to_all(send, every, 0, 0, tiled=True)  13.7 us
    dot_general x9, matrix products, body(): jnp.einsum('sto,stc->oc', streams_out, streams_pad[:, k:k + whole], prefe...  12.9 us
    all_to_all x1, blocking collectives, table_and_gain(): back = lax.all_to_all(back, every, 0, 0, tiled=True)  9.7 us
    pallas_call x1, Pallas kernels, conv_dconv(): pl.pallas_call(forward_kernel, grid=(groups // step,), in_specs=[pl.Block...  6.56 us
    pallas_call x1, Pallas kernels, conv_transpose(): pl.pallas_call(backward_kernel, grid=(groups // step,), in_specs=[pl.Bloc...  5.17 us
  transfers between devices with their start and end apart: 11, of which 7 were waited for; matrix products, arithmetic and copies ran while one was open for 21% of the time, Pallas kernels for 6%

profile of v9, /device:TPU:0, one launch (start us, length us, event | category | flops | bytes accessed | tf_op | source)
XLA Modules:
  0.0 192.5 jit_solution(15923770067476905857)
XLA Ops:
  7.2 0.7 all-gather.3.cloned.1.call-update
  7.9 0.2 copy-done.4
  8.1 0.1 tile.2
  8.3 23.8 %all_to_all.59 = bf16[4,64,2048]{2,1,0:T(8,128)(2,1)S(1)} all-to-all(bf16[4,64,2048]{2,1,0:T(8,128)(2,1)S(1)} %tile.2), channel_id=1, replica_groups=mesh['fsdp'=4,'seq'=8] {'fsdp'}, dimensions={0} | all-to-all | bytes 2097152 | tf_op jit(solution)/shard_map/all_to_all | solution.py:35
  32.0 0.4 multiply_reduce_fusion.2
  32.5 0.3 copy-done.5
  32.7 0.2 multiply_convert_fusion
  32.9 0.3 copy.55
  33.2 1.0 copy.56
  34.2 5.2 %all-to-all-start.5 = ((bf16[16,128,128]{2,1,0:T(8,128)(2,1)}), bf16[16,128,128]{2,1,0:T(8,128)(2,1)S(1)}, u32[]{:S(2)}, u32[]{:S(2)}) async-start(bf16[16,128,128]{2,1,0:T(8,128)(2,1)} %bitcast.5), calls=%async_computation.5 | async-start | bytes 1048576 | tf_op jit(solution)/shard_map/all_to_all | solution.py:195
  39.3 0.8 fusion.42
  40.1 2.4 %collective-permute-start = (bf16[16,4,128]{2,1,0:T(4,128)(2,1)S(1)}, bf16[16,4,128]{2,1,0:T(4,128)(2,1)S(1)}, u32[]{:S(2)}, u32[]{:S(2)}) collective-permute-start(bf16[16,4,128]{2,1,0:T(4,128)(2,1)S(1)} %get-tuple-element.30), channel_id=1, source_target_pairs={{0,1},{1,2},{2,3},{3,4},{4,5},{5,6},{6,7},{8,9},{9,10},{10,11},{11... | collective-permute-start | bytes 49160 | tf_op jit(solution)/shard_map/ppermute | solution.py:19
  42.6 1.3 collective-permute-start.1
  43.9 0.2 copy.57
  44.1 1.4 copy.58
  45.4 1.3 collective-permute-done.1
  46.8 2.2 %maximum_convert_fusion.pad_ref = f32[16,136,128]{2,1,0:T(8,128)} fusion(bf16[16,4,128]{2,1,0:T(4,128)(2,1)S(1)} %collective-permute-done.1, bf16[16,128,128]{2,1,0:T(8,128)(2,1)} %bitcast.5, bf16[16,4,128]{2,1,0:T(4,128)(2,1)S(1)} %collective-permute-done), kind=kLoop, calls=%fused_computation.39 | loop fusion | flops 1671168 | bytes 1671168 | tf_op jit(solution)/shard_map/convert_element_type | solution.py:191
  48.9 24.2 %all-gather.3.cloned.1.call-done = bf16[2048,1152]{1,0:T(8,128)(2,1)} async-done(((bf16[512,1152]{1,0:T(8,128)(2,1)}), bf16[2048,1152]{1,0:T(8,128)(2,1)}) %all-gather.3.cloned.1.call-update) | async-done | bytes 4718608 | tf_op jit(solution)/shard_map/all_gather | solution.py:188
  73.1 6.6 %shard_map.98 = bf16[16,128,128]{2,1,0:T(8,128)(2,1)} custom-call(f32[16,136,128]{2,1,0:T(8,128)} %maximum_convert_fusion.pad_ref, bf16[16,128,1152]{2,1,0:T(8,128)(2,1)} %bitcast.92, f32[16,128,128]{2,1,0:T(8,128)} %bitcast.94), custom_call_target="tpu_custom_call" | custom-call | flops 603979776 | bytes 7405568 | tf_op jit(solution)/shard_map/pallas_call | solution.py:74
  79.7 4.6 %all-to-all-start.3 = ((bf16[16,128,128]{2,1,0:T(8,128)(2,1)}), bf16[16,128,128]{2,1,0:T(8,128)(2,1)S(1)}, u32[]{:S(2)}, u32[]{:S(2)}) async-start(bf16[16,128,128]{2,1,0:T(8,128)(2,1)} %shard_map.98), calls=%async_computation.3 | async-start | bytes 1048576 | tf_op jit(solution)/shard_map/all_to_all | solution.py:196
  84.4 1.1 pad_maximum_fusion.1
  85.5 14.2 %all-to-all-done.3 = bf16[16,128,128]{2,1,0:T(8,128)(2,1)S(1)} async-done(((bf16[16,128,128]{2,1,0:T(8,128)(2,1)}), bf16[16,128,128]{2,1,0:T(8,128)(2,1)S(1)}, u32[]{:S(2)}, u32[]{:S(2)}) %all-to-all-start.3) | async-done | bytes 524320 | tf_op jit(solution)/shard_map/all_to_all | solution.py:196
  99.7 0.8 copy-done.2
  100.5 3.5 %all-to-all-start.6 = ((bf16[4,1024,128]{2,1,0:T(8,128)(2,1)}), bf16[4,1024,128]{2,1,0:T(8,128)(2,1)S(1)}, u32[]{:S(2)}, u32[]{:S(2)}) async-start(bf16[4,1024,128]{2,1,0:T(8,128)(2,1)} %pad_maximum_fusion.1), calls=%async_computation.6 | async-start | bytes 2097152 | tf_op jit(solution)/shard_map/all_to_all | solution.py:205
  104.0 1.5 collective-permute-start.2
  105.6 1.3 collective-permute-start.3
  107.0 0.1 copy.62
  107.1 1.6 collective-permute-done.3
  108.7 1.1 maximum_convert_fusion.1.pad_ref
  109.8 5.2 %shard_map.99 = f32[16,128,128]{2,1,0:T(8,128)} custom-call(f32[16,136,128]{2,1,0:T(8,128)} %maximum_convert_fusion.1.pad_ref, bf16[16,128,1152]{2,1,0:T(8,128)(2,1)} %bitcast.93), custom_call_target="tpu_custom_call" | custom-call | flops 603979776 | bytes 6881280 | tf_op jit(solution)/shard_map/pallas_call | solution.py:96
  114.9 2.5 %copy.59 = f32[128,16,128]{0,2,1:T(8,128)} copy(f32[128,16,128]{2,0,1:T(8,128)} %bitcast.98) | data formatting | bytes 2097152 | tf_op jit(solution)/shard_map/transpose | solution.py:213
  117.5 1.6 copy.60
  119.0 0.3 multiply_reduce_fusion
  119.3 2.1 %copy.70 = bf16[8,2,128,128]{2,0,3,1:T(8,128)(2,1)} copy(bf16[8,2,128,128]{3,2,1,0:T(8,128)(2,1)} %bitcast.99) | data formatting | bytes 1048576 | tf_op jit(solution)/shard_map/all_to_all | solution.py:196
  121.4 2.1 %reshape.120 = bf16[2,1024,2,64]{1,3,2,0:T(8,128)(2,1)} reshape(bf16[2,8,128,128]{2,1,3,0:T(8,128)(2,1)} %bitcast.103) | data formatting | bytes 1048576 | tf_op jit(solution)/shard_map/reshape | solution.py:202
  123.5 4.1 %all-to-all-start.4 = ((bf16[4,1024,64]{1,2,0:T(8,128)(2,1)}), bf16[4,1024,64]{1,2,0:T(8,128)(2,1)}, u32[]{:S(2)}, u32[]{:S(2)}) async-start(bf16[4,1024,64]{1,2,0:T(8,128)(2,1)} %bitcast.101), calls=%async_computation.4 | async-start | bytes 1048576 | tf_op jit(solution)/shard_map/all_to_all | solution.py:204
  127.6 2.2 %fusion.12 = bf16[128,2048]{1,0:T(8,128)(2,1)} fusion(f32[128,2048]{1,0:T(8,128)S(1)} %copy.60, f32[128,2048]{1,0:T(8,128)S(1)} %get-tuple-element.33, f32[128]{0:T(128)S(1)} %broadcast_multiply_fusion.2, f32[2048]{0:T(1024)S(1)} %copy-done.5, f32[128]{0:T(128)S(1)} %add_rsqrt_fusion, bf16[1,128,2048]{2,1,0:T(8,128)(2,1)} %param.15), kind=kLoop, calls=%fused_computation.26 | loop fusion | flops 2621440 | bytes 3154944 | tf_op jit(solution)/shard_map/convert_element_type | solution.py:217
  129.9 1.3 copy.61
  131.2 0.1 broadcast_in_dim.8
  131.3 1.2 pad_maximum_fusion
  132.5 3.2 %all-to-all-done.4 = bf16[4,1024,64]{1,2,0:T(8,128)(2,1)} async-done(((bf16[4,1024,64]{1,2,0:T(8,128)(2,1)}), bf16[4,1024,64]{1,2,0:T(8,128)(2,1)}, u32[]{:S(2)}, u32[]{:S(2)}) %all-to-all-start.4) | async-done | bytes 524320 | tf_op jit(solution)/shard_map/all_to_all | solution.py:204
  135.7 4.3 %all-to-all-start.1 = ((bf16[32,130,64]{1,2,0:T(8,128)(2,1)}), bf16[32,130,64]{1,2,0:T(8,128)(2,1)S(1)}, u32[]{:S(2)}, u32[]{:S(2)}) async-start(bf16[32,130,64]{1,2,0:T(8,128)(2,1)} %pad_maximum_fusion), calls=%async_computation.1 | async-start | bytes 2097152 | tf_op jit(solution)/shard_map/all_to_all | solution.py:155
  140.0 1.4 fusion.11
  141.5 1.4 fusion.10
  142.9 1.4 fusion.9
  144.4 1.5 fusion.8
  145.9 1.3 fusion.7
  147.2 1.4 fusion.6
  148.7 1.4 fusion.5
  150.1 1.4 fusion.4
  151.6 1.4 fusion.3
  153.0 0.7 broadcast_multiply_fusion
  153.9 13.7 %all-to-all-done.1 = bf16[32,130,64]{1,2,0:T(8,128)(2,1)S(1)} async-done(((bf16[32,130,64]{1,2,0:T(8,128)(2,1)}), bf16[32,130,64]{1,2,0:T(8,128)(2,1)S(1)}, u32[]{:S(2)}, u32[]{:S(2)}) %all-to-all-start.1) | async-done | bytes 532512 | tf_op jit(solution)/shard_map/all_to_all | solution.py:155
  167.6 0.1 slice.96
  167.7 0.3 copy.71
  168.1 0.9 fusion.2
  169.1 0.1 reshape.142
  169.3 9.7 %all_to_all.60 = f32[32,1,576]{2,1,0:T(1,128)S(1)} all-to-all(f32[32,1,576]{2,1,0:T(1,128)S(1)} %reshape.142), channel_id=1, replica_groups=mesh['fsdp'=4,'seq'=8] {'fsdp','seq'}, dimensions={0} | all-to-all | bytes 147456 | tf_op jit(solution)/shard_map/all_to_all | solution.py:165
  179.0 0.5 broadcast.56
  179.5 0.8 reduce.7
  180.5 0.7 reshape.119
  181.2 0.6 slice_reduce_fusion
  181.7 1.6 all-gather.5.cloned.1.call-done
  183.3 2.4 %copy.86 = f32[256,1152]{1,0:T(8,128)} copy(f32[256,1152]{1,0:T(8,128)} %all-gather.5.cloned.1.call-done) | data formatting | bytes 2359296
  (34 shorter events, 0.8 us)
Async XLA Ops:
  7.2 1.0 copy-start.4
  7.2 66.0 %all-gather.3.cloned.1.call-start = ((), (), s32[]{:S(2)}) async-start(), calls=%async_computation.7 | async-start | bytes 5898240 | tf_op jit(solution)/shard_map/all_gather | solution.py:188
  8.2 23.8 %copy-start.3 = (bf16[1,128,2048]{2,1,0:T(8,128)(2,1)S(1)}, bf16[1,128,2048]{2,1,0:T(8,128)(2,1)}, u32[]{:S(2)}) copy-start(bf16[1,128,2048]{2,1,0:T(8,128)(2,1)} %param.10) | copy-start | bytes 1572868
  8.2 23.8 %copy-start.6 = (s32[1,128]{1,0:T(1,128)S(1)}, s32[1,128]{1,0:T(1,128)}, u32[]{:S(2)}) copy-start(s32[1,128]{1,0:T(1,128)} %param.11) | copy-start | bytes 1540
  32.0 0.7 copy-start.5
  33.2 10.7 %copy-start.1 = (bf16[1,128,2048]{2,1,0:T(8,128)(2,1)S(1)}, bf16[1,128,2048]{2,1,0:T(8,128)(2,1)}, u32[]{:S(2)}) copy-start(bf16[1,128,2048]{2,1,0:T(8,128)(2,1)} %param.15) | copy-start | bytes 1572868
  34.2 45.5 %all-to-all-start.5 = ((bf16[16,128,128]{2,1,0:T(8,128)(2,1)}), bf16[16,128,128]{2,1,0:T(8,128)(2,1)S(1)}, u32[]{:S(2)}, u32[]{:S(2)}) async-start(bf16[16,128,128]{2,1,0:T(8,128)(2,1)} %bitcast.5), calls=%async_computation.5 | async-start | bytes 1048576 | tf_op jit(solution)/shard_map/all_to_all | solution.py:195
  40.1 5.3 %collective-permute-start = (bf16[16,4,128]{2,1,0:T(4,128)(2,1)S(1)}, bf16[16,4,128]{2,1,0:T(4,128)(2,1)S(1)}, u32[]{:S(2)}, u32[]{:S(2)}) collective-permute-start(bf16[16,4,128]{2,1,0:T(4,128)(2,1)S(1)} %get-tuple-element.30), channel_id=1, source_target_pairs={{0,1},{1,2},{2,3},{3,4},{4,5},{5,6},{6,7},{8,9},{9,10},{10,11},{11... | collective-permute-start | bytes 49160 | tf_op jit(solution)/shard_map/ppermute | solution.py:19
  42.6 4.2 %collective-permute-start.1 = (bf16[16,4,128]{2,1,0:T(4,128)(2,1)S(1)}, bf16[16,4,128]{2,1,0:T(4,128)(2,1)S(1)}, u32[]{:S(2)}, u32[]{:S(2)}) collective-permute-start(bf16[16,4,128]{2,1,0:T(4,128)(2,1)S(1)} %get-tuple-element.31), channel_id=1, source_target_pairs={{1,0},{2,1},{3,2},{4,3},{5,4},{6,5},{7,6},{9,8},{10,9},{11,10},{12... | collective-permute-start | bytes 49160 | tf_op jit(solution)/shard_map/ppermute | solution.py:21
  79.7 20.0 %all-to-all-start.3 = ((bf16[16,128,128]{2,1,0:T(8,128)(2,1)}), bf16[16,128,128]{2,1,0:T(8,128)(2,1)S(1)}, u32[]{:S(2)}, u32[]{:S(2)}) async-start(bf16[16,128,128]{2,1,0:T(8,128)(2,1)} %shard_map.98), calls=%async_computation.3 | async-start | bytes 1048576 | tf_op jit(solution)/shard_map/all_to_all | solution.py:196
  85.5 18.5 %copy-start = (bf16[16,128,128]{2,1,0:T(8,128)(2,1)S(1)}, bf16[16,128,128]{2,1,0:T(8,128)(2,1)}, u32[]{:S(2)}) copy-start(bf16[16,128,128]{2,1,0:T(8,128)(2,1)} %shard_map.98) | copy-start | bytes 1572868
  99.7 0.8 copy-start.2
  100.5 23.0 %all-to-all-start.6 = ((bf16[4,1024,128]{2,1,0:T(8,128)(2,1)}), bf16[4,1024,128]{2,1,0:T(8,128)(2,1)S(1)}, u32[]{:S(2)}, u32[]{:S(2)}) async-start(bf16[4,1024,128]{2,1,0:T(8,128)(2,1)} %pad_maximum_fusion.1), calls=%async_computation.6 | async-start | bytes 2097152 | tf_op jit(solution)/shard_map/all_to_all | solution.py:205
  104.0 3.1 %collective-permute-start.2 = (bf16[16,4,128]{2,1,0:T(4,128)(2,1)S(1)}, bf16[16,4,128]{2,1,0:T(4,128)(2,1)S(1)}, u32[]{:S(2)}, u32[]{:S(2)}) collective-permute-start(bf16[16,4,128]{2,1,0:T(4,128)(2,1)S(1)} %get-tuple-element.28), channel_id=1, source_target_pairs={{0,1},{1,2},{2,3},{3,4},{4,5},{5,6},{6,7},{8,9},{9,10},{10,11},{11... | collective-permute-start | bytes 49160 | tf_op jit(solution)/shard_map/ppermute | solution.py:19
  105.6 3.1 %collective-permute-start.3 = (bf16[16,4,128]{2,1,0:T(4,128)(2,1)S(1)}, bf16[16,4,128]{2,1,0:T(4,128)(2,1)S(1)}, u32[]{:S(2)}, u32[]{:S(2)}) collective-permute-start(bf16[16,4,128]{2,1,0:T(4,128)(2,1)S(1)} %get-tuple-element.29), channel_id=1, source_target_pairs={{1,0},{2,1},{3,2},{4,3},{5,4},{6,5},{7,6},{9,8},{10,9},{11,10},{12... | collective-permute-start | bytes 49160 | tf_op jit(solution)/shard_map/ppermute | solution.py:21
  123.5 12.2 %all-to-all-start.4 = ((bf16[4,1024,64]{1,2,0:T(8,128)(2,1)}), bf16[4,1024,64]{1,2,0:T(8,128)(2,1)}, u32[]{:S(2)}, u32[]{:S(2)}) async-start(bf16[4,1024,64]{1,2,0:T(8,128)(2,1)} %bitcast.101), calls=%async_computation.4 | async-start | bytes 1048576 | tf_op jit(solution)/shard_map/all_to_all | solution.py:204
  135.7 31.9 %all-to-all-start.1 = ((bf16[32,130,64]{1,2,0:T(8,128)(2,1)}), bf16[32,130,64]{1,2,0:T(8,128)(2,1)S(1)}, u32[]{:S(2)}, u32[]{:S(2)}) async-start(bf16[32,130,64]{1,2,0:T(8,128)(2,1)} %pad_maximum_fusion), calls=%async_computation.1 | async-start | bytes 2097152 | tf_op jit(solution)/shard_map/all_to_all | solution.py:155
  140.0 43.3 %all-gather.5.cloned.1.call-start = ((), (), s32[]{:S(2)}) async-start(), calls=%async_computation.8 | async-start | bytes 1474560 | tf_op jit(solution)/shard_map/all_gather | solution.py:212
Sparse Core Ops, SparseCore 0:
  9.8 63.2 all-gather.2
  153.9 29.3 all-gather.4

commit v10 on v5

--- a/solution.py
+++ b/solution.py
@@ -166,6 +166,27 @@
     table_grad = back[:, :per].transpose(1, 0, 2).reshape(per, width)
     gain_grad = back[:, per].sum(axis=0)
     return table_grad, gain_grad
+
+
+def psum_by_permutes(block, axis):
+    count = lax.axis_size(axis)
+    if count & (count - 1):
+        return lax.psum(block, axis)
+    me = lax.axis_index(axis)
+    rows = block.shape[0] // count
+    chunk = lambda index: lax.dynamic_slice_in_dim(block, index * rows, rows, axis=0)
+    total = chunk(me)
+    for apart in range(1, count):
+        pairs = [(source, source ^ apart) for source in range(count)]
+        total = total + lax.ppermute(chunk(me ^ apart), axis, pairs)
+    pieces = [total]
+    for apart in range(1, count):
+        pairs = [(source, source ^ apart) for source in range(count)]
+        pieces.append(lax.ppermute(total, axis, pairs))
+    stacked = jnp.stack(pieces)
+    return jnp.concatenate(
+        [lax.dynamic_index_in_dim(stacked, index ^ me, keepdims=False) for index in range(count)], axis=0
+    )
 
 
 def body(events, type_ids, type_table, norm_gain, kernel, upstream):
@@ -209,7 +230,7 @@
     scaled = norm_gain * dnormed
     dmixed = inv * scaled - mixed * inv * inv * inv * jnp.mean(scaled * mixed, axis=-1, keepdims=True)
     input_grad = (up_float + dmixed).astype(jnp.bfloat16)
-    kernel_grad = lax.psum(kernel_part, "fsdp")
+    kernel_grad = psum_by_permutes(kernel_part, "fsdp")
     table_grad, gain_grad = table_and_gain(input_grad, type_ids[0], gain_term, types, scale)
     return (input_grad[None], table_grad, gain_grad, kernel_grad)
 

time: 185 us -> 177 us (0.957)
  starting transfers between devices: 21.1 us -> 30.7 us
  blocking collectives: 33.3 us -> 23.8 us
  waiting for transfers between devices: 74.9 us -> 66.7 us
  other arithmetic: 7.03 us -> 9.37 us
  local copies, waits for them, and re-layouts: 16.6 us -> 14.6 us
    psum x1 -> x0, waiting for transfers between devices: 23.6 us -> none  [body(): kernel_grad = lax.psum(kernel_part, 'fsdp')]
    ppermute x0 -> x6, waiting for transfers between devices: none -> 10.9 us  [the longest x3 10.9 us: psum_by_permutes(): pieces.append(lax.ppermute(total, axis, pairs))]
    all_to_all x1 -> x0, blocking collectives: 9.53 us -> none  [table_and_gain(): back = lax.all_to_all(back, every, 0, 0, tiled=True)]
    all_to_all x0 -> x1, waiting for transfers between devices: none -> 7.55 us  [table_and_gain(): back = lax.all_to_all(back, every, 0, 0, tiled=True)]
    ppermute x0 -> x6, starting transfers between devices: none -> 7.04 us  [the longest x3 3.55 us: psum_by_permutes(): pieces.append(lax.ppermute(total, axis, pairs))]
    all_to_all x1, waiting for transfers between devices: 21.7 us -> 18.5 us  [table_and_gain(): got = lax.all_to_all(send, every, 0, 0, tiled=True)]
    all_to_all x0 -> x1, starting transfers between devices: none -> 2.57 us  [table_and_gain(): back = lax.all_to_all(back, every, 0, 0, tiled=True)]
    unnamed x22 -> x21, local copies, waits for them, and re-layouts: 4.11 us -> 2.31 us
  transfers between devices with their start and end apart: 9 -> 15, of which waited for: 4 -> 6; matrix products, arithmetic and copies ran while one was open for 13% -> 14% of each run, Pallas kernels for 6% -> 7%
where the time goes in v10:
time: 177 us; the launch traced here: 176 us
  waiting for transfers between devices  66.7 us (38%)
  starting transfers between devices  30.7 us (17%)
  blocking collectives  23.8 us (13%)
  local copies, waits for them, and re-layouts  14.6 us (8%)
  between operations  14.5 us (8%)
  Pallas kernels  11.7 us (7%)
  other arithmetic  9.37 us (5%)
  matrix products  4.47 us (3%)
    all_gather x1, waiting for transfers between devices, body(): lax.all_gather(kernel, 'fsdp', axis=0, tiled=True)  24.8 us
    all_to_all x1, blocking collectives, gather_rows(): lax.all_to_all(jnp.tile(block, (count,) + (1,) * (block.ndim - 1)), axis,...  23.8 us
    all_to_all x1, waiting for transfers between devices, table_and_gain(): got = lax.all_to_all(send, every, 0, 0, tiled=True)  18.5 us
    ppermute x3, waiting for transfers between devices, psum_by_permutes(): pieces.append(lax.ppermute(total, axis, pairs))  10.9 us
    all_to_all x1, waiting for transfers between devices, table_and_gain(): back = lax.all_to_all(back, every, 0, 0, tiled=True)  7.55 us
    pallas_call x1, Pallas kernels, conv_dconv(): pl.pallas_call(forward_kernel, grid=(groups // step,), in_specs=[pl.Block...  6.55 us
    ppermute x2, starting transfers between devices, with_halo(): lax.ppermute(tail, axis, [(i, (i + 1) % count) for i in range(ends)])  6.07 us
    pallas_call x1, Pallas kernels, conv_transpose(): pl.pallas_call(backward_kernel, grid=(groups // step,), in_specs=[pl.Bloc...  5.17 us
  transfers between devices with their start and end apart: 15, of which 6 were waited for; matrix products, arithmetic and copies ran while one was open for 14% of the time, Pallas kernels for 7%

profile of v10, /device:TPU:0, one launch (start us, length us, event | category | flops | bytes accessed | tf_op | source)
XLA Modules:
  0.0 175.8 jit_solution(10148262082649329000)
XLA Ops:
  7.2 0.7 all-gather.2.cloned.1.call-update
  7.9 0.2 copy-done.6
  8.3 23.8 %all_to_all.55 = bf16[4,64,2048]{2,1,0:T(8,128)(2,1)S(1)} all-to-all(bf16[4,64,2048]{2,1,0:T(8,128)(2,1)S(1)} %tile.2), channel_id=1, replica_groups=mesh['fsdp'=4,'seq'=8] {'fsdp'}, dimensions={0} | all-to-all | bytes 2097152 | tf_op jit(solution)/shard_map/all_to_all | solution.py:35
  32.0 0.4 multiply_reduce_fusion.2
  32.5 0.3 copy-done.7
  32.9 0.3 copy.63
  33.2 1.0 copy.64
  34.2 5.2 %all-to-all-start.4 = ((bf16[16,128,128]{2,1,0:T(8,128)(2,1)}), bf16[16,128,128]{2,1,0:T(8,128)(2,1)S(1)}, u32[]{:S(2)}, u32[]{:S(2)}) async-start(bf16[16,128,128]{2,1,0:T(8,128)(2,1)} %bitcast.5), calls=%async_computation.4 | async-start | bytes 1048576 | tf_op jit(solution)/shard_map/all_to_all | solution.py:216
  39.3 0.8 fusion.32
  40.1 1.3 collective-permute-start.1
  41.4 3.0 %collective-permute-start = (bf16[16,4,128]{2,1,0:T(4,128)(2,1)S(1)}, bf16[16,4,128]{2,1,0:T(4,128)(2,1)S(1)}, u32[]{:S(2)}, u32[]{:S(2)}) collective-permute-start(bf16[16,4,128]{2,1,0:T(4,128)(2,1)S(1)} %get-tuple-element.35), channel_id=1, source_target_pairs={{0,1},{1,2},{2,3},{3,4},{4,5},{5,6},{6,7},{8,9},{9,10},{10,11},{11... | collective-permute-start | bytes 49160 | tf_op jit(solution)/shard_map/ppermute | solution.py:19
  44.7 1.3 copy.66
  46.0 2.3 %maximum_convert_fusion.pad_ref = f32[16,136,128]{2,1,0:T(8,128)} fusion(bf16[16,4,128]{2,1,0:T(4,128)(2,1)S(1)} %collective-permute-done.1, bf16[16,128,128]{2,1,0:T(8,128)(2,1)} %bitcast.5, bf16[16,4,128]{2,1,0:T(4,128)(2,1)S(1)} %collective-permute-done), kind=kLoop, calls=%fused_computation.24 | loop fusion | flops 1671168 | bytes 1671168 | tf_op jit(solution)/shard_map/convert_element_type | solution.py:212
  48.3 24.8 %all-gather.2.cloned.1.call-done = bf16[2048,1152]{1,0:T(8,128)(2,1)} async-done(((bf16[512,1152]{1,0:T(8,128)(2,1)}), bf16[2048,1152]{1,0:T(8,128)(2,1)}) %all-gather.2.cloned.1.call-update) | async-done | bytes 4718608 | tf_op jit(solution)/shard_map/all_gather | solution.py:209
  73.1 6.6 %shard_map.98 = bf16[16,128,128]{2,1,0:T(8,128)(2,1)} custom-call(f32[16,136,128]{2,1,0:T(8,128)} %maximum_convert_fusion.pad_ref, bf16[16,128,1152]{2,1,0:T(8,128)(2,1)} %bitcast.66, f32[16,128,128]{2,1,0:T(8,128)} %bitcast.70), custom_call_target="tpu_custom_call" | custom-call | flops 603979776 | bytes 7405568 | tf_op jit(solution)/shard_map/pallas_call | solution.py:74
  79.7 0.8 fusion.31
  80.5 1.3 collective-permute-start.3
  81.8 3.0 %collective-permute-start.2 = (bf16[16,4,128]{2,1,0:T(4,128)(2,1)S(1)}, bf16[16,4,128]{2,1,0:T(4,128)(2,1)S(1)}, u32[]{:S(2)}, u32[]{:S(2)}) collective-permute-start(bf16[16,4,128]{2,1,0:T(4,128)(2,1)S(1)} %get-tuple-element.33), channel_id=1, source_target_pairs={{0,1},{1,2},{2,3},{3,4},{4,5},{5,6},{6,7},{8,9},{9,10},{10,11},{11... | collective-permute-start | bytes 49160 | tf_op jit(solution)/shard_map/ppermute | solution.py:19
  85.1 0.3 copy.79
  85.4 1.0 all_to_all.49
  86.4 4.6 %all-to-all-start.3 = ((bf16[16,128,128]{2,1,0:T(8,128)(2,1)}), bf16[16,128,128]{2,1,0:T(8,128)(2,1)}, u32[]{:S(2)}, u32[]{:S(2)}) async-start(bf16[16,128,128]{2,1,0:T(8,128)(2,1)} %shard_map.98), calls=%async_computation.3 | async-start | bytes 1048576 | tf_op jit(solution)/shard_map/all_to_all | solution.py:217
  91.1 1.1 maximum_convert_fusion.1.pad_ref
  92.2 5.2 %shard_map.99 = f32[16,128,128]{2,1,0:T(8,128)} custom-call(f32[16,136,128]{2,1,0:T(8,128)} %maximum_convert_fusion.1.pad_ref, bf16[16,128,1152]{2,1,0:T(8,128)(2,1)} %bitcast.67), custom_call_target="tpu_custom_call" | custom-call | flops 603979776 | bytes 6881280 | tf_op jit(solution)/shard_map/pallas_call | solution.py:96
  97.3 1.6 copy.67
  98.9 0.3 copy.68
  99.3 0.3 multiply_reduce_fusion
  99.6 0.7 copy-done.2
  100.3 0.4 fusion.3
  100.7 0.3 copy.69
  101.1 1.2 pad_maximum_fusion.2
  102.3 4.2 %all-to-all-done.3 = bf16[16,128,128]{2,1,0:T(8,128)(2,1)} async-done(((bf16[16,128,128]{2,1,0:T(8,128)(2,1)}), bf16[16,128,128]{2,1,0:T(8,128)(2,1)}, u32[]{:S(2)}, u32[]{:S(2)}) %all-to-all-start.3) | async-done | bytes 524320 | tf_op jit(solution)/shard_map/all_to_all | solution.py:217
  106.5 2.6 %all-to-all-start.1 = ((bf16[32,130,64]{1,2,0:T(8,128)(2,1)}), bf16[32,130,64]{1,2,0:T(8,128)(2,1)S(1)}, u32[]{:S(2)}, u32[]{:S(2)}) async-start(bf16[32,130,64]{1,2,0:T(8,128)(2,1)} %pad_maximum_fusion.2), calls=%async_computation.1 | async-start | bytes 2097152 | tf_op jit(solution)/shard_map/all_to_all | solution.py:155
  109.2 1.1 copy.78
  110.2 0.4 convolution_dynamic-update-slice_fusion.8
  110.6 0.4 convolution_dynamic-update-slice_fusion.7
  111.0 0.4 convolution_dynamic-update-slice_fusion.6
  111.3 0.4 convolution_dynamic-update-slice_fusion.5
  111.7 0.3 convolution_dynamic-update-slice_fusion.4
  112.0 0.4 convolution_dynamic-update-slice_fusion.3
  112.4 0.4 convolution_dynamic-update-slice_fusion.2
  112.7 0.4 convolution_dynamic-update-slice_fusion.1
  113.1 0.4 convolution_dynamic-update-slice_fusion
  113.6 0.4 copy.80
  113.9 0.8 constant_dynamic-slice_fusion.2
  114.7 2.6 %collective-permute-start.6 = (f32[64,1152]{1,0:T(8,128)}, f32[64,1152]{1,0:T(8,128)}, u32[]{:S(2)}, u32[]{:S(2)}) collective-permute-start(f32[64,1152]{1,0:T(8,128)} %get-tuple-element.31), channel_id=1, source_target_pairs={{0,24},{8,16},{16,8},{24,0},{1,25},{9,17},{17,9},{25,1},{2,26},{10... | collective-permute-start | bytes 884744 | tf_op jit(solution)/shard_map/ppermute | solution.py:181
  117.3 0.6 collective-permute-start.5
  117.8 0.4 collective-permute-start.4
  118.2 18.5 %all-to-all-done.1 = bf16[32,130,64]{1,2,0:T(8,128)(2,1)S(1)} async-done(((bf16[32,130,64]{1,2,0:T(8,128)(2,1)}), bf16[32,130,64]{1,2,0:T(8,128)(2,1)S(1)}, u32[]{:S(2)}, u32[]{:S(2)}) %all-to-all-start.1) | async-done | bytes 532512 | tf_op jit(solution)/shard_map/all_to_all | solution.py:155
  136.8 0.3 copy.81
  137.3 0.9 fusion.2
  138.3 0.8 reshape.125
  139.0 2.6 %all-to-all-start.2 = ((f32[32,1,576]{2,1,0:T(1,128)}), f32[32,1,576]{2,1,0:T(1,128)S(1)}, u32[]{:S(2)}, u32[]{:S(2)}) async-start(f32[32,1,576]{2,1,0:T(1,128)} %reshape.125), calls=%async_computation.2 | async-start | bytes 163840 | tf_op jit(solution)/shard_map/all_to_all | solution.py:165
  141.7 7.6 %all-to-all-done.2 = f32[32,1,576]{2,1,0:T(1,128)S(1)} async-done(((f32[32,1,576]{2,1,0:T(1,128)}), f32[32,1,576]{2,1,0:T(1,128)S(1)}, u32[]{:S(2)}, u32[]{:S(2)}) %all-to-all-start.2) | async-done | bytes 73760 | tf_op jit(solution)/shard_map/all_to_all | solution.py:165
  149.2 0.5 broadcast.58
  149.7 0.8 reduce.7
  150.7 1.2 add_add_fusion
  151.9 0.9 collective-permute-start.9
  152.8 1.4 collective-permute-start.8
  154.1 1.3 collective-permute-start.7
  155.5 0.7 reshape.113
  156.2 0.6 slice_reduce_fusion
  156.8 6.0 %collective-permute-done.9 = f32[64,1152]{1,0:T(8,128)S(1)} collective-permute-done((f32[64,1152]{1,0:T(8,128)S(1)}, f32[64,1152]{1,0:T(8,128)S(1)}, u32[]{:S(2)}, u32[]{:S(2)}) %collective-permute-start.9) | collective-permute-done | bytes 294944 | tf_op jit(solution)/shard_map/ppermute | solution.py:185
  162.8 4.9 %collective-permute-done.8 = f32[64,1152]{1,0:T(8,128)S(1)} collective-permute-done((f32[64,1152]{1,0:T(8,128)S(1)}, f32[64,1152]{1,0:T(8,128)S(1)}, u32[]{:S(2)}, u32[]{:S(2)}) %collective-permute-start.8) | collective-permute-done | bytes 294944 | tf_op jit(solution)/shard_map/ppermute | solution.py:185
  167.9 1.1 pad_maximum_fusion.1
  (48 shorter events, 1.7 us)
Async XLA Ops:
  7.2 1.0 copy-start.6
  7.2 66.0 %all-gather.2.cloned.1.call-start = ((), (), s32[]{:S(2)}) async-start(), calls=%async_computation.5 | async-start | bytes 5898240 | tf_op jit(solution)/shard_map/all_gather | solution.py:209
  8.2 23.8 %copy-start.5 = (bf16[1,128,2048]{2,1,0:T(8,128)(2,1)S(1)}, bf16[1,128,2048]{2,1,0:T(8,128)(2,1)}, u32[]{:S(2)}) copy-start(bf16[1,128,2048]{2,1,0:T(8,128)(2,1)} %param.10) | copy-start | bytes 1572868
  8.2 23.8 %copy-start.8 = (s32[1,128]{1,0:T(1,128)S(1)}, s32[1,128]{1,0:T(1,128)}, u32[]{:S(2)}) copy-start(s32[1,128]{1,0:T(1,128)} %param.11) | copy-start | bytes 1540
  32.0 0.7 copy-start.7
  33.2 11.3 %copy-start.1 = (bf16[1,128,2048]{2,1,0:T(8,128)(2,1)S(1)}, bf16[1,128,2048]{2,1,0:T(8,128)(2,1)}, u32[]{:S(2)}) copy-start(bf16[1,128,2048]{2,1,0:T(8,128)(2,1)} %param.15) | copy-start | bytes 1572868
  34.2 50.9 %all-to-all-start.4 = ((bf16[16,128,128]{2,1,0:T(8,128)(2,1)}), bf16[16,128,128]{2,1,0:T(8,128)(2,1)S(1)}, u32[]{:S(2)}, u32[]{:S(2)}) async-start(bf16[16,128,128]{2,1,0:T(8,128)(2,1)} %bitcast.5), calls=%async_computation.4 | async-start | bytes 1048576 | tf_op jit(solution)/shard_map/all_to_all | solution.py:216
  40.1 5.9 %collective-permute-start.1 = (bf16[16,4,128]{2,1,0:T(4,128)(2,1)S(1)}, bf16[16,4,128]{2,1,0:T(4,128)(2,1)S(1)}, u32[]{:S(2)}, u32[]{:S(2)}) collective-permute-start(bf16[16,4,128]{2,1,0:T(4,128)(2,1)S(1)} %get-tuple-element.36), channel_id=1, source_target_pairs={{1,0},{2,1},{3,2},{4,3},{5,4},{6,5},{7,6},{9,8},{10,9},{11,10},{12... | collective-permute-start | bytes 49160 | tf_op jit(solution)/shard_map/ppermute | solution.py:21
  41.4 4.6 %collective-permute-start = (bf16[16,4,128]{2,1,0:T(4,128)(2,1)S(1)}, bf16[16,4,128]{2,1,0:T(4,128)(2,1)S(1)}, u32[]{:S(2)}, u32[]{:S(2)}) collective-permute-start(bf16[16,4,128]{2,1,0:T(4,128)(2,1)S(1)} %get-tuple-element.35), channel_id=1, source_target_pairs={{0,1},{1,2},{2,3},{3,4},{4,5},{5,6},{6,7},{8,9},{9,10},{10,11},{11... | collective-permute-start | bytes 49160 | tf_op jit(solution)/shard_map/ppermute | solution.py:19
  80.5 10.5 %collective-permute-start.3 = (bf16[16,4,128]{2,1,0:T(4,128)(2,1)S(1)}, bf16[16,4,128]{2,1,0:T(4,128)(2,1)S(1)}, u32[]{:S(2)}, u32[]{:S(2)}) collective-permute-start(bf16[16,4,128]{2,1,0:T(4,128)(2,1)S(1)} %get-tuple-element.34), channel_id=1, source_target_pairs={{1,0},{2,1},{3,2},{4,3},{5,4},{6,5},{7,6},{9,8},{10,9},{11,10},{12... | collective-permute-start | bytes 49160 | tf_op jit(solution)/shard_map/ppermute | solution.py:21
  81.8 9.3 %collective-permute-start.2 = (bf16[16,4,128]{2,1,0:T(4,128)(2,1)S(1)}, bf16[16,4,128]{2,1,0:T(4,128)(2,1)S(1)}, u32[]{:S(2)}, u32[]{:S(2)}) collective-permute-start(bf16[16,4,128]{2,1,0:T(4,128)(2,1)S(1)} %get-tuple-element.33), channel_id=1, source_target_pairs={{0,1},{1,2},{2,3},{3,4},{4,5},{5,6},{6,7},{8,9},{9,10},{10,11},{11... | collective-permute-start | bytes 49160 | tf_op jit(solution)/shard_map/ppermute | solution.py:19
  85.4 5.7 %copy-start = (bf16[16,128,128]{2,1,0:T(8,128)(2,1)S(1)}, bf16[16,128,128]{2,1,0:T(8,128)(2,1)}, u32[]{:S(2)}) copy-start(bf16[16,128,128]{2,1,0:T(8,128)(2,1)} %shard_map.98) | copy-start | bytes 1572868
  86.4 20.1 %all-to-all-start.3 = ((bf16[16,128,128]{2,1,0:T(8,128)(2,1)}), bf16[16,128,128]{2,1,0:T(8,128)(2,1)}, u32[]{:S(2)}, u32[]{:S(2)}) async-start(bf16[16,128,128]{2,1,0:T(8,128)(2,1)} %shard_map.98), calls=%async_computation.3 | async-start | bytes 1048576 | tf_op jit(solution)/shard_map/all_to_all | solution.py:217
  99.2 1.0 copy-start.2
  100.7 1.6 copy-start.4
  102.3 7.9 %copy-start.3 = (bf16[2,1024,128]{1,2,0:T(8,128)(2,1)S(1)}, bf16[2,1024,128]{1,2,0:T(8,128)(2,1)}, u32[]{:S(2)}) copy-start(bf16[2,1024,128]{1,2,0:T(8,128)(2,1)} %all_to_all.49) | copy-start | bytes 1572868
  106.5 30.2 %all-to-all-start.1 = ((bf16[32,130,64]{1,2,0:T(8,128)(2,1)}), bf16[32,130,64]{1,2,0:T(8,128)(2,1)S(1)}, u32[]{:S(2)}, u32[]{:S(2)}) async-start(bf16[32,130,64]{1,2,0:T(8,128)(2,1)} %pad_maximum_fusion.2), calls=%async_computation.1 | async-start | bytes 2097152 | tf_op jit(solution)/shard_map/all_to_all | solution.py:155
  114.7 35.9 %collective-permute-start.6 = (f32[64,1152]{1,0:T(8,128)}, f32[64,1152]{1,0:T(8,128)}, u32[]{:S(2)}, u32[]{:S(2)}) collective-permute-start(f32[64,1152]{1,0:T(8,128)} %get-tuple-element.31), channel_id=1, source_target_pairs={{0,24},{8,16},{16,8},{24,0},{1,25},{9,17},{17,9},{25,1},{2,26},{10... | collective-permute-start | bytes 884744 | tf_op jit(solution)/shard_map/ppermute | solution.py:181
  117.3 33.4 %collective-permute-start.5 = (f32[64,1152]{1,0:T(8,128)S(1)}, f32[64,1152]{1,0:T(8,128)}, u32[]{:S(2)}, u32[]{:S(2)}) collective-permute-start(f32[64,1152]{1,0:T(8,128)S(1)} %get-tuple-element.32), channel_id=1, source_target_pairs={{0,16},{8,24},{16,0},{24,8},{1,17},{9,25},{17,1},{25,9},{2,18},{10... | collective-permute-start | bytes 884744 | tf_op jit(solution)/shard_map/ppermute | solution.py:181
  117.8 32.8 %collective-permute-start.4 = (f32[64,1152]{1,0:T(8,128)S(1)}, f32[64,1152]{1,0:T(8,128)}, u32[]{:S(2)}, u32[]{:S(2)}) collective-permute-start(f32[64,1152]{1,0:T(8,128)S(1)} %get-tuple-element.30), channel_id=1, source_target_pairs={{0,8},{8,0},{16,24},{24,16},{1,9},{9,1},{17,25},{25,17},{2,10},{10... | collective-permute-start | bytes 884744 | tf_op jit(solution)/shard_map/ppermute | solution.py:181
  139.0 10.2 %all-to-all-start.2 = ((f32[32,1,576]{2,1,0:T(1,128)}), f32[32,1,576]{2,1,0:T(1,128)S(1)}, u32[]{:S(2)}, u32[]{:S(2)}) async-start(f32[32,1,576]{2,1,0:T(1,128)} %reshape.125), calls=%async_computation.2 | async-start | bytes 163840 | tf_op jit(solution)/shard_map/all_to_all | solution.py:165
  151.9 10.9 %collective-permute-start.9 = (f32[64,1152]{1,0:T(8,128)S(1)}, f32[64,1152]{1,0:T(8,128)S(1)}, u32[]{:S(2)}, u32[]{:S(2)}) collective-permute-start(f32[64,1152]{1,0:T(8,128)S(1)} %add_add_fusion), channel_id=1, source_target_pairs={{0,24},{8,16},{16,8},{24,0},{1,25},{9,17},{17,9},{25,1},{2,26},{10... | collective-permute-start | bytes 884744 | tf_op jit(solution)/shard_map/ppermute | solution.py:185
  152.8 14.9 %collective-permute-start.8 = (f32[64,1152]{1,0:T(8,128)S(1)}, f32[64,1152]{1,0:T(8,128)S(1)}, u32[]{:S(2)}, u32[]{:S(2)}) collective-permute-start(f32[64,1152]{1,0:T(8,128)S(1)} %add_add_fusion), channel_id=1, source_target_pairs={{0,16},{8,24},{16,0},{24,8},{1,17},{9,25},{17,1},{25,9},{2,18},{10... | collective-permute-start | bytes 884744 | tf_op jit(solution)/shard_map/ppermute | solution.py:185
  154.1 13.6 %collective-permute-start.7 = (f32[64,1152]{1,0:T(8,128)S(1)}, f32[64,1152]{1,0:T(8,128)S(1)}, u32[]{:S(2)}, u32[]{:S(2)}) collective-permute-start(f32[64,1152]{1,0:T(8,128)S(1)} %add_add_fusion), channel_id=1, source_target_pairs={{0,8},{8,0},{16,24},{24,16},{1,9},{9,1},{17,25},{25,17},{2,10},{10... | collective-permute-start | bytes 884744 | tf_op jit(solution)/shard_map/ppermute | solution.py:185
Sparse Core Ops, SparseCore 0:
  9.8 63.2 all-gather.1

commit v11 on v10

--- a/solution.py
+++ b/solution.py
@@ -138,7 +138,7 @@
     return gather_rows(sum_rows(block, axis), axis)
 
 
-def table_and_gain(input_grad, ids, gain_term, types, scale):
+def table_and_gain(input_grad, ids, gain_term, types, scale, tied):
     every = ("fsdp", "seq")
     count = lax.axis_size("fsdp") * lax.axis_size("seq")
     length, width = input_grad.shape
@@ -162,16 +162,15 @@
     back = jnp.concatenate(
         [columns.reshape(count, per, narrow), gain_term.reshape(count, 1, narrow)], axis=1
     )
+    back, tied = lax.optimization_barrier((back, tied))
     back = lax.all_to_all(back, every, 0, 0, tiled=True)
     table_grad = back[:, :per].transpose(1, 0, 2).reshape(per, width)
     gain_grad = back[:, per].sum(axis=0)
-    return table_grad, gain_grad
-
-
-def psum_by_permutes(block, axis):
-    count = lax.axis_size(axis)
-    if count & (count - 1):
-        return lax.psum(block, axis)
+    return table_grad, gain_grad, tied
+
+
+def scatter_by_permutes(block, axis):
+    count = lax.axis_size(axis)
     me = lax.axis_index(axis)
     rows = block.shape[0] // count
     chunk = lambda index: lax.dynamic_slice_in_dim(block, index * rows, rows, axis=0)
@@ -179,6 +178,12 @@
     for apart in range(1, count):
         pairs = [(source, source ^ apart) for source in range(count)]
         total = total + lax.ppermute(chunk(me ^ apart), axis, pairs)
+    return total
+
+
+def gather_by_permutes(total, axis):
+    count = lax.axis_size(axis)
+    me = lax.axis_index(axis)
     pieces = [total]
     for apart in range(1, count):
         pairs = [(source, source ^ apart) for source in range(count)]
@@ -230,8 +235,11 @@
     scaled = norm_gain * dnormed
     dmixed = inv * scaled - mixed * inv * inv * inv * jnp.mean(scaled * mixed, axis=-1, keepdims=True)
     input_grad = (up_float + dmixed).astype(jnp.bfloat16)
-    kernel_grad = psum_by_permutes(kernel_part, "fsdp")
-    table_grad, gain_grad = table_and_gain(input_grad, type_ids[0], gain_term, types, scale)
+    if fsdp & (fsdp - 1):
+        raise ValueError("fsdp not pow2")
+    kernel_sum = scatter_by_permutes(kernel_part, "fsdp")
+    table_grad, gain_grad, kernel_sum = table_and_gain(input_grad, type_ids[0], gain_term, types, scale, kernel_sum)
+    kernel_grad = gather_by_permutes(kernel_sum, "fsdp")
     return (input_grad[None], table_grad, gain_grad, kernel_grad)
 
 

time: 177 us -> 170 us (0.960)
  waiting for transfers between devices: 66.7 us -> 58 us
    ppermute x6, waiting for transfers between devices: 10.9 us -> 6.82 us  [the longest x3 6.81 us: gather_by_permutes(): pieces.append(lax.ppermute(total, axis, pairs))]
    all_to_all x1, waiting for transfers between devices: 7.55 us -> 4.05 us  [table_and_gain(): back = lax.all_to_all(back, every, 0, 0, tiled=True)]
where the time goes in v11:
time: 170 us; the launch traced here: 169 us
  waiting for transfers between devices  58 us (34%)
  starting transfers between devices  31.2 us (18%)
  blocking collectives  23.8 us (14%)
  local copies, waits for them, and re-layouts  14.6 us (9%)
  between operations  14.5 us (9%)
  Pallas kernels  11.7 us (7%)
  other arithmetic  10.4 us (6%)
  matrix products  4.48 us (3%)
    all_gather x1, waiting for transfers between devices, body(): lax.all_gather(kernel, 'fsdp', axis=0, tiled=True)  24.8 us
    all_to_all x1, blocking collectives, gather_rows(): lax.all_to_all(jnp.tile(block, (count,) + (1,) * (block.ndim - 1)), axis,...  23.8 us
    all_to_all x1, waiting for transfers between devices, table_and_gain(): got = lax.all_to_all(send, every, 0, 0, tiled=True)  18.5 us
    ppermute x3, waiting for transfers between devices, gather_by_permutes(): pieces.append(lax.ppermute(total, axis, pairs))  6.81 us
    pallas_call x1, Pallas kernels, conv_dconv(): pl.pallas_call(forward_kernel, grid=(groups // step,), in_specs=[pl.Block...  6.56 us
    ppermute x2, starting transfers between devices, with_halo(): lax.ppermute(tail, axis, [(i, (i + 1) % count) for i in range(ends)])  6.07 us
    pallas_call x1, Pallas kernels, conv_transpose(): pl.pallas_call(backward_kernel, grid=(groups // step,), in_specs=[pl.Bloc...  5.17 us
    all_to_all x1, starting transfers between devices, body(): group_in = lax.all_to_all(normed_g, 'seq', 0, 1, tiled=True)  5.15 us
  transfers between devices with their start and end apart: 15, of which 6 were waited for; matrix products, arithmetic and copies ran while one was open for 14% of the time, Pallas kernels for 7%

profile of v11, /device:TPU:0, one launch (start us, length us, event | category | flops | bytes accessed | tf_op | source)
XLA Modules:
  0.0 168.7 jit_solution(9251347247989580905)
XLA Ops:
  7.2 0.7 all-gather.2.cloned.1.call-update
  7.9 0.2 copy-done.5
  8.3 23.8 %all_to_all.55 = bf16[4,64,2048]{2,1,0:T(8,128)(2,1)S(1)} all-to-all(bf16[4,64,2048]{2,1,0:T(8,128)(2,1)S(1)} %tile.2), channel_id=1, replica_groups=mesh['fsdp'=4,'seq'=8] {'fsdp'}, dimensions={0} | all-to-all | bytes 2097152 | tf_op jit(solution)/shard_map/all_to_all | solution.py:35
  32.0 0.4 multiply_reduce_fusion.2
  32.5 0.3 copy-done.6
  32.9 0.3 copy.63
  33.2 1.0 copy.64
  34.2 5.2 %all-to-all-start.3 = ((bf16[16,128,128]{2,1,0:T(8,128)(2,1)}), bf16[16,128,128]{2,1,0:T(8,128)(2,1)S(1)}, u32[]{:S(2)}, u32[]{:S(2)}) async-start(bf16[16,128,128]{2,1,0:T(8,128)(2,1)} %bitcast.5), calls=%async_computation.3 | async-start | bytes 1048576 | tf_op jit(solution)/shard_map/all_to_all | solution.py:221
  39.3 0.8 fusion.32
  40.1 1.3 collective-permute-start.1
  41.4 3.0 %collective-permute-start = (bf16[16,4,128]{2,1,0:T(4,128)(2,1)S(1)}, bf16[16,4,128]{2,1,0:T(4,128)(2,1)S(1)}, u32[]{:S(2)}, u32[]{:S(2)}) collective-permute-start(bf16[16,4,128]{2,1,0:T(4,128)(2,1)S(1)} %get-tuple-element.39), channel_id=1, source_target_pairs={{0,1},{1,2},{2,3},{3,4},{4,5},{5,6},{6,7},{8,9},{9,10},{10,11},{11... | collective-permute-start | bytes 49160 | tf_op jit(solution)/shard_map/ppermute | solution.py:19
  44.7 1.3 copy.66
  46.0 2.3 %maximum_convert_fusion.pad_ref = f32[16,136,128]{2,1,0:T(8,128)} fusion(bf16[16,4,128]{2,1,0:T(4,128)(2,1)S(1)} %collective-permute-done.1, bf16[16,128,128]{2,1,0:T(8,128)(2,1)} %bitcast.5, bf16[16,4,128]{2,1,0:T(4,128)(2,1)S(1)} %collective-permute-done), kind=kLoop, calls=%fused_computation.24 | loop fusion | flops 1671168 | bytes 1671168 | tf_op jit(solution)/shard_map/convert_element_type | solution.py:217
  48.3 24.8 %all-gather.2.cloned.1.call-done = bf16[2048,1152]{1,0:T(8,128)(2,1)} async-done(((bf16[512,1152]{1,0:T(8,128)(2,1)}), bf16[2048,1152]{1,0:T(8,128)(2,1)}) %all-gather.2.cloned.1.call-update) | async-done | bytes 4718608 | tf_op jit(solution)/shard_map/all_gather | solution.py:214
  73.1 6.6 %shard_map.98 = bf16[16,128,128]{2,1,0:T(8,128)(2,1)} custom-call(f32[16,136,128]{2,1,0:T(8,128)} %maximum_convert_fusion.pad_ref, bf16[16,128,1152]{2,1,0:T(8,128)(2,1)} %bitcast.66, f32[16,128,128]{2,1,0:T(8,128)} %bitcast.70), custom_call_target="tpu_custom_call" | custom-call | flops 603979776 | bytes 7405568 | tf_op jit(solution)/shard_map/pallas_call | solution.py:74
  79.7 0.8 fusion.31
  80.5 1.3 collective-permute-start.3
  81.8 3.0 %collective-permute-start.2 = (bf16[16,4,128]{2,1,0:T(4,128)(2,1)S(1)}, bf16[16,4,128]{2,1,0:T(4,128)(2,1)S(1)}, u32[]{:S(2)}, u32[]{:S(2)}) collective-permute-start(bf16[16,4,128]{2,1,0:T(4,128)(2,1)S(1)} %get-tuple-element.37), channel_id=1, source_target_pairs={{0,1},{1,2},{2,3},{3,4},{4,5},{5,6},{6,7},{8,9},{9,10},{10,11},{11... | collective-permute-start | bytes 49160 | tf_op jit(solution)/shard_map/ppermute | solution.py:19
  85.1 0.3 copy.78
  85.4 1.0 all_to_all.48
  86.4 4.6 %all-to-all-start.2 = ((bf16[16,128,128]{2,1,0:T(8,128)(2,1)}), bf16[16,128,128]{2,1,0:T(8,128)(2,1)}, u32[]{:S(2)}, u32[]{:S(2)}) async-start(bf16[16,128,128]{2,1,0:T(8,128)(2,1)} %shard_map.98), calls=%async_computation.2 | async-start | bytes 1048576 | tf_op jit(solution)/shard_map/all_to_all | solution.py:222
  91.0 2.2 %maximum_convert_fusion.1.pad_ref = f32[16,136,128]{2,1,0:T(8,128)} fusion(bf16[16,4,128]{2,1,0:T(4,128)(2,1)S(1)} %collective-permute-done.3, bf16[16,128,128]{2,1,0:T(8,128)(2,1)} %shard_map.98, bf16[16,4,128]{2,1,0:T(4,128)(2,1)S(1)} %collective-permute-done.2), kind=kLoop, calls=%fused_computation.25 | loop fusion | flops 1671168 | bytes 1671168 | tf_op jit(solution)/shard_map/convert_element_type | solution.py:219
  93.2 5.2 %shard_map.99 = f32[16,128,128]{2,1,0:T(8,128)} custom-call(f32[16,136,128]{2,1,0:T(8,128)} %maximum_convert_fusion.1.pad_ref, bf16[16,128,1152]{2,1,0:T(8,128)(2,1)} %bitcast.67), custom_call_target="tpu_custom_call" | custom-call | flops 603979776 | bytes 6881280 | tf_op jit(solution)/shard_map/pallas_call | solution.py:96
  98.4 1.6 copy.67
  100.0 0.3 copy.68
  100.3 0.3 multiply_reduce_fusion
  100.7 0.7 copy-done.1
  101.3 0.4 fusion.3
  101.7 0.3 copy.69
  102.1 1.2 pad_maximum_fusion.2
  103.4 3.1 %all-to-all-done.2 = bf16[16,128,128]{2,1,0:T(8,128)(2,1)} async-done(((bf16[16,128,128]{2,1,0:T(8,128)(2,1)}), bf16[16,128,128]{2,1,0:T(8,128)(2,1)}, u32[]{:S(2)}, u32[]{:S(2)}) %all-to-all-start.2) | async-done | bytes 524320 | tf_op jit(solution)/shard_map/all_to_all | solution.py:222
  106.5 2.6 %all-to-all-start.1 = ((bf16[32,130,64]{1,2,0:T(8,128)(2,1)}), bf16[32,130,64]{1,2,0:T(8,128)(2,1)S(1)}, u32[]{:S(2)}, u32[]{:S(2)}) async-start(bf16[32,130,64]{1,2,0:T(8,128)(2,1)} %pad_maximum_fusion.2), calls=%async_computation.1 | async-start | bytes 2097152 | tf_op jit(solution)/shard_map/all_to_all | solution.py:155
  109.2 1.1 copy.77
  110.2 0.4 convolution_dynamic-update-slice_fusion.8
  110.6 0.4 convolution_dynamic-update-slice_fusion.7
  111.0 0.4 convolution_dynamic-update-slice_fusion.6
  111.3 0.4 convolution_dynamic-update-slice_fusion.5
  111.7 0.3 convolution_dynamic-update-slice_fusion.4
  112.0 0.4 convolution_dynamic-update-slice_fusion.3
  112.4 0.4 convolution_dynamic-update-slice_fusion.2
  112.7 0.4 convolution_dynamic-update-slice_fusion.1
  113.1 0.4 convolution_dynamic-update-slice_fusion
  113.6 0.4 copy.79
  113.9 0.8 constant_dynamic-slice_fusion.2
  114.7 2.6 %collective-permute-start.6 = (f32[64,1152]{1,0:T(8,128)}, f32[64,1152]{1,0:T(8,128)}, u32[]{:S(2)}, u32[]{:S(2)}) collective-permute-start(f32[64,1152]{1,0:T(8,128)} %get-tuple-element.35), channel_id=1, source_target_pairs={{0,24},{8,16},{16,8},{24,0},{1,25},{9,17},{17,9},{25,1},{2,26},{10... | collective-permute-start | bytes 884744 | tf_op jit(solution)/shard_map/ppermute | solution.py:180
  117.3 0.6 collective-permute-start.5
  117.8 0.4 collective-permute-start.4
  118.2 18.5 %all-to-all-done.1 = bf16[32,130,64]{1,2,0:T(8,128)(2,1)S(1)} async-done(((bf16[32,130,64]{1,2,0:T(8,128)(2,1)}), bf16[32,130,64]{1,2,0:T(8,128)(2,1)S(1)}, u32[]{:S(2)}, u32[]{:S(2)}) %all-to-all-start.1) | async-done | bytes 532512 | tf_op jit(solution)/shard_map/all_to_all | solution.py:155
  136.8 0.3 copy.81
  137.3 0.9 fusion.2
  138.3 1.2 add_add_fusion
  139.5 0.8 reshape.125
  140.3 3.1 %all-to-all-start.4 = ((f32[32,1,576]{2,1,0:T(1,128)}), f32[32,1,576]{2,1,0:T(1,128)S(1)}, u32[]{:S(2)}, u32[]{:S(2)}) async-start(f32[32,1,576]{2,1,0:T(1,128)} %reshape.125), calls=%async_computation.4 | async-start | bytes 163840 | tf_op jit(solution)/shard_map/all_to_all | solution.py:166
  143.4 2.7 %collective-permute-start.9 = (f32[64,1152]{1,0:T(8,128)S(1)}, f32[64,1152]{1,0:T(8,128)S(1)}, u32[]{:S(2)}, u32[]{:S(2)}) collective-permute-start(f32[64,1152]{1,0:T(8,128)S(1)} %add_add_fusion), channel_id=1, source_target_pairs={{0,24},{8,16},{16,8},{24,0},{1,25},{9,17},{17,9},{25,1},{2,26},{10... | collective-permute-start | bytes 884744 | tf_op jit(solution)/shard_map/ppermute | solution.py:190
  146.1 0.6 collective-permute-start.8
  146.7 0.3 collective-permute-start.7
  147.0 4.1 %all-to-all-done.4 = f32[32,1,576]{2,1,0:T(1,128)S(1)} async-done(((f32[32,1,576]{2,1,0:T(1,128)}), f32[32,1,576]{2,1,0:T(1,128)S(1)}, u32[]{:S(2)}, u32[]{:S(2)}) %all-to-all-start.4) | async-done | bytes 73760 | tf_op jit(solution)/shard_map/all_to_all | solution.py:166
  151.0 0.5 broadcast.58
  151.5 0.8 reduce.7
  152.5 0.7 reshape.113
  153.2 0.6 slice_reduce_fusion
  153.8 1.1 collective-permute-done.9
  154.9 5.7 %collective-permute-done.8 = f32[64,1152]{1,0:T(8,128)S(1)} collective-permute-done((f32[64,1152]{1,0:T(8,128)S(1)}, f32[64,1152]{1,0:T(8,128)S(1)}, u32[]{:S(2)}, u32[]{:S(2)}) %collective-permute-start.8) | collective-permute-done | bytes 294944 | tf_op jit(solution)/shard_map/ppermute | solution.py:190
  160.8 1.1 pad_maximum_fusion.1
  (46 shorter events, 1.7 us)
Async XLA Ops:
  7.2 1.0 copy-start.5
  7.2 66.0 %all-gather.2.cloned.1.call-start = ((), (), s32[]{:S(2)}) async-start(), calls=%async_computation.5 | async-start | bytes 5898240 | tf_op jit(solution)/shard_map/all_gather | solution.py:214
  8.2 23.8 %copy-start.4 = (bf16[1,128,2048]{2,1,0:T(8,128)(2,1)S(1)}, bf16[1,128,2048]{2,1,0:T(8,128)(2,1)}, u32[]{:S(2)}) copy-start(bf16[1,128,2048]{2,1,0:T(8,128)(2,1)} %param.10) | copy-start | bytes 1572868
  8.2 23.8 %copy-start.7 = (s32[1,128]{1,0:T(1,128)S(1)}, s32[1,128]{1,0:T(1,128)}, u32[]{:S(2)}) copy-start(s32[1,128]{1,0:T(1,128)} %param.11) | copy-start | bytes 1540
  32.0 0.7 copy-start.6
  33.2 11.3 %copy-start = (bf16[1,128,2048]{2,1,0:T(8,128)(2,1)S(1)}, bf16[1,128,2048]{2,1,0:T(8,128)(2,1)}, u32[]{:S(2)}) copy-start(bf16[1,128,2048]{2,1,0:T(8,128)(2,1)} %param.15) | copy-start | bytes 1572868
  34.2 50.9 %all-to-all-start.3 = ((bf16[16,128,128]{2,1,0:T(8,128)(2,1)}), bf16[16,128,128]{2,1,0:T(8,128)(2,1)S(1)}, u32[]{:S(2)}, u32[]{:S(2)}) async-start(bf16[16,128,128]{2,1,0:T(8,128)(2,1)} %bitcast.5), calls=%async_computation.3 | async-start | bytes 1048576 | tf_op jit(solution)/shard_map/all_to_all | solution.py:221
  40.1 5.9 %collective-permute-start.1 = (bf16[16,4,128]{2,1,0:T(4,128)(2,1)S(1)}, bf16[16,4,128]{2,1,0:T(4,128)(2,1)S(1)}, u32[]{:S(2)}, u32[]{:S(2)}) collective-permute-start(bf16[16,4,128]{2,1,0:T(4,128)(2,1)S(1)} %get-tuple-element.40), channel_id=1, source_target_pairs={{1,0},{2,1},{3,2},{4,3},{5,4},{6,5},{7,6},{9,8},{10,9},{11,10},{12... | collective-permute-start | bytes 49160 | tf_op jit(solution)/shard_map/ppermute | solution.py:21
  41.4 4.6 %collective-permute-start = (bf16[16,4,128]{2,1,0:T(4,128)(2,1)S(1)}, bf16[16,4,128]{2,1,0:T(4,128)(2,1)S(1)}, u32[]{:S(2)}, u32[]{:S(2)}) collective-permute-start(bf16[16,4,128]{2,1,0:T(4,128)(2,1)S(1)} %get-tuple-element.39), channel_id=1, source_target_pairs={{0,1},{1,2},{2,3},{3,4},{4,5},{5,6},{6,7},{8,9},{9,10},{10,11},{11... | collective-permute-start | bytes 49160 | tf_op jit(solution)/shard_map/ppermute | solution.py:19
  80.5 10.5 %collective-permute-start.3 = (bf16[16,4,128]{2,1,0:T(4,128)(2,1)S(1)}, bf16[16,4,128]{2,1,0:T(4,128)(2,1)S(1)}, u32[]{:S(2)}, u32[]{:S(2)}) collective-permute-start(bf16[16,4,128]{2,1,0:T(4,128)(2,1)S(1)} %get-tuple-element.38), channel_id=1, source_target_pairs={{1,0},{2,1},{3,2},{4,3},{5,4},{6,5},{7,6},{9,8},{10,9},{11,10},{12... | collective-permute-start | bytes 49160 | tf_op jit(solution)/shard_map/ppermute | solution.py:21
  81.8 9.2 %collective-permute-start.2 = (bf16[16,4,128]{2,1,0:T(4,128)(2,1)S(1)}, bf16[16,4,128]{2,1,0:T(4,128)(2,1)S(1)}, u32[]{:S(2)}, u32[]{:S(2)}) collective-permute-start(bf16[16,4,128]{2,1,0:T(4,128)(2,1)S(1)} %get-tuple-element.37), channel_id=1, source_target_pairs={{0,1},{1,2},{2,3},{3,4},{4,5},{5,6},{6,7},{8,9},{9,10},{10,11},{11... | collective-permute-start | bytes 49160 | tf_op jit(solution)/shard_map/ppermute | solution.py:19
  86.4 20.1 %all-to-all-start.2 = ((bf16[16,128,128]{2,1,0:T(8,128)(2,1)}), bf16[16,128,128]{2,1,0:T(8,128)(2,1)}, u32[]{:S(2)}, u32[]{:S(2)}) async-start(bf16[16,128,128]{2,1,0:T(8,128)(2,1)} %shard_map.98), calls=%async_computation.2 | async-start | bytes 1048576 | tf_op jit(solution)/shard_map/all_to_all | solution.py:222
  100.3 1.0 copy-start.1
  101.7 1.6 copy-start.3
  103.4 6.9 %copy-start.2 = (bf16[2,1024,128]{1,2,0:T(8,128)(2,1)S(1)}, bf16[2,1024,128]{1,2,0:T(8,128)(2,1)}, u32[]{:S(2)}) copy-start(bf16[2,1024,128]{1,2,0:T(8,128)(2,1)} %all_to_all.48) | copy-start | bytes 1572868
  106.5 30.2 %all-to-all-start.1 = ((bf16[32,130,64]{1,2,0:T(8,128)(2,1)}), bf16[32,130,64]{1,2,0:T(8,128)(2,1)S(1)}, u32[]{:S(2)}, u32[]{:S(2)}) async-start(bf16[32,130,64]{1,2,0:T(8,128)(2,1)} %pad_maximum_fusion.2), calls=%async_computation.1 | async-start | bytes 2097152 | tf_op jit(solution)/shard_map/all_to_all | solution.py:155
  114.7 23.6 %collective-permute-start.6 = (f32[64,1152]{1,0:T(8,128)}, f32[64,1152]{1,0:T(8,128)}, u32[]{:S(2)}, u32[]{:S(2)}) collective-permute-start(f32[64,1152]{1,0:T(8,128)} %get-tuple-element.35), channel_id=1, source_target_pairs={{0,24},{8,16},{16,8},{24,0},{1,25},{9,17},{17,9},{25,1},{2,26},{10... | collective-permute-start | bytes 884744 | tf_op jit(solution)/shard_map/ppermute | solution.py:180
  117.3 21.0 %collective-permute-start.5 = (f32[64,1152]{1,0:T(8,128)S(1)}, f32[64,1152]{1,0:T(8,128)}, u32[]{:S(2)}, u32[]{:S(2)}) collective-permute-start(f32[64,1152]{1,0:T(8,128)S(1)} %get-tuple-element.36), channel_id=1, source_target_pairs={{0,16},{8,24},{16,0},{24,8},{1,17},{9,25},{17,1},{25,9},{2,18},{10... | collective-permute-start | bytes 884744 | tf_op jit(solution)/shard_map/ppermute | solution.py:180
  117.8 20.5 %collective-permute-start.4 = (f32[64,1152]{1,0:T(8,128)S(1)}, f32[64,1152]{1,0:T(8,128)}, u32[]{:S(2)}, u32[]{:S(2)}) collective-permute-start(f32[64,1152]{1,0:T(8,128)S(1)} %get-tuple-element.34), channel_id=1, source_target_pairs={{0,8},{8,0},{16,24},{24,16},{1,9},{9,1},{17,25},{25,17},{2,10},{10... | collective-permute-start | bytes 884744 | tf_op jit(solution)/shard_map/ppermute | solution.py:180
  140.3 10.7 %all-to-all-start.4 = ((f32[32,1,576]{2,1,0:T(1,128)}), f32[32,1,576]{2,1,0:T(1,128)S(1)}, u32[]{:S(2)}, u32[]{:S(2)}) async-start(f32[32,1,576]{2,1,0:T(1,128)} %reshape.125), calls=%async_computation.4 | async-start | bytes 163840 | tf_op jit(solution)/shard_map/all_to_all | solution.py:166
  143.4 11.5 %collective-permute-start.9 = (f32[64,1152]{1,0:T(8,128)S(1)}, f32[64,1152]{1,0:T(8,128)S(1)}, u32[]{:S(2)}, u32[]{:S(2)}) collective-permute-start(f32[64,1152]{1,0:T(8,128)S(1)} %add_add_fusion), channel_id=1, source_target_pairs={{0,24},{8,16},{16,8},{24,0},{1,25},{9,17},{17,9},{25,1},{2,26},{10... | collective-permute-start | bytes 884744 | tf_op jit(solution)/shard_map/ppermute | solution.py:190
  146.1 14.4 %collective-permute-start.8 = (f32[64,1152]{1,0:T(8,128)S(1)}, f32[64,1152]{1,0:T(8,128)S(1)}, u32[]{:S(2)}, u32[]{:S(2)}) collective-permute-start(f32[64,1152]{1,0:T(8,128)S(1)} %add_add_fusion), channel_id=1, source_target_pairs={{0,16},{8,24},{16,0},{24,8},{1,17},{9,25},{17,1},{25,9},{2,18},{10... | collective-permute-start | bytes 884744 | tf_op jit(solution)/shard_map/ppermute | solution.py:190
  146.7 13.9 %collective-permute-start.7 = (f32[64,1152]{1,0:T(8,128)S(1)}, f32[64,1152]{1,0:T(8,128)S(1)}, u32[]{:S(2)}, u32[]{:S(2)}) collective-permute-start(f32[64,1152]{1,0:T(8,128)S(1)} %add_add_fusion), channel_id=1, source_target_pairs={{0,8},{8,0},{16,24},{24,16},{1,9},{9,1},{17,25},{25,17},{2,10},{10... | collective-permute-start | bytes 884744 | tf_op jit(solution)/shard_map/ppermute | solution.py:190
Sparse Core Ops, SparseCore 0:
  9.8 63.2 all-gather.1

commit v12 on v11

--- a/solution.py
+++ b/solution.py
@@ -194,6 +194,25 @@
     )
 
 
+def gather_shards(block, axis):
+    count = lax.axis_size(axis)
+    me = lax.axis_index(axis)
+    core = lax.axis_index("seq") % 2
+    half_rows = block.shape[0] // 2
+    mine = lax.dynamic_slice_in_dim(block, core * half_rows, half_rows, axis=0)
+    blocks = [block]
+    for apart in range(1, count):
+        fetched = lax.ppermute(mine, axis, [(source, source ^ apart) for source in range(count)])
+        swapped = from_partner(fetched, "seq", 0)
+        lower = jnp.where(core == 0, fetched, swapped)
+        upper = jnp.where(core == 0, swapped, fetched)
+        blocks.append(jnp.concatenate([lower, upper], axis=0))
+    stacked = jnp.stack(blocks)
+    return jnp.concatenate(
+        [lax.dynamic_index_in_dim(stacked, index ^ me, keepdims=False) for index in range(count)], axis=0
+    )
+
+
 def body(events, type_ids, type_table, norm_gain, kernel, upstream):
     length = events.shape[1]
     width = events.shape[2]
@@ -203,7 +222,9 @@
     seq_count = lax.axis_size("seq")
     total = length * seq_count * fsdp
     scale = 1.0 / jnp.sqrt(jnp.float32(total))
-    table = gather_rows(type_table, "fsdp")
+    if fsdp & (fsdp - 1):
+        raise ValueError("fsdp not pow2")
+    table = gather_shards(type_table, "fsdp")
     types = table.shape[0]
     onehot = (type_ids[0][:, None] == jnp.arange(types, dtype=jnp.int32)[None, :]).astype(jnp.bfloat16)
     mixed = events[0].astype(jnp.float32) + jnp.dot(onehot, table, preferred_element_type=jnp.float32)
@@ -211,7 +232,7 @@
     normed = (mixed * inv * norm_gain).astype(jnp.bfloat16)
     normed_g = normed.reshape(length, GROUPS, chans).transpose(1, 0, 2)
     padded = with_halo(normed_g, "seq", 1, half)
-    weights = lax.all_gather(kernel, "fsdp", axis=0, tiled=True).reshape(GROUPS, chans, KERNEL * chans)
+    weights = gather_shards(kernel, "fsdp").reshape(GROUPS, chans, KERNEL * chans)
     up_float = upstream[0].astype(jnp.float32)
     up_g = up_float.reshape(length, GROUPS, chans).transpose(1, 0, 2)
     dconv = conv_dconv(padded.astype(jnp.float32), weights, up_g)
@@ -235,8 +256,6 @@
     scaled = norm_gain * dnormed
     dmixed = inv * scaled - mixed * inv * inv * inv * jnp.mean(scaled * mixed, axis=-1, keepdims=True)
     input_grad = (up_float + dmixed).astype(jnp.bfloat16)
-    if fsdp & (fsdp - 1):
-        raise ValueError("fsdp not pow2")
     kernel_sum = scatter_by_permutes(kernel_part, "fsdp")
     table_grad, gain_grad, kernel_sum = table_and_gain(input_grad, type_ids[0], gain_term, types, scale, kernel_sum)
     kernel_grad = gather_by_permutes(kernel_sum, "fsdp")

time: 170 us -> 157 us (0.924)
  blocking collectives: 23.8 us -> 0 us
  between operations: 14.5 us -> 1.22 us
  starting transfers between devices: 31.2 us -> 43.5 us
  other arithmetic: 10.4 us -> 16.1 us
  local copies, waits for them, and re-layouts: 14.6 us -> 20.3 us
    ppermute x0 -> x12, waiting for transfers between devices: none -> 26.1 us  [the longest x6 24.6 us: gather_shards(): lax.ppermute(mine, axis, [(source, source ^ apart) for source in range(co...]
    all_gather x1 -> x0, waiting for transfers between devices: 24.8 us -> none  [body(): lax.all_gather(kernel, 'fsdp', axis=0, tiled=True)]
    all_to_all x1 -> x0, blocking collectives: 23.8 us -> none  [gather_rows(): lax.all_to_all(jnp.tile(block, (count,) + (1,) * (block.ndim - 1)), axis,...]
    ppermute x0 -> x12, starting transfers between devices: none -> 9.69 us  [the longest x6 8.55 us: gather_shards(): lax.ppermute(mine, axis, [(source, source ^ apart) for source in range(co...]
    dynamic_slice x0 -> x2, local copies, waits for them, and re-layouts: none -> 2.9 us  [gather_shards(): mine = lax.dynamic_slice_in_dim(block, core * half_rows, half_rows, axis=0)]
    concatenate x0 -> x1, other arithmetic: none -> 2.83 us  [gather_shards(): jnp.concatenate([lax.dynamic_index_in_dim(stacked, index ^ me, keepdims=F...]
    select_n x0 -> x6, other arithmetic: none -> 2.77 us  [gather_shards(): lower = jnp.where(core == 0, fetched, swapped)]
    unnamed x19 -> x23, local copies, waits for them, and re-layouts: 2.31 us -> 4.73 us
  transfers between devices with their start and end apart: 15 -> 26, of which waited for: 6 -> 9; matrix products, arithmetic and copies ran while one was open for 14% -> 21% of each run, Pallas kernels for 7% -> 8%
where the time goes in v12:
time: 157 us; the launch traced here: 156 us
  waiting for transfers between devices  58.8 us (37%)
  starting transfers between devices  43.5 us (28%)
  local copies, waits for them, and re-layouts  20.3 us (13%)
  other arithmetic  16.1 us (10%)
  Pallas kernels  11.7 us (7%)
  matrix products  4.47 us (3%)
    ppermute x6, waiting for transfers between devices, gather_shards(): lax.ppermute(mine, axis, [(source, source ^ apart) for source in range(co...  24.6 us
    all_to_all x1, waiting for transfers between devices, table_and_gain(): got = lax.all_to_all(send, every, 0, 0, tiled=True)  18.7 us
    ppermute x6, starting transfers between devices, gather_shards(): lax.ppermute(mine, axis, [(source, source ^ apart) for source in range(co...  8.55 us
    ppermute x3, waiting for transfers between devices, gather_by_permutes(): pieces.append(lax.ppermute(total, axis, pairs))  7.14 us
    all_to_all x1, starting transfers between devices, body(): group_out = lax.all_to_all(dconv, 'seq', 0, 1, tiled=True)  6.85 us
    all_to_all x1, starting transfers between devices, body(): group_in = lax.all_to_all(normed_g, 'seq', 0, 1, tiled=True)  6.74 us
    pallas_call x1, Pallas kernels, conv_dconv(): pl.pallas_call(forward_kernel, grid=(groups // step,), in_specs=[pl.Block...  6.56 us
    pallas_call x1, Pallas kernels, conv_transpose(): pl.pallas_call(backward_kernel, grid=(groups // step,), in_specs=[pl.Bloc...  5.15 us
  transfers between devices with their start and end apart: 26, of which 9 were waited for; matrix products, arithmetic and copies ran while one was open for 21% of the time, Pallas kernels for 8%

profile of v12, /device:TPU:0, one launch (start us, length us, event | category | flops | bytes accessed | tf_op | source)
XLA Modules:
  0.0 156.1 jit_solution(12615638697692573431)
XLA Ops:
  0.6 0.9 constant_dynamic-slice_fusion.4
  1.6 3.0 %collective-permute-start = (bf16[32,2048]{1,0:T(8,128)(2,1)S(1)}, bf16[32,2048]{1,0:T(8,128)(2,1)S(1)}, u32[]{:S(2)}, u32[]{:S(2)}) collective-permute-start(bf16[32,2048]{1,0:T(8,128)(2,1)S(1)} %constant_dynamic-slice_fusion.4), channel_id=1, source_target_pairs={{0,8},{8,0},{16,24},{24,16},{1,9},{9,1},{17,25},{25,17},{2,10},{10... | collective-permute-start | bytes 393224 | tf_op jit(solution)/shard_map/ppermute | solution.py:205
  4.6 1.5 collective-permute-start.2
  6.1 2.4 %collective-permute-done = bf16[32,2048]{1,0:T(8,128)(2,1)S(1)} collective-permute-done((bf16[32,2048]{1,0:T(8,128)(2,1)S(1)}, bf16[32,2048]{1,0:T(8,128)(2,1)S(1)}, u32[]{:S(2)}, u32[]{:S(2)}) %collective-permute-start) | collective-permute-done | bytes 131104 | tf_op jit(solution)/shard_map/ppermute | solution.py:205
  8.5 2.0 %constant_dynamic-slice_fusion.3 = bf16[256,1152]{1,0:T(8,128)(2,1)} fusion(bf16[512,1152]{1,0:T(8,128)(2,1)} %param.14, s32[]{:T(128)S(6)} %select_n.120), kind=kLoop, calls=%fused_computation.94 | loop fusion | bytes 1179652 | tf_op jit(solution)/shard_map/dynamic_slice | solution.py:202
  10.5 2.5 %collective-permute-start.8 = (bf16[256,1152]{1,0:T(8,128)(2,1)}, bf16[256,1152]{1,0:T(8,128)(2,1)}, u32[]{:S(2)}, u32[]{:S(2)}) collective-permute-start(bf16[256,1152]{1,0:T(8,128)(2,1)} %constant_dynamic-slice_fusion.3), channel_id=1, source_target_pairs={{0,8},{8,0},{16,24},{24,16},{1,9},{9,1},{17,25},{25,17},{2,10},{10... | collective-permute-start | bytes 1769480 | tf_op jit(solution)/shard_map/ppermute | solution.py:205
  12.9 1.5 collective-permute-start.10
  14.6 0.5 collective-permute-start.5
  15.1 1.0 collective-permute-done.5
  16.2 0.8 copy-done.6
  17.3 0.9 copy-done.8
  18.2 0.4 multiply_reduce_fusion.2
  18.7 22.3 %collective-permute-done.12 = bf16[256,1152]{1,0:T(8,128)(2,1)} collective-permute-done((bf16[256,1152]{1,0:T(8,128)(2,1)}, bf16[256,1152]{1,0:T(8,128)(2,1)}, u32[]{:S(2)}, u32[]{:S(2)}) %collective-permute-start.12) | collective-permute-done | bytes 589856 | tf_op jit(solution)/shard_map/ppermute | solution.py:205
  41.4 1.0 copy.64
  42.4 0.8 fusion.40
  43.2 2.4 %collective-permute-start.6 = (bf16[16,4,128]{2,1,0:T(4,128)(2,1)S(1)}, bf16[16,4,128]{2,1,0:T(4,128)(2,1)S(1)}, u32[]{:S(2)}, u32[]{:S(2)}) collective-permute-start(bf16[16,4,128]{2,1,0:T(4,128)(2,1)S(1)} %get-tuple-element.53), channel_id=1, source_target_pairs={{0,1},{1,2},{2,3},{3,4},{4,5},{5,6},{6,7},{8,9},{9,10},{10,11},{11... | collective-permute-start | bytes 49160 | tf_op jit(solution)/shard_map/ppermute | solution.py:19
  45.6 1.3 collective-permute-start.7
  47.2 1.3 copy.66
  48.5 6.7 %all-to-all-start.2 = ((bf16[16,128,128]{2,1,0:T(8,128)(2,1)}), bf16[16,128,128]{2,1,0:T(8,128)(2,1)S(1)}, u32[]{:S(2)}, u32[]{:S(2)}) async-start(bf16[16,128,128]{2,1,0:T(8,128)(2,1)} %bitcast.12), calls=%async_computation.2 | async-start | bytes 1048576 | tf_op jit(solution)/shard_map/all_to_all | solution.py:242
  55.2 2.2 %maximum_convert_fusion.pad_ref = f32[16,136,128]{2,1,0:T(8,128)} fusion(bf16[16,4,128]{2,1,0:T(4,128)(2,1)S(1)} %collective-permute-done.7, bf16[16,128,128]{2,1,0:T(8,128)(2,1)} %bitcast.12, bf16[16,4,128]{2,1,0:T(4,128)(2,1)S(1)} %collective-permute-done.6), kind=kLoop, calls=%fused_computation.47 | loop fusion | flops 1671168 | bytes 1671168 | tf_op jit(solution)/shard_map/convert_element_type | solution.py:238
  57.4 0.5 collective-permute-start.9
  58.0 1.4 broadcast_select_fusion.1
  59.5 0.4 collective-permute-done.9
  59.9 1.2 broadcast_select_fusion.5
  61.4 1.1 copy-done.1
  62.5 0.7 pad_maximum_fusion
  63.3 0.4 dynamic-slice_bitcast_fusion.3
  63.6 2.8 %pad_maximum_fusion.1 = bf16[2048,1152]{1,0:T(8,128)(2,1)} fusion(bf16[512,1152]{1,0:T(8,128)(2,1)S(1)} %get-tuple-element.31, bf16[512,1152]{1,0:T(8,128)(2,1)S(1)} %get-tuple-element.32, bf16[512,1152]{1,0:T(8,128)(2,1)S(1)} %get-tuple-element.33, bf16[512,1152]{1,0:T(8,128)(2,1)S(1)} %get-tuple-element.30), kind=kLoop, calls=%fused_computation.1 | loop fusion | flops 18874368 | bytes 9437184 | tf_op jit(solution)/shard_map/concatenate | solution.py:211
  66.5 6.6 %shard_map.98 = bf16[16,128,128]{2,1,0:T(8,128)(2,1)} custom-call(f32[16,136,128]{2,1,0:T(8,128)} %maximum_convert_fusion.pad_ref, bf16[16,128,1152]{2,1,0:T(8,128)(2,1)} %bitcast.94, f32[16,128,128]{2,1,0:T(8,128)} %bitcast.98), custom_call_target="tpu_custom_call" | custom-call | flops 603979776 | bytes 7405568 | tf_op jit(solution)/shard_map/pallas_call | solution.py:74
  73.0 0.8 fusion.39
  73.8 2.3 %collective-permute-start.14 = (bf16[16,4,128]{2,1,0:T(4,128)(2,1)S(1)}, bf16[16,4,128]{2,1,0:T(4,128)(2,1)S(1)}, u32[]{:S(2)}, u32[]{:S(2)}) collective-permute-start(bf16[16,4,128]{2,1,0:T(4,128)(2,1)S(1)} %get-tuple-element.51), channel_id=1, source_target_pairs={{0,1},{1,2},{2,3},{3,4},{4,5},{5,6},{6,7},{8,9},{9,10},{10,11},{11... | collective-permute-start | bytes 49160 | tf_op jit(solution)/shard_map/ppermute | solution.py:19
  76.1 1.3 collective-permute-start.15
  77.7 6.8 %all-to-all-start.1 = ((bf16[16,128,128]{2,1,0:T(8,128)(2,1)}), bf16[16,128,128]{2,1,0:T(8,128)(2,1)}, u32[]{:S(2)}, u32[]{:S(2)}) async-start(bf16[16,128,128]{2,1,0:T(8,128)(2,1)} %shard_map.98), calls=%async_computation.1 | async-start | bytes 1048576 | tf_op jit(solution)/shard_map/all_to_all | solution.py:243
  84.8 1.0 all_to_all.40
  85.8 1.1 maximum_convert_fusion.1.pad_ref
  87.0 5.2 %shard_map.99 = f32[16,128,128]{2,1,0:T(8,128)} custom-call(f32[16,136,128]{2,1,0:T(8,128)} %maximum_convert_fusion.1.pad_ref, bf16[16,128,1152]{2,1,0:T(8,128)(2,1)} %bitcast.95), custom_call_target="tpu_custom_call" | custom-call | flops 603979776 | bytes 6881280 | tf_op jit(solution)/shard_map/pallas_call | solution.py:96
  92.1 1.6 copy.67
  94.3 0.7 copy-done.3
  95.1 0.4 fusion.10
  95.9 1.2 pad_maximum_fusion.5
  97.2 2.8 %all-to-all-done.1 = bf16[16,128,128]{2,1,0:T(8,128)(2,1)} async-done(((bf16[16,128,128]{2,1,0:T(8,128)(2,1)}), bf16[16,128,128]{2,1,0:T(8,128)(2,1)}, u32[]{:S(2)}, u32[]{:S(2)}) %all-to-all-start.1) | async-done | bytes 524320 | tf_op jit(solution)/shard_map/all_to_all | solution.py:243
  100.0 2.9 %all-to-all-start = ((bf16[32,130,64]{1,2,0:T(8,128)(2,1)}), bf16[32,130,64]{1,2,0:T(8,128)(2,1)S(1)}, u32[]{:S(2)}, u32[]{:S(2)}) async-start(bf16[32,130,64]{1,2,0:T(8,128)(2,1)} %pad_maximum_fusion.5), calls=%async_computation | async-start | bytes 2097152 | tf_op jit(solution)/shard_map/all_to_all | solution.py:155
  102.9 1.1 copy.77
  104.7 0.4 convolution_dynamic-update-slice_fusion.6
  105.1 0.4 convolution_dynamic-update-slice_fusion.5
  107.3 0.4 copy.79
  107.7 0.8 constant_dynamic-slice_fusion.2
  108.4 1.6 %collective-permute-start.16 = (f32[64,1152]{1,0:T(8,128)}, f32[64,1152]{1,0:T(8,128)}, u32[]{:S(2)}, u32[]{:S(2)}) collective-permute-start(f32[64,1152]{1,0:T(8,128)} %get-tuple-element.38), channel_id=1, source_target_pairs={{0,8},{8,0},{16,24},{24,16},{1,9},{9,1},{17,25},{25,17},{2,10},{10... | collective-permute-start | bytes 884744 | tf_op jit(solution)/shard_map/ppermute | solution.py:180
  110.0 1.5 collective-permute-start.17
  111.5 0.4 collective-permute-start.18
  111.9 18.7 %all-to-all-done = bf16[32,130,64]{1,2,0:T(8,128)(2,1)S(1)} async-done(((bf16[32,130,64]{1,2,0:T(8,128)(2,1)}), bf16[32,130,64]{1,2,0:T(8,128)(2,1)S(1)}, u32[]{:S(2)}, u32[]{:S(2)}) %all-to-all-start) | async-done | bytes 532512 | tf_op jit(solution)/shard_map/all_to_all | solution.py:155
  131.1 0.9 fusion.2
  132.2 1.2 add_add_fusion
  133.4 0.8 reshape.118
  134.1 3.1 %all-to-all-start.3 = ((f32[32,1,576]{2,1,0:T(1,128)}), f32[32,1,576]{2,1,0:T(1,128)S(1)}, u32[]{:S(2)}, u32[]{:S(2)}) async-start(f32[32,1,576]{2,1,0:T(1,128)} %reshape.118), calls=%async_computation.3 | async-start | bytes 163840 | tf_op jit(solution)/shard_map/all_to_all | solution.py:166
  137.2 1.8 %collective-permute-start.19 = (f32[64,1152]{1,0:T(8,128)S(1)}, f32[64,1152]{1,0:T(8,128)S(1)}, u32[]{:S(2)}, u32[]{:S(2)}) collective-permute-start(f32[64,1152]{1,0:T(8,128)S(1)} %add_add_fusion), channel_id=1, source_target_pairs={{0,8},{8,0},{16,24},{24,16},{1,9},{9,1},{17,25},{25,17},{2,10},{10... | collective-permute-start | bytes 884744 | tf_op jit(solution)/shard_map/ppermute | solution.py:190
  139.0 1.5 collective-permute-start.20
  140.7 4.1 %all-to-all-done.3 = f32[32,1,576]{2,1,0:T(1,128)S(1)} async-done(((f32[32,1,576]{2,1,0:T(1,128)}), f32[32,1,576]{2,1,0:T(1,128)S(1)}, u32[]{:S(2)}, u32[]{:S(2)}) %all-to-all-start.3) | async-done | bytes 73760 | tf_op jit(solution)/shard_map/all_to_all | solution.py:166
  144.9 0.5 broadcast.56
  145.4 0.8 reduce.7
  146.4 0.7 reshape.106
  147.1 0.6 slice_reduce_fusion
  147.8 7.0 %collective-permute-done.20 = f32[64,1152]{1,0:T(8,128)S(1)} collective-permute-done((f32[64,1152]{1,0:T(8,128)S(1)}, f32[64,1152]{1,0:T(8,128)S(1)}, u32[]{:S(2)}, u32[]{:S(2)}) %collective-permute-start.20) | collective-permute-done | bytes 294944 | tf_op jit(solution)/shard_map/ppermute | solution.py:190
  155.0 1.1 pad_maximum_fusion.3
  (86 shorter events, 7.1 us)
Async XLA Ops:
  1.6 6.9 %collective-permute-start = (bf16[32,2048]{1,0:T(8,128)(2,1)S(1)}, bf16[32,2048]{1,0:T(8,128)(2,1)S(1)}, u32[]{:S(2)}, u32[]{:S(2)}) collective-permute-start(bf16[32,2048]{1,0:T(8,128)(2,1)S(1)} %constant_dynamic-slice_fusion.4), channel_id=1, source_target_pairs={{0,8},{8,0},{16,24},{24,16},{1,9},{9,1},{17,25},{25,17},{2,10},{10... | collective-permute-start | bytes 393224 | tf_op jit(solution)/shard_map/ppermute | solution.py:205
  4.6 9.9 %collective-permute-start.2 = (bf16[32,2048]{1,0:T(8,128)(2,1)S(1)}, bf16[32,2048]{1,0:T(8,128)(2,1)S(1)}, u32[]{:S(2)}, u32[]{:S(2)}) collective-permute-start(bf16[32,2048]{1,0:T(8,128)(2,1)S(1)} %constant_dynamic-slice_fusion.4), channel_id=1, source_target_pairs={{0,16},{8,24},{16,0},{24,8},{1,17},{9,25},{17,1},{25,9},{2,18},{10... | collective-permute-start | bytes 393224 | tf_op jit(solution)/shard_map/ppermute | solution.py:205
  6.1 8.4 %collective-permute-start.4 = (bf16[32,2048]{1,0:T(8,128)(2,1)S(1)}, bf16[32,2048]{1,0:T(8,128)(2,1)S(1)}, u32[]{:S(2)}, u32[]{:S(2)}) collective-permute-start(bf16[32,2048]{1,0:T(8,128)(2,1)S(1)} %constant_dynamic-slice_fusion.4), channel_id=1, source_target_pairs={{0,24},{8,16},{16,8},{24,0},{1,25},{9,17},{17,9},{25,1},{2,26},{10... | collective-permute-start | bytes 393224 | tf_op jit(solution)/shard_map/ppermute | solution.py:205
  8.5 6.1 %collective-permute-start.1 = (bf16[32,2048]{1,0:T(8,128)(2,1)S(1)}, bf16[32,2048]{1,0:T(8,128)(2,1)S(1)}, u32[]{:S(2)}, u32[]{:S(2)}) collective-permute-start(bf16[32,2048]{1,0:T(8,128)(2,1)S(1)} %collective-permute-done), channel_id=1, source_target_pairs={{0,1},{1,0},{2,3},{3,2},{4,5},{5,4},{6,7},{7,6},{8,9},{9,8},{10,11... | collective-permute-start | bytes 393224 | tf_op jit(solution)/shard_map/ppermute | solution.py:30
  10.5 47.0 %collective-permute-start.8 = (bf16[256,1152]{1,0:T(8,128)(2,1)}, bf16[256,1152]{1,0:T(8,128)(2,1)}, u32[]{:S(2)}, u32[]{:S(2)}) collective-permute-start(bf16[256,1152]{1,0:T(8,128)(2,1)} %constant_dynamic-slice_fusion.3), channel_id=1, source_target_pairs={{0,8},{8,0},{16,24},{24,16},{1,9},{9,1},{17,25},{25,17},{2,10},{10... | collective-permute-start | bytes 1769480 | tf_op jit(solution)/shard_map/ppermute | solution.py:205
  12.9 45.0 %collective-permute-start.10 = (bf16[256,1152]{1,0:T(8,128)(2,1)}, bf16[256,1152]{1,0:T(8,128)(2,1)S(1)}, u32[]{:S(2)}, u32[]{:S(2)}) collective-permute-start(bf16[256,1152]{1,0:T(8,128)(2,1)} %constant_dynamic-slice_fusion.3), channel_id=1, source_target_pairs={{0,16},{8,24},{16,0},{24,8},{1,17},{9,25},{17,1},{25,9},{2,18},{10... | collective-permute-start | bytes 1769480 | tf_op jit(solution)/shard_map/ppermute | solution.py:205
  14.5 26.5 %collective-permute-start.12 = (bf16[256,1152]{1,0:T(8,128)(2,1)}, bf16[256,1152]{1,0:T(8,128)(2,1)}, u32[]{:S(2)}, u32[]{:S(2)}) collective-permute-start(bf16[256,1152]{1,0:T(8,128)(2,1)} %constant_dynamic-slice_fusion.3), channel_id=1, source_target_pairs={{0,24},{8,16},{16,8},{24,0},{1,25},{9,17},{17,9},{25,1},{2,26},{10... | collective-permute-start | bytes 1769480 | tf_op jit(solution)/shard_map/ppermute | solution.py:205
  14.5 1.7 %collective-permute-start.3 = (bf16[32,2048]{1,0:T(8,128)(2,1)S(1)}, bf16[32,2048]{1,0:T(8,128)(2,1)S(1)}, u32[]{:S(2)}, u32[]{:S(2)}) collective-permute-start(bf16[32,2048]{1,0:T(8,128)(2,1)S(1)} %collective-permute-done.2), channel_id=1, source_target_pairs={{0,1},{1,0},{2,3},{3,2},{4,5},{5,4},{6,7},{7,6},{8,9},{9,8},{10,11... | collective-permute-start | bytes 393224 | tf_op jit(solution)/shard_map/ppermute | solution.py:30
  14.6 1.5 collective-permute-start.5
  16.1 1.0 copy-start.6
  17.2 1.0 copy-start.8
  17.2 1.0 copy-start.9
  18.2 22.7 %copy-start.7 = (f32[2048]{0:T(1024)S(1)}, f32[2048]{0:T(1024)}, u32[]{:S(2)}) copy-start(f32[2048]{0:T(1024)} %param.13) | copy-start | bytes 24580
  41.0 17.1 %collective-permute-start.13 = (bf16[256,1152]{1,0:T(8,128)(2,1)}, bf16[256,1152]{1,0:T(8,128)(2,1)}, u32[]{:S(2)}, u32[]{:S(2)}) collective-permute-start(bf16[256,1152]{1,0:T(8,128)(2,1)} %collective-permute-done.12), channel_id=1, source_target_pairs={{0,1},{1,0},{2,3},{3,2},{4,5},{5,4},{6,7},{7,6},{8,9},{9,8},{10,11... | collective-permute-start | bytes 1769480 | tf_op jit(solution)/shard_map/ppermute | solution.py:30
  41.1 5.8 %copy-start.2 = (bf16[1,128,2048]{2,1,0:T(8,128)(2,1)S(1)}, bf16[1,128,2048]{2,1,0:T(8,128)(2,1)}, u32[]{:S(2)}) copy-start(bf16[1,128,2048]{2,1,0:T(8,128)(2,1)} %param.15) | copy-start | bytes 1572868
  43.2 12.0 %collective-permute-start.6 = (bf16[16,4,128]{2,1,0:T(4,128)(2,1)S(1)}, bf16[16,4,128]{2,1,0:T(4,128)(2,1)S(1)}, u32[]{:S(2)}, u32[]{:S(2)}) collective-permute-start(bf16[16,4,128]{2,1,0:T(4,128)(2,1)S(1)} %get-tuple-element.53), channel_id=1, source_target_pairs={{0,1},{1,2},{2,3},{3,4},{4,5},{5,6},{6,7},{8,9},{9,10},{10,11},{11... | collective-permute-start | bytes 49160 | tf_op jit(solution)/shard_map/ppermute | solution.py:19
  45.6 9.6 %collective-permute-start.7 = (bf16[16,4,128]{2,1,0:T(4,128)(2,1)S(1)}, bf16[16,4,128]{2,1,0:T(4,128)(2,1)S(1)}, u32[]{:S(2)}, u32[]{:S(2)}) collective-permute-start(bf16[16,4,128]{2,1,0:T(4,128)(2,1)S(1)} %get-tuple-element.54), channel_id=1, source_target_pairs={{1,0},{2,1},{3,2},{4,3},{5,4},{6,5},{7,6},{9,8},{10,9},{11,10},{12... | collective-permute-start | bytes 49160 | tf_op jit(solution)/shard_map/ppermute | solution.py:21
  48.5 29.2 %all-to-all-start.2 = ((bf16[16,128,128]{2,1,0:T(8,128)(2,1)}), bf16[16,128,128]{2,1,0:T(8,128)(2,1)S(1)}, u32[]{:S(2)}, u32[]{:S(2)}) async-start(bf16[16,128,128]{2,1,0:T(8,128)(2,1)} %bitcast.12), calls=%async_computation.2 | async-start | bytes 1048576 | tf_op jit(solution)/shard_map/all_to_all | solution.py:242
  57.4 2.5 %collective-permute-start.9 = (bf16[256,1152]{1,0:T(8,128)(2,1)}, bf16[256,1152]{1,0:T(8,128)(2,1)S(1)}, u32[]{:S(2)}, u32[]{:S(2)}) collective-permute-start(bf16[256,1152]{1,0:T(8,128)(2,1)} %collective-permute-done.8), channel_id=1, source_target_pairs={{0,1},{1,0},{2,3},{3,2},{4,5},{5,4},{6,7},{7,6},{8,9},{9,8},{10,11... | collective-permute-start | bytes 1769480 | tf_op jit(solution)/shard_map/ppermute | solution.py:30
  57.9 3.2 %collective-permute-start.11 = (bf16[256,1152]{1,0:T(8,128)(2,1)S(1)}, bf16[256,1152]{1,0:T(8,128)(2,1)S(1)}, u32[]{:S(2)}, u32[]{:S(2)}) collective-permute-start(bf16[256,1152]{1,0:T(8,128)(2,1)S(1)} %collective-permute-done.10), channel_id=1, source_target_pairs={{0,1},{1,0},{2,3},{3,2},{4,5},{5,4},{6,7},{7,6},{8,9},{9,8},{10,11... | collective-permute-start | bytes 1769480 | tf_op jit(solution)/shard_map/ppermute | solution.py:30
  61.2 1.3 copy-start.1
  73.8 12.0 %collective-permute-start.14 = (bf16[16,4,128]{2,1,0:T(4,128)(2,1)S(1)}, bf16[16,4,128]{2,1,0:T(4,128)(2,1)S(1)}, u32[]{:S(2)}, u32[]{:S(2)}) collective-permute-start(bf16[16,4,128]{2,1,0:T(4,128)(2,1)S(1)} %get-tuple-element.51), channel_id=1, source_target_pairs={{0,1},{1,2},{2,3},{3,4},{4,5},{5,6},{6,7},{8,9},{9,10},{10,11},{11... | collective-permute-start | bytes 49160 | tf_op jit(solution)/shard_map/ppermute | solution.py:19
  76.1 9.7 %collective-permute-start.15 = (bf16[16,4,128]{2,1,0:T(4,128)(2,1)S(1)}, bf16[16,4,128]{2,1,0:T(4,128)(2,1)S(1)}, u32[]{:S(2)}, u32[]{:S(2)}) collective-permute-start(bf16[16,4,128]{2,1,0:T(4,128)(2,1)S(1)} %get-tuple-element.52), channel_id=1, source_target_pairs={{1,0},{2,1},{3,2},{4,3},{5,4},{6,5},{7,6},{9,8},{10,9},{11,10},{12... | collective-permute-start | bytes 49160 | tf_op jit(solution)/shard_map/ppermute | solution.py:21
  77.7 22.3 %all-to-all-start.1 = ((bf16[16,128,128]{2,1,0:T(8,128)(2,1)}), bf16[16,128,128]{2,1,0:T(8,128)(2,1)}, u32[]{:S(2)}, u32[]{:S(2)}) async-start(bf16[16,128,128]{2,1,0:T(8,128)(2,1)} %shard_map.98), calls=%async_computation.1 | async-start | bytes 1048576 | tf_op jit(solution)/shard_map/all_to_all | solution.py:243
  84.5 1.3 copy-start
  94.0 1.0 copy-start.3
  95.5 1.7 %copy-start.5 = (bf16[128,2048]{1,0:T(8,128)(2,1)}, bf16[128,2048]{1,0:T(8,128)(2,1)S(1)}, u32[]{:S(2)}) copy-start(bf16[128,2048]{1,0:T(8,128)(2,1)S(1)} %fusion.10) | copy-start | bytes 1572868
  97.2 6.8 %copy-start.4 = (bf16[2,1024,128]{1,2,0:T(8,128)(2,1)S(1)}, bf16[2,1024,128]{1,2,0:T(8,128)(2,1)}, u32[]{:S(2)}) copy-start(bf16[2,1024,128]{1,2,0:T(8,128)(2,1)} %all_to_all.40) | copy-start | bytes 1572868
  100.0 30.6 %all-to-all-start = ((bf16[32,130,64]{1,2,0:T(8,128)(2,1)}), bf16[32,130,64]{1,2,0:T(8,128)(2,1)S(1)}, u32[]{:S(2)}, u32[]{:S(2)}) async-start(bf16[32,130,64]{1,2,0:T(8,128)(2,1)} %pad_maximum_fusion.5), calls=%async_computation | async-start | bytes 2097152 | tf_op jit(solution)/shard_map/all_to_all | solution.py:155
  108.4 23.7 %collective-permute-start.16 = (f32[64,1152]{1,0:T(8,128)}, f32[64,1152]{1,0:T(8,128)}, u32[]{:S(2)}, u32[]{:S(2)}) collective-permute-start(f32[64,1152]{1,0:T(8,128)} %get-tuple-element.38), channel_id=1, source_target_pairs={{0,8},{8,0},{16,24},{24,16},{1,9},{9,1},{17,25},{25,17},{2,10},{10... | collective-permute-start | bytes 884744 | tf_op jit(solution)/shard_map/ppermute | solution.py:180
  110.0 22.1 %collective-permute-start.17 = (f32[64,1152]{1,0:T(8,128)S(1)}, f32[64,1152]{1,0:T(8,128)}, u32[]{:S(2)}, u32[]{:S(2)}) collective-permute-start(f32[64,1152]{1,0:T(8,128)S(1)} %get-tuple-element.40), channel_id=1, source_target_pairs={{0,16},{8,24},{16,0},{24,8},{1,17},{9,25},{17,1},{25,9},{2,18},{10... | collective-permute-start | bytes 884744 | tf_op jit(solution)/shard_map/ppermute | solution.py:180
  111.5 20.7 %collective-permute-start.18 = (f32[64,1152]{1,0:T(8,128)S(1)}, f32[64,1152]{1,0:T(8,128)}, u32[]{:S(2)}, u32[]{:S(2)}) collective-permute-start(f32[64,1152]{1,0:T(8,128)S(1)} %get-tuple-element.39), channel_id=1, source_target_pairs={{0,24},{8,16},{16,8},{24,0},{1,25},{9,17},{17,9},{25,1},{2,26},{10... | collective-permute-start | bytes 884744 | tf_op jit(solution)/shard_map/ppermute | solution.py:180
  134.1 10.7 %all-to-all-start.3 = ((f32[32,1,576]{2,1,0:T(1,128)}), f32[32,1,576]{2,1,0:T(1,128)S(1)}, u32[]{:S(2)}, u32[]{:S(2)}) async-start(f32[32,1,576]{2,1,0:T(1,128)} %reshape.118), calls=%async_computation.3 | async-start | bytes 163840 | tf_op jit(solution)/shard_map/all_to_all | solution.py:166
  137.2 10.6 %collective-permute-start.19 = (f32[64,1152]{1,0:T(8,128)S(1)}, f32[64,1152]{1,0:T(8,128)S(1)}, u32[]{:S(2)}, u32[]{:S(2)}) collective-permute-start(f32[64,1152]{1,0:T(8,128)S(1)} %add_add_fusion), channel_id=1, source_target_pairs={{0,8},{8,0},{16,24},{24,16},{1,9},{9,1},{17,25},{25,17},{2,10},{10... | collective-permute-start | bytes 884744 | tf_op jit(solution)/shard_map/ppermute | solution.py:190
  139.0 15.8 %collective-permute-start.20 = (f32[64,1152]{1,0:T(8,128)S(1)}, f32[64,1152]{1,0:T(8,128)S(1)}, u32[]{:S(2)}, u32[]{:S(2)}) collective-permute-start(f32[64,1152]{1,0:T(8,128)S(1)} %add_add_fusion), channel_id=1, source_target_pairs={{0,16},{8,24},{16,0},{24,8},{1,17},{9,25},{17,1},{25,9},{2,18},{10... | collective-permute-start | bytes 884744 | tf_op jit(solution)/shard_map/ppermute | solution.py:190
  140.5 14.3 %collective-permute-start.21 = (f32[64,1152]{1,0:T(8,128)S(1)}, f32[64,1152]{1,0:T(8,128)S(1)}, u32[]{:S(2)}, u32[]{:S(2)}) collective-permute-start(f32[64,1152]{1,0:T(8,128)S(1)} %add_add_fusion), channel_id=1, source_target_pairs={{0,24},{8,16},{16,8},{24,0},{1,25},{9,17},{17,9},{25,1},{2,26},{10... | collective-permute-start | bytes 884744 | tf_op jit(solution)/shard_map/ppermute | solution.py:190

commit v13 on v12

--- a/solution.py
+++ b/solution.py
@@ -194,23 +194,39 @@
     )
 
 
-def gather_shards(block, axis):
-    count = lax.axis_size(axis)
-    me = lax.axis_index(axis)
+def fetch_halves(block, axis):
+    count = lax.axis_size(axis)
     core = lax.axis_index("seq") % 2
     half_rows = block.shape[0] // 2
     mine = lax.dynamic_slice_in_dim(block, core * half_rows, half_rows, axis=0)
+    return {
+        apart: lax.ppermute(mine, axis, [(source, source ^ apart) for source in range(count)])
+        for apart in range(count - 1, 0, -1)
+    }
+
+
+def swap_halves(fetched):
+    return {apart: from_partner(piece, "seq", 0) for apart, piece in fetched.items()}
+
+
+def assemble_shards(block, axis, fetched, swapped):
+    count = lax.axis_size(axis)
+    me = lax.axis_index(axis)
+    core = lax.axis_index("seq") % 2
     blocks = [block]
     for apart in range(1, count):
-        fetched = lax.ppermute(mine, axis, [(source, source ^ apart) for source in range(count)])
-        swapped = from_partner(fetched, "seq", 0)
-        lower = jnp.where(core == 0, fetched, swapped)
-        upper = jnp.where(core == 0, swapped, fetched)
+        lower = jnp.where(core == 0, fetched[apart], swapped[apart])
+        upper = jnp.where(core == 0, swapped[apart], fetched[apart])
         blocks.append(jnp.concatenate([lower, upper], axis=0))
     stacked = jnp.stack(blocks)
     return jnp.concatenate(
         [lax.dynamic_index_in_dim(stacked, index ^ me, keepdims=False) for index in range(count)], axis=0
     )
+
+
+def gather_shards(block, axis):
+    fetched = fetch_halves(block, axis)
+    return assemble_shards(block, axis, fetched, swap_halves(fetched))
 
 
 def body(events, type_ids, type_table, norm_gain, kernel, upstream):
@@ -225,14 +241,22 @@
     if fsdp & (fsdp - 1):
         raise ValueError("fsdp not pow2")
     table = gather_shards(type_table, "fsdp")
+    kernel_fetched = fetch_halves(kernel, "fsdp")
+    far = fsdp - 1
     types = table.shape[0]
     onehot = (type_ids[0][:, None] == jnp.arange(types, dtype=jnp.int32)[None, :]).astype(jnp.bfloat16)
     mixed = events[0].astype(jnp.float32) + jnp.dot(onehot, table, preferred_element_type=jnp.float32)
+    near = {apart: piece for apart, piece in kernel_fetched.items() if apart != far}
+    near_swapped = swap_halves(near)
+    near, near_swapped, mixed = lax.optimization_barrier((near, near_swapped, mixed))
     inv = lax.rsqrt(jnp.mean(mixed * mixed, axis=-1, keepdims=True) + 1e-06)
     normed = (mixed * inv * norm_gain).astype(jnp.bfloat16)
     normed_g = normed.reshape(length, GROUPS, chans).transpose(1, 0, 2)
     padded = with_halo(normed_g, "seq", 1, half)
-    weights = gather_shards(kernel, "fsdp").reshape(GROUPS, chans, KERNEL * chans)
+    far_piece, padded = lax.optimization_barrier((kernel_fetched[far], padded))
+    kernel_fetched = {**near, far: far_piece}
+    kernel_swapped = {**near_swapped, **swap_halves({far: far_piece})}
+    weights = assemble_shards(kernel, "fsdp", kernel_fetched, kernel_swapped).reshape(GROUPS, chans, KERNEL * chans)
     up_float = upstream[0].astype(jnp.float32)
     up_g = up_float.reshape(length, GROUPS, chans).transpose(1, 0, 2)
     dconv = conv_dconv(padded.astype(jnp.float32), weights, up_g)

time: 157 us -> 170 us (1.083)
  waiting for transfers between devices: 58.8 us -> 72.6 us
    all_to_all x1, waiting for transfers between devices: 2.79 us -> 9.84 us  [body(): group_out = lax.all_to_all(dconv, 'seq', 0, 1, tiled=True)]
    ppermute x6, waiting for transfers between devices: 24.6 us -> 27.5 us  [fetch_halves(): lax.ppermute(mine, axis, [(source, source ^ apart) for source in range(co...]
    ppermute x2, waiting for transfers between devices: 0.01 us -> 2.67 us  [with_halo(): lax.ppermute(head, axis, [((i + 1) % count, i) for i in range(ends)])]
    concatenate x1 -> x2, other arithmetic: 2.83 us -> 4.05 us  [the longest x1 2.78 us: assemble_shards(): jnp.concatenate([lax.dynamic_index_in_dim(stacked, index ^ me, keepdims=F...]
    unnamed x23 -> x29, local copies, waits for them, and re-layouts: 4.73 us -> 4.01 us
  transfers between devices with their start and end apart: 26 -> 26, of which waited for: 9 -> 13; matrix products, arithmetic and copies ran while one was open for 21% -> 20% of each run, Pallas kernels for 8% -> 7%
where the time goes in v13:
time: 170 us; the launch traced here: 169 us
  waiting for transfers between devices  72.6 us (43%)
  starting transfers between devices  42 us (25%)
  local copies, waits for them, and re-layouts  19.7 us (12%)
  other arithmetic  16.9 us (10%)
  Pallas kernels  11.7 us (7%)
  matrix products  4.39 us (3%)
    ppermute x6, waiting for transfers between devices, fetch_halves(): lax.ppermute(mine, axis, [(source, source ^ apart) for source in range(co...  27.5 us
    all_to_all x1, waiting for transfers between devices, table_and_gain(): got = lax.all_to_all(send, every, 0, 0, tiled=True)  19.7 us
    all_to_all x1, waiting for transfers between devices, body(): group_out = lax.all_to_all(dconv, 'seq', 0, 1, tiled=True)  9.84 us
    ppermute x6, starting transfers between devices, fetch_halves(): lax.ppermute(mine, axis, [(source, source ^ apart) for source in range(co...  8.55 us
    all_to_all x1, starting transfers between devices, body(): group_in = lax.all_to_all(normed_g, 'seq', 0, 1, tiled=True)  7.14 us
    ppermute x3, waiting for transfers between devices, gather_by_permutes(): pieces.append(lax.ppermute(total, axis, pairs))  7.13 us
    pallas_call x1, Pallas kernels, conv_dconv(): pl.pallas_call(forward_kernel, grid=(groups // step,), in_specs=[pl.Block...  6.55 us
    all_to_all x1, starting transfers between devices, body(): group_out = lax.all_to_all(dconv, 'seq', 0, 1, tiled=True)  5.73 us
  transfers between devices with their start and end apart: 26, of which 13 were waited for; matrix products, arithmetic and copies ran while one was open for 20% of the time, Pallas kernels for 7%

profile of v13, /device:TPU:0, one launch (start us, length us, event | category | flops | bytes accessed | tf_op | source)
XLA Modules:
  0.0 168.6 jit_solution(15328577401074464547)
XLA Ops:
  0.6 0.9 constant_dynamic-slice_fusion.3
  1.6 3.0 %collective-permute-start.4 = (bf16[32,2048]{1,0:T(8,128)(2,1)S(1)}, bf16[32,2048]{1,0:T(8,128)(2,1)S(1)}, u32[]{:S(2)}, u32[]{:S(2)}) collective-permute-start(bf16[32,2048]{1,0:T(8,128)(2,1)S(1)} %constant_dynamic-slice_fusion.3), channel_id=1, source_target_pairs={{0,8},{8,0},{16,24},{24,16},{1,9},{9,1},{17,25},{25,17},{2,10},{10... | collective-permute-start | bytes 393224 | tf_op jit(solution)/shard_map/ppermute | solution.py:203
  4.6 1.5 collective-permute-start.6
  6.1 2.4 %collective-permute-done.4 = bf16[32,2048]{1,0:T(8,128)(2,1)S(1)} collective-permute-done((bf16[32,2048]{1,0:T(8,128)(2,1)S(1)}, bf16[32,2048]{1,0:T(8,128)(2,1)S(1)}, u32[]{:S(2)}, u32[]{:S(2)}) %collective-permute-start.4) | collective-permute-done | bytes 131104 | tf_op jit(solution)/shard_map/ppermute | solution.py:203
  8.5 1.9 %constant_dynamic-slice_fusion.4 = bf16[256,1152]{1,0:T(8,128)(2,1)} fusion(bf16[512,1152]{1,0:T(8,128)(2,1)} %param.14, s32[]{:T(128)S(6)} %select_n.111), kind=kLoop, calls=%fused_computation.95 | loop fusion | bytes 1179652 | tf_op jit(solution)/shard_map/dynamic_slice | solution.py:201
  10.4 2.5 %collective-permute-start = (bf16[256,1152]{1,0:T(8,128)(2,1)}, bf16[256,1152]{1,0:T(8,128)(2,1)S(1)}, u32[]{:S(2)}, u32[]{:S(2)}) collective-permute-start(bf16[256,1152]{1,0:T(8,128)(2,1)} %constant_dynamic-slice_fusion.4), channel_id=1, source_target_pairs={{0,8},{8,0},{16,24},{24,16},{1,9},{9,1},{17,25},{25,17},{2,10},{10... | collective-permute-start | bytes 1769480 | tf_op jit(solution)/shard_map/ppermute | solution.py:203
  12.9 1.5 collective-permute-start.1
  14.5 0.5 collective-permute-start.9
  15.1 0.8 collective-permute-done.7
  16.1 11.2 %collective-permute-done = bf16[256,1152]{1,0:T(8,128)(2,1)S(1)} collective-permute-done((bf16[256,1152]{1,0:T(8,128)(2,1)}, bf16[256,1152]{1,0:T(8,128)(2,1)S(1)}, u32[]{:S(2)}, u32[]{:S(2)}) %collective-permute-start) | collective-permute-done | bytes 589856 | tf_op jit(solution)/shard_map/ppermute | solution.py:203
  27.3 13.9 %collective-permute-done.1 = bf16[256,1152]{1,0:T(8,128)(2,1)S(1)} collective-permute-done((bf16[256,1152]{1,0:T(8,128)(2,1)}, bf16[256,1152]{1,0:T(8,128)(2,1)S(1)}, u32[]{:S(2)}, u32[]{:S(2)}) %collective-permute-start.1) | collective-permute-done | bytes 589856 | tf_op jit(solution)/shard_map/ppermute | solution.py:203
  41.5 0.6 copy-done.3
  42.1 0.4 copy-done.11
  43.7 0.4 copy-done.7
  44.5 1.0 copy.64
  45.5 0.8 fusion.40
  46.3 2.1 %collective-permute-start.11 = (bf16[16,4,128]{2,1,0:T(4,128)(2,1)S(1)}, bf16[16,4,128]{2,1,0:T(4,128)(2,1)S(1)}, u32[]{:S(2)}, u32[]{:S(2)}) collective-permute-start(bf16[16,4,128]{2,1,0:T(4,128)(2,1)S(1)} %get-tuple-element.67), channel_id=1, source_target_pairs={{0,1},{1,2},{2,3},{3,4},{4,5},{5,6},{6,7},{8,9},{9,10},{10,11},{11... | collective-permute-start | bytes 49160 | tf_op jit(solution)/shard_map/ppermute | solution.py:19
  48.5 1.3 collective-permute-start.12
  50.0 1.3 copy.66
  51.3 7.1 %all-to-all-start.2 = ((bf16[16,128,128]{2,1,0:T(8,128)(2,1)}), bf16[16,128,128]{2,1,0:T(8,128)(2,1)}, u32[]{:S(2)}, u32[]{:S(2)}) async-start(bf16[16,128,128]{2,1,0:T(8,128)(2,1)} %bitcast.12), calls=%async_computation.2 | async-start | bytes 1048576 | tf_op jit(solution)/shard_map/all_to_all | solution.py:266
  58.5 1.3 pad_maximum_fusion.6
  59.8 0.6 collective-permute-start.13
  60.8 1.1 convert_element_type.51.pad_ref
  62.2 1.2 broadcast_select_fusion.1
  63.5 1.2 copy-done
  64.7 0.7 pad_maximum_fusion
  65.4 0.4 dynamic-slice_bitcast_fusion.3
  65.8 2.8 %pad_maximum_fusion.1 = bf16[2048,1152]{1,0:T(8,128)(2,1)} fusion(bf16[512,1152]{1,0:T(8,128)(2,1)S(1)} %get-tuple-element.45, bf16[512,1152]{1,0:T(8,128)(2,1)S(1)} %get-tuple-element.46, bf16[512,1152]{1,0:T(8,128)(2,1)S(1)} %get-tuple-element.47, bf16[512,1152]{1,0:T(8,128)(2,1)S(1)} %get-tuple-element.44), kind=kLoop, calls=%fused_computation.1 | loop fusion | flops 18874368 | bytes 9437184 | tf_op jit(solution)/shard_map/concatenate | solution.py:222
  68.6 6.5 %shard_map.98 = bf16[16,128,128]{2,1,0:T(8,128)(2,1)} custom-call(f32[16,136,128]{2,1,0:T(8,128)} %convert_element_type.51.pad_ref, bf16[16,128,1152]{2,1,0:T(8,128)(2,1)} %bitcast.94, f32[16,128,128]{2,1,0:T(8,128)} %bitcast.98), custom_call_target="tpu_custom_call" | custom-call | flops 603979776 | bytes 7405568 | tf_op jit(solution)/shard_map/pallas_call | solution.py:74
  75.1 0.8 fusion.39
  75.9 2.3 %collective-permute-start.14 = (bf16[16,4,128]{2,1,0:T(4,128)(2,1)S(1)}, bf16[16,4,128]{2,1,0:T(4,128)(2,1)S(1)}, u32[]{:S(2)}, u32[]{:S(2)}) collective-permute-start(bf16[16,4,128]{2,1,0:T(4,128)(2,1)S(1)} %get-tuple-element.65), channel_id=1, source_target_pairs={{0,1},{1,2},{2,3},{3,4},{4,5},{5,6},{6,7},{8,9},{9,10},{10,11},{11... | collective-permute-start | bytes 49160 | tf_op jit(solution)/shard_map/ppermute | solution.py:19
  78.2 1.3 collective-permute-start.15
  79.7 2.7 %collective-permute-done.15 = bf16[16,4,128]{2,1,0:T(4,128)(2,1)S(1)} collective-permute-done((bf16[16,4,128]{2,1,0:T(4,128)(2,1)S(1)}, bf16[16,4,128]{2,1,0:T(4,128)(2,1)S(1)}, u32[]{:S(2)}, u32[]{:S(2)}) %collective-permute-start.15) | collective-permute-done | bytes 16416 | tf_op jit(solution)/shard_map/ppermute | solution.py:21
  82.4 2.2 %maximum_convert_fusion.pad_ref = f32[16,136,128]{2,1,0:T(8,128)} fusion(bf16[16,4,128]{2,1,0:T(4,128)(2,1)S(1)} %collective-permute-done.15, bf16[16,128,128]{2,1,0:T(8,128)(2,1)} %shard_map.98, bf16[16,4,128]{2,1,0:T(4,128)(2,1)S(1)} %collective-permute-done.14), kind=kLoop, calls=%fused_computation.48 | loop fusion | flops 1671168 | bytes 1671168 | tf_op jit(solution)/shard_map/convert_element_type | solution.py:264
  84.6 5.1 %shard_map.99 = f32[16,128,128]{2,1,0:T(8,128)} custom-call(f32[16,136,128]{2,1,0:T(8,128)} %maximum_convert_fusion.pad_ref, bf16[16,128,1152]{2,1,0:T(8,128)(2,1)} %bitcast.95), custom_call_target="tpu_custom_call" | custom-call | flops 603979776 | bytes 6881280 | tf_op jit(solution)/shard_map/pallas_call | solution.py:96
  89.7 1.6 copy.67
  91.9 5.7 %all-to-all-start.1 = ((bf16[16,128,128]{2,1,0:T(8,128)(2,1)}), bf16[16,128,128]{2,1,0:T(8,128)(2,1)S(1)}, u32[]{:S(2)}, u32[]{:S(2)}) async-start(bf16[16,128,128]{2,1,0:T(8,128)(2,1)} %shard_map.98), calls=%async_computation.1 | async-start | bytes 1048576 | tf_op jit(solution)/shard_map/all_to_all | solution.py:267
  97.7 1.2 fusion.10
  98.8 1.3 copy.69
  100.4 1.2 pad_maximum_fusion.5
  101.6 1.3 copy.78
  103.2 9.8 %all-to-all-done.1 = bf16[16,128,128]{2,1,0:T(8,128)(2,1)S(1)} async-done(((bf16[16,128,128]{2,1,0:T(8,128)(2,1)}), bf16[16,128,128]{2,1,0:T(8,128)(2,1)S(1)}, u32[]{:S(2)}, u32[]{:S(2)}) %all-to-all-start.1) | async-done | bytes 524320 | tf_op jit(solution)/shard_map/all_to_all | solution.py:267
  113.0 2.8 %all-to-all-start = ((bf16[32,130,64]{1,2,0:T(8,128)(2,1)}), bf16[32,130,64]{1,2,0:T(8,128)(2,1)S(1)}, u32[]{:S(2)}, u32[]{:S(2)}) async-start(bf16[32,130,64]{1,2,0:T(8,128)(2,1)} %pad_maximum_fusion.5), calls=%async_computation | async-start | bytes 2097152 | tf_op jit(solution)/shard_map/all_to_all | solution.py:155
  116.6 0.4 convolution_dynamic-update-slice_fusion.6
  117.0 0.4 convolution_dynamic-update-slice_fusion.5
  119.2 0.4 copy.79
  119.6 0.8 constant_dynamic-slice_fusion.2
  120.4 1.5 collective-permute-start.16
  121.9 1.5 collective-permute-start.17
  123.4 0.5 collective-permute-start.18
  123.9 19.7 %all-to-all-done = bf16[32,130,64]{1,2,0:T(8,128)(2,1)S(1)} async-done(((bf16[32,130,64]{1,2,0:T(8,128)(2,1)}), bf16[32,130,64]{1,2,0:T(8,128)(2,1)S(1)}, u32[]{:S(2)}, u32[]{:S(2)}) %all-to-all-start) | async-done | bytes 532512 | tf_op jit(solution)/shard_map/all_to_all | solution.py:155
  144.1 0.9 fusion.2
  145.1 1.2 add_add_fusion
  146.3 0.8 reshape.118
  147.1 2.6 %all-to-all-start.3 = ((f32[32,1,576]{2,1,0:T(1,128)}), f32[32,1,576]{2,1,0:T(1,128)S(1)}, u32[]{:S(2)}, u32[]{:S(2)}) async-start(f32[32,1,576]{2,1,0:T(1,128)} %reshape.118), calls=%async_computation.3 | async-start | bytes 163840 | tf_op jit(solution)/shard_map/all_to_all | solution.py:166
  149.7 1.8 %collective-permute-start.19 = (f32[64,1152]{1,0:T(8,128)S(1)}, f32[64,1152]{1,0:T(8,128)S(1)}, u32[]{:S(2)}, u32[]{:S(2)}) collective-permute-start(f32[64,1152]{1,0:T(8,128)S(1)} %add_add_fusion), channel_id=1, source_target_pairs={{0,8},{8,0},{16,24},{24,16},{1,9},{9,1},{17,25},{25,17},{2,10},{10... | collective-permute-start | bytes 884744 | tf_op jit(solution)/shard_map/ppermute | solution.py:190
  151.5 1.5 collective-permute-start.20
  153.3 4.1 %all-to-all-done.3 = f32[32,1,576]{2,1,0:T(1,128)S(1)} async-done(((f32[32,1,576]{2,1,0:T(1,128)}), f32[32,1,576]{2,1,0:T(1,128)S(1)}, u32[]{:S(2)}, u32[]{:S(2)}) %all-to-all-start.3) | async-done | bytes 73760 | tf_op jit(solution)/shard_map/all_to_all | solution.py:166
  157.4 0.5 broadcast.56
  157.9 0.8 reduce.7
  158.9 0.7 reshape.106
  159.6 0.6 slice_reduce_fusion
  160.3 7.0 %collective-permute-done.20 = f32[64,1152]{1,0:T(8,128)S(1)} collective-permute-done((f32[64,1152]{1,0:T(8,128)S(1)}, f32[64,1152]{1,0:T(8,128)S(1)}, u32[]{:S(2)}, u32[]{:S(2)}) %collective-permute-start.20) | collective-permute-done | bytes 294944 | tf_op jit(solution)/shard_map/ppermute | solution.py:190
  167.5 1.1 pad_maximum_fusion.3
  (95 shorter events, 8.4 us)
Async XLA Ops:
  1.6 6.9 %collective-permute-start.4 = (bf16[32,2048]{1,0:T(8,128)(2,1)S(1)}, bf16[32,2048]{1,0:T(8,128)(2,1)S(1)}, u32[]{:S(2)}, u32[]{:S(2)}) collective-permute-start(bf16[32,2048]{1,0:T(8,128)(2,1)S(1)} %constant_dynamic-slice_fusion.3), channel_id=1, source_target_pairs={{0,8},{8,0},{16,24},{24,16},{1,9},{9,1},{17,25},{25,17},{2,10},{10... | collective-permute-start | bytes 393224 | tf_op jit(solution)/shard_map/ppermute | solution.py:203
  4.6 9.8 %collective-permute-start.6 = (bf16[32,2048]{1,0:T(8,128)(2,1)S(1)}, bf16[32,2048]{1,0:T(8,128)(2,1)S(1)}, u32[]{:S(2)}, u32[]{:S(2)}) collective-permute-start(bf16[32,2048]{1,0:T(8,128)(2,1)S(1)} %constant_dynamic-slice_fusion.3), channel_id=1, source_target_pairs={{0,16},{8,24},{16,0},{24,8},{1,17},{9,25},{17,1},{25,9},{2,18},{10... | collective-permute-start | bytes 393224 | tf_op jit(solution)/shard_map/ppermute | solution.py:203
  6.1 8.3 %collective-permute-start.8 = (bf16[32,2048]{1,0:T(8,128)(2,1)S(1)}, bf16[32,2048]{1,0:T(8,128)(2,1)S(1)}, u32[]{:S(2)}, u32[]{:S(2)}) collective-permute-start(bf16[32,2048]{1,0:T(8,128)(2,1)S(1)} %constant_dynamic-slice_fusion.3), channel_id=1, source_target_pairs={{0,24},{8,16},{16,8},{24,0},{1,25},{9,17},{17,9},{25,1},{2,26},{10... | collective-permute-start | bytes 393224 | tf_op jit(solution)/shard_map/ppermute | solution.py:203
  8.5 6.0 %collective-permute-start.5 = (bf16[32,2048]{1,0:T(8,128)(2,1)S(1)}, bf16[32,2048]{1,0:T(8,128)(2,1)S(1)}, u32[]{:S(2)}, u32[]{:S(2)}) collective-permute-start(bf16[32,2048]{1,0:T(8,128)(2,1)S(1)} %collective-permute-done.4), channel_id=1, source_target_pairs={{0,1},{1,0},{2,3},{3,2},{4,5},{5,4},{6,7},{7,6},{8,9},{9,8},{10,11... | collective-permute-start | bytes 393224 | tf_op jit(solution)/shard_map/ppermute | solution.py:30
  10.4 16.9 %collective-permute-start = (bf16[256,1152]{1,0:T(8,128)(2,1)}, bf16[256,1152]{1,0:T(8,128)(2,1)S(1)}, u32[]{:S(2)}, u32[]{:S(2)}) collective-permute-start(bf16[256,1152]{1,0:T(8,128)(2,1)} %constant_dynamic-slice_fusion.4), channel_id=1, source_target_pairs={{0,8},{8,0},{16,24},{24,16},{1,9},{9,1},{17,25},{25,17},{2,10},{10... | collective-permute-start | bytes 1769480 | tf_op jit(solution)/shard_map/ppermute | solution.py:203
  12.9 28.3 %collective-permute-start.1 = (bf16[256,1152]{1,0:T(8,128)(2,1)}, bf16[256,1152]{1,0:T(8,128)(2,1)S(1)}, u32[]{:S(2)}, u32[]{:S(2)}) collective-permute-start(bf16[256,1152]{1,0:T(8,128)(2,1)} %constant_dynamic-slice_fusion.4), channel_id=1, source_target_pairs={{0,16},{8,24},{16,0},{24,8},{1,17},{9,25},{17,1},{25,9},{2,18},{10... | collective-permute-start | bytes 1769480 | tf_op jit(solution)/shard_map/ppermute | solution.py:203
  14.4 45.3 %collective-permute-start.10 = (bf16[256,1152]{1,0:T(8,128)(2,1)}, bf16[256,1152]{1,0:T(8,128)(2,1)}, u32[]{:S(2)}, u32[]{:S(2)}) collective-permute-start(bf16[256,1152]{1,0:T(8,128)(2,1)} %constant_dynamic-slice_fusion.4), channel_id=1, source_target_pairs={{0,24},{8,16},{16,8},{24,0},{1,25},{9,17},{17,9},{25,1},{2,26},{10... | collective-permute-start | bytes 1769480 | tf_op jit(solution)/shard_map/ppermute | solution.py:203
  14.4 1.4 collective-permute-start.7
  14.5 1.5 collective-permute-start.9
  15.0 26.2 %copy-start.9 = (bf16[64,2048]{1,0:T(8,128)(2,1)S(1)}, bf16[64,2048]{1,0:T(8,128)(2,1)}, u32[]{:S(2)}) copy-start(bf16[64,2048]{1,0:T(8,128)(2,1)} %param.12) | copy-start | bytes 786436
  27.3 15.6 %collective-permute-start.2 = (bf16[256,1152]{1,0:T(8,128)(2,1)S(1)}, bf16[256,1152]{1,0:T(8,128)(2,1)S(1)}, u32[]{:S(2)}, u32[]{:S(2)}) collective-permute-start(bf16[256,1152]{1,0:T(8,128)(2,1)S(1)} %collective-permute-done), channel_id=1, source_target_pairs={{0,1},{1,0},{2,3},{3,2},{4,5},{5,4},{6,7},{7,6},{8,9},{9,8},{10,11... | collective-permute-start | bytes 1769480 | tf_op jit(solution)/shard_map/ppermute | solution.py:30
  41.2 0.9 copy-start.3
  41.2 2.0 %collective-permute-start.3 = (bf16[256,1152]{1,0:T(8,128)(2,1)S(1)}, bf16[256,1152]{1,0:T(8,128)(2,1)S(1)}, u32[]{:S(2)}, u32[]{:S(2)}) collective-permute-start(bf16[256,1152]{1,0:T(8,128)(2,1)S(1)} %collective-permute-done.1), channel_id=1, source_target_pairs={{0,1},{1,0},{2,3},{3,2},{4,5},{5,4},{6,7},{7,6},{8,9},{9,8},{10,11... | collective-permute-start | bytes 1769480 | tf_op jit(solution)/shard_map/ppermute | solution.py:30
  41.3 1.1 copy-start.11
  41.4 1.1 copy-start.12
  42.5 1.6 copy-start.10
  42.8 0.8 copy-start.5
  43.2 0.8 copy-start.7
  44.2 5.5 %copy-start.1 = (bf16[1,128,2048]{2,1,0:T(8,128)(2,1)S(1)}, bf16[1,128,2048]{2,1,0:T(8,128)(2,1)}, u32[]{:S(2)}) copy-start(bf16[1,128,2048]{2,1,0:T(8,128)(2,1)} %param.15) | copy-start | bytes 1572868
  46.3 12.2 %collective-permute-start.11 = (bf16[16,4,128]{2,1,0:T(4,128)(2,1)S(1)}, bf16[16,4,128]{2,1,0:T(4,128)(2,1)S(1)}, u32[]{:S(2)}, u32[]{:S(2)}) collective-permute-start(bf16[16,4,128]{2,1,0:T(4,128)(2,1)S(1)} %get-tuple-element.67), channel_id=1, source_target_pairs={{0,1},{1,2},{2,3},{3,4},{4,5},{5,6},{6,7},{8,9},{9,10},{10,11},{11... | collective-permute-start | bytes 49160 | tf_op jit(solution)/shard_map/ppermute | solution.py:19
  48.5 10.0 %collective-permute-start.12 = (bf16[16,4,128]{2,1,0:T(4,128)(2,1)S(1)}, bf16[16,4,128]{2,1,0:T(4,128)(2,1)S(1)}, u32[]{:S(2)}, u32[]{:S(2)}) collective-permute-start(bf16[16,4,128]{2,1,0:T(4,128)(2,1)S(1)} %get-tuple-element.68), channel_id=1, source_target_pairs={{1,0},{2,1},{3,2},{4,3},{5,4},{6,5},{7,6},{9,8},{10,9},{11,10},{12... | collective-permute-start | bytes 49160 | tf_op jit(solution)/shard_map/ppermute | solution.py:21
  51.3 9.0 %copy-start.4 = (bf16[256,1152]{1,0:T(8,128)(2,1)S(1)}, bf16[256,1152]{1,0:T(8,128)(2,1)}, u32[]{:S(2)}) copy-start(bf16[256,1152]{1,0:T(8,128)(2,1)} %copy-done.3) | copy-start | bytes 1769476
  51.3 9.0 %copy-start.6 = (bf16[256,1152]{1,0:T(8,128)(2,1)S(1)}, bf16[256,1152]{1,0:T(8,128)(2,1)}, u32[]{:S(2)}) copy-start(bf16[256,1152]{1,0:T(8,128)(2,1)} %copy-done.5) | copy-start | bytes 1769476
  51.3 40.6 %all-to-all-start.2 = ((bf16[16,128,128]{2,1,0:T(8,128)(2,1)}), bf16[16,128,128]{2,1,0:T(8,128)(2,1)}, u32[]{:S(2)}, u32[]{:S(2)}) async-start(bf16[16,128,128]{2,1,0:T(8,128)(2,1)} %bitcast.12), calls=%async_computation.2 | async-start | bytes 1048576 | tf_op jit(solution)/shard_map/all_to_all | solution.py:266
  58.5 1.9 %copy-start.8 = (bf16[256,1152]{1,0:T(8,128)(2,1)S(1)}, bf16[256,1152]{1,0:T(8,128)(2,1)}, u32[]{:S(2)}) copy-start(bf16[256,1152]{1,0:T(8,128)(2,1)} %copy-done.7) | copy-start | bytes 1769476
  59.8 2.4 %collective-permute-start.13 = (bf16[256,1152]{1,0:T(8,128)(2,1)}, bf16[256,1152]{1,0:T(8,128)(2,1)S(1)}, u32[]{:S(2)}, u32[]{:S(2)}) collective-permute-start(bf16[256,1152]{1,0:T(8,128)(2,1)} %collective-permute-done.10), channel_id=1, source_target_pairs={{0,1},{1,0},{2,3},{3,2},{4,5},{5,4},{6,7},{7,6},{8,9},{9,8},{10,11... | collective-permute-start | bytes 1769480 | tf_op jit(solution)/shard_map/ppermute | solution.py:30
  63.4 1.3 copy-start
  75.9 3.8 %collective-permute-start.14 = (bf16[16,4,128]{2,1,0:T(4,128)(2,1)S(1)}, bf16[16,4,128]{2,1,0:T(4,128)(2,1)S(1)}, u32[]{:S(2)}, u32[]{:S(2)}) collective-permute-start(bf16[16,4,128]{2,1,0:T(4,128)(2,1)S(1)} %get-tuple-element.65), channel_id=1, source_target_pairs={{0,1},{1,2},{2,3},{3,4},{4,5},{5,6},{6,7},{8,9},{9,10},{10,11},{11... | collective-permute-start | bytes 49160 | tf_op jit(solution)/shard_map/ppermute | solution.py:19
  78.2 4.2 %collective-permute-start.15 = (bf16[16,4,128]{2,1,0:T(4,128)(2,1)S(1)}, bf16[16,4,128]{2,1,0:T(4,128)(2,1)S(1)}, u32[]{:S(2)}, u32[]{:S(2)}) collective-permute-start(bf16[16,4,128]{2,1,0:T(4,128)(2,1)S(1)} %get-tuple-element.66), channel_id=1, source_target_pairs={{1,0},{2,1},{3,2},{4,3},{5,4},{6,5},{7,6},{9,8},{10,9},{11,10},{12... | collective-permute-start | bytes 49160 | tf_op jit(solution)/shard_map/ppermute | solution.py:21
  91.6 6.0 %copy-start.2 = (bf16[1,128,2048]{2,1,0:T(8,128)(2,1)S(1)}, bf16[1,128,2048]{2,1,0:T(8,128)(2,1)}, u32[]{:S(2)}) copy-start(bf16[1,128,2048]{2,1,0:T(8,128)(2,1)} %param.15) | copy-start | bytes 1572868
  91.9 21.1 %all-to-all-start.1 = ((bf16[16,128,128]{2,1,0:T(8,128)(2,1)}), bf16[16,128,128]{2,1,0:T(8,128)(2,1)S(1)}, u32[]{:S(2)}, u32[]{:S(2)}) async-start(bf16[16,128,128]{2,1,0:T(8,128)(2,1)} %shard_map.98), calls=%async_computation.1 | async-start | bytes 1048576 | tf_op jit(solution)/shard_map/all_to_all | solution.py:267
  113.0 30.6 %all-to-all-start = ((bf16[32,130,64]{1,2,0:T(8,128)(2,1)}), bf16[32,130,64]{1,2,0:T(8,128)(2,1)S(1)}, u32[]{:S(2)}, u32[]{:S(2)}) async-start(bf16[32,130,64]{1,2,0:T(8,128)(2,1)} %pad_maximum_fusion.5), calls=%async_computation | async-start | bytes 2097152 | tf_op jit(solution)/shard_map/all_to_all | solution.py:155
  120.4 24.7 %collective-permute-start.16 = (f32[64,1152]{1,0:T(8,128)}, f32[64,1152]{1,0:T(8,128)}, u32[]{:S(2)}, u32[]{:S(2)}) collective-permute-start(f32[64,1152]{1,0:T(8,128)} %get-tuple-element.52), channel_id=1, source_target_pairs={{0,8},{8,0},{16,24},{24,16},{1,9},{9,1},{17,25},{25,17},{2,10},{10... | collective-permute-start | bytes 884744 | tf_op jit(solution)/shard_map/ppermute | solution.py:180
  121.9 23.2 %collective-permute-start.17 = (f32[64,1152]{1,0:T(8,128)S(1)}, f32[64,1152]{1,0:T(8,128)}, u32[]{:S(2)}, u32[]{:S(2)}) collective-permute-start(f32[64,1152]{1,0:T(8,128)S(1)} %get-tuple-element.54), channel_id=1, source_target_pairs={{0,16},{8,24},{16,0},{24,8},{1,17},{9,25},{17,1},{25,9},{2,18},{10... | collective-permute-start | bytes 884744 | tf_op jit(solution)/shard_map/ppermute | solution.py:180
  123.4 21.8 %collective-permute-start.18 = (f32[64,1152]{1,0:T(8,128)S(1)}, f32[64,1152]{1,0:T(8,128)}, u32[]{:S(2)}, u32[]{:S(2)}) collective-permute-start(f32[64,1152]{1,0:T(8,128)S(1)} %get-tuple-element.53), channel_id=1, source_target_pairs={{0,24},{8,16},{16,8},{24,0},{1,25},{9,17},{17,9},{25,1},{2,26},{10... | collective-permute-start | bytes 884744 | tf_op jit(solution)/shard_map/ppermute | solution.py:180
  147.1 10.3 %all-to-all-start.3 = ((f32[32,1,576]{2,1,0:T(1,128)}), f32[32,1,576]{2,1,0:T(1,128)S(1)}, u32[]{:S(2)}, u32[]{:S(2)}) async-start(f32[32,1,576]{2,1,0:T(1,128)} %reshape.118), calls=%async_computation.3 | async-start | bytes 163840 | tf_op jit(solution)/shard_map/all_to_all | solution.py:166
  149.7 10.6 %collective-permute-start.19 = (f32[64,1152]{1,0:T(8,128)S(1)}, f32[64,1152]{1,0:T(8,128)S(1)}, u32[]{:S(2)}, u32[]{:S(2)}) collective-permute-start(f32[64,1152]{1,0:T(8,128)S(1)} %add_add_fusion), channel_id=1, source_target_pairs={{0,8},{8,0},{16,24},{24,16},{1,9},{9,1},{17,25},{25,17},{2,10},{10... | collective-permute-start | bytes 884744 | tf_op jit(solution)/shard_map/ppermute | solution.py:190
  151.5 15.8 %collective-permute-start.20 = (f32[64,1152]{1,0:T(8,128)S(1)}, f32[64,1152]{1,0:T(8,128)S(1)}, u32[]{:S(2)}, u32[]{:S(2)}) collective-permute-start(f32[64,1152]{1,0:T(8,128)S(1)} %add_add_fusion), channel_id=1, source_target_pairs={{0,16},{8,24},{16,0},{24,8},{1,17},{9,25},{17,1},{25,9},{2,18},{10... | collective-permute-start | bytes 884744 | tf_op jit(solution)/shard_map/ppermute | solution.py:190
  153.0 14.3 %collective-permute-start.21 = (f32[64,1152]{1,0:T(8,128)S(1)}, f32[64,1152]{1,0:T(8,128)S(1)}, u32[]{:S(2)}, u32[]{:S(2)}) collective-permute-start(f32[64,1152]{1,0:T(8,128)S(1)} %add_add_fusion), channel_id=1, source_target_pairs={{0,24},{8,16},{16,8},{24,0},{1,25},{9,17},{17,9},{25,1},{2,26},{10... | collective-permute-start | bytes 884744 | tf_op jit(solution)/shard_map/ppermute | solution.py:190

commit v14 on v13

--- a/solution.py
+++ b/solution.py
@@ -248,7 +248,6 @@
     mixed = events[0].astype(jnp.float32) + jnp.dot(onehot, table, preferred_element_type=jnp.float32)
     near = {apart: piece for apart, piece in kernel_fetched.items() if apart != far}
     near_swapped = swap_halves(near)
-    near, near_swapped, mixed = lax.optimization_barrier((near, near_swapped, mixed))
     inv = lax.rsqrt(jnp.mean(mixed * mixed, axis=-1, keepdims=True) + 1e-06)
     normed = (mixed * inv * norm_gain).astype(jnp.bfloat16)
     normed_g = normed.reshape(length, GROUPS, chans).transpose(1, 0, 2)

time: 170 us -> 142 us (0.84)
  waiting for transfers between devices: 72.6 us -> 41.5 us
  starting transfers between devices: 42 us -> 44 us
    ppermute x6, waiting for transfers between devices: 27.5 us -> 5.64 us  [fetch_halves(): lax.ppermute(mine, axis, [(source, source ^ apart) for source in range(co...]
    all_to_all x1, waiting for transfers between devices: 9.84 us -> 2.78 us  [body(): group_out = lax.all_to_all(dconv, 'seq', 0, 1, tiled=True)]
    all_to_all x1, starting transfers between devices: 7.14 us -> 3.49 us  [body(): group_in = lax.all_to_all(normed_g, 'seq', 0, 1, tiled=True)]
    ppermute x6, starting transfers between devices: 1.13 us -> 3.99 us  [from_partner(): return lax.ppermute(value, axis, pairs)]
    select_n x5 -> x6, other arithmetic: 1.53 us -> 3.88 us  [assemble_shards(): lower = jnp.where(core == 0, fetched[apart], swapped[apart])]
    unnamed x29 -> x23, local copies, waits for them, and re-layouts: 4.01 us -> 4.98 us
  transfers between devices with their start and end apart: 26 -> 26, of which waited for: 13 -> 11; matrix products, arithmetic and copies ran while one was open for 20% -> 24% of each run, Pallas kernels for 7% -> 8%
where the time goes in v14:
time: 142 us; the launch traced here: 141 us
  starting transfers between devices  44 us (31%)
  waiting for transfers between devices  41.5 us (29%)
  local copies, waits for them, and re-layouts  20.5 us (14%)
  other arithmetic  17.3 us (12%)
  Pallas kernels  11.7 us (8%)
  matrix products  4.46 us (3%)
    all_to_all x1, waiting for transfers between devices, table_and_gain(): got = lax.all_to_all(send, every, 0, 0, tiled=True)  18.7 us
    ppermute x6, starting transfers between devices, fetch_halves(): lax.ppermute(mine, axis, [(source, source ^ apart) for source in range(co...  8.79 us
    all_to_all x1, starting transfers between devices, body(): group_out = lax.all_to_all(dconv, 'seq', 0, 1, tiled=True)  7.4 us
    ppermute x3, waiting for transfers between devices, gather_by_permutes(): pieces.append(lax.ppermute(total, axis, pairs))  7.14 us
    pallas_call x1, Pallas kernels, conv_dconv(): pl.pallas_call(forward_kernel, grid=(groups // step,), in_specs=[pl.Block...  6.56 us
    ppermute x6, waiting for transfers between devices, fetch_halves(): lax.ppermute(mine, axis, [(source, source ^ apart) for source in range(co...  5.64 us
    pallas_call x1, Pallas kernels, conv_transpose(): pl.pallas_call(backward_kernel, grid=(groups // step,), in_specs=[pl.Bloc...  5.16 us
    unnamed x23, local copies, waits for them, and re-layouts  4.98 us
  transfers between devices with their start and end apart: 26, of which 11 were waited for; matrix products, arithmetic and copies ran while one was open for 24% of the time, Pallas kernels for 8%

profile of v14, /device:TPU:0, one launch (start us, length us, event | category | flops | bytes accessed | tf_op | source)
XLA Modules:
  0.0 140.6 jit_solution(4677801428427945703)
XLA Ops:
  0.6 0.9 constant_dynamic-slice_fusion.4
  1.6 3.0 %collective-permute-start = (bf16[32,2048]{1,0:T(8,128)(2,1)S(1)}, bf16[32,2048]{1,0:T(8,128)(2,1)S(1)}, u32[]{:S(2)}, u32[]{:S(2)}) collective-permute-start(bf16[32,2048]{1,0:T(8,128)(2,1)S(1)} %constant_dynamic-slice_fusion.4), channel_id=1, source_target_pairs={{0,8},{8,0},{16,24},{24,16},{1,9},{9,1},{17,25},{25,17},{2,10},{10... | collective-permute-start | bytes 393224 | tf_op jit(solution)/shard_map/ppermute | solution.py:203
  4.6 1.5 %collective-permute-start.2 = (bf16[32,2048]{1,0:T(8,128)(2,1)S(1)}, bf16[32,2048]{1,0:T(8,128)(2,1)S(1)}, u32[]{:S(2)}, u32[]{:S(2)}) collective-permute-start(bf16[32,2048]{1,0:T(8,128)(2,1)S(1)} %constant_dynamic-slice_fusion.4), channel_id=1, source_target_pairs={{0,16},{8,24},{16,0},{24,8},{1,17},{9,25},{17,1},{25,9},{2,18},{10... | collective-permute-start | bytes 393224 | tf_op jit(solution)/shard_map/ppermute | solution.py:203
  6.1 2.4 %collective-permute-done = bf16[32,2048]{1,0:T(8,128)(2,1)S(1)} collective-permute-done((bf16[32,2048]{1,0:T(8,128)(2,1)S(1)}, bf16[32,2048]{1,0:T(8,128)(2,1)S(1)}, u32[]{:S(2)}, u32[]{:S(2)}) %collective-permute-start) | collective-permute-done | bytes 131104 | tf_op jit(solution)/shard_map/ppermute | solution.py:203
  8.5 1.9 %constant_dynamic-slice_fusion.3 = bf16[256,1152]{1,0:T(8,128)(2,1)} fusion(bf16[512,1152]{1,0:T(8,128)(2,1)} %param.14, s32[]{:T(128)S(6)} %select_n.123), kind=kLoop, calls=%fused_computation.94 | loop fusion | bytes 1179652 | tf_op jit(solution)/shard_map/dynamic_slice | solution.py:201
  10.4 3.4 %collective-permute-start.6 = (bf16[256,1152]{1,0:T(8,128)(2,1)}, bf16[256,1152]{1,0:T(8,128)(2,1)}, u32[]{:S(2)}, u32[]{:S(2)}) collective-permute-start(bf16[256,1152]{1,0:T(8,128)(2,1)} %constant_dynamic-slice_fusion.3), channel_id=1, source_target_pairs={{0,24},{8,16},{16,8},{24,0},{1,25},{9,17},{17,9},{25,1},{2,26},{10... | collective-permute-start | bytes 1769480 | tf_op jit(solution)/shard_map/ppermute | solution.py:203
  14.4 1.0 collective-permute-done.5
  15.6 0.8 copy-done.6
  16.7 0.9 copy-done.8
  17.6 0.4 multiply_reduce_fusion.2
  18.8 1.0 copy.64
  19.8 0.8 fusion.40
  20.6 2.2 %collective-permute-start.7 = (bf16[16,4,128]{2,1,0:T(4,128)(2,1)S(1)}, bf16[16,4,128]{2,1,0:T(4,128)(2,1)S(1)}, u32[]{:S(2)}, u32[]{:S(2)}) collective-permute-start(bf16[16,4,128]{2,1,0:T(4,128)(2,1)S(1)} %get-tuple-element.57), channel_id=1, source_target_pairs={{0,1},{1,2},{2,3},{3,4},{4,5},{5,6},{6,7},{8,9},{9,10},{10,11},{11... | collective-permute-start | bytes 49160 | tf_op jit(solution)/shard_map/ppermute | solution.py:19
  22.8 1.3 collective-permute-start.8
  24.1 0.7 collective-permute-start.11
  24.9 1.9 %collective-permute-done.8 = bf16[16,4,128]{2,1,0:T(4,128)(2,1)S(1)} collective-permute-done((bf16[16,4,128]{2,1,0:T(4,128)(2,1)S(1)}, bf16[16,4,128]{2,1,0:T(4,128)(2,1)S(1)}, u32[]{:S(2)}, u32[]{:S(2)}) %collective-permute-start.8) | collective-permute-done | bytes 16416 | tf_op jit(solution)/shard_map/ppermute | solution.py:21
  26.7 1.2 pad_maximum_fusion.6
  28.2 2.7 %collective-permute-start.13 = (bf16[256,1152]{1,0:T(8,128)(2,1)}, bf16[256,1152]{1,0:T(8,128)(2,1)}, u32[]{:S(2)}, u32[]{:S(2)}) collective-permute-start(bf16[256,1152]{1,0:T(8,128)(2,1)} %collective-permute-done.6), channel_id=1, source_target_pairs={{0,1},{1,0},{2,3},{3,2},{4,5},{5,4},{6,7},{7,6},{8,9},{9,8},{10,11... | collective-permute-start | bytes 1769480 | tf_op jit(solution)/shard_map/ppermute | solution.py:30
  31.1 1.3 copy.66
  32.5 3.5 %all-to-all-start.2 = ((bf16[16,128,128]{2,1,0:T(8,128)(2,1)}), bf16[16,128,128]{2,1,0:T(8,128)(2,1)S(1)}, u32[]{:S(2)}, u32[]{:S(2)}) async-start(bf16[16,128,128]{2,1,0:T(8,128)(2,1)} %bitcast.12), calls=%async_computation.2 | async-start | bytes 1048576 | tf_op jit(solution)/shard_map/all_to_all | solution.py:265
  36.0 1.1 convert_element_type.51.pad_ref
  37.0 3.0 %collective-permute-done.9 = bf16[256,1152]{1,0:T(8,128)(2,1)} collective-permute-done((bf16[256,1152]{1,0:T(8,128)(2,1)}, bf16[256,1152]{1,0:T(8,128)(2,1)}, u32[]{:S(2)}, u32[]{:S(2)}) %collective-permute-start.9) | collective-permute-done | bytes 589856 | tf_op jit(solution)/shard_map/ppermute | solution.py:203
  40.1 0.6 collective-permute-start.10
  40.8 1.4 broadcast_select_fusion.1
  42.5 1.2 broadcast_select_fusion.5
  43.7 1.2 broadcast_select_fusion.3
  45.2 1.1 copy-done.1
  46.2 0.7 pad_maximum_fusion
  47.0 0.4 dynamic-slice_bitcast_fusion.3
  47.3 2.8 %pad_maximum_fusion.1 = bf16[2048,1152]{1,0:T(8,128)(2,1)} fusion(bf16[512,1152]{1,0:T(8,128)(2,1)S(1)} %get-tuple-element.35, bf16[512,1152]{1,0:T(8,128)(2,1)S(1)} %get-tuple-element.36, bf16[512,1152]{1,0:T(8,128)(2,1)S(1)} %get-tuple-element.37, bf16[512,1152]{1,0:T(8,128)(2,1)S(1)} %get-tuple-element.34), kind=kLoop, calls=%fused_computation.1 | loop fusion | flops 18874368 | bytes 9437184 | tf_op jit(solution)/shard_map/concatenate | solution.py:222
  50.2 6.6 %shard_map.98 = bf16[16,128,128]{2,1,0:T(8,128)(2,1)} custom-call(f32[16,136,128]{2,1,0:T(8,128)} %convert_element_type.51.pad_ref, bf16[16,128,1152]{2,1,0:T(8,128)(2,1)} %bitcast.94, f32[16,128,128]{2,1,0:T(8,128)} %bitcast.98), custom_call_target="tpu_custom_call" | custom-call | flops 603979776 | bytes 7405568 | tf_op jit(solution)/shard_map/pallas_call | solution.py:74
  56.7 0.8 fusion.39
  57.5 2.3 %collective-permute-start.14 = (bf16[16,4,128]{2,1,0:T(4,128)(2,1)S(1)}, bf16[16,4,128]{2,1,0:T(4,128)(2,1)S(1)}, u32[]{:S(2)}, u32[]{:S(2)}) collective-permute-start(bf16[16,4,128]{2,1,0:T(4,128)(2,1)S(1)} %get-tuple-element.55), channel_id=1, source_target_pairs={{0,1},{1,2},{2,3},{3,4},{4,5},{5,6},{6,7},{8,9},{9,10},{10,11},{11... | collective-permute-start | bytes 49160 | tf_op jit(solution)/shard_map/ppermute | solution.py:19
  59.8 1.3 collective-permute-start.15
  61.4 7.4 %all-to-all-start.1 = ((bf16[16,128,128]{2,1,0:T(8,128)(2,1)}), bf16[16,128,128]{2,1,0:T(8,128)(2,1)}, u32[]{:S(2)}, u32[]{:S(2)}) async-start(bf16[16,128,128]{2,1,0:T(8,128)(2,1)} %shard_map.98), calls=%async_computation.1 | async-start | bytes 1048576 | tf_op jit(solution)/shard_map/all_to_all | solution.py:266
  69.1 1.0 all_to_all.40
  70.1 1.1 maximum_convert_fusion.pad_ref
  71.2 5.2 %shard_map.99 = f32[16,128,128]{2,1,0:T(8,128)} custom-call(f32[16,136,128]{2,1,0:T(8,128)} %maximum_convert_fusion.pad_ref, bf16[16,128,1152]{2,1,0:T(8,128)(2,1)} %bitcast.95), custom_call_target="tpu_custom_call" | custom-call | flops 603979776 | bytes 6881280 | tf_op jit(solution)/shard_map/pallas_call | solution.py:96
  76.4 1.6 %copy.67 = f32[128,16,128]{0,2,1:T(8,128)S(1)} copy(f32[128,16,128]{2,0,1:T(8,128)} %bitcast.101) | data formatting | bytes 2097152 | tf_op jit(solution)/shard_map/transpose | solution.py:277
  78.6 0.7 copy-done.3
  79.3 0.4 fusion.10
  80.2 1.2 pad_maximum_fusion.5
  81.4 2.8 %all-to-all-done.1 = bf16[16,128,128]{2,1,0:T(8,128)(2,1)} async-done(((bf16[16,128,128]{2,1,0:T(8,128)(2,1)}), bf16[16,128,128]{2,1,0:T(8,128)(2,1)}, u32[]{:S(2)}, u32[]{:S(2)}) %all-to-all-start.1) | async-done | bytes 524320 | tf_op jit(solution)/shard_map/all_to_all | solution.py:266
  84.2 3.2 %all-to-all-start = ((bf16[32,130,64]{1,2,0:T(8,128)(2,1)}), bf16[32,130,64]{1,2,0:T(8,128)(2,1)S(1)}, u32[]{:S(2)}, u32[]{:S(2)}) async-start(bf16[32,130,64]{1,2,0:T(8,128)(2,1)} %pad_maximum_fusion.5), calls=%async_computation | async-start | bytes 2097152 | tf_op jit(solution)/shard_map/all_to_all | solution.py:155
  87.4 1.1 copy.77
  89.2 0.4 convolution_dynamic-update-slice_fusion.6
  92.2 0.8 constant_dynamic-slice_fusion.2
  93.0 1.6 %collective-permute-start.16 = (f32[64,1152]{1,0:T(8,128)}, f32[64,1152]{1,0:T(8,128)}, u32[]{:S(2)}, u32[]{:S(2)}) collective-permute-start(f32[64,1152]{1,0:T(8,128)} %get-tuple-element.42), channel_id=1, source_target_pairs={{0,8},{8,0},{16,24},{24,16},{1,9},{9,1},{17,25},{25,17},{2,10},{10... | collective-permute-start | bytes 884744 | tf_op jit(solution)/shard_map/ppermute | solution.py:180
  94.6 1.5 %collective-permute-start.17 = (f32[64,1152]{1,0:T(8,128)S(1)}, f32[64,1152]{1,0:T(8,128)}, u32[]{:S(2)}, u32[]{:S(2)}) collective-permute-start(f32[64,1152]{1,0:T(8,128)S(1)} %get-tuple-element.44), channel_id=1, source_target_pairs={{0,16},{8,24},{16,0},{24,8},{1,17},{9,25},{17,1},{25,9},{2,18},{10... | collective-permute-start | bytes 884744 | tf_op jit(solution)/shard_map/ppermute | solution.py:180
  96.0 0.4 collective-permute-start.18
  96.5 18.7 %all-to-all-done = bf16[32,130,64]{1,2,0:T(8,128)(2,1)S(1)} async-done(((bf16[32,130,64]{1,2,0:T(8,128)(2,1)}), bf16[32,130,64]{1,2,0:T(8,128)(2,1)S(1)}, u32[]{:S(2)}, u32[]{:S(2)}) %all-to-all-start) | async-done | bytes 532512 | tf_op jit(solution)/shard_map/all_to_all | solution.py:155
  115.6 0.9 fusion.2
  116.7 1.2 add_add_fusion
  117.9 0.8 reshape.118
  118.7 3.0 %all-to-all-start.3 = ((f32[32,1,576]{2,1,0:T(1,128)}), f32[32,1,576]{2,1,0:T(1,128)S(1)}, u32[]{:S(2)}, u32[]{:S(2)}) async-start(f32[32,1,576]{2,1,0:T(1,128)} %reshape.118), calls=%async_computation.3 | async-start | bytes 163840 | tf_op jit(solution)/shard_map/all_to_all | solution.py:166
  121.7 1.8 %collective-permute-start.19 = (f32[64,1152]{1,0:T(8,128)S(1)}, f32[64,1152]{1,0:T(8,128)S(1)}, u32[]{:S(2)}, u32[]{:S(2)}) collective-permute-start(f32[64,1152]{1,0:T(8,128)S(1)} %add_add_fusion), channel_id=1, source_target_pairs={{0,8},{8,0},{16,24},{24,16},{1,9},{9,1},{17,25},{25,17},{2,10},{10... | collective-permute-start | bytes 884744 | tf_op jit(solution)/shard_map/ppermute | solution.py:190
  123.5 1.5 %collective-permute-start.20 = (f32[64,1152]{1,0:T(8,128)S(1)}, f32[64,1152]{1,0:T(8,128)S(1)}, u32[]{:S(2)}, u32[]{:S(2)}) collective-permute-start(f32[64,1152]{1,0:T(8,128)S(1)} %add_add_fusion), channel_id=1, source_target_pairs={{0,16},{8,24},{16,0},{24,8},{1,17},{9,25},{17,1},{25,9},{2,18},{10... | collective-permute-start | bytes 884744 | tf_op jit(solution)/shard_map/ppermute | solution.py:190
  125.3 4.1 %all-to-all-done.3 = f32[32,1,576]{2,1,0:T(1,128)S(1)} async-done(((f32[32,1,576]{2,1,0:T(1,128)}), f32[32,1,576]{2,1,0:T(1,128)S(1)}, u32[]{:S(2)}, u32[]{:S(2)}) %all-to-all-start.3) | async-done | bytes 73760 | tf_op jit(solution)/shard_map/all_to_all | solution.py:166
  129.4 0.5 broadcast.56
  129.9 0.8 reduce.7
  130.9 0.7 reshape.106
  131.6 0.6 slice_reduce_fusion
  132.3 7.0 %collective-permute-done.20 = f32[64,1152]{1,0:T(8,128)S(1)} collective-permute-done((f32[64,1152]{1,0:T(8,128)S(1)}, f32[64,1152]{1,0:T(8,128)S(1)}, u32[]{:S(2)}, u32[]{:S(2)}) %collective-permute-start.20) | collective-permute-done | bytes 294944 | tf_op jit(solution)/shard_map/ppermute | solution.py:190
  139.5 1.1 pad_maximum_fusion.3
  (87 shorter events, 9.0 us)
Async XLA Ops:
  1.6 6.9 %collective-permute-start = (bf16[32,2048]{1,0:T(8,128)(2,1)S(1)}, bf16[32,2048]{1,0:T(8,128)(2,1)S(1)}, u32[]{:S(2)}, u32[]{:S(2)}) collective-permute-start(bf16[32,2048]{1,0:T(8,128)(2,1)S(1)} %constant_dynamic-slice_fusion.4), channel_id=1, source_target_pairs={{0,8},{8,0},{16,24},{24,16},{1,9},{9,1},{17,25},{25,17},{2,10},{10... | collective-permute-start | bytes 393224 | tf_op jit(solution)/shard_map/ppermute | solution.py:203
  4.6 9.3 %collective-permute-start.2 = (bf16[32,2048]{1,0:T(8,128)(2,1)S(1)}, bf16[32,2048]{1,0:T(8,128)(2,1)S(1)}, u32[]{:S(2)}, u32[]{:S(2)}) collective-permute-start(bf16[32,2048]{1,0:T(8,128)(2,1)S(1)} %constant_dynamic-slice_fusion.4), channel_id=1, source_target_pairs={{0,16},{8,24},{16,0},{24,8},{1,17},{9,25},{17,1},{25,9},{2,18},{10... | collective-permute-start | bytes 393224 | tf_op jit(solution)/shard_map/ppermute | solution.py:203
  6.1 8.0 %collective-permute-start.4 = (bf16[32,2048]{1,0:T(8,128)(2,1)S(1)}, bf16[32,2048]{1,0:T(8,128)(2,1)S(1)}, u32[]{:S(2)}, u32[]{:S(2)}) collective-permute-start(bf16[32,2048]{1,0:T(8,128)(2,1)S(1)} %constant_dynamic-slice_fusion.4), channel_id=1, source_target_pairs={{0,24},{8,16},{16,8},{24,0},{1,25},{9,17},{17,9},{25,1},{2,26},{10... | collective-permute-start | bytes 393224 | tf_op jit(solution)/shard_map/ppermute | solution.py:203
  8.5 5.9 %collective-permute-start.1 = (bf16[32,2048]{1,0:T(8,128)(2,1)S(1)}, bf16[32,2048]{1,0:T(8,128)(2,1)S(1)}, u32[]{:S(2)}, u32[]{:S(2)}) collective-permute-start(bf16[32,2048]{1,0:T(8,128)(2,1)S(1)} %collective-permute-done), channel_id=1, source_target_pairs={{0,1},{1,0},{2,3},{3,2},{4,5},{5,4},{6,7},{7,6},{8,9},{9,8},{10,11... | collective-permute-start | bytes 393224 | tf_op jit(solution)/shard_map/ppermute | solution.py:30
  10.4 17.8 %collective-permute-start.6 = (bf16[256,1152]{1,0:T(8,128)(2,1)}, bf16[256,1152]{1,0:T(8,128)(2,1)}, u32[]{:S(2)}, u32[]{:S(2)}) collective-permute-start(bf16[256,1152]{1,0:T(8,128)(2,1)} %constant_dynamic-slice_fusion.3), channel_id=1, source_target_pairs={{0,24},{8,16},{16,8},{24,0},{1,25},{9,17},{17,9},{25,1},{2,26},{10... | collective-permute-start | bytes 1769480 | tf_op jit(solution)/shard_map/ppermute | solution.py:203
  13.9 1.7 %collective-permute-start.3 = (bf16[32,2048]{1,0:T(8,128)(2,1)S(1)}, bf16[32,2048]{1,0:T(8,128)(2,1)S(1)}, u32[]{:S(2)}, u32[]{:S(2)}) collective-permute-start(bf16[32,2048]{1,0:T(8,128)(2,1)S(1)} %collective-permute-done.2), channel_id=1, source_target_pairs={{0,1},{1,0},{2,3},{3,2},{4,5},{5,4},{6,7},{7,6},{8,9},{9,8},{10,11... | collective-permute-start | bytes 393224 | tf_op jit(solution)/shard_map/ppermute | solution.py:30
  14.1 1.3 collective-permute-start.5
  15.5 1.0 copy-start.6
  16.6 1.0 copy-start.8
  16.6 1.0 copy-start.9
  17.6 0.7 copy-start.7
  18.7 12.2 %copy-start.2 = (bf16[1,128,2048]{2,1,0:T(8,128)(2,1)S(1)}, bf16[1,128,2048]{2,1,0:T(8,128)(2,1)}, u32[]{:S(2)}) copy-start(bf16[1,128,2048]{2,1,0:T(8,128)(2,1)} %param.15) | copy-start | bytes 1572868
  20.6 4.3 %collective-permute-start.7 = (bf16[16,4,128]{2,1,0:T(4,128)(2,1)S(1)}, bf16[16,4,128]{2,1,0:T(4,128)(2,1)S(1)}, u32[]{:S(2)}, u32[]{:S(2)}) collective-permute-start(bf16[16,4,128]{2,1,0:T(4,128)(2,1)S(1)} %get-tuple-element.57), channel_id=1, source_target_pairs={{0,1},{1,2},{2,3},{3,4},{4,5},{5,6},{6,7},{8,9},{9,10},{10,11},{11... | collective-permute-start | bytes 49160 | tf_op jit(solution)/shard_map/ppermute | solution.py:19
  22.8 4.0 %collective-permute-start.8 = (bf16[16,4,128]{2,1,0:T(4,128)(2,1)S(1)}, bf16[16,4,128]{2,1,0:T(4,128)(2,1)S(1)}, u32[]{:S(2)}, u32[]{:S(2)}) collective-permute-start(bf16[16,4,128]{2,1,0:T(4,128)(2,1)S(1)} %get-tuple-element.58), channel_id=1, source_target_pairs={{1,0},{2,1},{3,2},{4,3},{5,4},{6,5},{7,6},{9,8},{10,9},{11,10},{12... | collective-permute-start | bytes 49160 | tf_op jit(solution)/shard_map/ppermute | solution.py:21
  24.1 16.0 %collective-permute-start.9 = (bf16[256,1152]{1,0:T(8,128)(2,1)}, bf16[256,1152]{1,0:T(8,128)(2,1)}, u32[]{:S(2)}, u32[]{:S(2)}) collective-permute-start(bf16[256,1152]{1,0:T(8,128)(2,1)} %constant_dynamic-slice_fusion.3), channel_id=1, source_target_pairs={{0,8},{8,0},{16,24},{24,16},{1,9},{9,1},{17,25},{25,17},{2,10},{10... | collective-permute-start | bytes 1769480 | tf_op jit(solution)/shard_map/ppermute | solution.py:203
  24.1 16.5 %collective-permute-start.11 = (bf16[256,1152]{1,0:T(8,128)(2,1)}, bf16[256,1152]{1,0:T(8,128)(2,1)}, u32[]{:S(2)}, u32[]{:S(2)}) collective-permute-start(bf16[256,1152]{1,0:T(8,128)(2,1)} %constant_dynamic-slice_fusion.3), channel_id=1, source_target_pairs={{0,16},{8,24},{16,0},{24,8},{1,17},{9,25},{17,1},{25,9},{2,18},{10... | collective-permute-start | bytes 1769480 | tf_op jit(solution)/shard_map/ppermute | solution.py:203
  28.2 12.6 %collective-permute-start.13 = (bf16[256,1152]{1,0:T(8,128)(2,1)}, bf16[256,1152]{1,0:T(8,128)(2,1)}, u32[]{:S(2)}, u32[]{:S(2)}) collective-permute-start(bf16[256,1152]{1,0:T(8,128)(2,1)} %collective-permute-done.6), channel_id=1, source_target_pairs={{0,1},{1,0},{2,3},{3,2},{4,5},{5,4},{6,7},{7,6},{8,9},{9,8},{10,11... | collective-permute-start | bytes 1769480 | tf_op jit(solution)/shard_map/ppermute | solution.py:30
  32.5 28.9 %all-to-all-start.2 = ((bf16[16,128,128]{2,1,0:T(8,128)(2,1)}), bf16[16,128,128]{2,1,0:T(8,128)(2,1)S(1)}, u32[]{:S(2)}, u32[]{:S(2)}) async-start(bf16[16,128,128]{2,1,0:T(8,128)(2,1)} %bitcast.12), calls=%async_computation.2 | async-start | bytes 1048576 | tf_op jit(solution)/shard_map/all_to_all | solution.py:265
  40.1 2.4 %collective-permute-start.10 = (bf16[256,1152]{1,0:T(8,128)(2,1)}, bf16[256,1152]{1,0:T(8,128)(2,1)S(1)}, u32[]{:S(2)}, u32[]{:S(2)}) collective-permute-start(bf16[256,1152]{1,0:T(8,128)(2,1)} %collective-permute-done.9), channel_id=1, source_target_pairs={{0,1},{1,0},{2,3},{3,2},{4,5},{5,4},{6,7},{7,6},{8,9},{9,8},{10,11... | collective-permute-start | bytes 1769480 | tf_op jit(solution)/shard_map/ppermute | solution.py:30
  40.7 3.1 %collective-permute-start.12 = (bf16[256,1152]{1,0:T(8,128)(2,1)}, bf16[256,1152]{1,0:T(8,128)(2,1)S(1)}, u32[]{:S(2)}, u32[]{:S(2)}) collective-permute-start(bf16[256,1152]{1,0:T(8,128)(2,1)} %collective-permute-done.11), channel_id=1, source_target_pairs={{0,1},{1,0},{2,3},{3,2},{4,5},{5,4},{6,7},{7,6},{8,9},{9,8},{10,11... | collective-permute-start | bytes 1769480 | tf_op jit(solution)/shard_map/ppermute | solution.py:30
  45.0 1.3 copy-start.1
  57.5 12.6 %collective-permute-start.14 = (bf16[16,4,128]{2,1,0:T(4,128)(2,1)S(1)}, bf16[16,4,128]{2,1,0:T(4,128)(2,1)S(1)}, u32[]{:S(2)}, u32[]{:S(2)}) collective-permute-start(bf16[16,4,128]{2,1,0:T(4,128)(2,1)S(1)} %get-tuple-element.55), channel_id=1, source_target_pairs={{0,1},{1,2},{2,3},{3,4},{4,5},{5,6},{6,7},{8,9},{9,10},{10,11},{11... | collective-permute-start | bytes 49160 | tf_op jit(solution)/shard_map/ppermute | solution.py:19
  59.8 10.3 %collective-permute-start.15 = (bf16[16,4,128]{2,1,0:T(4,128)(2,1)S(1)}, bf16[16,4,128]{2,1,0:T(4,128)(2,1)S(1)}, u32[]{:S(2)}, u32[]{:S(2)}) collective-permute-start(bf16[16,4,128]{2,1,0:T(4,128)(2,1)S(1)} %get-tuple-element.56), channel_id=1, source_target_pairs={{1,0},{2,1},{3,2},{4,3},{5,4},{6,5},{7,6},{9,8},{10,9},{11,10},{12... | collective-permute-start | bytes 49160 | tf_op jit(solution)/shard_map/ppermute | solution.py:21
  61.4 22.9 %all-to-all-start.1 = ((bf16[16,128,128]{2,1,0:T(8,128)(2,1)}), bf16[16,128,128]{2,1,0:T(8,128)(2,1)}, u32[]{:S(2)}, u32[]{:S(2)}) async-start(bf16[16,128,128]{2,1,0:T(8,128)(2,1)} %shard_map.98), calls=%async_computation.1 | async-start | bytes 1048576 | tf_op jit(solution)/shard_map/all_to_all | solution.py:266
  68.8 1.3 copy-start
  78.3 1.0 copy-start.3
  79.7 1.7 %copy-start.5 = (bf16[128,2048]{1,0:T(8,128)(2,1)}, bf16[128,2048]{1,0:T(8,128)(2,1)S(1)}, u32[]{:S(2)}) copy-start(bf16[128,2048]{1,0:T(8,128)(2,1)S(1)} %fusion.10) | copy-start | bytes 1572868
  81.4 7.0 %copy-start.4 = (bf16[2,1024,128]{1,2,0:T(8,128)(2,1)S(1)}, bf16[2,1024,128]{1,2,0:T(8,128)(2,1)}, u32[]{:S(2)}) copy-start(bf16[2,1024,128]{1,2,0:T(8,128)(2,1)} %all_to_all.40) | copy-start | bytes 1572868
  84.2 30.9 %all-to-all-start = ((bf16[32,130,64]{1,2,0:T(8,128)(2,1)}), bf16[32,130,64]{1,2,0:T(8,128)(2,1)S(1)}, u32[]{:S(2)}, u32[]{:S(2)}) async-start(bf16[32,130,64]{1,2,0:T(8,128)(2,1)} %pad_maximum_fusion.5), calls=%async_computation | async-start | bytes 2097152 | tf_op jit(solution)/shard_map/all_to_all | solution.py:155
  93.0 23.7 %collective-permute-start.16 = (f32[64,1152]{1,0:T(8,128)}, f32[64,1152]{1,0:T(8,128)}, u32[]{:S(2)}, u32[]{:S(2)}) collective-permute-start(f32[64,1152]{1,0:T(8,128)} %get-tuple-element.42), channel_id=1, source_target_pairs={{0,8},{8,0},{16,24},{24,16},{1,9},{9,1},{17,25},{25,17},{2,10},{10... | collective-permute-start | bytes 884744 | tf_op jit(solution)/shard_map/ppermute | solution.py:180
  94.6 22.1 %collective-permute-start.17 = (f32[64,1152]{1,0:T(8,128)S(1)}, f32[64,1152]{1,0:T(8,128)}, u32[]{:S(2)}, u32[]{:S(2)}) collective-permute-start(f32[64,1152]{1,0:T(8,128)S(1)} %get-tuple-element.44), channel_id=1, source_target_pairs={{0,16},{8,24},{16,0},{24,8},{1,17},{9,25},{17,1},{25,9},{2,18},{10... | collective-permute-start | bytes 884744 | tf_op jit(solution)/shard_map/ppermute | solution.py:180
  96.0 20.6 %collective-permute-start.18 = (f32[64,1152]{1,0:T(8,128)S(1)}, f32[64,1152]{1,0:T(8,128)}, u32[]{:S(2)}, u32[]{:S(2)}) collective-permute-start(f32[64,1152]{1,0:T(8,128)S(1)} %get-tuple-element.43), channel_id=1, source_target_pairs={{0,24},{8,16},{16,8},{24,0},{1,25},{9,17},{17,9},{25,1},{2,26},{10... | collective-permute-start | bytes 884744 | tf_op jit(solution)/shard_map/ppermute | solution.py:180
  118.7 10.7 %all-to-all-start.3 = ((f32[32,1,576]{2,1,0:T(1,128)}), f32[32,1,576]{2,1,0:T(1,128)S(1)}, u32[]{:S(2)}, u32[]{:S(2)}) async-start(f32[32,1,576]{2,1,0:T(1,128)} %reshape.118), calls=%async_computation.3 | async-start | bytes 163840 | tf_op jit(solution)/shard_map/all_to_all | solution.py:166
  121.7 10.6 %collective-permute-start.19 = (f32[64,1152]{1,0:T(8,128)S(1)}, f32[64,1152]{1,0:T(8,128)S(1)}, u32[]{:S(2)}, u32[]{:S(2)}) collective-permute-start(f32[64,1152]{1,0:T(8,128)S(1)} %add_add_fusion), channel_id=1, source_target_pairs={{0,8},{8,0},{16,24},{24,16},{1,9},{9,1},{17,25},{25,17},{2,10},{10... | collective-permute-start | bytes 884744 | tf_op jit(solution)/shard_map/ppermute | solution.py:190
  123.5 15.8 %collective-permute-start.20 = (f32[64,1152]{1,0:T(8,128)S(1)}, f32[64,1152]{1,0:T(8,128)S(1)}, u32[]{:S(2)}, u32[]{:S(2)}) collective-permute-start(f32[64,1152]{1,0:T(8,128)S(1)} %add_add_fusion), channel_id=1, source_target_pairs={{0,16},{8,24},{16,0},{24,8},{1,17},{9,25},{17,1},{25,9},{2,18},{10... | collective-permute-start | bytes 884744 | tf_op jit(solution)/shard_map/ppermute | solution.py:190
  125.0 14.3 %collective-permute-start.21 = (f32[64,1152]{1,0:T(8,128)S(1)}, f32[64,1152]{1,0:T(8,128)S(1)}, u32[]{:S(2)}, u32[]{:S(2)}) collective-permute-start(f32[64,1152]{1,0:T(8,128)S(1)} %add_add_fusion), channel_id=1, source_target_pairs={{0,24},{8,16},{16,8},{24,0},{1,25},{9,17},{17,9},{25,1},{2,26},{10... | collective-permute-start | bytes 884744 | tf_op jit(solution)/shard_map/ppermute | solution.py:190

commit v15 on v14

--- a/solution.py
+++ b/solution.py
@@ -40,14 +40,11 @@
 
 def forward_kernel(pad_ref, w_ref, up_ref, out_ref):
     length = out_ref.shape[1]
-    chans = pad_ref.shape[2]
     for g in range(out_ref.shape[0]):
-        acc = None
-        for k in range(KERNEL):
-            x = pad_ref[g, k : k + length, :].astype(jnp.bfloat16)
-            w = w_ref[g, :, k * chans : (k + 1) * chans]
-            term = lax.dot_general(x, w, (((1,), (1,)), ((), ())), preferred_element_type=jnp.float32)
-            acc = term if acc is None else acc + term
+        x = jnp.concatenate(
+            [pad_ref[g, k : k + length, :].astype(jnp.bfloat16) for k in range(KERNEL)], axis=1
+        )
+        acc = lax.dot_general(x, w_ref[g], (((1,), (1,)), ((), ())), preferred_element_type=jnp.float32)
         sig = 1.0 / (1.0 + jnp.exp(-acc))
         out_ref[g] = (up_ref[g] * sig * (1.0 + acc * (1.0 - sig))).astype(out_ref.dtype)
 
@@ -57,13 +54,11 @@
     chans = out_ref.shape[2]
     half = KERNEL // 2
     for g in range(out_ref.shape[0]):
-        acc = None
-        for k in range(KERNEL):
-            x = pad_ref[g, 2 * half - k : 2 * half - k + length, :].astype(jnp.bfloat16)
-            w = w_ref[g, :, k * chans : (k + 1) * chans]
-            term = jnp.dot(x, w, preferred_element_type=jnp.float32)
-            acc = term if acc is None else acc + term
-        out_ref[g] = acc
+        x = jnp.concatenate(
+            [pad_ref[g, 2 * half - k : 2 * half - k + length, :].astype(jnp.bfloat16) for k in range(KERNEL)], axis=1
+        )
+        w = jnp.concatenate([w_ref[g, :, k * chans : (k + 1) * chans] for k in range(KERNEL)], axis=0)
+        out_ref[g] = jnp.dot(x, w, preferred_element_type=jnp.float32)
 
 
 def conv_dconv(padded, weights, up):

time: 142 us -> 141 us (level)
  transfers between devices with their start and end apart: 26 -> 26, of which waited for: 11 -> 11; matrix products, arithmetic and copies ran while one was open for 24% -> 24% of each run, Pallas kernels for 8% -> 7%
where the time goes in v15:
time: 141 us; the launch traced here: 139 us
  starting transfers between devices  44 us (31%)
  waiting for transfers between devices  41.5 us (29%)
  local copies, waits for them, and re-layouts  20.5 us (15%)
  other arithmetic  17.3 us (12%)
  Pallas kernels  10.4 us (7%)
  matrix products  4.47 us (3%)
    all_to_all x1, waiting for transfers between devices, table_and_gain(): got = lax.all_to_all(send, every, 0, 0, tiled=True)  18.7 us
    ppermute x6, starting transfers between devices, fetch_halves(): lax.ppermute(mine, axis, [(source, source ^ apart) for source in range(co...  8.79 us
    all_to_all x1, starting transfers between devices, body(): group_out = lax.all_to_all(dconv, 'seq', 0, 1, tiled=True)  7.41 us
    ppermute x3, waiting for transfers between devices, gather_by_permutes(): pieces.append(lax.ppermute(total, axis, pairs))  7.14 us
    ppermute x6, waiting for transfers between devices, fetch_halves(): lax.ppermute(mine, axis, [(source, source ^ apart) for source in range(co...  5.64 us
    pallas_call x1, Pallas kernels, conv_dconv(): pl.pallas_call(forward_kernel, grid=(groups // step,), in_specs=[pl.Block...  5.29 us
    pallas_call x1, Pallas kernels, conv_transpose(): pl.pallas_call(backward_kernel, grid=(groups // step,), in_specs=[pl.Bloc...  5.15 us
    unnamed x23, local copies, waits for them, and re-layouts  4.98 us
  transfers between devices with their start and end apart: 26, of which 11 were waited for; matrix products, arithmetic and copies ran while one was open for 24% of the time, Pallas kernels for 7%

profile of v15, /device:TPU:0, one launch (start us, length us, event | category | flops | bytes accessed | tf_op | source)
XLA Modules:
  0.0 139.3 jit_solution(2820002561381778637)
XLA Ops:
  0.6 0.9 constant_dynamic-slice_fusion.4
  1.6 3.0 %collective-permute-start = (bf16[32,2048]{1,0:T(8,128)(2,1)S(1)}, bf16[32,2048]{1,0:T(8,128)(2,1)S(1)}, u32[]{:S(2)}, u32[]{:S(2)}) collective-permute-start(bf16[32,2048]{1,0:T(8,128)(2,1)S(1)} %constant_dynamic-slice_fusion.4), channel_id=1, source_target_pairs={{0,8},{8,0},{16,24},{24,16},{1,9},{9,1},{17,25},{25,17},{2,10},{10... | collective-permute-start | bytes 393224 | tf_op jit(solution)/shard_map/ppermute | solution.py:198
  4.6 1.5 %collective-permute-start.2 = (bf16[32,2048]{1,0:T(8,128)(2,1)S(1)}, bf16[32,2048]{1,0:T(8,128)(2,1)S(1)}, u32[]{:S(2)}, u32[]{:S(2)}) collective-permute-start(bf16[32,2048]{1,0:T(8,128)(2,1)S(1)} %constant_dynamic-slice_fusion.4), channel_id=1, source_target_pairs={{0,16},{8,24},{16,0},{24,8},{1,17},{9,25},{17,1},{25,9},{2,18},{10... | collective-permute-start | bytes 393224 | tf_op jit(solution)/shard_map/ppermute | solution.py:198
  6.1 2.4 %collective-permute-done = bf16[32,2048]{1,0:T(8,128)(2,1)S(1)} collective-permute-done((bf16[32,2048]{1,0:T(8,128)(2,1)S(1)}, bf16[32,2048]{1,0:T(8,128)(2,1)S(1)}, u32[]{:S(2)}, u32[]{:S(2)}) %collective-permute-start) | collective-permute-done | bytes 131104 | tf_op jit(solution)/shard_map/ppermute | solution.py:198
  8.5 1.9 %constant_dynamic-slice_fusion.3 = bf16[256,1152]{1,0:T(8,128)(2,1)} fusion(bf16[512,1152]{1,0:T(8,128)(2,1)} %param.14, s32[]{:T(128)S(6)} %select_n.123), kind=kLoop, calls=%fused_computation.94 | loop fusion | bytes 1179652 | tf_op jit(solution)/shard_map/dynamic_slice | solution.py:196
  10.4 3.4 %collective-permute-start.6 = (bf16[256,1152]{1,0:T(8,128)(2,1)}, bf16[256,1152]{1,0:T(8,128)(2,1)}, u32[]{:S(2)}, u32[]{:S(2)}) collective-permute-start(bf16[256,1152]{1,0:T(8,128)(2,1)} %constant_dynamic-slice_fusion.3), channel_id=1, source_target_pairs={{0,24},{8,16},{16,8},{24,0},{1,25},{9,17},{17,9},{25,1},{2,26},{10... | collective-permute-start | bytes 1769480 | tf_op jit(solution)/shard_map/ppermute | solution.py:198
  14.4 1.0 collective-permute-done.5
  15.6 0.8 copy-done.6
  16.7 0.9 copy-done.8
  17.6 0.4 multiply_reduce_fusion.2
  18.8 1.0 copy.64
  19.8 0.8 fusion.40
  20.6 2.2 %collective-permute-start.7 = (bf16[16,4,128]{2,1,0:T(4,128)(2,1)S(1)}, bf16[16,4,128]{2,1,0:T(4,128)(2,1)S(1)}, u32[]{:S(2)}, u32[]{:S(2)}) collective-permute-start(bf16[16,4,128]{2,1,0:T(4,128)(2,1)S(1)} %get-tuple-element.57), channel_id=1, source_target_pairs={{0,1},{1,2},{2,3},{3,4},{4,5},{5,6},{6,7},{8,9},{9,10},{10,11},{11... | collective-permute-start | bytes 49160 | tf_op jit(solution)/shard_map/ppermute | solution.py:19
  22.8 1.3 collective-permute-start.8
  24.1 0.7 collective-permute-start.11
  24.9 1.9 %collective-permute-done.8 = bf16[16,4,128]{2,1,0:T(4,128)(2,1)S(1)} collective-permute-done((bf16[16,4,128]{2,1,0:T(4,128)(2,1)S(1)}, bf16[16,4,128]{2,1,0:T(4,128)(2,1)S(1)}, u32[]{:S(2)}, u32[]{:S(2)}) %collective-permute-start.8) | collective-permute-done | bytes 16416 | tf_op jit(solution)/shard_map/ppermute | solution.py:21
  26.7 1.2 pad_maximum_fusion.6
  28.2 2.7 %collective-permute-start.13 = (bf16[256,1152]{1,0:T(8,128)(2,1)}, bf16[256,1152]{1,0:T(8,128)(2,1)}, u32[]{:S(2)}, u32[]{:S(2)}) collective-permute-start(bf16[256,1152]{1,0:T(8,128)(2,1)} %collective-permute-done.6), channel_id=1, source_target_pairs={{0,1},{1,0},{2,3},{3,2},{4,5},{5,4},{6,7},{7,6},{8,9},{9,8},{10,11... | collective-permute-start | bytes 1769480 | tf_op jit(solution)/shard_map/ppermute | solution.py:30
  31.1 1.3 copy.66
  32.5 3.5 %all-to-all-start.2 = ((bf16[16,128,128]{2,1,0:T(8,128)(2,1)}), bf16[16,128,128]{2,1,0:T(8,128)(2,1)S(1)}, u32[]{:S(2)}, u32[]{:S(2)}) async-start(bf16[16,128,128]{2,1,0:T(8,128)(2,1)} %bitcast.12), calls=%async_computation.2 | async-start | bytes 1048576 | tf_op jit(solution)/shard_map/all_to_all | solution.py:260
  36.0 1.1 convert_element_type.51.pad_ref
  37.0 3.0 %collective-permute-done.9 = bf16[256,1152]{1,0:T(8,128)(2,1)} collective-permute-done((bf16[256,1152]{1,0:T(8,128)(2,1)}, bf16[256,1152]{1,0:T(8,128)(2,1)}, u32[]{:S(2)}, u32[]{:S(2)}) %collective-permute-start.9) | collective-permute-done | bytes 589856 | tf_op jit(solution)/shard_map/ppermute | solution.py:198
  40.1 0.6 collective-permute-start.10
  40.8 1.4 broadcast_select_fusion.1
  42.5 1.2 broadcast_select_fusion.5
  43.7 1.2 broadcast_select_fusion.3
  45.2 1.1 copy-done.1
  46.2 0.7 pad_maximum_fusion
  47.0 0.4 dynamic-slice_bitcast_fusion.3
  47.3 2.8 %pad_maximum_fusion.1 = bf16[2048,1152]{1,0:T(8,128)(2,1)} fusion(bf16[512,1152]{1,0:T(8,128)(2,1)S(1)} %get-tuple-element.35, bf16[512,1152]{1,0:T(8,128)(2,1)S(1)} %get-tuple-element.36, bf16[512,1152]{1,0:T(8,128)(2,1)S(1)} %get-tuple-element.37, bf16[512,1152]{1,0:T(8,128)(2,1)S(1)} %get-tuple-element.34), kind=kLoop, calls=%fused_computation.1 | loop fusion | flops 18874368 | bytes 9437184 | tf_op jit(solution)/shard_map/concatenate | solution.py:217
  50.2 5.3 %shard_map.98 = bf16[16,128,128]{2,1,0:T(8,128)(2,1)} custom-call(f32[16,136,128]{2,1,0:T(8,128)} %convert_element_type.51.pad_ref, bf16[16,128,1152]{2,1,0:T(8,128)(2,1)} %bitcast.94, f32[16,128,128]{2,1,0:T(8,128)} %bitcast.98), custom_call_target="tpu_custom_call" | custom-call | flops 603979776 | bytes 7405568 | tf_op jit(solution)/shard_map/pallas_call | solution.py:69
  55.5 0.8 fusion.39
  56.3 2.3 %collective-permute-start.14 = (bf16[16,4,128]{2,1,0:T(4,128)(2,1)S(1)}, bf16[16,4,128]{2,1,0:T(4,128)(2,1)S(1)}, u32[]{:S(2)}, u32[]{:S(2)}) collective-permute-start(bf16[16,4,128]{2,1,0:T(4,128)(2,1)S(1)} %get-tuple-element.55), channel_id=1, source_target_pairs={{0,1},{1,2},{2,3},{3,4},{4,5},{5,6},{6,7},{8,9},{9,10},{10,11},{11... | collective-permute-start | bytes 49160 | tf_op jit(solution)/shard_map/ppermute | solution.py:19
  58.5 1.3 collective-permute-start.15
  60.1 7.4 %all-to-all-start.1 = ((bf16[16,128,128]{2,1,0:T(8,128)(2,1)}), bf16[16,128,128]{2,1,0:T(8,128)(2,1)}, u32[]{:S(2)}, u32[]{:S(2)}) async-start(bf16[16,128,128]{2,1,0:T(8,128)(2,1)} %shard_map.98), calls=%async_computation.1 | async-start | bytes 1048576 | tf_op jit(solution)/shard_map/all_to_all | solution.py:261
  67.8 1.0 all_to_all.40
  68.8 1.1 maximum_convert_fusion.pad_ref
  70.0 5.1 %shard_map.99 = f32[16,128,128]{2,1,0:T(8,128)} custom-call(f32[16,136,128]{2,1,0:T(8,128)} %maximum_convert_fusion.pad_ref, bf16[16,128,1152]{2,1,0:T(8,128)(2,1)} %bitcast.95), custom_call_target="tpu_custom_call" | custom-call | flops 603979776 | bytes 6881280 | tf_op jit(solution)/shard_map/pallas_call | solution.py:91
  75.1 1.6 %copy.67 = f32[128,16,128]{0,2,1:T(8,128)S(1)} copy(f32[128,16,128]{2,0,1:T(8,128)} %bitcast.101) | data formatting | bytes 2097152 | tf_op jit(solution)/shard_map/transpose | solution.py:272
  77.3 0.7 copy-done.3
  78.1 0.4 fusion.10
  78.9 1.2 pad_maximum_fusion.5
  80.2 2.8 %all-to-all-done.1 = bf16[16,128,128]{2,1,0:T(8,128)(2,1)} async-done(((bf16[16,128,128]{2,1,0:T(8,128)(2,1)}), bf16[16,128,128]{2,1,0:T(8,128)(2,1)}, u32[]{:S(2)}, u32[]{:S(2)}) %all-to-all-start.1) | async-done | bytes 524320 | tf_op jit(solution)/shard_map/all_to_all | solution.py:261
  83.0 3.2 %all-to-all-start = ((bf16[32,130,64]{1,2,0:T(8,128)(2,1)}), bf16[32,130,64]{1,2,0:T(8,128)(2,1)S(1)}, u32[]{:S(2)}, u32[]{:S(2)}) async-start(bf16[32,130,64]{1,2,0:T(8,128)(2,1)} %pad_maximum_fusion.5), calls=%async_computation | async-start | bytes 2097152 | tf_op jit(solution)/shard_map/all_to_all | solution.py:150
  86.1 1.1 copy.77
  88.0 0.4 convolution_dynamic-update-slice_fusion.6
  90.9 0.8 constant_dynamic-slice_fusion.2
  91.7 1.6 %collective-permute-start.16 = (f32[64,1152]{1,0:T(8,128)}, f32[64,1152]{1,0:T(8,128)}, u32[]{:S(2)}, u32[]{:S(2)}) collective-permute-start(f32[64,1152]{1,0:T(8,128)} %get-tuple-element.42), channel_id=1, source_target_pairs={{0,8},{8,0},{16,24},{24,16},{1,9},{9,1},{17,25},{25,17},{2,10},{10... | collective-permute-start | bytes 884744 | tf_op jit(solution)/shard_map/ppermute | solution.py:175
  93.3 1.5 %collective-permute-start.17 = (f32[64,1152]{1,0:T(8,128)S(1)}, f32[64,1152]{1,0:T(8,128)}, u32[]{:S(2)}, u32[]{:S(2)}) collective-permute-start(f32[64,1152]{1,0:T(8,128)S(1)} %get-tuple-element.44), channel_id=1, source_target_pairs={{0,16},{8,24},{16,0},{24,8},{1,17},{9,25},{17,1},{25,9},{2,18},{10... | collective-permute-start | bytes 884744 | tf_op jit(solution)/shard_map/ppermute | solution.py:175
  94.8 0.4 collective-permute-start.18
  95.2 18.7 %all-to-all-done = bf16[32,130,64]{1,2,0:T(8,128)(2,1)S(1)} async-done(((bf16[32,130,64]{1,2,0:T(8,128)(2,1)}), bf16[32,130,64]{1,2,0:T(8,128)(2,1)S(1)}, u32[]{:S(2)}, u32[]{:S(2)}) %all-to-all-start) | async-done | bytes 532512 | tf_op jit(solution)/shard_map/all_to_all | solution.py:150
  114.4 0.9 fusion.2
  115.4 1.2 add_add_fusion
  116.6 0.8 reshape.118
  117.4 3.0 %all-to-all-start.3 = ((f32[32,1,576]{2,1,0:T(1,128)}), f32[32,1,576]{2,1,0:T(1,128)S(1)}, u32[]{:S(2)}, u32[]{:S(2)}) async-start(f32[32,1,576]{2,1,0:T(1,128)} %reshape.118), calls=%async_computation.3 | async-start | bytes 163840 | tf_op jit(solution)/shard_map/all_to_all | solution.py:161
  120.4 1.8 %collective-permute-start.19 = (f32[64,1152]{1,0:T(8,128)S(1)}, f32[64,1152]{1,0:T(8,128)S(1)}, u32[]{:S(2)}, u32[]{:S(2)}) collective-permute-start(f32[64,1152]{1,0:T(8,128)S(1)} %add_add_fusion), channel_id=1, source_target_pairs={{0,8},{8,0},{16,24},{24,16},{1,9},{9,1},{17,25},{25,17},{2,10},{10... | collective-permute-start | bytes 884744 | tf_op jit(solution)/shard_map/ppermute | solution.py:185
  122.3 1.5 %collective-permute-start.20 = (f32[64,1152]{1,0:T(8,128)S(1)}, f32[64,1152]{1,0:T(8,128)S(1)}, u32[]{:S(2)}, u32[]{:S(2)}) collective-permute-start(f32[64,1152]{1,0:T(8,128)S(1)} %add_add_fusion), channel_id=1, source_target_pairs={{0,16},{8,24},{16,0},{24,8},{1,17},{9,25},{17,1},{25,9},{2,18},{10... | collective-permute-start | bytes 884744 | tf_op jit(solution)/shard_map/ppermute | solution.py:185
  124.0 4.1 %all-to-all-done.3 = f32[32,1,576]{2,1,0:T(1,128)S(1)} async-done(((f32[32,1,576]{2,1,0:T(1,128)}), f32[32,1,576]{2,1,0:T(1,128)S(1)}, u32[]{:S(2)}, u32[]{:S(2)}) %all-to-all-start.3) | async-done | bytes 73760 | tf_op jit(solution)/shard_map/all_to_all | solution.py:161
  128.1 0.5 broadcast.56
  128.6 0.8 reduce.7
  129.6 0.7 reshape.106
  130.3 0.6 slice_reduce_fusion
  131.0 7.0 %collective-permute-done.20 = f32[64,1152]{1,0:T(8,128)S(1)} collective-permute-done((f32[64,1152]{1,0:T(8,128)S(1)}, f32[64,1152]{1,0:T(8,128)S(1)}, u32[]{:S(2)}, u32[]{:S(2)}) %collective-permute-start.20) | collective-permute-done | bytes 294944 | tf_op jit(solution)/shard_map/ppermute | solution.py:185
  138.2 1.1 pad_maximum_fusion.3
  (87 shorter events, 9.0 us)
Async XLA Ops:
  1.6 6.9 %collective-permute-start = (bf16[32,2048]{1,0:T(8,128)(2,1)S(1)}, bf16[32,2048]{1,0:T(8,128)(2,1)S(1)}, u32[]{:S(2)}, u32[]{:S(2)}) collective-permute-start(bf16[32,2048]{1,0:T(8,128)(2,1)S(1)} %constant_dynamic-slice_fusion.4), channel_id=1, source_target_pairs={{0,8},{8,0},{16,24},{24,16},{1,9},{9,1},{17,25},{25,17},{2,10},{10... | collective-permute-start | bytes 393224 | tf_op jit(solution)/shard_map/ppermute | solution.py:198
  4.6 9.3 %collective-permute-start.2 = (bf16[32,2048]{1,0:T(8,128)(2,1)S(1)}, bf16[32,2048]{1,0:T(8,128)(2,1)S(1)}, u32[]{:S(2)}, u32[]{:S(2)}) collective-permute-start(bf16[32,2048]{1,0:T(8,128)(2,1)S(1)} %constant_dynamic-slice_fusion.4), channel_id=1, source_target_pairs={{0,16},{8,24},{16,0},{24,8},{1,17},{9,25},{17,1},{25,9},{2,18},{10... | collective-permute-start | bytes 393224 | tf_op jit(solution)/shard_map/ppermute | solution.py:198
  6.1 8.0 %collective-permute-start.4 = (bf16[32,2048]{1,0:T(8,128)(2,1)S(1)}, bf16[32,2048]{1,0:T(8,128)(2,1)S(1)}, u32[]{:S(2)}, u32[]{:S(2)}) collective-permute-start(bf16[32,2048]{1,0:T(8,128)(2,1)S(1)} %constant_dynamic-slice_fusion.4), channel_id=1, source_target_pairs={{0,24},{8,16},{16,8},{24,0},{1,25},{9,17},{17,9},{25,1},{2,26},{10... | collective-permute-start | bytes 393224 | tf_op jit(solution)/shard_map/ppermute | solution.py:198
  8.5 5.9 %collective-permute-start.1 = (bf16[32,2048]{1,0:T(8,128)(2,1)S(1)}, bf16[32,2048]{1,0:T(8,128)(2,1)S(1)}, u32[]{:S(2)}, u32[]{:S(2)}) collective-permute-start(bf16[32,2048]{1,0:T(8,128)(2,1)S(1)} %collective-permute-done), channel_id=1, source_target_pairs={{0,1},{1,0},{2,3},{3,2},{4,5},{5,4},{6,7},{7,6},{8,9},{9,8},{10,11... | collective-permute-start | bytes 393224 | tf_op jit(solution)/shard_map/ppermute | solution.py:30
  10.4 17.8 %collective-permute-start.6 = (bf16[256,1152]{1,0:T(8,128)(2,1)}, bf16[256,1152]{1,0:T(8,128)(2,1)}, u32[]{:S(2)}, u32[]{:S(2)}) collective-permute-start(bf16[256,1152]{1,0:T(8,128)(2,1)} %constant_dynamic-slice_fusion.3), channel_id=1, source_target_pairs={{0,24},{8,16},{16,8},{24,0},{1,25},{9,17},{17,9},{25,1},{2,26},{10... | collective-permute-start | bytes 1769480 | tf_op jit(solution)/shard_map/ppermute | solution.py:198
  13.9 1.7 %collective-permute-start.3 = (bf16[32,2048]{1,0:T(8,128)(2,1)S(1)}, bf16[32,2048]{1,0:T(8,128)(2,1)S(1)}, u32[]{:S(2)}, u32[]{:S(2)}) collective-permute-start(bf16[32,2048]{1,0:T(8,128)(2,1)S(1)} %collective-permute-done.2), channel_id=1, source_target_pairs={{0,1},{1,0},{2,3},{3,2},{4,5},{5,4},{6,7},{7,6},{8,9},{9,8},{10,11... | collective-permute-start | bytes 393224 | tf_op jit(solution)/shard_map/ppermute | solution.py:30
  14.1 1.3 collective-permute-start.5
  15.5 1.0 copy-start.6
  16.6 1.0 copy-start.8
  16.6 1.0 copy-start.9
  17.6 0.7 copy-start.7
  18.7 12.2 %copy-start.2 = (bf16[1,128,2048]{2,1,0:T(8,128)(2,1)S(1)}, bf16[1,128,2048]{2,1,0:T(8,128)(2,1)}, u32[]{:S(2)}) copy-start(bf16[1,128,2048]{2,1,0:T(8,128)(2,1)} %param.15) | copy-start | bytes 1572868
  20.6 4.3 %collective-permute-start.7 = (bf16[16,4,128]{2,1,0:T(4,128)(2,1)S(1)}, bf16[16,4,128]{2,1,0:T(4,128)(2,1)S(1)}, u32[]{:S(2)}, u32[]{:S(2)}) collective-permute-start(bf16[16,4,128]{2,1,0:T(4,128)(2,1)S(1)} %get-tuple-element.57), channel_id=1, source_target_pairs={{0,1},{1,2},{2,3},{3,4},{4,5},{5,6},{6,7},{8,9},{9,10},{10,11},{11... | collective-permute-start | bytes 49160 | tf_op jit(solution)/shard_map/ppermute | solution.py:19
  22.8 4.0 %collective-permute-start.8 = (bf16[16,4,128]{2,1,0:T(4,128)(2,1)S(1)}, bf16[16,4,128]{2,1,0:T(4,128)(2,1)S(1)}, u32[]{:S(2)}, u32[]{:S(2)}) collective-permute-start(bf16[16,4,128]{2,1,0:T(4,128)(2,1)S(1)} %get-tuple-element.58), channel_id=1, source_target_pairs={{1,0},{2,1},{3,2},{4,3},{5,4},{6,5},{7,6},{9,8},{10,9},{11,10},{12... | collective-permute-start | bytes 49160 | tf_op jit(solution)/shard_map/ppermute | solution.py:21
  24.1 16.0 %collective-permute-start.9 = (bf16[256,1152]{1,0:T(8,128)(2,1)}, bf16[256,1152]{1,0:T(8,128)(2,1)}, u32[]{:S(2)}, u32[]{:S(2)}) collective-permute-start(bf16[256,1152]{1,0:T(8,128)(2,1)} %constant_dynamic-slice_fusion.3), channel_id=1, source_target_pairs={{0,8},{8,0},{16,24},{24,16},{1,9},{9,1},{17,25},{25,17},{2,10},{10... | collective-permute-start | bytes 1769480 | tf_op jit(solution)/shard_map/ppermute | solution.py:198
  24.1 16.5 %collective-permute-start.11 = (bf16[256,1152]{1,0:T(8,128)(2,1)}, bf16[256,1152]{1,0:T(8,128)(2,1)}, u32[]{:S(2)}, u32[]{:S(2)}) collective-permute-start(bf16[256,1152]{1,0:T(8,128)(2,1)} %constant_dynamic-slice_fusion.3), channel_id=1, source_target_pairs={{0,16},{8,24},{16,0},{24,8},{1,17},{9,25},{17,1},{25,9},{2,18},{10... | collective-permute-start | bytes 1769480 | tf_op jit(solution)/shard_map/ppermute | solution.py:198
  28.2 12.6 %collective-permute-start.13 = (bf16[256,1152]{1,0:T(8,128)(2,1)}, bf16[256,1152]{1,0:T(8,128)(2,1)}, u32[]{:S(2)}, u32[]{:S(2)}) collective-permute-start(bf16[256,1152]{1,0:T(8,128)(2,1)} %collective-permute-done.6), channel_id=1, source_target_pairs={{0,1},{1,0},{2,3},{3,2},{4,5},{5,4},{6,7},{7,6},{8,9},{9,8},{10,11... | collective-permute-start | bytes 1769480 | tf_op jit(solution)/shard_map/ppermute | solution.py:30
  32.5 27.6 %all-to-all-start.2 = ((bf16[16,128,128]{2,1,0:T(8,128)(2,1)}), bf16[16,128,128]{2,1,0:T(8,128)(2,1)S(1)}, u32[]{:S(2)}, u32[]{:S(2)}) async-start(bf16[16,128,128]{2,1,0:T(8,128)(2,1)} %bitcast.12), calls=%async_computation.2 | async-start | bytes 1048576 | tf_op jit(solution)/shard_map/all_to_all | solution.py:260
  40.1 2.4 %collective-permute-start.10 = (bf16[256,1152]{1,0:T(8,128)(2,1)}, bf16[256,1152]{1,0:T(8,128)(2,1)S(1)}, u32[]{:S(2)}, u32[]{:S(2)}) collective-permute-start(bf16[256,1152]{1,0:T(8,128)(2,1)} %collective-permute-done.9), channel_id=1, source_target_pairs={{0,1},{1,0},{2,3},{3,2},{4,5},{5,4},{6,7},{7,6},{8,9},{9,8},{10,11... | collective-permute-start | bytes 1769480 | tf_op jit(solution)/shard_map/ppermute | solution.py:30
  40.7 3.1 %collective-permute-start.12 = (bf16[256,1152]{1,0:T(8,128)(2,1)}, bf16[256,1152]{1,0:T(8,128)(2,1)S(1)}, u32[]{:S(2)}, u32[]{:S(2)}) collective-permute-start(bf16[256,1152]{1,0:T(8,128)(2,1)} %collective-permute-done.11), channel_id=1, source_target_pairs={{0,1},{1,0},{2,3},{3,2},{4,5},{5,4},{6,7},{7,6},{8,9},{9,8},{10,11... | collective-permute-start | bytes 1769480 | tf_op jit(solution)/shard_map/ppermute | solution.py:30
  45.0 1.3 copy-start.1
  56.3 12.6 %collective-permute-start.14 = (bf16[16,4,128]{2,1,0:T(4,128)(2,1)S(1)}, bf16[16,4,128]{2,1,0:T(4,128)(2,1)S(1)}, u32[]{:S(2)}, u32[]{:S(2)}) collective-permute-start(bf16[16,4,128]{2,1,0:T(4,128)(2,1)S(1)} %get-tuple-element.55), channel_id=1, source_target_pairs={{0,1},{1,2},{2,3},{3,4},{4,5},{5,6},{6,7},{8,9},{9,10},{10,11},{11... | collective-permute-start | bytes 49160 | tf_op jit(solution)/shard_map/ppermute | solution.py:19
  58.5 10.3 %collective-permute-start.15 = (bf16[16,4,128]{2,1,0:T(4,128)(2,1)S(1)}, bf16[16,4,128]{2,1,0:T(4,128)(2,1)S(1)}, u32[]{:S(2)}, u32[]{:S(2)}) collective-permute-start(bf16[16,4,128]{2,1,0:T(4,128)(2,1)S(1)} %get-tuple-element.56), channel_id=1, source_target_pairs={{1,0},{2,1},{3,2},{4,3},{5,4},{6,5},{7,6},{9,8},{10,9},{11,10},{12... | collective-permute-start | bytes 49160 | tf_op jit(solution)/shard_map/ppermute | solution.py:21
  60.1 22.9 %all-to-all-start.1 = ((bf16[16,128,128]{2,1,0:T(8,128)(2,1)}), bf16[16,128,128]{2,1,0:T(8,128)(2,1)}, u32[]{:S(2)}, u32[]{:S(2)}) async-start(bf16[16,128,128]{2,1,0:T(8,128)(2,1)} %shard_map.98), calls=%async_computation.1 | async-start | bytes 1048576 | tf_op jit(solution)/shard_map/all_to_all | solution.py:261
  67.5 1.3 copy-start
  77.0 1.0 copy-start.3
  78.4 1.7 %copy-start.5 = (bf16[128,2048]{1,0:T(8,128)(2,1)}, bf16[128,2048]{1,0:T(8,128)(2,1)S(1)}, u32[]{:S(2)}) copy-start(bf16[128,2048]{1,0:T(8,128)(2,1)S(1)} %fusion.10) | copy-start | bytes 1572868
  80.2 7.0 %copy-start.4 = (bf16[2,1024,128]{1,2,0:T(8,128)(2,1)S(1)}, bf16[2,1024,128]{1,2,0:T(8,128)(2,1)}, u32[]{:S(2)}) copy-start(bf16[2,1024,128]{1,2,0:T(8,128)(2,1)} %all_to_all.40) | copy-start | bytes 1572868
  83.0 30.9 %all-to-all-start = ((bf16[32,130,64]{1,2,0:T(8,128)(2,1)}), bf16[32,130,64]{1,2,0:T(8,128)(2,1)S(1)}, u32[]{:S(2)}, u32[]{:S(2)}) async-start(bf16[32,130,64]{1,2,0:T(8,128)(2,1)} %pad_maximum_fusion.5), calls=%async_computation | async-start | bytes 2097152 | tf_op jit(solution)/shard_map/all_to_all | solution.py:150
  91.7 23.7 %collective-permute-start.16 = (f32[64,1152]{1,0:T(8,128)}, f32[64,1152]{1,0:T(8,128)}, u32[]{:S(2)}, u32[]{:S(2)}) collective-permute-start(f32[64,1152]{1,0:T(8,128)} %get-tuple-element.42), channel_id=1, source_target_pairs={{0,8},{8,0},{16,24},{24,16},{1,9},{9,1},{17,25},{25,17},{2,10},{10... | collective-permute-start | bytes 884744 | tf_op jit(solution)/shard_map/ppermute | solution.py:175
  93.3 22.1 %collective-permute-start.17 = (f32[64,1152]{1,0:T(8,128)S(1)}, f32[64,1152]{1,0:T(8,128)}, u32[]{:S(2)}, u32[]{:S(2)}) collective-permute-start(f32[64,1152]{1,0:T(8,128)S(1)} %get-tuple-element.44), channel_id=1, source_target_pairs={{0,16},{8,24},{16,0},{24,8},{1,17},{9,25},{17,1},{25,9},{2,18},{10... | collective-permute-start | bytes 884744 | tf_op jit(solution)/shard_map/ppermute | solution.py:175
  94.8 20.7 %collective-permute-start.18 = (f32[64,1152]{1,0:T(8,128)S(1)}, f32[64,1152]{1,0:T(8,128)}, u32[]{:S(2)}, u32[]{:S(2)}) collective-permute-start(f32[64,1152]{1,0:T(8,128)S(1)} %get-tuple-element.43), channel_id=1, source_target_pairs={{0,24},{8,16},{16,8},{24,0},{1,25},{9,17},{17,9},{25,1},{2,26},{10... | collective-permute-start | bytes 884744 | tf_op jit(solution)/shard_map/ppermute | solution.py:175
  117.4 10.7 %all-to-all-start.3 = ((f32[32,1,576]{2,1,0:T(1,128)}), f32[32,1,576]{2,1,0:T(1,128)S(1)}, u32[]{:S(2)}, u32[]{:S(2)}) async-start(f32[32,1,576]{2,1,0:T(1,128)} %reshape.118), calls=%async_computation.3 | async-start | bytes 163840 | tf_op jit(solution)/shard_map/all_to_all | solution.py:161
  120.4 10.6 %collective-permute-start.19 = (f32[64,1152]{1,0:T(8,128)S(1)}, f32[64,1152]{1,0:T(8,128)S(1)}, u32[]{:S(2)}, u32[]{:S(2)}) collective-permute-start(f32[64,1152]{1,0:T(8,128)S(1)} %add_add_fusion), channel_id=1, source_target_pairs={{0,8},{8,0},{16,24},{24,16},{1,9},{9,1},{17,25},{25,17},{2,10},{10... | collective-permute-start | bytes 884744 | tf_op jit(solution)/shard_map/ppermute | solution.py:185
  122.3 15.8 %collective-permute-start.20 = (f32[64,1152]{1,0:T(8,128)S(1)}, f32[64,1152]{1,0:T(8,128)S(1)}, u32[]{:S(2)}, u32[]{:S(2)}) collective-permute-start(f32[64,1152]{1,0:T(8,128)S(1)} %add_add_fusion), channel_id=1, source_target_pairs={{0,16},{8,24},{16,0},{24,8},{1,17},{9,25},{17,1},{25,9},{2,18},{10... | collective-permute-start | bytes 884744 | tf_op jit(solution)/shard_map/ppermute | solution.py:185
  123.7 14.3 %collective-permute-start.21 = (f32[64,1152]{1,0:T(8,128)S(1)}, f32[64,1152]{1,0:T(8,128)S(1)}, u32[]{:S(2)}, u32[]{:S(2)}) collective-permute-start(f32[64,1152]{1,0:T(8,128)S(1)} %add_add_fusion), channel_id=1, source_target_pairs={{0,24},{8,16},{16,8},{24,0},{1,25},{9,17},{17,9},{25,1},{2,26},{10... | collective-permute-start | bytes 884744 | tf_op jit(solution)/shard_map/ppermute | solution.py:185

commit v16 on v15

--- a/solution.py
+++ b/solution.py
@@ -208,15 +208,15 @@
     count = lax.axis_size(axis)
     me = lax.axis_index(axis)
     core = lax.axis_index("seq") % 2
-    blocks = [block]
+    rows = block.shape[0]
+    half_rows = rows // 2
+    whole = jnp.zeros((count * rows,) + block.shape[1:], block.dtype)
+    whole = lax.dynamic_update_slice_in_dim(whole, block, me * rows, axis=0)
     for apart in range(1, count):
-        lower = jnp.where(core == 0, fetched[apart], swapped[apart])
-        upper = jnp.where(core == 0, swapped[apart], fetched[apart])
-        blocks.append(jnp.concatenate([lower, upper], axis=0))
-    stacked = jnp.stack(blocks)
-    return jnp.concatenate(
-        [lax.dynamic_index_in_dim(stacked, index ^ me, keepdims=False) for index in range(count)], axis=0
-    )
+        base = (me ^ apart) * rows
+        whole = lax.dynamic_update_slice_in_dim(whole, fetched[apart], base + core * half_rows, axis=0)
+        whole = lax.dynamic_update_slice_in_dim(whole, swapped[apart], base + (1 - core) * half_rows, axis=0)
+    return whole
 
 
 def gather_shards(block, axis):

time: 141 us -> 149 us (1.057)
  local copies, waits for them, and re-layouts: 20.5 us -> 28.6 us
  other arithmetic: 17.3 us -> 9.4 us
  waiting for transfers between devices: 41.5 us -> 49 us
    ppermute x6, waiting for transfers between devices: 5.64 us -> 15.3 us  [fetch_halves(): lax.ppermute(mine, axis, [(source, source ^ apart) for source in range(co...]
    dynamic_update_slice x0 -> x14, local copies, waits for them, and re-layouts: none -> 9.63 us  [the longest x6 4.76 us: assemble_shards(): lax.dynamic_update_slice_in_dim(whole, fetched[apart], base + core * half...]
    select_n x6 -> x0, other arithmetic: 3.88 us -> none  [assemble_shards(): lower = jnp.where(core == 0, fetched[apart], swapped[apart])]
    concatenate x1 -> x0, other arithmetic: 2.83 us -> none  [assemble_shards(): jnp.concatenate([lax.dynamic_index_in_dim(stacked, index ^ me, keepdims=F...]
    unnamed x23, local copies, waits for them, and re-layouts: 4.98 us -> 2.2 us
    broadcast_in_dim x0 -> x2, local copies, waits for them, and re-layouts: none -> 2.6 us  [assemble_shards(): whole = jnp.zeros((count * rows,) + block.shape[1:], block.dtype)]
    ppermute x2, waiting for transfers between devices: 1.88 us -> 0.01 us  [with_halo(): lax.ppermute(head, axis, [((i + 1) % count, i) for i in range(ends)])]
    all_to_all x1, starting transfers between devices: 3.49 us -> 5.03 us  [body(): group_in = lax.all_to_all(normed_g, 'seq', 0, 1, tiled=True)]
  transfers between devices with their start and end apart: 26 -> 26, of which waited for: 11 -> 9; matrix products, arithmetic and copies ran while one was open for 24% -> 24% of each run, Pallas kernels for 7% -> 7%
where the time goes in v16:
time: 149 us; the launch traced here: 148 us
  waiting for transfers between devices  49 us (33%)
  starting transfers between devices  44.9 us (30%)
  local copies, waits for them, and re-layouts  28.6 us (19%)
  Pallas kernels  10.4 us (7%)
  other arithmetic  9.4 us (6%)
  matrix products  4.45 us (3%)
    all_to_all x1, waiting for transfers between devices, table_and_gain(): got = lax.all_to_all(send, every, 0, 0, tiled=True)  18.7 us
    ppermute x6, waiting for transfers between devices, fetch_halves(): lax.ppermute(mine, axis, [(source, source ^ apart) for source in range(co...  15.3 us
    ppermute x6, starting transfers between devices, fetch_halves(): lax.ppermute(mine, axis, [(source, source ^ apart) for source in range(co...  9.5 us
    ppermute x3, waiting for transfers between devices, gather_by_permutes(): pieces.append(lax.ppermute(total, axis, pairs))  7.16 us
    all_to_all x1, starting transfers between devices, body(): group_out = lax.all_to_all(dconv, 'seq', 0, 1, tiled=True)  6.97 us
    pallas_call x1, Pallas kernels, conv_dconv(): pl.pallas_call(forward_kernel, grid=(groups // step,), in_specs=[pl.Block...  5.29 us
    pallas_call x1, Pallas kernels, conv_transpose(): pl.pallas_call(backward_kernel, grid=(groups // step,), in_specs=[pl.Bloc...  5.15 us
    all_to_all x1, starting transfers between devices, body(): group_in = lax.all_to_all(normed_g, 'seq', 0, 1, tiled=True)  5.03 us
  transfers between devices with their start and end apart: 26, of which 9 were waited for; matrix products, arithmetic and copies ran while one was open for 24% of the time, Pallas kernels for 7%

profile of v16, /device:TPU:0, one launch (start us, length us, event | category | flops | bytes accessed | tf_op | source)
XLA Modules:
  0.0 148.0 jit_solution(1842833682243077573)
XLA Ops:
  0.7 2.0 %constant_dynamic-slice_fusion.3 = bf16[256,1152]{1,0:T(8,128)(2,1)} fusion(bf16[512,1152]{1,0:T(8,128)(2,1)} %param.14, s32[]{:T(128)S(6)} %select_n.93), kind=kLoop, calls=%fused_computation.65 | loop fusion | bytes 1179652 | tf_op jit(solution)/shard_map/dynamic_slice | solution.py:196
  2.6 2.9 %collective-permute-start.9 = (bf16[256,1152]{1,0:T(8,128)(2,1)}, bf16[256,1152]{1,0:T(8,128)(2,1)}, u32[]{:S(2)}, u32[]{:S(2)}) collective-permute-start(bf16[256,1152]{1,0:T(8,128)(2,1)} %constant_dynamic-slice_fusion.3), channel_id=1, source_target_pairs={{0,8},{8,0},{16,24},{24,16},{1,9},{9,1},{17,25},{25,17},{2,10},{10... | collective-permute-start | bytes 1769480 | tf_op jit(solution)/shard_map/ppermute | solution.py:198
  5.6 1.5 %collective-permute-start.11 = (bf16[256,1152]{1,0:T(8,128)(2,1)}, bf16[256,1152]{1,0:T(8,128)(2,1)S(1)}, u32[]{:S(2)}, u32[]{:S(2)}) collective-permute-start(bf16[256,1152]{1,0:T(8,128)(2,1)} %constant_dynamic-slice_fusion.3), channel_id=1, source_target_pairs={{0,16},{8,24},{16,0},{24,8},{1,17},{9,25},{17,1},{25,9},{2,18},{10... | collective-permute-start | bytes 1769480 | tf_op jit(solution)/shard_map/ppermute | solution.py:198
  7.1 0.6 collective-permute-start
  7.8 2.9 %collective-permute-start.4 = (bf16[32,2048]{1,0:T(8,128)(2,1)S(1)}, bf16[32,2048]{1,0:T(8,128)(2,1)S(1)}, u32[]{:S(2)}, u32[]{:S(2)}) collective-permute-start(bf16[32,2048]{1,0:T(8,128)(2,1)S(1)} %constant_dynamic-slice_fusion.4), channel_id=1, source_target_pairs={{0,24},{8,16},{16,8},{24,0},{1,25},{9,17},{17,9},{25,1},{2,26},{10... | collective-permute-start | bytes 393224 | tf_op jit(solution)/shard_map/ppermute | solution.py:198
  10.8 11.9 %collective-permute-done = bf16[32,2048]{1,0:T(8,128)(2,1)S(1)} collective-permute-done((bf16[32,2048]{1,0:T(8,128)(2,1)S(1)}, bf16[32,2048]{1,0:T(8,128)(2,1)S(1)}, u32[]{:S(2)}, u32[]{:S(2)}) %collective-permute-start) | collective-permute-done | bytes 131104 | tf_op jit(solution)/shard_map/ppermute | solution.py:198
  22.8 3.4 %collective-permute-done.2 = bf16[32,2048]{1,0:T(8,128)(2,1)S(1)} collective-permute-done((bf16[32,2048]{1,0:T(8,128)(2,1)S(1)}, bf16[32,2048]{1,0:T(8,128)(2,1)S(1)}, u32[]{:S(2)}, u32[]{:S(2)}) %collective-permute-start.2) | collective-permute-done | bytes 131104 | tf_op jit(solution)/shard_map/ppermute | solution.py:198
  26.2 1.5 %collective-permute-start.6 = (bf16[256,1152]{1,0:T(8,128)(2,1)}, bf16[256,1152]{1,0:T(8,128)(2,1)}, u32[]{:S(2)}, u32[]{:S(2)}) collective-permute-start(bf16[256,1152]{1,0:T(8,128)(2,1)} %constant_dynamic-slice_fusion.3), channel_id=1, source_target_pairs={{0,24},{8,16},{16,8},{24,0},{1,25},{9,17},{17,9},{25,1},{2,26},{10... | collective-permute-start | bytes 1769480 | tf_op jit(solution)/shard_map/ppermute | solution.py:198
  27.7 0.5 collective-permute-start.5
  28.2 0.8 collective-permute-done.3
  29.3 0.4 multiply_reduce_fusion.2
  30.4 1.0 copy.64
  31.4 0.8 fusion.32
  32.2 2.2 %collective-permute-start.7 = (bf16[16,4,128]{2,1,0:T(4,128)(2,1)S(1)}, bf16[16,4,128]{2,1,0:T(4,128)(2,1)S(1)}, u32[]{:S(2)}, u32[]{:S(2)}) collective-permute-start(bf16[16,4,128]{2,1,0:T(4,128)(2,1)S(1)} %get-tuple-element.43), channel_id=1, source_target_pairs={{0,1},{1,2},{2,3},{3,4},{4,5},{5,6},{6,7},{8,9},{9,10},{10,11},{11... | collective-permute-start | bytes 49160 | tf_op jit(solution)/shard_map/ppermute | solution.py:19
  34.4 1.4 collective-permute-start.8
  35.9 2.1 %collective-permute-start.10 = (bf16[256,1152]{1,0:T(8,128)(2,1)}, bf16[256,1152]{1,0:T(8,128)(2,1)}, u32[]{:S(2)}, u32[]{:S(2)}) collective-permute-start(bf16[256,1152]{1,0:T(8,128)(2,1)} %collective-permute-done.9), channel_id=1, source_target_pairs={{0,1},{1,0},{2,3},{3,2},{4,5},{5,4},{6,7},{7,6},{8,9},{9,8},{10,11... | collective-permute-start | bytes 1769480 | tf_op jit(solution)/shard_map/ppermute | solution.py:30
  37.9 2.5 %broadcast_in_dim.11 = bf16[2048,1152]{1,0:T(8,128)(2,1)} broadcast(bf16[]{:T(256)} %constant.84.clone.1), dimensions={} | broadcast | bytes 4718594 | tf_op jit(solution)/shard_map/broadcast_in_dim | solution.py:213
  40.4 1.1 constant_dynamic-update-slice_fusion.6
  41.8 1.4 copy.66
  43.2 5.0 %all-to-all-start.2 = ((bf16[16,128,128]{2,1,0:T(8,128)(2,1)}), bf16[16,128,128]{2,1,0:T(8,128)(2,1)S(1)}, u32[]{:S(2)}, u32[]{:S(2)}) async-start(bf16[16,128,128]{2,1,0:T(8,128)(2,1)} %bitcast.4), calls=%async_computation.2 | async-start | bytes 1048576 | tf_op jit(solution)/shard_map/all_to_all | solution.py:260
  48.2 1.2 pad_maximum_fusion.3
  49.5 0.6 collective-permute-start.13
  50.1 1.9 %constant_dynamic-update-slice_fusion.5 = bf16[2048,1152]{1,0:T(8,128)(2,1)} fusion(bf16[2048,1152]{1,0:T(8,128)(2,1)} %constant_dynamic-update-slice_fusion.6, bf16[256,1152]{1,0:T(8,128)(2,1)} %collective-permute-done.9, s32[]{:T(128)S(6)} %select_n.95), kind=kLoop, calls=%fused_computation.63 | loop fusion | bytes 1179652 | tf_op jit(solution)/shard_map/dynamic_update_slice | solution.py:217
  52.0 1.1 convert_element_type.51.pad_ref
  53.1 1.9 %constant_dynamic-update-slice_fusion.4 = bf16[2048,1152]{1,0:T(8,128)(2,1)} fusion(bf16[2048,1152]{1,0:T(8,128)(2,1)} %constant_dynamic-update-slice_fusion.5, bf16[256,1152]{1,0:T(8,128)(2,1)} %collective-permute-done.10, s32[]{:T(128)S(6)} %select_n.96), kind=kLoop, calls=%fused_computation.62 | loop fusion | bytes 1179652 | tf_op jit(solution)/shard_map/dynamic_update_slice | solution.py:218
  55.0 0.9 constant_dynamic-update-slice_fusion.3
  55.9 0.9 constant_dynamic-update-slice_fusion.2
  56.8 1.9 %constant_dynamic-update-slice_fusion.1 = bf16[2048,1152]{1,0:T(8,128)(2,1)} fusion(bf16[2048,1152]{1,0:T(8,128)(2,1)} %constant_dynamic-update-slice_fusion.2, bf16[256,1152]{1,0:T(8,128)(2,1)} %collective-permute-done.6, s32[]{:T(128)S(6)} %select_n.99), kind=kLoop, calls=%fused_computation.59 | loop fusion | bytes 1179652 | tf_op jit(solution)/shard_map/dynamic_update_slice | solution.py:217
  58.7 0.9 constant_dynamic-update-slice_fusion
  59.6 5.3 %shard_map.98 = bf16[16,128,128]{2,1,0:T(8,128)(2,1)} custom-call(f32[16,136,128]{2,1,0:T(8,128)} %convert_element_type.51.pad_ref, bf16[16,128,1152]{2,1,0:T(8,128)(2,1)} %bitcast.5.w_ref, f32[16,128,128]{2,1,0:T(8,128)} %bitcast.67), custom_call_target="tpu_custom_call" | custom-call | flops 603979776 | bytes 7405568 | tf_op jit(solution)/shard_map/pallas_call | solution.py:69
  64.9 0.8 fusion.31
  65.7 2.3 %collective-permute-start.14 = (bf16[16,4,128]{2,1,0:T(4,128)(2,1)S(1)}, bf16[16,4,128]{2,1,0:T(4,128)(2,1)S(1)}, u32[]{:S(2)}, u32[]{:S(2)}) collective-permute-start(bf16[16,4,128]{2,1,0:T(4,128)(2,1)S(1)} %get-tuple-element.41), channel_id=1, source_target_pairs={{0,1},{1,2},{2,3},{3,4},{4,5},{5,6},{6,7},{8,9},{9,10},{10,11},{11... | collective-permute-start | bytes 49160 | tf_op jit(solution)/shard_map/ppermute | solution.py:19
  68.0 1.3 collective-permute-start.15
  69.5 7.0 %all-to-all-start.1 = ((bf16[16,128,128]{2,1,0:T(8,128)(2,1)}), bf16[16,128,128]{2,1,0:T(8,128)(2,1)}, u32[]{:S(2)}, u32[]{:S(2)}) async-start(bf16[16,128,128]{2,1,0:T(8,128)(2,1)} %shard_map.98), calls=%async_computation.1 | async-start | bytes 1048576 | tf_op jit(solution)/shard_map/all_to_all | solution.py:261
  76.8 1.0 all_to_all.40
  77.9 1.1 maximum_convert_fusion.pad_ref
  79.0 5.2 %shard_map.99 = f32[16,128,128]{2,1,0:T(8,128)} custom-call(f32[16,136,128]{2,1,0:T(8,128)} %maximum_convert_fusion.pad_ref, bf16[16,128,1152]{2,1,0:T(8,128)(2,1)} %bitcast.5.w_ref), custom_call_target="tpu_custom_call" | custom-call | flops 603979776 | bytes 6881280 | tf_op jit(solution)/shard_map/pallas_call | solution.py:91
  84.2 1.6 %copy.67 = f32[128,16,128]{0,2,1:T(8,128)S(1)} copy(f32[128,16,128]{2,0,1:T(8,128)} %bitcast.70) | data formatting | bytes 2097152 | tf_op jit(solution)/shard_map/transpose | solution.py:272
  86.4 0.7 copy-done.3
  87.1 0.4 fusion.3
  88.0 1.2 pad_maximum_fusion.2
  89.2 2.8 %all-to-all-done.1 = bf16[16,128,128]{2,1,0:T(8,128)(2,1)} async-done(((bf16[16,128,128]{2,1,0:T(8,128)(2,1)}), bf16[16,128,128]{2,1,0:T(8,128)(2,1)}, u32[]{:S(2)}, u32[]{:S(2)}) %all-to-all-start.1) | async-done | bytes 524320 | tf_op jit(solution)/shard_map/all_to_all | solution.py:261
  92.0 2.8 %all-to-all-start = ((bf16[32,130,64]{1,2,0:T(8,128)(2,1)}), bf16[32,130,64]{1,2,0:T(8,128)(2,1)S(1)}, u32[]{:S(2)}, u32[]{:S(2)}) async-start(bf16[32,130,64]{1,2,0:T(8,128)(2,1)} %pad_maximum_fusion.2), calls=%async_computation | async-start | bytes 2097152 | tf_op jit(solution)/shard_map/all_to_all | solution.py:150
  94.8 1.1 copy.77
  95.9 0.4 convolution_dynamic-update-slice_fusion.8
  99.2 0.4 copy.79
  99.6 0.8 constant_dynamic-slice_fusion.2
  100.4 1.5 %collective-permute-start.16 = (f32[64,1152]{1,0:T(8,128)}, f32[64,1152]{1,0:T(8,128)}, u32[]{:S(2)}, u32[]{:S(2)}) collective-permute-start(f32[64,1152]{1,0:T(8,128)} %get-tuple-element.38), channel_id=1, source_target_pairs={{0,8},{8,0},{16,24},{24,16},{1,9},{9,1},{17,25},{25,17},{2,10},{10... | collective-permute-start | bytes 884744 | tf_op jit(solution)/shard_map/ppermute | solution.py:175
  101.9 1.5 collective-permute-start.17
  103.4 0.5 collective-permute-start.18
  103.9 18.7 %all-to-all-done = bf16[32,130,64]{1,2,0:T(8,128)(2,1)S(1)} async-done(((bf16[32,130,64]{1,2,0:T(8,128)(2,1)}), bf16[32,130,64]{1,2,0:T(8,128)(2,1)S(1)}, u32[]{:S(2)}, u32[]{:S(2)}) %all-to-all-start) | async-done | bytes 532512 | tf_op jit(solution)/shard_map/all_to_all | solution.py:150
  123.1 0.9 fusion.2
  124.1 1.2 add_add_fusion
  125.3 0.8 reshape.118
  126.1 3.0 %all-to-all-start.3 = ((f32[32,1,576]{2,1,0:T(1,128)}), f32[32,1,576]{2,1,0:T(1,128)S(1)}, u32[]{:S(2)}, u32[]{:S(2)}) async-start(f32[32,1,576]{2,1,0:T(1,128)} %reshape.118), calls=%async_computation.3 | async-start | bytes 163840 | tf_op jit(solution)/shard_map/all_to_all | solution.py:161
  129.1 1.8 %collective-permute-start.19 = (f32[64,1152]{1,0:T(8,128)S(1)}, f32[64,1152]{1,0:T(8,128)S(1)}, u32[]{:S(2)}, u32[]{:S(2)}) collective-permute-start(f32[64,1152]{1,0:T(8,128)S(1)} %add_add_fusion), channel_id=1, source_target_pairs={{0,8},{8,0},{16,24},{24,16},{1,9},{9,1},{17,25},{25,17},{2,10},{10... | collective-permute-start | bytes 884744 | tf_op jit(solution)/shard_map/ppermute | solution.py:185
  131.0 1.5 collective-permute-start.20
  132.7 4.1 %all-to-all-done.3 = f32[32,1,576]{2,1,0:T(1,128)S(1)} async-done(((f32[32,1,576]{2,1,0:T(1,128)}), f32[32,1,576]{2,1,0:T(1,128)S(1)}, u32[]{:S(2)}, u32[]{:S(2)}) %all-to-all-start.3) | async-done | bytes 73760 | tf_op jit(solution)/shard_map/all_to_all | solution.py:161
  136.8 0.5 broadcast.56
  137.3 0.8 reduce.7
  138.3 0.7 reshape.106
  139.0 0.6 slice_reduce_fusion
  139.7 7.0 %collective-permute-done.20 = f32[64,1152]{1,0:T(8,128)S(1)} collective-permute-done((f32[64,1152]{1,0:T(8,128)S(1)}, f32[64,1152]{1,0:T(8,128)S(1)}, u32[]{:S(2)}, u32[]{:S(2)}) %collective-permute-start.20) | collective-permute-done | bytes 294944 | tf_op jit(solution)/shard_map/ppermute | solution.py:185
  146.9 1.1 pad_maximum_fusion.1
  (88 shorter events, 7.3 us)
Async XLA Ops:
  0.6 6.5 %copy-start.6 = (bf16[64,2048]{1,0:T(8,128)(2,1)S(1)}, bf16[64,2048]{1,0:T(8,128)(2,1)}, u32[]{:S(2)}) copy-start(bf16[64,2048]{1,0:T(8,128)(2,1)} %param.12) | copy-start | bytes 786436
  2.6 33.3 %collective-permute-start.9 = (bf16[256,1152]{1,0:T(8,128)(2,1)}, bf16[256,1152]{1,0:T(8,128)(2,1)}, u32[]{:S(2)}, u32[]{:S(2)}) collective-permute-start(bf16[256,1152]{1,0:T(8,128)(2,1)} %constant_dynamic-slice_fusion.3), channel_id=1, source_target_pairs={{0,8},{8,0},{16,24},{24,16},{1,9},{9,1},{17,25},{25,17},{2,10},{10... | collective-permute-start | bytes 1769480 | tf_op jit(solution)/shard_map/ppermute | solution.py:198
  5.6 44.5 %collective-permute-start.11 = (bf16[256,1152]{1,0:T(8,128)(2,1)}, bf16[256,1152]{1,0:T(8,128)(2,1)S(1)}, u32[]{:S(2)}, u32[]{:S(2)}) collective-permute-start(bf16[256,1152]{1,0:T(8,128)(2,1)} %constant_dynamic-slice_fusion.3), channel_id=1, source_target_pairs={{0,16},{8,24},{16,0},{24,8},{1,17},{9,25},{17,1},{25,9},{2,18},{10... | collective-permute-start | bytes 1769480 | tf_op jit(solution)/shard_map/ppermute | solution.py:198
  7.1 15.6 %collective-permute-start = (bf16[32,2048]{1,0:T(8,128)(2,1)S(1)}, bf16[32,2048]{1,0:T(8,128)(2,1)S(1)}, u32[]{:S(2)}, u32[]{:S(2)}) collective-permute-start(bf16[32,2048]{1,0:T(8,128)(2,1)S(1)} %constant_dynamic-slice_fusion.4), channel_id=1, source_target_pairs={{0,8},{8,0},{16,24},{24,16},{1,9},{9,1},{17,25},{25,17},{2,10},{10... | collective-permute-start | bytes 393224 | tf_op jit(solution)/shard_map/ppermute | solution.py:198
  7.7 18.5 %collective-permute-start.2 = (bf16[32,2048]{1,0:T(8,128)(2,1)S(1)}, bf16[32,2048]{1,0:T(8,128)(2,1)S(1)}, u32[]{:S(2)}, u32[]{:S(2)}) collective-permute-start(bf16[32,2048]{1,0:T(8,128)(2,1)S(1)} %constant_dynamic-slice_fusion.4), channel_id=1, source_target_pairs={{0,16},{8,24},{16,0},{24,8},{1,17},{9,25},{17,1},{25,9},{2,18},{10... | collective-permute-start | bytes 393224 | tf_op jit(solution)/shard_map/ppermute | solution.py:198
  7.8 19.9 %collective-permute-start.4 = (bf16[32,2048]{1,0:T(8,128)(2,1)S(1)}, bf16[32,2048]{1,0:T(8,128)(2,1)S(1)}, u32[]{:S(2)}, u32[]{:S(2)}) collective-permute-start(bf16[32,2048]{1,0:T(8,128)(2,1)S(1)} %constant_dynamic-slice_fusion.4), channel_id=1, source_target_pairs={{0,24},{8,16},{16,8},{24,0},{1,25},{9,17},{17,9},{25,1},{2,26},{10... | collective-permute-start | bytes 393224 | tf_op jit(solution)/shard_map/ppermute | solution.py:198
  10.8 18.5 %copy-start.7 = (bf16[1,128,2048]{2,1,0:T(8,128)(2,1)S(1)}, bf16[1,128,2048]{2,1,0:T(8,128)(2,1)}, u32[]{:S(2)}) copy-start(bf16[1,128,2048]{2,1,0:T(8,128)(2,1)} %param.10) | copy-start | bytes 1572868
  10.8 18.5 %copy-start.9 = (s32[1,128]{1,0:T(1,128)S(1)}, s32[1,128]{1,0:T(1,128)}, u32[]{:S(2)}) copy-start(s32[1,128]{1,0:T(1,128)} %param.11) | copy-start | bytes 1540
  22.7 4.9 %collective-permute-start.1 = (bf16[32,2048]{1,0:T(8,128)(2,1)S(1)}, bf16[32,2048]{1,0:T(8,128)(2,1)S(1)}, u32[]{:S(2)}, u32[]{:S(2)}) collective-permute-start(bf16[32,2048]{1,0:T(8,128)(2,1)S(1)} %collective-permute-done), channel_id=1, source_target_pairs={{0,1},{1,0},{2,3},{3,2},{4,5},{5,4},{6,7},{7,6},{8,9},{9,8},{10,11... | collective-permute-start | bytes 393224 | tf_op jit(solution)/shard_map/ppermute | solution.py:30
  26.2 23.3 %collective-permute-start.6 = (bf16[256,1152]{1,0:T(8,128)(2,1)}, bf16[256,1152]{1,0:T(8,128)(2,1)}, u32[]{:S(2)}, u32[]{:S(2)}) collective-permute-start(bf16[256,1152]{1,0:T(8,128)(2,1)} %constant_dynamic-slice_fusion.3), channel_id=1, source_target_pairs={{0,24},{8,16},{16,8},{24,0},{1,25},{9,17},{17,9},{25,1},{2,26},{10... | collective-permute-start | bytes 1769480 | tf_op jit(solution)/shard_map/ppermute | solution.py:198
  27.7 1.3 collective-permute-start.3
  27.7 1.5 %collective-permute-start.5 = (bf16[32,2048]{1,0:T(8,128)(2,1)S(1)}, bf16[32,2048]{1,0:T(8,128)(2,1)S(1)}, u32[]{:S(2)}, u32[]{:S(2)}) collective-permute-start(bf16[32,2048]{1,0:T(8,128)(2,1)S(1)} %collective-permute-done.4), channel_id=1, source_target_pairs={{0,1},{1,0},{2,3},{3,2},{4,5},{5,4},{6,7},{7,6},{8,9},{9,8},{10,11... | collective-permute-start | bytes 393224 | tf_op jit(solution)/shard_map/ppermute | solution.py:30
  29.2 0.7 copy-start.8
  32.2 16.0 %collective-permute-start.7 = (bf16[16,4,128]{2,1,0:T(4,128)(2,1)S(1)}, bf16[16,4,128]{2,1,0:T(4,128)(2,1)S(1)}, u32[]{:S(2)}, u32[]{:S(2)}) collective-permute-start(bf16[16,4,128]{2,1,0:T(4,128)(2,1)S(1)} %get-tuple-element.43), channel_id=1, source_target_pairs={{0,1},{1,2},{2,3},{3,4},{4,5},{5,6},{6,7},{8,9},{9,10},{10,11},{11... | collective-permute-start | bytes 49160 | tf_op jit(solution)/shard_map/ppermute | solution.py:19
  34.4 6.0 %copy-start.1 = (bf16[512,1152]{1,0:T(8,128)(2,1)S(1)}, bf16[512,1152]{1,0:T(8,128)(2,1)}, u32[]{:S(2)}) copy-start(bf16[512,1152]{1,0:T(8,128)(2,1)} %param.14) | copy-start | bytes 3538948
  34.4 13.8 %collective-permute-start.8 = (bf16[16,4,128]{2,1,0:T(4,128)(2,1)S(1)}, bf16[16,4,128]{2,1,0:T(4,128)(2,1)S(1)}, u32[]{:S(2)}, u32[]{:S(2)}) collective-permute-start(bf16[16,4,128]{2,1,0:T(4,128)(2,1)S(1)} %get-tuple-element.44), channel_id=1, source_target_pairs={{1,0},{2,1},{3,2},{4,3},{5,4},{6,5},{7,6},{9,8},{10,9},{11,10},{12... | collective-permute-start | bytes 49160 | tf_op jit(solution)/shard_map/ppermute | solution.py:21
  35.9 17.2 %collective-permute-start.10 = (bf16[256,1152]{1,0:T(8,128)(2,1)}, bf16[256,1152]{1,0:T(8,128)(2,1)}, u32[]{:S(2)}, u32[]{:S(2)}) collective-permute-start(bf16[256,1152]{1,0:T(8,128)(2,1)} %collective-permute-done.9), channel_id=1, source_target_pairs={{0,1},{1,0},{2,3},{3,2},{4,5},{5,4},{6,7},{7,6},{8,9},{9,8},{10,11... | collective-permute-start | bytes 1769480 | tf_op jit(solution)/shard_map/ppermute | solution.py:30
  40.4 1.2 copy-start.2
  43.2 26.4 %all-to-all-start.2 = ((bf16[16,128,128]{2,1,0:T(8,128)(2,1)}), bf16[16,128,128]{2,1,0:T(8,128)(2,1)S(1)}, u32[]{:S(2)}, u32[]{:S(2)}) async-start(bf16[16,128,128]{2,1,0:T(8,128)(2,1)} %bitcast.4), calls=%async_computation.2 | async-start | bytes 1048576 | tf_op jit(solution)/shard_map/all_to_all | solution.py:260
  49.5 9.2 %collective-permute-start.13 = (bf16[256,1152]{1,0:T(8,128)(2,1)}, bf16[256,1152]{1,0:T(8,128)(2,1)S(1)}, u32[]{:S(2)}, u32[]{:S(2)}) collective-permute-start(bf16[256,1152]{1,0:T(8,128)(2,1)} %collective-permute-done.6), channel_id=1, source_target_pairs={{0,1},{1,0},{2,3},{3,2},{4,5},{5,4},{6,7},{7,6},{8,9},{9,8},{10,11... | collective-permute-start | bytes 1769480 | tf_op jit(solution)/shard_map/ppermute | solution.py:30
  50.0 5.9 %collective-permute-start.12 = (bf16[256,1152]{1,0:T(8,128)(2,1)S(1)}, bf16[256,1152]{1,0:T(8,128)(2,1)S(1)}, u32[]{:S(2)}, u32[]{:S(2)}) collective-permute-start(bf16[256,1152]{1,0:T(8,128)(2,1)S(1)} %collective-permute-done.11), channel_id=1, source_target_pairs={{0,1},{1,0},{2,3},{3,2},{4,5},{5,4},{6,7},{7,6},{8,9},{9,8},{10,11... | collective-permute-start | bytes 1769480 | tf_op jit(solution)/shard_map/ppermute | solution.py:30
  65.7 12.2 %collective-permute-start.14 = (bf16[16,4,128]{2,1,0:T(4,128)(2,1)S(1)}, bf16[16,4,128]{2,1,0:T(4,128)(2,1)S(1)}, u32[]{:S(2)}, u32[]{:S(2)}) collective-permute-start(bf16[16,4,128]{2,1,0:T(4,128)(2,1)S(1)} %get-tuple-element.41), channel_id=1, source_target_pairs={{0,1},{1,2},{2,3},{3,4},{4,5},{5,6},{6,7},{8,9},{9,10},{10,11},{11... | collective-permute-start | bytes 49160 | tf_op jit(solution)/shard_map/ppermute | solution.py:19
  68.0 9.9 %collective-permute-start.15 = (bf16[16,4,128]{2,1,0:T(4,128)(2,1)S(1)}, bf16[16,4,128]{2,1,0:T(4,128)(2,1)S(1)}, u32[]{:S(2)}, u32[]{:S(2)}) collective-permute-start(bf16[16,4,128]{2,1,0:T(4,128)(2,1)S(1)} %get-tuple-element.42), channel_id=1, source_target_pairs={{1,0},{2,1},{3,2},{4,3},{5,4},{6,5},{7,6},{9,8},{10,9},{11,10},{12... | collective-permute-start | bytes 49160 | tf_op jit(solution)/shard_map/ppermute | solution.py:21
  69.5 22.4 %all-to-all-start.1 = ((bf16[16,128,128]{2,1,0:T(8,128)(2,1)}), bf16[16,128,128]{2,1,0:T(8,128)(2,1)}, u32[]{:S(2)}, u32[]{:S(2)}) async-start(bf16[16,128,128]{2,1,0:T(8,128)(2,1)} %shard_map.98), calls=%async_computation.1 | async-start | bytes 1048576 | tf_op jit(solution)/shard_map/all_to_all | solution.py:261
  76.5 1.4 copy-start
  86.1 1.0 copy-start.3
  87.5 1.7 %copy-start.5 = (bf16[128,2048]{1,0:T(8,128)(2,1)}, bf16[128,2048]{1,0:T(8,128)(2,1)S(1)}, u32[]{:S(2)}) copy-start(bf16[128,2048]{1,0:T(8,128)(2,1)S(1)} %fusion.3) | copy-start | bytes 1572868
  89.2 6.7 %copy-start.4 = (bf16[2,1024,128]{1,2,0:T(8,128)(2,1)S(1)}, bf16[2,1024,128]{1,2,0:T(8,128)(2,1)}, u32[]{:S(2)}) copy-start(bf16[2,1024,128]{1,2,0:T(8,128)(2,1)} %all_to_all.40) | copy-start | bytes 1572868
  92.0 30.6 %all-to-all-start = ((bf16[32,130,64]{1,2,0:T(8,128)(2,1)}), bf16[32,130,64]{1,2,0:T(8,128)(2,1)S(1)}, u32[]{:S(2)}, u32[]{:S(2)}) async-start(bf16[32,130,64]{1,2,0:T(8,128)(2,1)} %pad_maximum_fusion.2), calls=%async_computation | async-start | bytes 2097152 | tf_op jit(solution)/shard_map/all_to_all | solution.py:150
  100.4 23.7 %collective-permute-start.16 = (f32[64,1152]{1,0:T(8,128)}, f32[64,1152]{1,0:T(8,128)}, u32[]{:S(2)}, u32[]{:S(2)}) collective-permute-start(f32[64,1152]{1,0:T(8,128)} %get-tuple-element.38), channel_id=1, source_target_pairs={{0,8},{8,0},{16,24},{24,16},{1,9},{9,1},{17,25},{25,17},{2,10},{10... | collective-permute-start | bytes 884744 | tf_op jit(solution)/shard_map/ppermute | solution.py:175
  101.9 22.2 %collective-permute-start.17 = (f32[64,1152]{1,0:T(8,128)S(1)}, f32[64,1152]{1,0:T(8,128)}, u32[]{:S(2)}, u32[]{:S(2)}) collective-permute-start(f32[64,1152]{1,0:T(8,128)S(1)} %get-tuple-element.40), channel_id=1, source_target_pairs={{0,16},{8,24},{16,0},{24,8},{1,17},{9,25},{17,1},{25,9},{2,18},{10... | collective-permute-start | bytes 884744 | tf_op jit(solution)/shard_map/ppermute | solution.py:175
  103.4 20.7 %collective-permute-start.18 = (f32[64,1152]{1,0:T(8,128)S(1)}, f32[64,1152]{1,0:T(8,128)}, u32[]{:S(2)}, u32[]{:S(2)}) collective-permute-start(f32[64,1152]{1,0:T(8,128)S(1)} %get-tuple-element.39), channel_id=1, source_target_pairs={{0,24},{8,16},{16,8},{24,0},{1,25},{9,17},{17,9},{25,1},{2,26},{10... | collective-permute-start | bytes 884744 | tf_op jit(solution)/shard_map/ppermute | solution.py:175
  126.1 10.7 %all-to-all-start.3 = ((f32[32,1,576]{2,1,0:T(1,128)}), f32[32,1,576]{2,1,0:T(1,128)S(1)}, u32[]{:S(2)}, u32[]{:S(2)}) async-start(f32[32,1,576]{2,1,0:T(1,128)} %reshape.118), calls=%async_computation.3 | async-start | bytes 163840 | tf_op jit(solution)/shard_map/all_to_all | solution.py:161
  129.1 10.6 %collective-permute-start.19 = (f32[64,1152]{1,0:T(8,128)S(1)}, f32[64,1152]{1,0:T(8,128)S(1)}, u32[]{:S(2)}, u32[]{:S(2)}) collective-permute-start(f32[64,1152]{1,0:T(8,128)S(1)} %add_add_fusion), channel_id=1, source_target_pairs={{0,8},{8,0},{16,24},{24,16},{1,9},{9,1},{17,25},{25,17},{2,10},{10... | collective-permute-start | bytes 884744 | tf_op jit(solution)/shard_map/ppermute | solution.py:185
  131.0 15.8 %collective-permute-start.20 = (f32[64,1152]{1,0:T(8,128)S(1)}, f32[64,1152]{1,0:T(8,128)S(1)}, u32[]{:S(2)}, u32[]{:S(2)}) collective-permute-start(f32[64,1152]{1,0:T(8,128)S(1)} %add_add_fusion), channel_id=1, source_target_pairs={{0,16},{8,24},{16,0},{24,8},{1,17},{9,25},{17,1},{25,9},{2,18},{10... | collective-permute-start | bytes 884744 | tf_op jit(solution)/shard_map/ppermute | solution.py:185
  132.4 14.3 %collective-permute-start.21 = (f32[64,1152]{1,0:T(8,128)S(1)}, f32[64,1152]{1,0:T(8,128)S(1)}, u32[]{:S(2)}, u32[]{:S(2)}) collective-permute-start(f32[64,1152]{1,0:T(8,128)S(1)} %add_add_fusion), channel_id=1, source_target_pairs={{0,24},{8,16},{16,8},{24,0},{1,25},{9,17},{17,9},{25,1},{2,26},{10... | collective-permute-start | bytes 884744 | tf_op jit(solution)/shard_map/ppermute | solution.py:185

commit v17 on v15

--- a/solution.py
+++ b/solution.py
@@ -41,9 +41,8 @@
 def forward_kernel(pad_ref, w_ref, up_ref, out_ref):
     length = out_ref.shape[1]
     for g in range(out_ref.shape[0]):
-        x = jnp.concatenate(
-            [pad_ref[g, k : k + length, :].astype(jnp.bfloat16) for k in range(KERNEL)], axis=1
-        )
+        rows = pad_ref[g].astype(jnp.float32)
+        x = jnp.concatenate([rows[k : k + length].astype(jnp.bfloat16) for k in range(KERNEL)], axis=1)
         acc = lax.dot_general(x, w_ref[g], (((1,), (1,)), ((), ())), preferred_element_type=jnp.float32)
         sig = 1.0 / (1.0 + jnp.exp(-acc))
         out_ref[g] = (up_ref[g] * sig * (1.0 + acc * (1.0 - sig))).astype(out_ref.dtype)
@@ -54,8 +53,9 @@
     chans = out_ref.shape[2]
     half = KERNEL // 2
     for g in range(out_ref.shape[0]):
+        rows = pad_ref[g].astype(jnp.float32)
         x = jnp.concatenate(
-            [pad_ref[g, 2 * half - k : 2 * half - k + length, :].astype(jnp.bfloat16) for k in range(KERNEL)], axis=1
+            [rows[2 * half - k : 2 * half - k + length].astype(jnp.bfloat16) for k in range(KERNEL)], axis=1
         )
         w = jnp.concatenate([w_ref[g, :, k * chans : (k + 1) * chans] for k in range(KERNEL)], axis=0)
         out_ref[g] = jnp.dot(x, w, preferred_element_type=jnp.float32)
@@ -79,7 +79,7 @@
         cost_estimate=pl.CostEstimate(
             flops=flops,
             transcendentals=up.size,
-            bytes_accessed=padded.size * 4 + weights.size * 2 + up.size * 6,
+            bytes_accessed=padded.size * 2 + weights.size * 2 + up.size * 6,
         ),
     )(padded, weights, up)
 
@@ -100,7 +100,7 @@
         cost_estimate=pl.CostEstimate(
             flops=2 * groups * length * chans * outs * KERNEL,
             transcendentals=0,
-            bytes_accessed=dpad.size * 4 + weights.size * 2 + groups * length * chans * 4,
+            bytes_accessed=dpad.size * 2 + weights.size * 2 + groups * length * chans * 4,
         ),
     )(dpad, weights)
 
@@ -253,9 +253,9 @@
     weights = assemble_shards(kernel, "fsdp", kernel_fetched, kernel_swapped).reshape(GROUPS, chans, KERNEL * chans)
     up_float = upstream[0].astype(jnp.float32)
     up_g = up_float.reshape(length, GROUPS, chans).transpose(1, 0, 2)
-    dconv = conv_dconv(padded.astype(jnp.float32), weights, up_g)
+    dconv = conv_dconv(padded, weights, up_g)
     dpad = with_halo(dconv, "seq", 1, half)
-    dnormed = conv_transpose(dpad.astype(jnp.float32), weights, length)
+    dnormed = conv_transpose(dpad, weights, length)
     if seq_count <= GROUPS:
         group_in = lax.all_to_all(normed_g, "seq", 0, 1, tiled=True)
         group_out = lax.all_to_all(dconv, "seq", 0, 1, tiled=True)

time: 141 us -> 140 us (level)
    ppermute x6, waiting for transfers between devices: 5.64 us -> 9.11 us  [fetch_halves(): lax.ppermute(mine, axis, [(source, source ^ apart) for source in range(co...]
    all_to_all x1, starting transfers between devices: 7.41 us -> 5.1 us  [body(): group_out = lax.all_to_all(dconv, 'seq', 0, 1, tiled=True)]
    convert_element_type x2 -> x0, other arithmetic: 2.19 us -> none  [the longest x1 1.12 us: body(): dnormed = conv_transpose(dpad.astype(jnp.float32), weights, length)]
    all_to_all x1, starting transfers between devices: 3.49 us -> 5.6 us  [body(): group_in = lax.all_to_all(normed_g, 'seq', 0, 1, tiled=True)]
    ppermute x2, waiting for transfers between devices: 1.88 us -> 0.01 us  [with_halo(): lax.ppermute(head, axis, [((i + 1) % count, i) for i in range(ends)])]
    concatenate x1 -> x2, other arithmetic: 1.2 us -> 3.04 us  [with_halo(): jnp.concatenate([lax.ppermute(tail, axis, [(i, (i + 1) % count) for i in...]
    ppermute x6, starting transfers between devices: 3.99 us -> 2.25 us  [from_partner(): return lax.ppermute(value, axis, pairs)]
    ppermute x2, starting transfers between devices: 4.47 us -> 6.06 us  [with_halo(): lax.ppermute(tail, axis, [(i, (i + 1) % count) for i in range(ends)])]
  transfers between devices with their start and end apart: 26 -> 26, of which waited for: 11 -> 12; matrix products, arithmetic and copies ran while one was open for 24% -> 24% of each run, Pallas kernels for 7% -> 7%
where the time goes in v17:
time: 140 us; the launch traced here: 138 us
  starting transfers between devices  42.9 us (31%)
  waiting for transfers between devices  42.6 us (30%)
  local copies, waits for them, and re-layouts  20.3 us (14%)
  other arithmetic  16.7 us (12%)
  Pallas kernels  10.3 us (7%)
  matrix products  4.46 us (3%)
    all_to_all x1, waiting for transfers between devices, table_and_gain(): got = lax.all_to_all(send, every, 0, 0, tiled=True)  18.4 us
    ppermute x6, waiting for transfers between devices, fetch_halves(): lax.ppermute(mine, axis, [(source, source ^ apart) for source in range(co...  9.11 us
    ppermute x6, starting transfers between devices, fetch_halves(): lax.ppermute(mine, axis, [(source, source ^ apart) for source in range(co...  8.34 us
    ppermute x3, waiting for transfers between devices, gather_by_permutes(): pieces.append(lax.ppermute(total, axis, pairs))  6.79 us
    ppermute x2, starting transfers between devices, with_halo(): lax.ppermute(tail, axis, [(i, (i + 1) % count) for i in range(ends)])  6.06 us
    all_to_all x1, starting transfers between devices, body(): group_in = lax.all_to_all(normed_g, 'seq', 0, 1, tiled=True)  5.6 us
    pallas_call x1, Pallas kernels, conv_dconv(): pl.pallas_call(forward_kernel, grid=(groups // step,), in_specs=[pl.Block...  5.19 us
    pallas_call x1, Pallas kernels, conv_transpose(): pl.pallas_call(backward_kernel, grid=(groups // step,), in_specs=[pl.Bloc...  5.11 us
  transfers between devices with their start and end apart: 26, of which 12 were waited for; matrix products, arithmetic and copies ran while one was open for 24% of the time, Pallas kernels for 7%

profile of v17, /device:TPU:0, one launch (start us, length us, event | category | flops | bytes accessed | tf_op | source)
XLA Modules:
  0.0 138.3 jit_solution(11302485454470964043)
XLA Ops:
  0.6 0.9 constant_dynamic-slice_fusion.4
  1.6 4.0 %collective-permute-start.4 = (bf16[32,2048]{1,0:T(8,128)(2,1)S(1)}, bf16[32,2048]{1,0:T(8,128)(2,1)S(1)}, u32[]{:S(2)}, u32[]{:S(2)}) collective-permute-start(bf16[32,2048]{1,0:T(8,128)(2,1)S(1)} %constant_dynamic-slice_fusion.4), channel_id=1, source_target_pairs={{0,24},{8,16},{16,8},{24,0},{1,25},{9,17},{17,9},{25,1},{2,26},{10... | collective-permute-start | bytes 393224 | tf_op jit(solution)/shard_map/ppermute | solution.py:198
  5.5 0.5 collective-permute-start
  6.2 3.7 %collective-permute-done.4 = bf16[32,2048]{1,0:T(8,128)(2,1)S(1)} collective-permute-done((bf16[32,2048]{1,0:T(8,128)(2,1)S(1)}, bf16[32,2048]{1,0:T(8,128)(2,1)S(1)}, u32[]{:S(2)}, u32[]{:S(2)}) %collective-permute-start.4) | collective-permute-done | bytes 131104 | tf_op jit(solution)/shard_map/ppermute | solution.py:198
  9.9 1.9 %constant_dynamic-slice_fusion.3 = bf16[256,1152]{1,0:T(8,128)(2,1)} fusion(bf16[512,1152]{1,0:T(8,128)(2,1)} %param.14, s32[]{:T(128)S(6)} %select_n.123), kind=kLoop, calls=%fused_computation.94 | loop fusion | bytes 1179652 | tf_op jit(solution)/shard_map/dynamic_slice | solution.py:196
  11.8 3.0 %collective-permute-start.6 = (bf16[256,1152]{1,0:T(8,128)(2,1)}, bf16[256,1152]{1,0:T(8,128)(2,1)S(1)}, u32[]{:S(2)}, u32[]{:S(2)}) collective-permute-start(bf16[256,1152]{1,0:T(8,128)(2,1)} %constant_dynamic-slice_fusion.3), channel_id=1, source_target_pairs={{0,24},{8,16},{16,8},{24,0},{1,25},{9,17},{17,9},{25,1},{2,26},{10... | collective-permute-start | bytes 1769480 | tf_op jit(solution)/shard_map/ppermute | solution.py:198
  15.3 0.8 collective-permute-done.1
  16.4 0.7 copy-done.6
  17.4 0.9 copy-done.8
  18.3 0.4 multiply_reduce_fusion.2
  19.4 1.0 copy.64
  20.4 0.8 fusion.40
  21.2 1.3 collective-permute-start.8
  22.5 3.0 %collective-permute-start.7 = (bf16[16,4,128]{2,1,0:T(4,128)(2,1)S(1)}, bf16[16,4,128]{2,1,0:T(4,128)(2,1)S(1)}, u32[]{:S(2)}, u32[]{:S(2)}) collective-permute-start(bf16[16,4,128]{2,1,0:T(4,128)(2,1)S(1)} %get-tuple-element.57), channel_id=1, source_target_pairs={{0,1},{1,2},{2,3},{3,4},{4,5},{5,6},{6,7},{8,9},{9,10},{10,11},{11... | collective-permute-start | bytes 49160 | tf_op jit(solution)/shard_map/ppermute | solution.py:19
  25.6 0.6 collective-permute-start.9
  26.4 2.0 %pad_maximum_fusion.6.pad_ref = bf16[16,136,128]{2,1,0:T(8,128)(2,1)} fusion(bf16[16,4,128]{2,1,0:T(4,128)(2,1)S(1)} %collective-permute-done.8, bf16[16,128,128]{2,1,0:T(8,128)(2,1)} %bitcast.12, bf16[16,4,128]{2,1,0:T(4,128)(2,1)S(1)} %collective-permute-done.7), kind=kLoop, calls=%fused_computation.47 | loop fusion | flops 1671168 | bytes 1114112 | tf_op jit(solution)/shard_map/concatenate | solution.py:17
  28.4 0.5 collective-permute-done.6
  29.0 1.0 collective-permute-start.13
  30.1 1.3 copy.66
  31.4 5.6 %all-to-all-start.2 = ((bf16[16,128,128]{2,1,0:T(8,128)(2,1)}), bf16[16,128,128]{2,1,0:T(8,128)(2,1)S(1)}, u32[]{:S(2)}, u32[]{:S(2)}) async-start(bf16[16,128,128]{2,1,0:T(8,128)(2,1)} %bitcast.12), calls=%async_computation.2 | async-start | bytes 1048576 | tf_op jit(solution)/shard_map/all_to_all | solution.py:260
  37.0 4.7 %collective-permute-done.9 = bf16[256,1152]{1,0:T(8,128)(2,1)} collective-permute-done((bf16[256,1152]{1,0:T(8,128)(2,1)}, bf16[256,1152]{1,0:T(8,128)(2,1)}, u32[]{:S(2)}, u32[]{:S(2)}) %collective-permute-start.9) | collective-permute-done | bytes 589856 | tf_op jit(solution)/shard_map/ppermute | solution.py:198
  41.7 0.5 collective-permute-start.10
  42.7 1.2 broadcast_select_fusion.1
  44.1 1.2 broadcast_select_fusion.5
  45.3 1.2 broadcast_select_fusion.3
  46.7 1.1 copy-done.1
  47.8 0.7 pad_maximum_fusion
  48.5 0.4 dynamic-slice_bitcast_fusion.3
  48.9 2.8 %pad_maximum_fusion.1 = bf16[2048,1152]{1,0:T(8,128)(2,1)} fusion(bf16[512,1152]{1,0:T(8,128)(2,1)S(1)} %get-tuple-element.35, bf16[512,1152]{1,0:T(8,128)(2,1)S(1)} %get-tuple-element.36, bf16[512,1152]{1,0:T(8,128)(2,1)S(1)} %get-tuple-element.37, bf16[512,1152]{1,0:T(8,128)(2,1)S(1)} %get-tuple-element.34), kind=kLoop, calls=%fused_computation.1 | loop fusion | flops 18874368 | bytes 9437184 | tf_op jit(solution)/shard_map/concatenate | solution.py:217
  51.7 5.2 %shard_map.98 = bf16[16,128,128]{2,1,0:T(8,128)(2,1)} custom-call(bf16[16,136,128]{2,1,0:T(8,128)(2,1)} %pad_maximum_fusion.6.pad_ref, bf16[16,128,1152]{2,1,0:T(8,128)(2,1)} %bitcast.94, f32[16,128,128]{2,1,0:T(8,128)} %bitcast.100), custom_call_target="tpu_custom_call" | custom-call | flops 603979776 | bytes 6848512 | tf_op jit(solution)/shard_map/pallas_call | solution.py:69
  56.9 0.8 fusion.39
  57.7 1.3 collective-permute-start.15
  59.0 3.0 %collective-permute-start.14 = (bf16[16,4,128]{2,1,0:T(4,128)(2,1)S(1)}, bf16[16,4,128]{2,1,0:T(4,128)(2,1)S(1)}, u32[]{:S(2)}, u32[]{:S(2)}) collective-permute-start(bf16[16,4,128]{2,1,0:T(4,128)(2,1)S(1)} %get-tuple-element.55), channel_id=1, source_target_pairs={{0,1},{1,2},{2,3},{3,4},{4,5},{5,6},{6,7},{8,9},{9,10},{10,11},{11... | collective-permute-start | bytes 49160 | tf_op jit(solution)/shard_map/ppermute | solution.py:19
  62.3 5.1 %all-to-all-start.1 = ((bf16[16,128,128]{2,1,0:T(8,128)(2,1)}), bf16[16,128,128]{2,1,0:T(8,128)(2,1)}, u32[]{:S(2)}, u32[]{:S(2)}) async-start(bf16[16,128,128]{2,1,0:T(8,128)(2,1)} %shard_map.98), calls=%async_computation.1 | async-start | bytes 1048576 | tf_op jit(solution)/shard_map/all_to_all | solution.py:261
  67.7 1.0 all_to_all.40
  68.8 1.0 pad_maximum_fusion.7.pad_ref
  69.8 5.1 %shard_map.99 = f32[16,128,128]{2,1,0:T(8,128)} custom-call(bf16[16,136,128]{2,1,0:T(8,128)(2,1)} %pad_maximum_fusion.7.pad_ref, bf16[16,128,1152]{2,1,0:T(8,128)(2,1)} %bitcast.95), custom_call_target="tpu_custom_call" | custom-call | flops 603979776 | bytes 6324224 | tf_op jit(solution)/shard_map/pallas_call | solution.py:91
  74.9 1.6 %copy.67 = f32[128,16,128]{0,2,1:T(8,128)S(1)} copy(f32[128,16,128]{2,0,1:T(8,128)} %bitcast.101) | data formatting | bytes 2097152 | tf_op jit(solution)/shard_map/transpose | solution.py:272
  77.2 0.7 copy-done.3
  77.8 0.4 fusion.10
  78.6 1.2 pad_maximum_fusion.5
  79.9 3.1 %all-to-all-done.1 = bf16[16,128,128]{2,1,0:T(8,128)(2,1)} async-done(((bf16[16,128,128]{2,1,0:T(8,128)(2,1)}), bf16[16,128,128]{2,1,0:T(8,128)(2,1)}, u32[]{:S(2)}, u32[]{:S(2)}) %all-to-all-start.1) | async-done | bytes 524320 | tf_op jit(solution)/shard_map/all_to_all | solution.py:261
  83.0 2.8 %all-to-all-start = ((bf16[32,130,64]{1,2,0:T(8,128)(2,1)}), bf16[32,130,64]{1,2,0:T(8,128)(2,1)S(1)}, u32[]{:S(2)}, u32[]{:S(2)}) async-start(bf16[32,130,64]{1,2,0:T(8,128)(2,1)} %pad_maximum_fusion.5), calls=%async_computation | async-start | bytes 2097152 | tf_op jit(solution)/shard_map/all_to_all | solution.py:150
  85.8 1.1 copy.77
  90.2 0.4 copy.79
  90.6 0.8 constant_dynamic-slice_fusion.2
  91.4 2.5 %collective-permute-start.18 = (f32[64,1152]{1,0:T(8,128)}, f32[64,1152]{1,0:T(8,128)}, u32[]{:S(2)}, u32[]{:S(2)}) collective-permute-start(f32[64,1152]{1,0:T(8,128)} %get-tuple-element.43), channel_id=1, source_target_pairs={{0,24},{8,16},{16,8},{24,0},{1,25},{9,17},{17,9},{25,1},{2,26},{10... | collective-permute-start | bytes 884744 | tf_op jit(solution)/shard_map/ppermute | solution.py:175
  93.8 0.6 collective-permute-start.17
  94.4 0.5 collective-permute-start.16
  94.9 18.4 %all-to-all-done = bf16[32,130,64]{1,2,0:T(8,128)(2,1)S(1)} async-done(((bf16[32,130,64]{1,2,0:T(8,128)(2,1)}), bf16[32,130,64]{1,2,0:T(8,128)(2,1)S(1)}, u32[]{:S(2)}, u32[]{:S(2)}) %all-to-all-start) | async-done | bytes 532512 | tf_op jit(solution)/shard_map/all_to_all | solution.py:150
  113.8 0.9 fusion.2
  114.8 1.2 add_add_fusion
  116.0 0.8 reshape.118
  116.8 3.1 %all-to-all-start.3 = ((f32[32,1,576]{2,1,0:T(1,128)}), f32[32,1,576]{2,1,0:T(1,128)S(1)}, u32[]{:S(2)}, u32[]{:S(2)}) async-start(f32[32,1,576]{2,1,0:T(1,128)} %reshape.118), calls=%async_computation.3 | async-start | bytes 163840 | tf_op jit(solution)/shard_map/all_to_all | solution.py:161
  119.9 2.7 %collective-permute-start.21 = (f32[64,1152]{1,0:T(8,128)S(1)}, f32[64,1152]{1,0:T(8,128)S(1)}, u32[]{:S(2)}, u32[]{:S(2)}) collective-permute-start(f32[64,1152]{1,0:T(8,128)S(1)} %add_add_fusion), channel_id=1, source_target_pairs={{0,24},{8,16},{16,8},{24,0},{1,25},{9,17},{17,9},{25,1},{2,26},{10... | collective-permute-start | bytes 884744 | tf_op jit(solution)/shard_map/ppermute | solution.py:185
  122.6 0.6 collective-permute-start.20
  123.4 4.1 %all-to-all-done.3 = f32[32,1,576]{2,1,0:T(1,128)S(1)} async-done(((f32[32,1,576]{2,1,0:T(1,128)}), f32[32,1,576]{2,1,0:T(1,128)S(1)}, u32[]{:S(2)}, u32[]{:S(2)}) %all-to-all-start.3) | async-done | bytes 73760 | tf_op jit(solution)/shard_map/all_to_all | solution.py:161
  127.5 0.5 broadcast.56
  128.0 0.8 reduce.7
  129.0 0.7 reshape.106
  129.7 0.6 slice_reduce_fusion
  130.3 1.1 collective-permute-done.21
  131.3 5.7 %collective-permute-done.20 = f32[64,1152]{1,0:T(8,128)S(1)} collective-permute-done((f32[64,1152]{1,0:T(8,128)S(1)}, f32[64,1152]{1,0:T(8,128)S(1)}, u32[]{:S(2)}, u32[]{:S(2)}) %collective-permute-start.20) | collective-permute-done | bytes 294944 | tf_op jit(solution)/shard_map/ppermute | solution.py:185
  137.2 1.1 pad_maximum_fusion.3
  (86 shorter events, 9.2 us)
Async XLA Ops:
  1.6 8.3 %collective-permute-start.4 = (bf16[32,2048]{1,0:T(8,128)(2,1)S(1)}, bf16[32,2048]{1,0:T(8,128)(2,1)S(1)}, u32[]{:S(2)}, u32[]{:S(2)}) collective-permute-start(bf16[32,2048]{1,0:T(8,128)(2,1)S(1)} %constant_dynamic-slice_fusion.4), channel_id=1, source_target_pairs={{0,24},{8,16},{16,8},{24,0},{1,25},{9,17},{17,9},{25,1},{2,26},{10... | collective-permute-start | bytes 393224 | tf_op jit(solution)/shard_map/ppermute | solution.py:198
  5.5 9.2 %collective-permute-start = (bf16[32,2048]{1,0:T(8,128)(2,1)S(1)}, bf16[32,2048]{1,0:T(8,128)(2,1)S(1)}, u32[]{:S(2)}, u32[]{:S(2)}) collective-permute-start(bf16[32,2048]{1,0:T(8,128)(2,1)S(1)} %constant_dynamic-slice_fusion.4), channel_id=1, source_target_pairs={{0,8},{8,0},{16,24},{24,16},{1,9},{9,1},{17,25},{25,17},{2,10},{10... | collective-permute-start | bytes 393224 | tf_op jit(solution)/shard_map/ppermute | solution.py:198
  6.1 8.9 %collective-permute-start.2 = (bf16[32,2048]{1,0:T(8,128)(2,1)S(1)}, bf16[32,2048]{1,0:T(8,128)(2,1)S(1)}, u32[]{:S(2)}, u32[]{:S(2)}) collective-permute-start(bf16[32,2048]{1,0:T(8,128)(2,1)S(1)} %constant_dynamic-slice_fusion.4), channel_id=1, source_target_pairs={{0,16},{8,24},{16,0},{24,8},{1,17},{9,25},{17,1},{25,9},{2,18},{10... | collective-permute-start | bytes 393224 | tf_op jit(solution)/shard_map/ppermute | solution.py:198
  9.9 5.4 %collective-permute-start.5 = (bf16[32,2048]{1,0:T(8,128)(2,1)S(1)}, bf16[32,2048]{1,0:T(8,128)(2,1)S(1)}, u32[]{:S(2)}, u32[]{:S(2)}) collective-permute-start(bf16[32,2048]{1,0:T(8,128)(2,1)S(1)} %collective-permute-done.4), channel_id=1, source_target_pairs={{0,1},{1,0},{2,3},{3,2},{4,5},{5,4},{6,7},{7,6},{8,9},{9,8},{10,11... | collective-permute-start | bytes 393224 | tf_op jit(solution)/shard_map/ppermute | solution.py:30
  11.8 17.2 %collective-permute-start.6 = (bf16[256,1152]{1,0:T(8,128)(2,1)}, bf16[256,1152]{1,0:T(8,128)(2,1)S(1)}, u32[]{:S(2)}, u32[]{:S(2)}) collective-permute-start(bf16[256,1152]{1,0:T(8,128)(2,1)} %constant_dynamic-slice_fusion.3), channel_id=1, source_target_pairs={{0,24},{8,16},{16,8},{24,0},{1,25},{9,17},{17,9},{25,1},{2,26},{10... | collective-permute-start | bytes 1769480 | tf_op jit(solution)/shard_map/ppermute | solution.py:198
  14.8 1.3 collective-permute-start.1
  15.0 1.3 collective-permute-start.3
  16.1 1.0 copy-start.6
  17.2 1.0 copy-start.8
  17.2 1.0 copy-start.9
  18.3 0.7 copy-start.7
  19.4 10.5 %copy-start.2 = (bf16[1,128,2048]{2,1,0:T(8,128)(2,1)S(1)}, bf16[1,128,2048]{2,1,0:T(8,128)(2,1)}, u32[]{:S(2)}) copy-start(bf16[1,128,2048]{2,1,0:T(8,128)(2,1)} %param.15) | copy-start | bytes 1572868
  21.2 5.1 %collective-permute-start.8 = (bf16[16,4,128]{2,1,0:T(4,128)(2,1)S(1)}, bf16[16,4,128]{2,1,0:T(4,128)(2,1)S(1)}, u32[]{:S(2)}, u32[]{:S(2)}) collective-permute-start(bf16[16,4,128]{2,1,0:T(4,128)(2,1)S(1)} %get-tuple-element.58), channel_id=1, source_target_pairs={{1,0},{2,1},{3,2},{4,3},{5,4},{6,5},{7,6},{9,8},{10,9},{11,10},{12... | collective-permute-start | bytes 49160 | tf_op jit(solution)/shard_map/ppermute | solution.py:21
  22.5 3.9 %collective-permute-start.7 = (bf16[16,4,128]{2,1,0:T(4,128)(2,1)S(1)}, bf16[16,4,128]{2,1,0:T(4,128)(2,1)S(1)}, u32[]{:S(2)}, u32[]{:S(2)}) collective-permute-start(bf16[16,4,128]{2,1,0:T(4,128)(2,1)S(1)} %get-tuple-element.57), channel_id=1, source_target_pairs={{0,1},{1,2},{2,3},{3,4},{4,5},{5,6},{6,7},{8,9},{9,10},{10,11},{11... | collective-permute-start | bytes 49160 | tf_op jit(solution)/shard_map/ppermute | solution.py:19
  25.6 16.2 %collective-permute-start.9 = (bf16[256,1152]{1,0:T(8,128)(2,1)}, bf16[256,1152]{1,0:T(8,128)(2,1)}, u32[]{:S(2)}, u32[]{:S(2)}) collective-permute-start(bf16[256,1152]{1,0:T(8,128)(2,1)} %constant_dynamic-slice_fusion.3), channel_id=1, source_target_pairs={{0,8},{8,0},{16,24},{24,16},{1,9},{9,1},{17,25},{25,17},{2,10},{10... | collective-permute-start | bytes 1769480 | tf_op jit(solution)/shard_map/ppermute | solution.py:198
  26.2 16.3 %collective-permute-start.11 = (bf16[256,1152]{1,0:T(8,128)(2,1)}, bf16[256,1152]{1,0:T(8,128)(2,1)}, u32[]{:S(2)}, u32[]{:S(2)}) collective-permute-start(bf16[256,1152]{1,0:T(8,128)(2,1)} %constant_dynamic-slice_fusion.3), channel_id=1, source_target_pairs={{0,16},{8,24},{16,0},{24,8},{1,17},{9,25},{17,1},{25,9},{2,18},{10... | collective-permute-start | bytes 1769480 | tf_op jit(solution)/shard_map/ppermute | solution.py:198
  29.0 13.7 %collective-permute-start.13 = (bf16[256,1152]{1,0:T(8,128)(2,1)S(1)}, bf16[256,1152]{1,0:T(8,128)(2,1)}, u32[]{:S(2)}, u32[]{:S(2)}) collective-permute-start(bf16[256,1152]{1,0:T(8,128)(2,1)S(1)} %collective-permute-done.6), channel_id=1, source_target_pairs={{0,1},{1,0},{2,3},{3,2},{4,5},{5,4},{6,7},{7,6},{8,9},{9,8},{10,11... | collective-permute-start | bytes 1769480 | tf_op jit(solution)/shard_map/ppermute | solution.py:30
  31.4 30.9 %all-to-all-start.2 = ((bf16[16,128,128]{2,1,0:T(8,128)(2,1)}), bf16[16,128,128]{2,1,0:T(8,128)(2,1)S(1)}, u32[]{:S(2)}, u32[]{:S(2)}) async-start(bf16[16,128,128]{2,1,0:T(8,128)(2,1)} %bitcast.12), calls=%async_computation.2 | async-start | bytes 1048576 | tf_op jit(solution)/shard_map/all_to_all | solution.py:260
  41.7 2.4 %collective-permute-start.10 = (bf16[256,1152]{1,0:T(8,128)(2,1)}, bf16[256,1152]{1,0:T(8,128)(2,1)S(1)}, u32[]{:S(2)}, u32[]{:S(2)}) collective-permute-start(bf16[256,1152]{1,0:T(8,128)(2,1)} %collective-permute-done.9), channel_id=1, source_target_pairs={{0,1},{1,0},{2,3},{3,2},{4,5},{5,4},{6,7},{7,6},{8,9},{9,8},{10,11... | collective-permute-start | bytes 1769480 | tf_op jit(solution)/shard_map/ppermute | solution.py:30
  42.5 2.9 %collective-permute-start.12 = (bf16[256,1152]{1,0:T(8,128)(2,1)}, bf16[256,1152]{1,0:T(8,128)(2,1)S(1)}, u32[]{:S(2)}, u32[]{:S(2)}) collective-permute-start(bf16[256,1152]{1,0:T(8,128)(2,1)} %collective-permute-done.11), channel_id=1, source_target_pairs={{0,1},{1,0},{2,3},{3,2},{4,5},{5,4},{6,7},{7,6},{8,9},{9,8},{10,11... | collective-permute-start | bytes 1769480 | tf_op jit(solution)/shard_map/ppermute | solution.py:30
  46.5 1.3 copy-start.1
  57.7 11.0 %collective-permute-start.15 = (bf16[16,4,128]{2,1,0:T(4,128)(2,1)S(1)}, bf16[16,4,128]{2,1,0:T(4,128)(2,1)S(1)}, u32[]{:S(2)}, u32[]{:S(2)}) collective-permute-start(bf16[16,4,128]{2,1,0:T(4,128)(2,1)S(1)} %get-tuple-element.56), channel_id=1, source_target_pairs={{1,0},{2,1},{3,2},{4,3},{5,4},{6,5},{7,6},{9,8},{10,9},{11,10},{12... | collective-permute-start | bytes 49160 | tf_op jit(solution)/shard_map/ppermute | solution.py:21
  59.0 9.7 %collective-permute-start.14 = (bf16[16,4,128]{2,1,0:T(4,128)(2,1)S(1)}, bf16[16,4,128]{2,1,0:T(4,128)(2,1)S(1)}, u32[]{:S(2)}, u32[]{:S(2)}) collective-permute-start(bf16[16,4,128]{2,1,0:T(4,128)(2,1)S(1)} %get-tuple-element.55), channel_id=1, source_target_pairs={{0,1},{1,2},{2,3},{3,4},{4,5},{5,6},{6,7},{8,9},{9,10},{10,11},{11... | collective-permute-start | bytes 49160 | tf_op jit(solution)/shard_map/ppermute | solution.py:19
  62.3 20.7 %all-to-all-start.1 = ((bf16[16,128,128]{2,1,0:T(8,128)(2,1)}), bf16[16,128,128]{2,1,0:T(8,128)(2,1)}, u32[]{:S(2)}, u32[]{:S(2)}) async-start(bf16[16,128,128]{2,1,0:T(8,128)(2,1)} %shard_map.98), calls=%async_computation.1 | async-start | bytes 1048576 | tf_op jit(solution)/shard_map/all_to_all | solution.py:261
  67.4 1.4 copy-start
  76.8 1.0 copy-start.3
  78.2 1.6 %copy-start.5 = (bf16[128,2048]{1,0:T(8,128)(2,1)}, bf16[128,2048]{1,0:T(8,128)(2,1)S(1)}, u32[]{:S(2)}) copy-start(bf16[128,2048]{1,0:T(8,128)(2,1)S(1)} %fusion.10) | copy-start | bytes 1572868
  79.9 7.0 %copy-start.4 = (bf16[2,1024,128]{1,2,0:T(8,128)(2,1)S(1)}, bf16[2,1024,128]{1,2,0:T(8,128)(2,1)}, u32[]{:S(2)}) copy-start(bf16[2,1024,128]{1,2,0:T(8,128)(2,1)} %all_to_all.40) | copy-start | bytes 1572868
  83.0 30.2 %all-to-all-start = ((bf16[32,130,64]{1,2,0:T(8,128)(2,1)}), bf16[32,130,64]{1,2,0:T(8,128)(2,1)S(1)}, u32[]{:S(2)}, u32[]{:S(2)}) async-start(bf16[32,130,64]{1,2,0:T(8,128)(2,1)} %pad_maximum_fusion.5), calls=%async_computation | async-start | bytes 2097152 | tf_op jit(solution)/shard_map/all_to_all | solution.py:150
  91.4 23.4 %collective-permute-start.18 = (f32[64,1152]{1,0:T(8,128)}, f32[64,1152]{1,0:T(8,128)}, u32[]{:S(2)}, u32[]{:S(2)}) collective-permute-start(f32[64,1152]{1,0:T(8,128)} %get-tuple-element.43), channel_id=1, source_target_pairs={{0,24},{8,16},{16,8},{24,0},{1,25},{9,17},{17,9},{25,1},{2,26},{10... | collective-permute-start | bytes 884744 | tf_op jit(solution)/shard_map/ppermute | solution.py:175
  93.8 20.9 %collective-permute-start.17 = (f32[64,1152]{1,0:T(8,128)S(1)}, f32[64,1152]{1,0:T(8,128)}, u32[]{:S(2)}, u32[]{:S(2)}) collective-permute-start(f32[64,1152]{1,0:T(8,128)S(1)} %get-tuple-element.44), channel_id=1, source_target_pairs={{0,16},{8,24},{16,0},{24,8},{1,17},{9,25},{17,1},{25,9},{2,18},{10... | collective-permute-start | bytes 884744 | tf_op jit(solution)/shard_map/ppermute | solution.py:175
  94.4 20.4 %collective-permute-start.16 = (f32[64,1152]{1,0:T(8,128)S(1)}, f32[64,1152]{1,0:T(8,128)}, u32[]{:S(2)}, u32[]{:S(2)}) collective-permute-start(f32[64,1152]{1,0:T(8,128)S(1)} %get-tuple-element.42), channel_id=1, source_target_pairs={{0,8},{8,0},{16,24},{24,16},{1,9},{9,1},{17,25},{25,17},{2,10},{10... | collective-permute-start | bytes 884744 | tf_op jit(solution)/shard_map/ppermute | solution.py:175
  116.8 10.7 %all-to-all-start.3 = ((f32[32,1,576]{2,1,0:T(1,128)}), f32[32,1,576]{2,1,0:T(1,128)S(1)}, u32[]{:S(2)}, u32[]{:S(2)}) async-start(f32[32,1,576]{2,1,0:T(1,128)} %reshape.118), calls=%async_computation.3 | async-start | bytes 163840 | tf_op jit(solution)/shard_map/all_to_all | solution.py:161
  119.9 11.5 %collective-permute-start.21 = (f32[64,1152]{1,0:T(8,128)S(1)}, f32[64,1152]{1,0:T(8,128)S(1)}, u32[]{:S(2)}, u32[]{:S(2)}) collective-permute-start(f32[64,1152]{1,0:T(8,128)S(1)} %add_add_fusion), channel_id=1, source_target_pairs={{0,24},{8,16},{16,8},{24,0},{1,25},{9,17},{17,9},{25,1},{2,26},{10... | collective-permute-start | bytes 884744 | tf_op jit(solution)/shard_map/ppermute | solution.py:185
  122.6 14.5 %collective-permute-start.20 = (f32[64,1152]{1,0:T(8,128)S(1)}, f32[64,1152]{1,0:T(8,128)S(1)}, u32[]{:S(2)}, u32[]{:S(2)}) collective-permute-start(f32[64,1152]{1,0:T(8,128)S(1)} %add_add_fusion), channel_id=1, source_target_pairs={{0,16},{8,24},{16,0},{24,8},{1,17},{9,25},{17,1},{25,9},{2,18},{10... | collective-permute-start | bytes 884744 | tf_op jit(solution)/shard_map/ppermute | solution.py:185
  123.2 13.9 %collective-permute-start.19 = (f32[64,1152]{1,0:T(8,128)S(1)}, f32[64,1152]{1,0:T(8,128)S(1)}, u32[]{:S(2)}, u32[]{:S(2)}) collective-permute-start(f32[64,1152]{1,0:T(8,128)S(1)} %add_add_fusion), channel_id=1, source_target_pairs={{0,8},{8,0},{16,24},{24,16},{1,9},{9,1},{17,25},{25,17},{2,10},{10... | collective-permute-start | bytes 884744 | tf_op jit(solution)/shard_map/ppermute | solution.py:185

commit v18 on v17

--- a/solution.py
+++ b/solution.py
@@ -246,15 +246,16 @@
     inv = lax.rsqrt(jnp.mean(mixed * mixed, axis=-1, keepdims=True) + 1e-06)
     normed = (mixed * inv * norm_gain).astype(jnp.bfloat16)
     normed_g = normed.reshape(length, GROUPS, chans).transpose(1, 0, 2)
-    padded = with_halo(normed_g, "seq", 1, half)
+    padded = with_halo(normed_g, "seq", 1, 2 * half)
+    up_pad = with_halo(upstream[0].reshape(length, GROUPS, chans).transpose(1, 0, 2), "seq", 1, half)
     far_piece, padded = lax.optimization_barrier((kernel_fetched[far], padded))
     kernel_fetched = {**near, far: far_piece}
     kernel_swapped = {**near_swapped, **swap_halves({far: far_piece})}
     weights = assemble_shards(kernel, "fsdp", kernel_fetched, kernel_swapped).reshape(GROUPS, chans, KERNEL * chans)
     up_float = upstream[0].astype(jnp.float32)
     up_g = up_float.reshape(length, GROUPS, chans).transpose(1, 0, 2)
-    dconv = conv_dconv(padded, weights, up_g)
-    dpad = with_halo(dconv, "seq", 1, half)
+    dpad = conv_dconv(padded, weights, up_pad.astype(jnp.float32))
+    dconv = dpad[:, half : half + length]
     dnormed = conv_transpose(dpad, weights, length)
     if seq_count <= GROUPS:
         group_in = lax.all_to_all(normed_g, "seq", 0, 1, tiled=True)

time: 140 us -> 146 us (1.043)
  waiting for transfers between devices: 42.6 us -> 46.6 us
  starting transfers between devices: 42.9 us -> 44.5 us
    all_to_all x1, waiting for transfers between devices: 3.11 us -> 9.85 us  [body(): group_out = lax.all_to_all(dconv, 'seq', 0, 1, tiled=True)]
    ppermute x6, waiting for transfers between devices: 9.11 us -> 4.35 us  [fetch_halves(): lax.ppermute(mine, axis, [(source, source ^ apart) for source in range(co...]
    all_to_all x1, starting transfers between devices: 5.6 us -> 7.88 us  [body(): group_in = lax.all_to_all(normed_g, 'seq', 0, 1, tiled=True)]
    slice x0 -> x1, local copies, waits for them, and re-layouts: none -> 2.03 us  [body(): dconv = dpad[:, half:half + length]]
    concatenate x2 -> x1, other arithmetic: 3.04 us -> 1.92 us  [with_halo(): jnp.concatenate([lax.ppermute(tail, axis, [(i, (i + 1) % count) for i in...]
    unnamed x23 -> x18, local copies, waits for them, and re-layouts: 4.76 us -> 4.36 us
where the time goes in v18:
time: 146 us; the launch traced here: 145 us
  waiting for transfers between devices  46.6 us (32%)
  starting transfers between devices  44.5 us (30%)
  local copies, waits for them, and re-layouts  20.1 us (14%)
  other arithmetic  17.4 us (12%)
  Pallas kernels  10.4 us (7%)
  matrix products  4.45 us (3%)
    all_to_all x1, waiting for transfers between devices, table_and_gain(): got = lax.all_to_all(send, every, 0, 0, tiled=True)  19.4 us
    all_to_all x1, waiting for transfers between devices, body(): group_out = lax.all_to_all(dconv, 'seq', 0, 1, tiled=True)  9.85 us
    ppermute x6, starting transfers between devices, fetch_halves(): lax.ppermute(mine, axis, [(source, source ^ apart) for source in range(co...  8.34 us
    all_to_all x1, starting transfers between devices, body(): group_in = lax.all_to_all(normed_g, 'seq', 0, 1, tiled=True)  7.88 us
    ppermute x3, waiting for transfers between devices, gather_by_permutes(): pieces.append(lax.ppermute(total, axis, pairs))  6.79 us
    ppermute x2, starting transfers between devices, with_halo(): lax.ppermute(tail, axis, [(i, (i + 1) % count) for i in range(ends)])  6.06 us
    pallas_call x1, Pallas kernels, conv_dconv(): pl.pallas_call(forward_kernel, grid=(groups // step,), in_specs=[pl.Block...  5.31 us
    pallas_call x1, Pallas kernels, conv_transpose(): pl.pallas_call(backward_kernel, grid=(groups // step,), in_specs=[pl.Bloc...  5.11 us
  transfers between devices with their start and end apart: 26, of which 12 were waited for; matrix products, arithmetic and copies ran while one was open for 24% of the time, Pallas kernels for 7%

profile of v18, /device:TPU:0, one launch (start us, length us, event | category | flops | bytes accessed | tf_op | source)
XLA Modules:
  0.0 144.7 jit_solution(202964500384107972)
XLA Ops:
  0.6 0.9 constant_dynamic-slice_fusion.4
  1.6 4.0 %collective-permute-start.4 = (bf16[32,2048]{1,0:T(8,128)(2,1)S(1)}, bf16[32,2048]{1,0:T(8,128)(2,1)S(1)}, u32[]{:S(2)}, u32[]{:S(2)}) collective-permute-start(bf16[32,2048]{1,0:T(8,128)(2,1)S(1)} %constant_dynamic-slice_fusion.4), channel_id=1, source_target_pairs={{0,24},{8,16},{16,8},{24,0},{1,25},{9,17},{17,9},{25,1},{2,26},{10... | collective-permute-start | bytes 393224 | tf_op jit(solution)/shard_map/ppermute | solution.py:198
  5.5 0.5 collective-permute-start
  6.2 3.7 %collective-permute-done.4 = bf16[32,2048]{1,0:T(8,128)(2,1)S(1)} collective-permute-done((bf16[32,2048]{1,0:T(8,128)(2,1)S(1)}, bf16[32,2048]{1,0:T(8,128)(2,1)S(1)}, u32[]{:S(2)}, u32[]{:S(2)}) %collective-permute-start.4) | collective-permute-done | bytes 131104 | tf_op jit(solution)/shard_map/ppermute | solution.py:198
  9.9 1.9 %constant_dynamic-slice_fusion.3 = bf16[256,1152]{1,0:T(8,128)(2,1)} fusion(bf16[512,1152]{1,0:T(8,128)(2,1)} %param.14, s32[]{:T(128)S(6)} %select_n.123), kind=kLoop, calls=%fused_computation.94 | loop fusion | bytes 1179652 | tf_op jit(solution)/shard_map/dynamic_slice | solution.py:196
  11.8 3.0 %collective-permute-start.6 = (bf16[256,1152]{1,0:T(8,128)(2,1)}, bf16[256,1152]{1,0:T(8,128)(2,1)S(1)}, u32[]{:S(2)}, u32[]{:S(2)}) collective-permute-start(bf16[256,1152]{1,0:T(8,128)(2,1)} %constant_dynamic-slice_fusion.3), channel_id=1, source_target_pairs={{0,24},{8,16},{16,8},{24,0},{1,25},{9,17},{17,9},{25,1},{2,26},{10... | collective-permute-start | bytes 1769480 | tf_op jit(solution)/shard_map/ppermute | solution.py:198
  15.3 0.8 collective-permute-done.1
  16.4 0.7 copy-done.3
  17.4 0.9 copy-done.5
  18.3 0.4 multiply_reduce_fusion.2
  19.4 1.0 copy.64
  20.4 0.8 fusion.40
  21.2 1.3 collective-permute-start.8
  22.5 3.0 %collective-permute-start.7 = (bf16[16,8,128]{2,1,0:T(8,128)(2,1)S(1)}, bf16[16,8,128]{2,1,0:T(8,128)(2,1)S(1)}, u32[]{:S(2)}, u32[]{:S(2)}) collective-permute-start(bf16[16,8,128]{2,1,0:T(8,128)(2,1)S(1)} %get-tuple-element.57), channel_id=1, source_target_pairs={{0,1},{1,2},{2,3},{3,4},{4,5},{5,6},{6,7},{8,9},{9,10},{10,11},{11... | collective-permute-start | bytes 98312 | tf_op jit(solution)/shard_map/ppermute | solution.py:19
  25.5 0.6 collective-permute-start.9
  26.4 1.9 %pad_maximum_fusion.6.pad_ref = bf16[16,144,128]{2,1,0:T(8,128)(2,1)} fusion(bf16[16,8,128]{2,1,0:T(8,128)(2,1)S(1)} %collective-permute-done.8, bf16[16,128,128]{2,1,0:T(8,128)(2,1)} %bitcast.12, bf16[16,8,128]{2,1,0:T(8,128)(2,1)S(1)} %collective-permute-done.7), kind=kLoop, calls=%fused_computation.40 | loop fusion | flops 1769472 | bytes 1179648 | tf_op jit(solution)/shard_map/concatenate | solution.py:17
  28.3 0.7 collective-permute-done.6
  29.0 1.0 collective-permute-start.13
  30.5 1.3 collective-permute-start.15
  31.8 3.0 %collective-permute-start.14 = (bf16[16,4,128]{2,1,0:T(4,128)(2,1)S(1)}, bf16[16,4,128]{2,1,0:T(4,128)(2,1)S(1)}, u32[]{:S(2)}, u32[]{:S(2)}) collective-permute-start(bf16[16,4,128]{2,1,0:T(4,128)(2,1)S(1)} %get-tuple-element.55), channel_id=1, source_target_pairs={{0,1},{1,2},{2,3},{3,4},{4,5},{5,6},{6,7},{8,9},{9,10},{10,11},{11... | collective-permute-start | bytes 49160 | tf_op jit(solution)/shard_map/ppermute | solution.py:19
  35.1 0.6 collective-permute-done.14
  35.7 1.1 maximum_convert_fusion.up_ref
  36.8 7.9 %all-to-all-start.2 = ((bf16[16,128,128]{2,1,0:T(8,128)(2,1)}), bf16[16,128,128]{2,1,0:T(8,128)(2,1)}, u32[]{:S(2)}, u32[]{:S(2)}) async-start(bf16[16,128,128]{2,1,0:T(8,128)(2,1)} %bitcast.12), calls=%async_computation.2 | async-start | bytes 1048576 | tf_op jit(solution)/shard_map/all_to_all | solution.py:261
  44.7 0.5 collective-permute-start.10
  45.3 1.2 broadcast_select_fusion.1
  46.6 0.5 collective-permute-done.10
  47.0 1.2 broadcast_select_fusion.5
  48.2 1.2 broadcast_select_fusion.3
  49.6 1.1 copy-done
  50.7 0.7 pad_maximum_fusion
  51.4 0.4 dynamic-slice_bitcast_fusion.3
  51.8 2.8 %pad_maximum_fusion.1 = bf16[2048,1152]{1,0:T(8,128)(2,1)} fusion(bf16[512,1152]{1,0:T(8,128)(2,1)S(1)} %get-tuple-element.35, bf16[512,1152]{1,0:T(8,128)(2,1)S(1)} %get-tuple-element.36, bf16[512,1152]{1,0:T(8,128)(2,1)S(1)} %get-tuple-element.37, bf16[512,1152]{1,0:T(8,128)(2,1)S(1)} %get-tuple-element.34), kind=kLoop, calls=%fused_computation.1 | loop fusion | flops 18874368 | bytes 9437184 | tf_op jit(solution)/shard_map/concatenate | solution.py:217
  54.6 5.3 %shard_map.98.pad_ref = bf16[16,136,128]{2,1,0:T(8,128)(2,1)} custom-call(bf16[16,144,128]{2,1,0:T(8,128)(2,1)} %pad_maximum_fusion.6.pad_ref, bf16[16,128,1152]{2,1,0:T(8,128)(2,1)} %bitcast.93, f32[16,136,128]{2,1,0:T(8,128)} %maximum_convert_fusion.up_ref), custom_call_target="tpu_custom_call" | custom-call | flops 641728512 | bytes 6979584 | tf_op jit(solution)/shard_map/pallas_call | solution.py:69
  59.9 2.0 %slice.84 = bf16[16,128,128]{2,1,0:T(8,128)(2,1)} slice(bf16[16,136,128]{2,1,0:T(8,128)(2,1)} %shard_map.98.pad_ref), slice={[0:16], [4:132], [0:128]} | slice | bytes 1048576 | tf_op jit(solution)/shard_map/slice | solution.py:258
  62.0 5.1 %shard_map.99 = f32[16,128,128]{2,1,0:T(8,128)} custom-call(bf16[16,136,128]{2,1,0:T(8,128)(2,1)} %shard_map.98.pad_ref, bf16[16,128,1152]{2,1,0:T(8,128)(2,1)} %bitcast.94), custom_call_target="tpu_custom_call" | custom-call | flops 603979776 | bytes 6324224 | tf_op jit(solution)/shard_map/pallas_call | solution.py:91
  67.1 1.6 %copy.67 = f32[128,16,128]{0,2,1:T(8,128)S(1)} copy(f32[128,16,128]{2,0,1:T(8,128)} %bitcast.98) | data formatting | bytes 2097152 | tf_op jit(solution)/shard_map/transpose | solution.py:273
  69.3 5.0 %all-to-all-start.1 = ((bf16[16,128,128]{2,1,0:T(8,128)(2,1)}), bf16[16,128,128]{2,1,0:T(8,128)(2,1)S(1)}, u32[]{:S(2)}, u32[]{:S(2)}) async-start(bf16[16,128,128]{2,1,0:T(8,128)(2,1)} %slice.84), calls=%async_computation.1 | async-start | bytes 1048576 | tf_op jit(solution)/shard_map/all_to_all | solution.py:262
  74.3 1.2 fusion.10
  75.5 1.3 copy.69
  76.8 1.3 copy.78
  78.5 1.2 pad_maximum_fusion.5
  79.8 9.9 %all-to-all-done.1 = bf16[16,128,128]{2,1,0:T(8,128)(2,1)S(1)} async-done(((bf16[16,128,128]{2,1,0:T(8,128)(2,1)}), bf16[16,128,128]{2,1,0:T(8,128)(2,1)S(1)}, u32[]{:S(2)}, u32[]{:S(2)}) %all-to-all-start.1) | async-done | bytes 524320 | tf_op jit(solution)/shard_map/all_to_all | solution.py:262
  89.6 2.8 %all-to-all-start = ((bf16[32,130,64]{1,2,0:T(8,128)(2,1)}), bf16[32,130,64]{1,2,0:T(8,128)(2,1)S(1)}, u32[]{:S(2)}, u32[]{:S(2)}) async-start(bf16[32,130,64]{1,2,0:T(8,128)(2,1)} %pad_maximum_fusion.5), calls=%async_computation | async-start | bytes 2097152 | tf_op jit(solution)/shard_map/all_to_all | solution.py:150
  92.5 0.4 convolution_dynamic-update-slice_fusion.8
  95.8 0.4 copy.79
  96.2 0.8 constant_dynamic-slice_fusion.2
  97.0 2.4 %collective-permute-start.18 = (f32[64,1152]{1,0:T(8,128)}, f32[64,1152]{1,0:T(8,128)}, u32[]{:S(2)}, u32[]{:S(2)}) collective-permute-start(f32[64,1152]{1,0:T(8,128)} %get-tuple-element.43), channel_id=1, source_target_pairs={{0,24},{8,16},{16,8},{24,0},{1,25},{9,17},{17,9},{25,1},{2,26},{10... | collective-permute-start | bytes 884744 | tf_op jit(solution)/shard_map/ppermute | solution.py:175
  99.4 0.5 collective-permute-start.17
  99.9 0.6 collective-permute-start.16
  100.5 19.4 %all-to-all-done = bf16[32,130,64]{1,2,0:T(8,128)(2,1)S(1)} async-done(((bf16[32,130,64]{1,2,0:T(8,128)(2,1)}), bf16[32,130,64]{1,2,0:T(8,128)(2,1)S(1)}, u32[]{:S(2)}, u32[]{:S(2)}) %all-to-all-start) | async-done | bytes 532512 | tf_op jit(solution)/shard_map/all_to_all | solution.py:150
  120.4 0.9 fusion.2
  121.4 1.2 add_add_fusion
  122.6 0.8 reshape.113
  123.4 2.8 %all-to-all-start.3 = ((f32[32,1,576]{2,1,0:T(1,128)}), f32[32,1,576]{2,1,0:T(1,128)S(1)}, u32[]{:S(2)}, u32[]{:S(2)}) async-start(f32[32,1,576]{2,1,0:T(1,128)} %reshape.113), calls=%async_computation.3 | async-start | bytes 163840 | tf_op jit(solution)/shard_map/all_to_all | solution.py:161
  126.2 2.7 %collective-permute-start.21 = (f32[64,1152]{1,0:T(8,128)S(1)}, f32[64,1152]{1,0:T(8,128)S(1)}, u32[]{:S(2)}, u32[]{:S(2)}) collective-permute-start(f32[64,1152]{1,0:T(8,128)S(1)} %add_add_fusion), channel_id=1, source_target_pairs={{0,24},{8,16},{16,8},{24,0},{1,25},{9,17},{17,9},{25,1},{2,26},{10... | collective-permute-start | bytes 884744 | tf_op jit(solution)/shard_map/ppermute | solution.py:185
  128.9 0.6 collective-permute-start.20
  129.7 4.1 %all-to-all-done.3 = f32[32,1,576]{2,1,0:T(1,128)S(1)} async-done(((f32[32,1,576]{2,1,0:T(1,128)}), f32[32,1,576]{2,1,0:T(1,128)S(1)}, u32[]{:S(2)}, u32[]{:S(2)}) %all-to-all-start.3) | async-done | bytes 73760 | tf_op jit(solution)/shard_map/all_to_all | solution.py:161
  133.8 0.5 broadcast.56
  134.3 0.8 reduce.7
  135.3 0.7 reshape.102
  136.0 0.6 slice_reduce_fusion
  136.6 1.1 collective-permute-done.21
  137.7 5.7 %collective-permute-done.20 = f32[64,1152]{1,0:T(8,128)S(1)} collective-permute-done((f32[64,1152]{1,0:T(8,128)S(1)}, f32[64,1152]{1,0:T(8,128)S(1)}, u32[]{:S(2)}, u32[]{:S(2)}) %collective-permute-start.20) | collective-permute-done | bytes 294944 | tf_op jit(solution)/shard_map/ppermute | solution.py:185
  143.6 1.1 pad_maximum_fusion.3
  (81 shorter events, 8.4 us)
Async XLA Ops:
  1.6 8.3 %collective-permute-start.4 = (bf16[32,2048]{1,0:T(8,128)(2,1)S(1)}, bf16[32,2048]{1,0:T(8,128)(2,1)S(1)}, u32[]{:S(2)}, u32[]{:S(2)}) collective-permute-start(bf16[32,2048]{1,0:T(8,128)(2,1)S(1)} %constant_dynamic-slice_fusion.4), channel_id=1, source_target_pairs={{0,24},{8,16},{16,8},{24,0},{1,25},{9,17},{17,9},{25,1},{2,26},{10... | collective-permute-start | bytes 393224 | tf_op jit(solution)/shard_map/ppermute | solution.py:198
  5.5 9.2 %collective-permute-start = (bf16[32,2048]{1,0:T(8,128)(2,1)S(1)}, bf16[32,2048]{1,0:T(8,128)(2,1)S(1)}, u32[]{:S(2)}, u32[]{:S(2)}) collective-permute-start(bf16[32,2048]{1,0:T(8,128)(2,1)S(1)} %constant_dynamic-slice_fusion.4), channel_id=1, source_target_pairs={{0,8},{8,0},{16,24},{24,16},{1,9},{9,1},{17,25},{25,17},{2,10},{10... | collective-permute-start | bytes 393224 | tf_op jit(solution)/shard_map/ppermute | solution.py:198
  6.1 8.9 %collective-permute-start.2 = (bf16[32,2048]{1,0:T(8,128)(2,1)S(1)}, bf16[32,2048]{1,0:T(8,128)(2,1)S(1)}, u32[]{:S(2)}, u32[]{:S(2)}) collective-permute-start(bf16[32,2048]{1,0:T(8,128)(2,1)S(1)} %constant_dynamic-slice_fusion.4), channel_id=1, source_target_pairs={{0,16},{8,24},{16,0},{24,8},{1,17},{9,25},{17,1},{25,9},{2,18},{10... | collective-permute-start | bytes 393224 | tf_op jit(solution)/shard_map/ppermute | solution.py:198
  9.9 5.4 %collective-permute-start.5 = (bf16[32,2048]{1,0:T(8,128)(2,1)S(1)}, bf16[32,2048]{1,0:T(8,128)(2,1)S(1)}, u32[]{:S(2)}, u32[]{:S(2)}) collective-permute-start(bf16[32,2048]{1,0:T(8,128)(2,1)S(1)} %collective-permute-done.4), channel_id=1, source_target_pairs={{0,1},{1,0},{2,3},{3,2},{4,5},{5,4},{6,7},{7,6},{8,9},{9,8},{10,11... | collective-permute-start | bytes 393224 | tf_op jit(solution)/shard_map/ppermute | solution.py:30
  11.8 17.2 %collective-permute-start.6 = (bf16[256,1152]{1,0:T(8,128)(2,1)}, bf16[256,1152]{1,0:T(8,128)(2,1)S(1)}, u32[]{:S(2)}, u32[]{:S(2)}) collective-permute-start(bf16[256,1152]{1,0:T(8,128)(2,1)} %constant_dynamic-slice_fusion.3), channel_id=1, source_target_pairs={{0,24},{8,16},{16,8},{24,0},{1,25},{9,17},{17,9},{25,1},{2,26},{10... | collective-permute-start | bytes 1769480 | tf_op jit(solution)/shard_map/ppermute | solution.py:198
  14.8 1.3 collective-permute-start.1
  15.0 1.3 collective-permute-start.3
  16.1 1.0 copy-start.3
  17.2 1.0 copy-start.5
  17.2 1.0 copy-start.6
  18.3 0.7 copy-start.4
  19.4 10.5 %copy-start.1 = (bf16[1,128,2048]{2,1,0:T(8,128)(2,1)S(1)}, bf16[1,128,2048]{2,1,0:T(8,128)(2,1)}, u32[]{:S(2)}) copy-start(bf16[1,128,2048]{2,1,0:T(8,128)(2,1)} %param.15) | copy-start | bytes 1572868
  21.2 5.1 %collective-permute-start.8 = (bf16[16,8,128]{2,1,0:T(8,128)(2,1)S(1)}, bf16[16,8,128]{2,1,0:T(8,128)(2,1)S(1)}, u32[]{:S(2)}, u32[]{:S(2)}) collective-permute-start(bf16[16,8,128]{2,1,0:T(8,128)(2,1)S(1)} %get-tuple-element.58), channel_id=1, source_target_pairs={{1,0},{2,1},{3,2},{4,3},{5,4},{6,5},{7,6},{9,8},{10,9},{11,10},{12... | collective-permute-start | bytes 98312 | tf_op jit(solution)/shard_map/ppermute | solution.py:21
  22.5 3.9 %collective-permute-start.7 = (bf16[16,8,128]{2,1,0:T(8,128)(2,1)S(1)}, bf16[16,8,128]{2,1,0:T(8,128)(2,1)S(1)}, u32[]{:S(2)}, u32[]{:S(2)}) collective-permute-start(bf16[16,8,128]{2,1,0:T(8,128)(2,1)S(1)} %get-tuple-element.57), channel_id=1, source_target_pairs={{0,1},{1,2},{2,3},{3,4},{4,5},{5,6},{6,7},{8,9},{9,10},{10,11},{11... | collective-permute-start | bytes 98312 | tf_op jit(solution)/shard_map/ppermute | solution.py:19
  25.5 19.2 %collective-permute-start.9 = (bf16[256,1152]{1,0:T(8,128)(2,1)}, bf16[256,1152]{1,0:T(8,128)(2,1)}, u32[]{:S(2)}, u32[]{:S(2)}) collective-permute-start(bf16[256,1152]{1,0:T(8,128)(2,1)} %constant_dynamic-slice_fusion.3), channel_id=1, source_target_pairs={{0,8},{8,0},{16,24},{24,16},{1,9},{9,1},{17,25},{25,17},{2,10},{10... | collective-permute-start | bytes 1769480 | tf_op jit(solution)/shard_map/ppermute | solution.py:198
  26.1 19.1 %collective-permute-start.11 = (bf16[256,1152]{1,0:T(8,128)(2,1)}, bf16[256,1152]{1,0:T(8,128)(2,1)}, u32[]{:S(2)}, u32[]{:S(2)}) collective-permute-start(bf16[256,1152]{1,0:T(8,128)(2,1)} %constant_dynamic-slice_fusion.3), channel_id=1, source_target_pairs={{0,16},{8,24},{16,0},{24,8},{1,17},{9,25},{17,1},{25,9},{2,18},{10... | collective-permute-start | bytes 1769480 | tf_op jit(solution)/shard_map/ppermute | solution.py:198
  29.0 16.3 %collective-permute-start.13 = (bf16[256,1152]{1,0:T(8,128)(2,1)S(1)}, bf16[256,1152]{1,0:T(8,128)(2,1)}, u32[]{:S(2)}, u32[]{:S(2)}) collective-permute-start(bf16[256,1152]{1,0:T(8,128)(2,1)S(1)} %collective-permute-done.6), channel_id=1, source_target_pairs={{0,1},{1,0},{2,3},{3,2},{4,5},{5,4},{6,7},{7,6},{8,9},{9,8},{10,11... | collective-permute-start | bytes 1769480 | tf_op jit(solution)/shard_map/ppermute | solution.py:30
  30.5 4.6 %collective-permute-start.15 = (bf16[16,4,128]{2,1,0:T(4,128)(2,1)S(1)}, bf16[16,4,128]{2,1,0:T(4,128)(2,1)S(1)}, u32[]{:S(2)}, u32[]{:S(2)}) collective-permute-start(bf16[16,4,128]{2,1,0:T(4,128)(2,1)S(1)} %get-tuple-element.56), channel_id=1, source_target_pairs={{1,0},{2,1},{3,2},{4,3},{5,4},{6,5},{7,6},{9,8},{10,9},{11,10},{12... | collective-permute-start | bytes 49160 | tf_op jit(solution)/shard_map/ppermute | solution.py:21
  31.8 3.9 %collective-permute-start.14 = (bf16[16,4,128]{2,1,0:T(4,128)(2,1)S(1)}, bf16[16,4,128]{2,1,0:T(4,128)(2,1)S(1)}, u32[]{:S(2)}, u32[]{:S(2)}) collective-permute-start(bf16[16,4,128]{2,1,0:T(4,128)(2,1)S(1)} %get-tuple-element.55), channel_id=1, source_target_pairs={{0,1},{1,2},{2,3},{3,4},{4,5},{5,6},{6,7},{8,9},{9,10},{10,11},{11... | collective-permute-start | bytes 49160 | tf_op jit(solution)/shard_map/ppermute | solution.py:19
  36.8 32.5 %all-to-all-start.2 = ((bf16[16,128,128]{2,1,0:T(8,128)(2,1)}), bf16[16,128,128]{2,1,0:T(8,128)(2,1)}, u32[]{:S(2)}, u32[]{:S(2)}) async-start(bf16[16,128,128]{2,1,0:T(8,128)(2,1)} %bitcast.12), calls=%async_computation.2 | async-start | bytes 1048576 | tf_op jit(solution)/shard_map/all_to_all | solution.py:261
  44.7 2.3 %collective-permute-start.10 = (bf16[256,1152]{1,0:T(8,128)(2,1)}, bf16[256,1152]{1,0:T(8,128)(2,1)S(1)}, u32[]{:S(2)}, u32[]{:S(2)}) collective-permute-start(bf16[256,1152]{1,0:T(8,128)(2,1)} %collective-permute-done.9), channel_id=1, source_target_pairs={{0,1},{1,0},{2,3},{3,2},{4,5},{5,4},{6,7},{7,6},{8,9},{9,8},{10,11... | collective-permute-start | bytes 1769480 | tf_op jit(solution)/shard_map/ppermute | solution.py:30
  45.2 3.0 %collective-permute-start.12 = (bf16[256,1152]{1,0:T(8,128)(2,1)}, bf16[256,1152]{1,0:T(8,128)(2,1)S(1)}, u32[]{:S(2)}, u32[]{:S(2)}) collective-permute-start(bf16[256,1152]{1,0:T(8,128)(2,1)} %collective-permute-done.11), channel_id=1, source_target_pairs={{0,1},{1,0},{2,3},{3,2},{4,5},{5,4},{6,7},{7,6},{8,9},{9,8},{10,11... | collective-permute-start | bytes 1769480 | tf_op jit(solution)/shard_map/ppermute | solution.py:30
  49.4 1.3 copy-start
  69.0 5.4 %copy-start.2 = (bf16[1,128,2048]{2,1,0:T(8,128)(2,1)S(1)}, bf16[1,128,2048]{2,1,0:T(8,128)(2,1)}, u32[]{:S(2)}) copy-start(bf16[1,128,2048]{2,1,0:T(8,128)(2,1)} %param.15) | copy-start | bytes 1572868
  69.3 20.3 %all-to-all-start.1 = ((bf16[16,128,128]{2,1,0:T(8,128)(2,1)}), bf16[16,128,128]{2,1,0:T(8,128)(2,1)S(1)}, u32[]{:S(2)}, u32[]{:S(2)}) async-start(bf16[16,128,128]{2,1,0:T(8,128)(2,1)} %slice.84), calls=%async_computation.1 | async-start | bytes 1048576 | tf_op jit(solution)/shard_map/all_to_all | solution.py:262
  89.6 30.2 %all-to-all-start = ((bf16[32,130,64]{1,2,0:T(8,128)(2,1)}), bf16[32,130,64]{1,2,0:T(8,128)(2,1)S(1)}, u32[]{:S(2)}, u32[]{:S(2)}) async-start(bf16[32,130,64]{1,2,0:T(8,128)(2,1)} %pad_maximum_fusion.5), calls=%async_computation | async-start | bytes 2097152 | tf_op jit(solution)/shard_map/all_to_all | solution.py:150
  97.0 24.4 %collective-permute-start.18 = (f32[64,1152]{1,0:T(8,128)}, f32[64,1152]{1,0:T(8,128)}, u32[]{:S(2)}, u32[]{:S(2)}) collective-permute-start(f32[64,1152]{1,0:T(8,128)} %get-tuple-element.43), channel_id=1, source_target_pairs={{0,24},{8,16},{16,8},{24,0},{1,25},{9,17},{17,9},{25,1},{2,26},{10... | collective-permute-start | bytes 884744 | tf_op jit(solution)/shard_map/ppermute | solution.py:175
  99.4 22.1 %collective-permute-start.17 = (f32[64,1152]{1,0:T(8,128)S(1)}, f32[64,1152]{1,0:T(8,128)}, u32[]{:S(2)}, u32[]{:S(2)}) collective-permute-start(f32[64,1152]{1,0:T(8,128)S(1)} %get-tuple-element.44), channel_id=1, source_target_pairs={{0,16},{8,24},{16,0},{24,8},{1,17},{9,25},{17,1},{25,9},{2,18},{10... | collective-permute-start | bytes 884744 | tf_op jit(solution)/shard_map/ppermute | solution.py:175
  99.9 21.5 %collective-permute-start.16 = (f32[64,1152]{1,0:T(8,128)S(1)}, f32[64,1152]{1,0:T(8,128)}, u32[]{:S(2)}, u32[]{:S(2)}) collective-permute-start(f32[64,1152]{1,0:T(8,128)S(1)} %get-tuple-element.42), channel_id=1, source_target_pairs={{0,8},{8,0},{16,24},{24,16},{1,9},{9,1},{17,25},{25,17},{2,10},{10... | collective-permute-start | bytes 884744 | tf_op jit(solution)/shard_map/ppermute | solution.py:175
  123.4 10.4 %all-to-all-start.3 = ((f32[32,1,576]{2,1,0:T(1,128)}), f32[32,1,576]{2,1,0:T(1,128)S(1)}, u32[]{:S(2)}, u32[]{:S(2)}) async-start(f32[32,1,576]{2,1,0:T(1,128)} %reshape.113), calls=%async_computation.3 | async-start | bytes 163840 | tf_op jit(solution)/shard_map/all_to_all | solution.py:161
  126.2 11.5 %collective-permute-start.21 = (f32[64,1152]{1,0:T(8,128)S(1)}, f32[64,1152]{1,0:T(8,128)S(1)}, u32[]{:S(2)}, u32[]{:S(2)}) collective-permute-start(f32[64,1152]{1,0:T(8,128)S(1)} %add_add_fusion), channel_id=1, source_target_pairs={{0,24},{8,16},{16,8},{24,0},{1,25},{9,17},{17,9},{25,1},{2,26},{10... | collective-permute-start | bytes 884744 | tf_op jit(solution)/shard_map/ppermute | solution.py:185
  128.9 14.5 %collective-permute-start.20 = (f32[64,1152]{1,0:T(8,128)S(1)}, f32[64,1152]{1,0:T(8,128)S(1)}, u32[]{:S(2)}, u32[]{:S(2)}) collective-permute-start(f32[64,1152]{1,0:T(8,128)S(1)} %add_add_fusion), channel_id=1, source_target_pairs={{0,16},{8,24},{16,0},{24,8},{1,17},{9,25},{17,1},{25,9},{2,18},{10... | collective-permute-start | bytes 884744 | tf_op jit(solution)/shard_map/ppermute | solution.py:185
  129.5 13.9 %collective-permute-start.19 = (f32[64,1152]{1,0:T(8,128)S(1)}, f32[64,1152]{1,0:T(8,128)S(1)}, u32[]{:S(2)}, u32[]{:S(2)}) collective-permute-start(f32[64,1152]{1,0:T(8,128)S(1)} %add_add_fusion), channel_id=1, source_target_pairs={{0,8},{8,0},{16,24},{24,16},{1,9},{9,1},{17,25},{25,17},{2,10},{10... | collective-permute-start | bytes 884744 | tf_op jit(solution)/shard_map/ppermute | solution.py:185

commit v19 on v17

--- a/solution.py
+++ b/solution.py
@@ -235,7 +235,7 @@
     scale = 1.0 / jnp.sqrt(jnp.float32(total))
     if fsdp & (fsdp - 1):
         raise ValueError("fsdp not pow2")
-    table = gather_shards(type_table, "fsdp")
+    table = gather_by_permutes(type_table, "fsdp")
     kernel_fetched = fetch_halves(kernel, "fsdp")
     far = fsdp - 1
     types = table.shape[0]

time: 140 us -> 142 us (1.014)
  waiting for transfers between devices: 42.6 us -> 47 us
  local copies, waits for them, and re-layouts: 20.3 us -> 18.6 us
    ppermute x3 -> x6, waiting for transfers between devices: 6.79 us -> 15 us  [gather_by_permutes(): pieces.append(lax.ppermute(total, axis, pairs))]
    ppermute x3 -> x6, starting transfers between devices: 3.55 us -> 8.15 us  [gather_by_permutes(): pieces.append(lax.ppermute(total, axis, pairs))]
    ppermute x6 -> x3, starting transfers between devices: 8.34 us -> 4.91 us  [fetch_halves(): lax.ppermute(mine, axis, [(source, source ^ apart) for source in range(co...]
    ppermute x6 -> x3, waiting for transfers between devices: 9.11 us -> 6.45 us  [fetch_halves(): lax.ppermute(mine, axis, [(source, source ^ apart) for source in range(co...]
    dynamic_slice x2 -> x1, local copies, waits for them, and re-layouts: 2.86 us -> 1.92 us  [fetch_halves(): mine = lax.dynamic_slice_in_dim(block, core * half_rows, half_rows, axis=0)]
    select_n x6 -> x3, other arithmetic: 3.65 us -> 3.58 us  [assemble_shards(): lower = jnp.where(core == 0, fetched[apart], swapped[apart])]
  transfers between devices with their start and end apart: 26 -> 23, of which waited for: 12 -> 10; matrix products, arithmetic and copies ran while one was open for 24% -> 23% of each run, Pallas kernels for 7% -> 7%
where the time goes in v19:
time: 142 us; the launch traced here: 140 us
  waiting for transfers between devices  47 us (33%)
  starting transfers between devices  42.3 us (30%)
  local copies, waits for them, and re-layouts  18.6 us (13%)
  other arithmetic  16.5 us (12%)
  Pallas kernels  10.3 us (7%)
  matrix products  4.47 us (3%)
    all_to_all x1, waiting for transfers between devices, table_and_gain(): got = lax.all_to_all(send, every, 0, 0, tiled=True)  18.4 us
    ppermute x6, waiting for transfers between devices, gather_by_permutes(): pieces.append(lax.ppermute(total, axis, pairs))  15 us
    ppermute x6, starting transfers between devices, gather_by_permutes(): pieces.append(lax.ppermute(total, axis, pairs))  8.15 us
    ppermute x3, waiting for transfers between devices, fetch_halves(): lax.ppermute(mine, axis, [(source, source ^ apart) for source in range(co...  6.45 us
    ppermute x2, starting transfers between devices, with_halo(): lax.ppermute(tail, axis, [(i, (i + 1) % count) for i in range(ends)])  6.06 us
    all_to_all x1, starting transfers between devices, body(): group_out = lax.all_to_all(dconv, 'seq', 0, 1, tiled=True)  5.18 us
    pallas_call x1, Pallas kernels, conv_dconv(): pl.pallas_call(forward_kernel, grid=(groups // step,), in_specs=[pl.Block...  5.18 us
    pallas_call x1, Pallas kernels, conv_transpose(): pl.pallas_call(backward_kernel, grid=(groups // step,), in_specs=[pl.Bloc...  5.12 us
  transfers between devices with their start and end apart: 23, of which 10 were waited for; matrix products, arithmetic and copies ran while one was open for 23% of the time, Pallas kernels for 7%

profile of v19, /device:TPU:0, one launch (start us, length us, event | category | flops | bytes accessed | tf_op | source)
XLA Modules:
  0.0 140.3 jit_solution(918203943532404152)
XLA Ops:
  0.6 4.0 %collective-permute-start.2 = (bf16[64,2048]{1,0:T(8,128)(2,1)}, bf16[64,2048]{1,0:T(8,128)(2,1)S(1)}, u32[]{:S(2)}, u32[]{:S(2)}) collective-permute-start(bf16[64,2048]{1,0:T(8,128)(2,1)} %param.12), channel_id=1, source_target_pairs={{0,24},{8,16},{16,8},{24,0},{1,25},{9,17},{17,9},{25,1},{2,26},{10... | collective-permute-start | bytes 786440 | tf_op jit(solution)/shard_map/ppermute | solution.py:185
  4.6 0.5 collective-permute-start.1
  5.2 1.9 %constant_dynamic-slice_fusion.3 = bf16[256,1152]{1,0:T(8,128)(2,1)} fusion(bf16[512,1152]{1,0:T(8,128)(2,1)} %param.14, s32[]{:T(128)S(6)} %select_n.80), kind=kLoop, calls=%fused_computation.85 | loop fusion | bytes 1179652 | tf_op jit(solution)/shard_map/dynamic_slice | solution.py:196
  7.2 2.8 %collective-permute-start.3 = (bf16[256,1152]{1,0:T(8,128)(2,1)}, bf16[256,1152]{1,0:T(8,128)(2,1)S(1)}, u32[]{:S(2)}, u32[]{:S(2)}) collective-permute-start(bf16[256,1152]{1,0:T(8,128)(2,1)} %constant_dynamic-slice_fusion.3), channel_id=1, source_target_pairs={{0,24},{8,16},{16,8},{24,0},{1,25},{9,17},{17,9},{25,1},{2,26},{10... | collective-permute-start | bytes 1769480 | tf_op jit(solution)/shard_map/ppermute | solution.py:198
  10.0 2.0 %collective-permute-done.2 = bf16[64,2048]{1,0:T(8,128)(2,1)S(1)} collective-permute-done((bf16[64,2048]{1,0:T(8,128)(2,1)}, bf16[64,2048]{1,0:T(8,128)(2,1)S(1)}, u32[]{:S(2)}, u32[]{:S(2)}) %collective-permute-start.2) | collective-permute-done | bytes 262176 | tf_op jit(solution)/shard_map/ppermute | solution.py:185
  12.0 5.5 %collective-permute-done.1 = bf16[64,2048]{1,0:T(8,128)(2,1)S(1)} collective-permute-done((bf16[64,2048]{1,0:T(8,128)(2,1)}, bf16[64,2048]{1,0:T(8,128)(2,1)S(1)}, u32[]{:S(2)}, u32[]{:S(2)}) %collective-permute-start.1) | collective-permute-done | bytes 262176 | tf_op jit(solution)/shard_map/ppermute | solution.py:185
  17.5 0.7 collective-permute-done
  18.4 0.9 copy-done.8
  19.4 0.4 multiply_reduce_fusion.2
  20.5 1.0 copy.64
  21.5 0.8 fusion.40
  22.3 1.3 collective-permute-start.5
  23.6 3.0 %collective-permute-start.4 = (bf16[16,4,128]{2,1,0:T(4,128)(2,1)S(1)}, bf16[16,4,128]{2,1,0:T(4,128)(2,1)S(1)}, u32[]{:S(2)}, u32[]{:S(2)}) collective-permute-start(bf16[16,4,128]{2,1,0:T(4,128)(2,1)S(1)} %get-tuple-element.57), channel_id=1, source_target_pairs={{0,1},{1,2},{2,3},{3,4},{4,5},{5,6},{6,7},{8,9},{9,10},{10,11},{11... | collective-permute-start | bytes 49160 | tf_op jit(solution)/shard_map/ppermute | solution.py:19
  26.6 1.5 %collective-permute-start.6 = (bf16[256,1152]{1,0:T(8,128)(2,1)}, bf16[256,1152]{1,0:T(8,128)(2,1)}, u32[]{:S(2)}, u32[]{:S(2)}) collective-permute-start(bf16[256,1152]{1,0:T(8,128)(2,1)} %constant_dynamic-slice_fusion.3), channel_id=1, source_target_pairs={{0,8},{8,0},{16,24},{24,16},{1,9},{9,1},{17,25},{25,17},{2,10},{10... | collective-permute-start | bytes 1769480 | tf_op jit(solution)/shard_map/ppermute | solution.py:198
  28.2 0.5 collective-permute-start.8
  28.7 2.0 %pad_maximum_fusion.6.pad_ref = bf16[16,136,128]{2,1,0:T(8,128)(2,1)} fusion(bf16[16,4,128]{2,1,0:T(4,128)(2,1)S(1)} %collective-permute-done.5, bf16[16,128,128]{2,1,0:T(8,128)(2,1)} %bitcast.12, bf16[16,4,128]{2,1,0:T(4,128)(2,1)S(1)} %collective-permute-done.4), kind=kLoop, calls=%fused_computation.47 | loop fusion | flops 1671168 | bytes 1114112 | tf_op jit(solution)/shard_map/concatenate | solution.py:17
  30.7 0.6 collective-permute-start.10
  31.6 1.3 copy.66
  32.9 4.9 %all-to-all-start.2 = ((bf16[16,128,128]{2,1,0:T(8,128)(2,1)}), bf16[16,128,128]{2,1,0:T(8,128)(2,1)S(1)}, u32[]{:S(2)}, u32[]{:S(2)}) async-start(bf16[16,128,128]{2,1,0:T(8,128)(2,1)} %bitcast.12), calls=%async_computation.2 | async-start | bytes 1048576 | tf_op jit(solution)/shard_map/all_to_all | solution.py:260
  37.8 5.2 %collective-permute-done.6 = bf16[256,1152]{1,0:T(8,128)(2,1)} collective-permute-done((bf16[256,1152]{1,0:T(8,128)(2,1)}, bf16[256,1152]{1,0:T(8,128)(2,1)}, u32[]{:S(2)}, u32[]{:S(2)}) %collective-permute-start.6) | collective-permute-done | bytes 589856 | tf_op jit(solution)/shard_map/ppermute | solution.py:198
  43.3 1.3 collective-permute-done.8
  44.7 1.2 broadcast_select_fusion.1
  46.0 1.2 broadcast_select_fusion.5
  47.2 1.2 broadcast_select_fusion.3
  48.6 1.1 copy-done.1
  49.7 0.7 pad_maximum_fusion
  50.4 0.4 dynamic-slice_bitcast_fusion.3
  50.8 2.8 %pad_maximum_fusion.1 = bf16[2048,1152]{1,0:T(8,128)(2,1)} fusion(bf16[512,1152]{1,0:T(8,128)(2,1)S(1)} %get-tuple-element.35, bf16[512,1152]{1,0:T(8,128)(2,1)S(1)} %get-tuple-element.36, bf16[512,1152]{1,0:T(8,128)(2,1)S(1)} %get-tuple-element.37, bf16[512,1152]{1,0:T(8,128)(2,1)S(1)} %get-tuple-element.34), kind=kLoop, calls=%fused_computation.1 | loop fusion | flops 18874368 | bytes 9437184 | tf_op jit(solution)/shard_map/concatenate | solution.py:217
  53.6 5.2 %shard_map.98 = bf16[16,128,128]{2,1,0:T(8,128)(2,1)} custom-call(bf16[16,136,128]{2,1,0:T(8,128)(2,1)} %pad_maximum_fusion.6.pad_ref, bf16[16,128,1152]{2,1,0:T(8,128)(2,1)} %bitcast.91, f32[16,128,128]{2,1,0:T(8,128)} %bitcast.97), custom_call_target="tpu_custom_call" | custom-call | flops 603979776 | bytes 6848512 | tf_op jit(solution)/shard_map/pallas_call | solution.py:69
  58.8 0.8 fusion.39
  59.6 1.3 collective-permute-start.12
  60.9 3.0 %collective-permute-start.11 = (bf16[16,4,128]{2,1,0:T(4,128)(2,1)S(1)}, bf16[16,4,128]{2,1,0:T(4,128)(2,1)S(1)}, u32[]{:S(2)}, u32[]{:S(2)}) collective-permute-start(bf16[16,4,128]{2,1,0:T(4,128)(2,1)S(1)} %get-tuple-element.55), channel_id=1, source_target_pairs={{0,1},{1,2},{2,3},{3,4},{4,5},{5,6},{6,7},{8,9},{9,10},{10,11},{11... | collective-permute-start | bytes 49160 | tf_op jit(solution)/shard_map/ppermute | solution.py:19
  64.2 5.2 %all-to-all-start.1 = ((bf16[16,128,128]{2,1,0:T(8,128)(2,1)}), bf16[16,128,128]{2,1,0:T(8,128)(2,1)}, u32[]{:S(2)}, u32[]{:S(2)}) async-start(bf16[16,128,128]{2,1,0:T(8,128)(2,1)} %shard_map.98), calls=%async_computation.1 | async-start | bytes 1048576 | tf_op jit(solution)/shard_map/all_to_all | solution.py:261
  69.6 1.0 all_to_all.40
  70.7 1.0 pad_maximum_fusion.7.pad_ref
  71.7 5.1 %shard_map.99 = f32[16,128,128]{2,1,0:T(8,128)} custom-call(bf16[16,136,128]{2,1,0:T(8,128)(2,1)} %pad_maximum_fusion.7.pad_ref, bf16[16,128,1152]{2,1,0:T(8,128)(2,1)} %bitcast.92), custom_call_target="tpu_custom_call" | custom-call | flops 603979776 | bytes 6324224 | tf_op jit(solution)/shard_map/pallas_call | solution.py:91
  76.8 1.6 %copy.67 = f32[128,16,128]{0,2,1:T(8,128)S(1)} copy(f32[128,16,128]{2,0,1:T(8,128)} %bitcast.98) | data formatting | bytes 2097152 | tf_op jit(solution)/shard_map/transpose | solution.py:272
  79.1 0.7 copy-done.3
  79.7 0.4 fusion.10
  80.5 1.2 pad_maximum_fusion.5
  81.8 3.1 %all-to-all-done.1 = bf16[16,128,128]{2,1,0:T(8,128)(2,1)} async-done(((bf16[16,128,128]{2,1,0:T(8,128)(2,1)}), bf16[16,128,128]{2,1,0:T(8,128)(2,1)}, u32[]{:S(2)}, u32[]{:S(2)}) %all-to-all-start.1) | async-done | bytes 524320 | tf_op jit(solution)/shard_map/all_to_all | solution.py:261
  84.9 2.8 %all-to-all-start = ((bf16[32,130,64]{1,2,0:T(8,128)(2,1)}), bf16[32,130,64]{1,2,0:T(8,128)(2,1)S(1)}, u32[]{:S(2)}, u32[]{:S(2)}) async-start(bf16[32,130,64]{1,2,0:T(8,128)(2,1)} %pad_maximum_fusion.5), calls=%async_computation | async-start | bytes 2097152 | tf_op jit(solution)/shard_map/all_to_all | solution.py:150
  87.7 1.1 copy.77
  91.3 0.4 convolution_dynamic-update-slice_fusion.1
  92.1 0.4 copy.79
  92.5 0.8 constant_dynamic-slice_fusion.2
  93.3 2.4 %collective-permute-start.15 = (f32[64,1152]{1,0:T(8,128)}, f32[64,1152]{1,0:T(8,128)}, u32[]{:S(2)}, u32[]{:S(2)}) collective-permute-start(f32[64,1152]{1,0:T(8,128)} %get-tuple-element.43), channel_id=1, source_target_pairs={{0,24},{8,16},{16,8},{24,0},{1,25},{9,17},{17,9},{25,1},{2,26},{10... | collective-permute-start | bytes 884744 | tf_op jit(solution)/shard_map/ppermute | solution.py:175
  95.7 0.5 collective-permute-start.14
  96.2 0.6 collective-permute-start.13
  96.8 18.4 %all-to-all-done = bf16[32,130,64]{1,2,0:T(8,128)(2,1)S(1)} async-done(((bf16[32,130,64]{1,2,0:T(8,128)(2,1)}), bf16[32,130,64]{1,2,0:T(8,128)(2,1)S(1)}, u32[]{:S(2)}, u32[]{:S(2)}) %all-to-all-start) | async-done | bytes 532512 | tf_op jit(solution)/shard_map/all_to_all | solution.py:150
  115.7 0.9 fusion.2
  116.7 1.2 add_add_fusion
  117.9 0.8 reshape.118
  118.7 3.1 %all-to-all-start.3 = ((f32[32,1,576]{2,1,0:T(1,128)}), f32[32,1,576]{2,1,0:T(1,128)S(1)}, u32[]{:S(2)}, u32[]{:S(2)}) async-start(f32[32,1,576]{2,1,0:T(1,128)} %reshape.118), calls=%async_computation.3 | async-start | bytes 163840 | tf_op jit(solution)/shard_map/all_to_all | solution.py:161
  121.8 2.7 %collective-permute-start.18 = (f32[64,1152]{1,0:T(8,128)S(1)}, f32[64,1152]{1,0:T(8,128)S(1)}, u32[]{:S(2)}, u32[]{:S(2)}) collective-permute-start(f32[64,1152]{1,0:T(8,128)S(1)} %add_add_fusion), channel_id=1, source_target_pairs={{0,24},{8,16},{16,8},{24,0},{1,25},{9,17},{17,9},{25,1},{2,26},{10... | collective-permute-start | bytes 884744 | tf_op jit(solution)/shard_map/ppermute | solution.py:185
  124.5 0.6 collective-permute-start.17
  125.3 4.1 %all-to-all-done.3 = f32[32,1,576]{2,1,0:T(1,128)S(1)} async-done(((f32[32,1,576]{2,1,0:T(1,128)}), f32[32,1,576]{2,1,0:T(1,128)S(1)}, u32[]{:S(2)}, u32[]{:S(2)}) %all-to-all-start.3) | async-done | bytes 73760 | tf_op jit(solution)/shard_map/all_to_all | solution.py:161
  129.4 0.5 broadcast.56
  129.9 0.8 reduce.7
  130.9 0.7 reshape.106
  131.6 0.6 slice_reduce_fusion
  132.2 1.1 collective-permute-done.18
  133.3 5.7 %collective-permute-done.17 = f32[64,1152]{1,0:T(8,128)S(1)} collective-permute-done((f32[64,1152]{1,0:T(8,128)S(1)}, f32[64,1152]{1,0:T(8,128)S(1)}, u32[]{:S(2)}, u32[]{:S(2)}) %collective-permute-start.17) | collective-permute-done | bytes 294944 | tf_op jit(solution)/shard_map/ppermute | solution.py:185
  139.2 1.1 pad_maximum_fusion.3
  (74 shorter events, 7.7 us)
Async XLA Ops:
  0.6 17.5 %copy-start.6 = (bf16[64,2048]{1,0:T(8,128)(2,1)S(1)}, bf16[64,2048]{1,0:T(8,128)(2,1)}, u32[]{:S(2)}) copy-start(bf16[64,2048]{1,0:T(8,128)(2,1)} %param.12) | copy-start | bytes 786436
  0.6 11.3 %collective-permute-start.2 = (bf16[64,2048]{1,0:T(8,128)(2,1)}, bf16[64,2048]{1,0:T(8,128)(2,1)S(1)}, u32[]{:S(2)}, u32[]{:S(2)}) collective-permute-start(bf16[64,2048]{1,0:T(8,128)(2,1)} %param.12), channel_id=1, source_target_pairs={{0,24},{8,16},{16,8},{24,0},{1,25},{9,17},{17,9},{25,1},{2,26},{10... | collective-permute-start | bytes 786440 | tf_op jit(solution)/shard_map/ppermute | solution.py:185
  4.6 12.9 %collective-permute-start.1 = (bf16[64,2048]{1,0:T(8,128)(2,1)}, bf16[64,2048]{1,0:T(8,128)(2,1)S(1)}, u32[]{:S(2)}, u32[]{:S(2)}) collective-permute-start(bf16[64,2048]{1,0:T(8,128)(2,1)} %param.12), channel_id=1, source_target_pairs={{0,16},{8,24},{16,0},{24,8},{1,17},{9,25},{17,1},{25,9},{2,18},{10... | collective-permute-start | bytes 786440 | tf_op jit(solution)/shard_map/ppermute | solution.py:185
  5.1 13.1 %collective-permute-start = (bf16[64,2048]{1,0:T(8,128)(2,1)}, bf16[64,2048]{1,0:T(8,128)(2,1)S(1)}, u32[]{:S(2)}, u32[]{:S(2)}) collective-permute-start(bf16[64,2048]{1,0:T(8,128)(2,1)} %param.12), channel_id=1, source_target_pairs={{0,8},{8,0},{16,24},{24,16},{1,9},{9,1},{17,25},{25,17},{2,10},{10... | collective-permute-start | bytes 786440 | tf_op jit(solution)/shard_map/ppermute | solution.py:185
  7.2 23.6 %collective-permute-start.3 = (bf16[256,1152]{1,0:T(8,128)(2,1)}, bf16[256,1152]{1,0:T(8,128)(2,1)S(1)}, u32[]{:S(2)}, u32[]{:S(2)}) collective-permute-start(bf16[256,1152]{1,0:T(8,128)(2,1)} %constant_dynamic-slice_fusion.3), channel_id=1, source_target_pairs={{0,24},{8,16},{16,8},{24,0},{1,25},{9,17},{17,9},{25,1},{2,26},{10... | collective-permute-start | bytes 1769480 | tf_op jit(solution)/shard_map/ppermute | solution.py:198
  18.3 1.0 copy-start.8
  18.3 1.0 copy-start.9
  19.4 0.7 copy-start.7
  20.5 10.9 %copy-start.2 = (bf16[1,128,2048]{2,1,0:T(8,128)(2,1)S(1)}, bf16[1,128,2048]{2,1,0:T(8,128)(2,1)}, u32[]{:S(2)}) copy-start(bf16[1,128,2048]{2,1,0:T(8,128)(2,1)} %param.15) | copy-start | bytes 1572868
  22.3 6.4 %collective-permute-start.5 = (bf16[16,4,128]{2,1,0:T(4,128)(2,1)S(1)}, bf16[16,4,128]{2,1,0:T(4,128)(2,1)S(1)}, u32[]{:S(2)}, u32[]{:S(2)}) collective-permute-start(bf16[16,4,128]{2,1,0:T(4,128)(2,1)S(1)} %get-tuple-element.58), channel_id=1, source_target_pairs={{1,0},{2,1},{3,2},{4,3},{5,4},{6,5},{7,6},{9,8},{10,9},{11,10},{12... | collective-permute-start | bytes 49160 | tf_op jit(solution)/shard_map/ppermute | solution.py:21
  23.6 5.1 %collective-permute-start.4 = (bf16[16,4,128]{2,1,0:T(4,128)(2,1)S(1)}, bf16[16,4,128]{2,1,0:T(4,128)(2,1)S(1)}, u32[]{:S(2)}, u32[]{:S(2)}) collective-permute-start(bf16[16,4,128]{2,1,0:T(4,128)(2,1)S(1)} %get-tuple-element.57), channel_id=1, source_target_pairs={{0,1},{1,2},{2,3},{3,4},{4,5},{5,6},{6,7},{8,9},{9,10},{10,11},{11... | collective-permute-start | bytes 49160 | tf_op jit(solution)/shard_map/ppermute | solution.py:19
  26.6 16.4 %collective-permute-start.6 = (bf16[256,1152]{1,0:T(8,128)(2,1)}, bf16[256,1152]{1,0:T(8,128)(2,1)}, u32[]{:S(2)}, u32[]{:S(2)}) collective-permute-start(bf16[256,1152]{1,0:T(8,128)(2,1)} %constant_dynamic-slice_fusion.3), channel_id=1, source_target_pairs={{0,8},{8,0},{16,24},{24,16},{1,9},{9,1},{17,25},{25,17},{2,10},{10... | collective-permute-start | bytes 1769480 | tf_op jit(solution)/shard_map/ppermute | solution.py:198
  28.2 16.5 %collective-permute-start.8 = (bf16[256,1152]{1,0:T(8,128)(2,1)}, bf16[256,1152]{1,0:T(8,128)(2,1)}, u32[]{:S(2)}, u32[]{:S(2)}) collective-permute-start(bf16[256,1152]{1,0:T(8,128)(2,1)} %constant_dynamic-slice_fusion.3), channel_id=1, source_target_pairs={{0,16},{8,24},{16,0},{24,8},{1,17},{9,25},{17,1},{25,9},{2,18},{10... | collective-permute-start | bytes 1769480 | tf_op jit(solution)/shard_map/ppermute | solution.py:198
  30.7 13.9 %collective-permute-start.10 = (bf16[256,1152]{1,0:T(8,128)(2,1)S(1)}, bf16[256,1152]{1,0:T(8,128)(2,1)}, u32[]{:S(2)}, u32[]{:S(2)}) collective-permute-start(bf16[256,1152]{1,0:T(8,128)(2,1)S(1)} %collective-permute-done.3), channel_id=1, source_target_pairs={{0,1},{1,0},{2,3},{3,2},{4,5},{5,4},{6,7},{7,6},{8,9},{9,8},{10,11... | collective-permute-start | bytes 1769480 | tf_op jit(solution)/shard_map/ppermute | solution.py:30
  32.9 31.2 %all-to-all-start.2 = ((bf16[16,128,128]{2,1,0:T(8,128)(2,1)}), bf16[16,128,128]{2,1,0:T(8,128)(2,1)S(1)}, u32[]{:S(2)}, u32[]{:S(2)}) async-start(bf16[16,128,128]{2,1,0:T(8,128)(2,1)} %bitcast.12), calls=%async_computation.2 | async-start | bytes 1048576 | tf_op jit(solution)/shard_map/all_to_all | solution.py:260
  43.0 3.0 %collective-permute-start.7 = (bf16[256,1152]{1,0:T(8,128)(2,1)}, bf16[256,1152]{1,0:T(8,128)(2,1)S(1)}, u32[]{:S(2)}, u32[]{:S(2)}) collective-permute-start(bf16[256,1152]{1,0:T(8,128)(2,1)} %collective-permute-done.6), channel_id=1, source_target_pairs={{0,1},{1,0},{2,3},{3,2},{4,5},{5,4},{6,7},{7,6},{8,9},{9,8},{10,11... | collective-permute-start | bytes 1769480 | tf_op jit(solution)/shard_map/ppermute | solution.py:30
  44.6 2.6 %collective-permute-start.9 = (bf16[256,1152]{1,0:T(8,128)(2,1)}, bf16[256,1152]{1,0:T(8,128)(2,1)S(1)}, u32[]{:S(2)}, u32[]{:S(2)}) collective-permute-start(bf16[256,1152]{1,0:T(8,128)(2,1)} %collective-permute-done.8), channel_id=1, source_target_pairs={{0,1},{1,0},{2,3},{3,2},{4,5},{5,4},{6,7},{7,6},{8,9},{9,8},{10,11... | collective-permute-start | bytes 1769480 | tf_op jit(solution)/shard_map/ppermute | solution.py:30
  48.4 1.3 copy-start.1
  59.6 11.1 %collective-permute-start.12 = (bf16[16,4,128]{2,1,0:T(4,128)(2,1)S(1)}, bf16[16,4,128]{2,1,0:T(4,128)(2,1)S(1)}, u32[]{:S(2)}, u32[]{:S(2)}) collective-permute-start(bf16[16,4,128]{2,1,0:T(4,128)(2,1)S(1)} %get-tuple-element.56), channel_id=1, source_target_pairs={{1,0},{2,1},{3,2},{4,3},{5,4},{6,5},{7,6},{9,8},{10,9},{11,10},{12... | collective-permute-start | bytes 49160 | tf_op jit(solution)/shard_map/ppermute | solution.py:21
  60.9 9.8 %collective-permute-start.11 = (bf16[16,4,128]{2,1,0:T(4,128)(2,1)S(1)}, bf16[16,4,128]{2,1,0:T(4,128)(2,1)S(1)}, u32[]{:S(2)}, u32[]{:S(2)}) collective-permute-start(bf16[16,4,128]{2,1,0:T(4,128)(2,1)S(1)} %get-tuple-element.55), channel_id=1, source_target_pairs={{0,1},{1,2},{2,3},{3,4},{4,5},{5,6},{6,7},{8,9},{9,10},{10,11},{11... | collective-permute-start | bytes 49160 | tf_op jit(solution)/shard_map/ppermute | solution.py:19
  64.2 20.7 %all-to-all-start.1 = ((bf16[16,128,128]{2,1,0:T(8,128)(2,1)}), bf16[16,128,128]{2,1,0:T(8,128)(2,1)}, u32[]{:S(2)}, u32[]{:S(2)}) async-start(bf16[16,128,128]{2,1,0:T(8,128)(2,1)} %shard_map.98), calls=%async_computation.1 | async-start | bytes 1048576 | tf_op jit(solution)/shard_map/all_to_all | solution.py:261
  69.3 1.4 copy-start
  78.7 1.0 copy-start.3
  80.1 1.6 %copy-start.5 = (bf16[128,2048]{1,0:T(8,128)(2,1)}, bf16[128,2048]{1,0:T(8,128)(2,1)S(1)}, u32[]{:S(2)}) copy-start(bf16[128,2048]{1,0:T(8,128)(2,1)S(1)} %fusion.10) | copy-start | bytes 1572868
  81.8 7.0 %copy-start.4 = (bf16[2,1024,128]{1,2,0:T(8,128)(2,1)S(1)}, bf16[2,1024,128]{1,2,0:T(8,128)(2,1)}, u32[]{:S(2)}) copy-start(bf16[2,1024,128]{1,2,0:T(8,128)(2,1)} %all_to_all.40) | copy-start | bytes 1572868
  84.9 30.2 %all-to-all-start = ((bf16[32,130,64]{1,2,0:T(8,128)(2,1)}), bf16[32,130,64]{1,2,0:T(8,128)(2,1)S(1)}, u32[]{:S(2)}, u32[]{:S(2)}) async-start(bf16[32,130,64]{1,2,0:T(8,128)(2,1)} %pad_maximum_fusion.5), calls=%async_computation | async-start | bytes 2097152 | tf_op jit(solution)/shard_map/all_to_all | solution.py:150
  93.3 23.4 %collective-permute-start.15 = (f32[64,1152]{1,0:T(8,128)}, f32[64,1152]{1,0:T(8,128)}, u32[]{:S(2)}, u32[]{:S(2)}) collective-permute-start(f32[64,1152]{1,0:T(8,128)} %get-tuple-element.43), channel_id=1, source_target_pairs={{0,24},{8,16},{16,8},{24,0},{1,25},{9,17},{17,9},{25,1},{2,26},{10... | collective-permute-start | bytes 884744 | tf_op jit(solution)/shard_map/ppermute | solution.py:175
  95.7 21.0 %collective-permute-start.14 = (f32[64,1152]{1,0:T(8,128)S(1)}, f32[64,1152]{1,0:T(8,128)}, u32[]{:S(2)}, u32[]{:S(2)}) collective-permute-start(f32[64,1152]{1,0:T(8,128)S(1)} %get-tuple-element.44), channel_id=1, source_target_pairs={{0,16},{8,24},{16,0},{24,8},{1,17},{9,25},{17,1},{25,9},{2,18},{10... | collective-permute-start | bytes 884744 | tf_op jit(solution)/shard_map/ppermute | solution.py:175
  96.2 20.5 %collective-permute-start.13 = (f32[64,1152]{1,0:T(8,128)S(1)}, f32[64,1152]{1,0:T(8,128)}, u32[]{:S(2)}, u32[]{:S(2)}) collective-permute-start(f32[64,1152]{1,0:T(8,128)S(1)} %get-tuple-element.42), channel_id=1, source_target_pairs={{0,8},{8,0},{16,24},{24,16},{1,9},{9,1},{17,25},{25,17},{2,10},{10... | collective-permute-start | bytes 884744 | tf_op jit(solution)/shard_map/ppermute | solution.py:175
  118.7 10.8 %all-to-all-start.3 = ((f32[32,1,576]{2,1,0:T(1,128)}), f32[32,1,576]{2,1,0:T(1,128)S(1)}, u32[]{:S(2)}, u32[]{:S(2)}) async-start(f32[32,1,576]{2,1,0:T(1,128)} %reshape.118), calls=%async_computation.3 | async-start | bytes 163840 | tf_op jit(solution)/shard_map/all_to_all | solution.py:161
  121.8 11.5 %collective-permute-start.18 = (f32[64,1152]{1,0:T(8,128)S(1)}, f32[64,1152]{1,0:T(8,128)S(1)}, u32[]{:S(2)}, u32[]{:S(2)}) collective-permute-start(f32[64,1152]{1,0:T(8,128)S(1)} %add_add_fusion), channel_id=1, source_target_pairs={{0,24},{8,16},{16,8},{24,0},{1,25},{9,17},{17,9},{25,1},{2,26},{10... | collective-permute-start | bytes 884744 | tf_op jit(solution)/shard_map/ppermute | solution.py:185
  124.5 14.5 %collective-permute-start.17 = (f32[64,1152]{1,0:T(8,128)S(1)}, f32[64,1152]{1,0:T(8,128)S(1)}, u32[]{:S(2)}, u32[]{:S(2)}) collective-permute-start(f32[64,1152]{1,0:T(8,128)S(1)} %add_add_fusion), channel_id=1, source_target_pairs={{0,16},{8,24},{16,0},{24,8},{1,17},{9,25},{17,1},{25,9},{2,18},{10... | collective-permute-start | bytes 884744 | tf_op jit(solution)/shard_map/ppermute | solution.py:185
  125.1 13.9 %collective-permute-start.16 = (f32[64,1152]{1,0:T(8,128)S(1)}, f32[64,1152]{1,0:T(8,128)S(1)}, u32[]{:S(2)}, u32[]{:S(2)}) collective-permute-start(f32[64,1152]{1,0:T(8,128)S(1)} %add_add_fusion), channel_id=1, source_target_pairs={{0,8},{8,0},{16,24},{24,16},{1,9},{9,1},{17,25},{25,17},{2,10},{10... | collective-permute-start | bytes 884744 | tf_op jit(solution)/shard_map/ppermute | solution.py:185

commit v20 on v17

--- a/solution.py
+++ b/solution.py
@@ -35,7 +35,7 @@
     return lax.all_to_all(jnp.tile(block, (count,) + (1,) * (block.ndim - 1)), axis, 0, 0, tiled=True)
 
 
-STEP_GROUPS = 4
+STEP_GROUPS = 8
 
 
 def forward_kernel(pad_ref, w_ref, up_ref, out_ref):

time: 140 us -> 139 us (level)
  Pallas kernels: 10.3 us -> 8.49 us
  transfers between devices with their start and end apart: 26 -> 26, of which waited for: 12 -> 12; matrix products, arithmetic and copies ran while one was open for 24% -> 24% of each run, Pallas kernels for 7% -> 6%
where the time goes in v20:
time: 139 us; the launch traced here: 138 us
  waiting for transfers between devices  43.6 us (31%)
  starting transfers between devices  42.9 us (31%)
  local copies, waits for them, and re-layouts  20.3 us (15%)
  other arithmetic  16.7 us (12%)
  Pallas kernels  8.49 us (6%)
  matrix products  4.48 us (3%)
    all_to_all x1, waiting for transfers between devices, table_and_gain(): got = lax.all_to_all(send, every, 0, 0, tiled=True)  18.4 us
    ppermute x6, waiting for transfers between devices, fetch_halves(): lax.ppermute(mine, axis, [(source, source ^ apart) for source in range(co...  9.11 us
    ppermute x6, starting transfers between devices, fetch_halves(): lax.ppermute(mine, axis, [(source, source ^ apart) for source in range(co...  8.34 us
    ppermute x3, waiting for transfers between devices, gather_by_permutes(): pieces.append(lax.ppermute(total, axis, pairs))  6.79 us
    ppermute x2, starting transfers between devices, with_halo(): lax.ppermute(tail, axis, [(i, (i + 1) % count) for i in range(ends)])  6.06 us
    all_to_all x1, starting transfers between devices, body(): group_in = lax.all_to_all(normed_g, 'seq', 0, 1, tiled=True)  5.6 us
    all_to_all x1, starting transfers between devices, body(): group_out = lax.all_to_all(dconv, 'seq', 0, 1, tiled=True)  5.1 us
    unnamed x23, local copies, waits for them, and re-layouts  4.76 us
  transfers between devices with their start and end apart: 26, of which 12 were waited for; matrix products, arithmetic and copies ran while one was open for 24% of the time, Pallas kernels for 6%

profile of v20, /device:TPU:0, one launch (start us, length us, event | category | flops | bytes accessed | tf_op | source)
XLA Modules:
  0.0 137.5 jit_solution(2661084361759567847)
XLA Ops:
  0.6 0.9 constant_dynamic-slice_fusion.4
  1.6 4.0 %collective-permute-start.4 = (bf16[32,2048]{1,0:T(8,128)(2,1)S(1)}, bf16[32,2048]{1,0:T(8,128)(2,1)S(1)}, u32[]{:S(2)}, u32[]{:S(2)}) collective-permute-start(bf16[32,2048]{1,0:T(8,128)(2,1)S(1)} %constant_dynamic-slice_fusion.4), channel_id=1, source_target_pairs={{0,24},{8,16},{16,8},{24,0},{1,25},{9,17},{17,9},{25,1},{2,26},{10... | collective-permute-start | bytes 393224 | tf_op jit(solution)/shard_map/ppermute | solution.py:198
  5.5 0.5 collective-permute-start
  6.2 3.7 %collective-permute-done.4 = bf16[32,2048]{1,0:T(8,128)(2,1)S(1)} collective-permute-done((bf16[32,2048]{1,0:T(8,128)(2,1)S(1)}, bf16[32,2048]{1,0:T(8,128)(2,1)S(1)}, u32[]{:S(2)}, u32[]{:S(2)}) %collective-permute-start.4) | collective-permute-done | bytes 131104 | tf_op jit(solution)/shard_map/ppermute | solution.py:198
  9.9 1.9 %constant_dynamic-slice_fusion.3 = bf16[256,1152]{1,0:T(8,128)(2,1)} fusion(bf16[512,1152]{1,0:T(8,128)(2,1)} %param.14, s32[]{:T(128)S(6)} %select_n.123), kind=kLoop, calls=%fused_computation.94 | loop fusion | bytes 1179652 | tf_op jit(solution)/shard_map/dynamic_slice | solution.py:196
  11.8 3.0 %collective-permute-start.6 = (bf16[256,1152]{1,0:T(8,128)(2,1)}, bf16[256,1152]{1,0:T(8,128)(2,1)S(1)}, u32[]{:S(2)}, u32[]{:S(2)}) collective-permute-start(bf16[256,1152]{1,0:T(8,128)(2,1)} %constant_dynamic-slice_fusion.3), channel_id=1, source_target_pairs={{0,24},{8,16},{16,8},{24,0},{1,25},{9,17},{17,9},{25,1},{2,26},{10... | collective-permute-start | bytes 1769480 | tf_op jit(solution)/shard_map/ppermute | solution.py:198
  15.3 0.8 collective-permute-done.1
  16.4 0.7 copy-done.6
  17.4 0.9 copy-done.8
  18.3 0.4 multiply_reduce_fusion.2
  19.4 1.0 copy.64
  20.4 0.8 fusion.40
  21.2 1.3 collective-permute-start.8
  22.5 3.0 %collective-permute-start.7 = (bf16[16,4,128]{2,1,0:T(4,128)(2,1)S(1)}, bf16[16,4,128]{2,1,0:T(4,128)(2,1)S(1)}, u32[]{:S(2)}, u32[]{:S(2)}) collective-permute-start(bf16[16,4,128]{2,1,0:T(4,128)(2,1)S(1)} %get-tuple-element.57), channel_id=1, source_target_pairs={{0,1},{1,2},{2,3},{3,4},{4,5},{5,6},{6,7},{8,9},{9,10},{10,11},{11... | collective-permute-start | bytes 49160 | tf_op jit(solution)/shard_map/ppermute | solution.py:19
  25.6 0.6 collective-permute-start.9
  26.4 2.0 %pad_maximum_fusion.6.pad_ref = bf16[16,136,128]{2,1,0:T(8,128)(2,1)} fusion(bf16[16,4,128]{2,1,0:T(4,128)(2,1)S(1)} %collective-permute-done.8, bf16[16,128,128]{2,1,0:T(8,128)(2,1)} %bitcast.12, bf16[16,4,128]{2,1,0:T(4,128)(2,1)S(1)} %collective-permute-done.7), kind=kLoop, calls=%fused_computation.47 | loop fusion | flops 1671168 | bytes 1114112 | tf_op jit(solution)/shard_map/concatenate | solution.py:17
  28.4 0.5 collective-permute-done.6
  29.0 1.0 collective-permute-start.13
  30.1 1.3 copy.66
  31.4 5.6 %all-to-all-start.2 = ((bf16[16,128,128]{2,1,0:T(8,128)(2,1)}), bf16[16,128,128]{2,1,0:T(8,128)(2,1)S(1)}, u32[]{:S(2)}, u32[]{:S(2)}) async-start(bf16[16,128,128]{2,1,0:T(8,128)(2,1)} %bitcast.12), calls=%async_computation.2 | async-start | bytes 1048576 | tf_op jit(solution)/shard_map/all_to_all | solution.py:260
  37.0 4.7 %collective-permute-done.9 = bf16[256,1152]{1,0:T(8,128)(2,1)} collective-permute-done((bf16[256,1152]{1,0:T(8,128)(2,1)}, bf16[256,1152]{1,0:T(8,128)(2,1)}, u32[]{:S(2)}, u32[]{:S(2)}) %collective-permute-start.9) | collective-permute-done | bytes 589856 | tf_op jit(solution)/shard_map/ppermute | solution.py:198
  41.7 0.5 collective-permute-start.10
  42.7 1.2 broadcast_select_fusion.1
  44.1 1.2 broadcast_select_fusion.5
  45.3 1.2 broadcast_select_fusion.3
  46.7 1.1 copy-done.1
  47.8 0.7 pad_maximum_fusion
  48.5 0.4 dynamic-slice_bitcast_fusion.3
  48.9 2.8 %pad_maximum_fusion.1 = bf16[2048,1152]{1,0:T(8,128)(2,1)} fusion(bf16[512,1152]{1,0:T(8,128)(2,1)S(1)} %get-tuple-element.35, bf16[512,1152]{1,0:T(8,128)(2,1)S(1)} %get-tuple-element.36, bf16[512,1152]{1,0:T(8,128)(2,1)S(1)} %get-tuple-element.37, bf16[512,1152]{1,0:T(8,128)(2,1)S(1)} %get-tuple-element.34), kind=kLoop, calls=%fused_computation.1 | loop fusion | flops 18874368 | bytes 9437184 | tf_op jit(solution)/shard_map/concatenate | solution.py:217
  51.7 4.4 %shard_map.98 = bf16[16,128,128]{2,1,0:T(8,128)(2,1)} custom-call(bf16[16,136,128]{2,1,0:T(8,128)(2,1)} %pad_maximum_fusion.6.pad_ref, bf16[16,128,1152]{2,1,0:T(8,128)(2,1)} %bitcast.94, f32[16,128,128]{2,1,0:T(8,128)} %bitcast.100), custom_call_target="tpu_custom_call" | custom-call | flops 603979776 | bytes 6848512 | tf_op jit(solution)/shard_map/pallas_call | solution.py:69
  56.1 0.8 fusion.39
  56.9 1.3 collective-permute-start.15
  58.2 3.0 %collective-permute-start.14 = (bf16[16,4,128]{2,1,0:T(4,128)(2,1)S(1)}, bf16[16,4,128]{2,1,0:T(4,128)(2,1)S(1)}, u32[]{:S(2)}, u32[]{:S(2)}) collective-permute-start(bf16[16,4,128]{2,1,0:T(4,128)(2,1)S(1)} %get-tuple-element.55), channel_id=1, source_target_pairs={{0,1},{1,2},{2,3},{3,4},{4,5},{5,6},{6,7},{8,9},{9,10},{10,11},{11... | collective-permute-start | bytes 49160 | tf_op jit(solution)/shard_map/ppermute | solution.py:19
  61.5 5.1 %all-to-all-start.1 = ((bf16[16,128,128]{2,1,0:T(8,128)(2,1)}), bf16[16,128,128]{2,1,0:T(8,128)(2,1)}, u32[]{:S(2)}, u32[]{:S(2)}) async-start(bf16[16,128,128]{2,1,0:T(8,128)(2,1)} %shard_map.98), calls=%async_computation.1 | async-start | bytes 1048576 | tf_op jit(solution)/shard_map/all_to_all | solution.py:261
  66.9 1.0 all_to_all.40
  68.0 1.0 pad_maximum_fusion.7.pad_ref
  69.0 4.1 %shard_map.99 = f32[16,128,128]{2,1,0:T(8,128)} custom-call(bf16[16,136,128]{2,1,0:T(8,128)(2,1)} %pad_maximum_fusion.7.pad_ref, bf16[16,128,1152]{2,1,0:T(8,128)(2,1)} %bitcast.95), custom_call_target="tpu_custom_call" | custom-call | flops 603979776 | bytes 6324224 | tf_op jit(solution)/shard_map/pallas_call | solution.py:91
  73.1 1.6 %copy.67 = f32[128,16,128]{0,2,1:T(8,128)S(1)} copy(f32[128,16,128]{2,0,1:T(8,128)} %bitcast.101) | data formatting | bytes 2097152 | tf_op jit(solution)/shard_map/transpose | solution.py:272
  75.4 0.7 copy-done.3
  76.0 0.4 fusion.10
  76.8 1.2 pad_maximum_fusion.5
  78.1 4.1 %all-to-all-done.1 = bf16[16,128,128]{2,1,0:T(8,128)(2,1)} async-done(((bf16[16,128,128]{2,1,0:T(8,128)(2,1)}), bf16[16,128,128]{2,1,0:T(8,128)(2,1)}, u32[]{:S(2)}, u32[]{:S(2)}) %all-to-all-start.1) | async-done | bytes 524320 | tf_op jit(solution)/shard_map/all_to_all | solution.py:261
  82.2 2.8 %all-to-all-start = ((bf16[32,130,64]{1,2,0:T(8,128)(2,1)}), bf16[32,130,64]{1,2,0:T(8,128)(2,1)S(1)}, u32[]{:S(2)}, u32[]{:S(2)}) async-start(bf16[32,130,64]{1,2,0:T(8,128)(2,1)} %pad_maximum_fusion.5), calls=%async_computation | async-start | bytes 2097152 | tf_op jit(solution)/shard_map/all_to_all | solution.py:150
  85.0 1.1 copy.77
  86.8 0.4 convolution_dynamic-update-slice_fusion.6
  89.8 0.8 constant_dynamic-slice_fusion.2
  90.6 2.5 %collective-permute-start.18 = (f32[64,1152]{1,0:T(8,128)}, f32[64,1152]{1,0:T(8,128)}, u32[]{:S(2)}, u32[]{:S(2)}) collective-permute-start(f32[64,1152]{1,0:T(8,128)} %get-tuple-element.43), channel_id=1, source_target_pairs={{0,24},{8,16},{16,8},{24,0},{1,25},{9,17},{17,9},{25,1},{2,26},{10... | collective-permute-start | bytes 884744 | tf_op jit(solution)/shard_map/ppermute | solution.py:175
  93.0 0.5 collective-permute-start.17
  93.6 0.5 collective-permute-start.16
  94.1 18.4 %all-to-all-done = bf16[32,130,64]{1,2,0:T(8,128)(2,1)S(1)} async-done(((bf16[32,130,64]{1,2,0:T(8,128)(2,1)}), bf16[32,130,64]{1,2,0:T(8,128)(2,1)S(1)}, u32[]{:S(2)}, u32[]{:S(2)}) %all-to-all-start) | async-done | bytes 532512 | tf_op jit(solution)/shard_map/all_to_all | solution.py:150
  112.9 0.9 fusion.2
  114.0 1.2 add_add_fusion
  115.2 0.8 reshape.118
  116.0 3.1 %all-to-all-start.3 = ((f32[32,1,576]{2,1,0:T(1,128)}), f32[32,1,576]{2,1,0:T(1,128)S(1)}, u32[]{:S(2)}, u32[]{:S(2)}) async-start(f32[32,1,576]{2,1,0:T(1,128)} %reshape.118), calls=%async_computation.3 | async-start | bytes 163840 | tf_op jit(solution)/shard_map/all_to_all | solution.py:161
  119.0 2.7 %collective-permute-start.21 = (f32[64,1152]{1,0:T(8,128)S(1)}, f32[64,1152]{1,0:T(8,128)S(1)}, u32[]{:S(2)}, u32[]{:S(2)}) collective-permute-start(f32[64,1152]{1,0:T(8,128)S(1)} %add_add_fusion), channel_id=1, source_target_pairs={{0,24},{8,16},{16,8},{24,0},{1,25},{9,17},{17,9},{25,1},{2,26},{10... | collective-permute-start | bytes 884744 | tf_op jit(solution)/shard_map/ppermute | solution.py:185
  121.8 0.6 collective-permute-start.20
  122.6 4.1 %all-to-all-done.3 = f32[32,1,576]{2,1,0:T(1,128)S(1)} async-done(((f32[32,1,576]{2,1,0:T(1,128)}), f32[32,1,576]{2,1,0:T(1,128)S(1)}, u32[]{:S(2)}, u32[]{:S(2)}) %all-to-all-start.3) | async-done | bytes 73760 | tf_op jit(solution)/shard_map/all_to_all | solution.py:161
  126.7 0.5 broadcast.56
  127.2 0.8 reduce.7
  128.2 0.7 reshape.106
  128.9 0.6 slice_reduce_fusion
  129.4 1.1 collective-permute-done.21
  130.5 5.7 %collective-permute-done.20 = f32[64,1152]{1,0:T(8,128)S(1)} collective-permute-done((f32[64,1152]{1,0:T(8,128)S(1)}, f32[64,1152]{1,0:T(8,128)S(1)}, u32[]{:S(2)}, u32[]{:S(2)}) %collective-permute-start.20) | collective-permute-done | bytes 294944 | tf_op jit(solution)/shard_map/ppermute | solution.py:185
  136.4 1.1 pad_maximum_fusion.3
  (86 shorter events, 9.2 us)
Async XLA Ops:
  1.6 8.3 %collective-permute-start.4 = (bf16[32,2048]{1,0:T(8,128)(2,1)S(1)}, bf16[32,2048]{1,0:T(8,128)(2,1)S(1)}, u32[]{:S(2)}, u32[]{:S(2)}) collective-permute-start(bf16[32,2048]{1,0:T(8,128)(2,1)S(1)} %constant_dynamic-slice_fusion.4), channel_id=1, source_target_pairs={{0,24},{8,16},{16,8},{24,0},{1,25},{9,17},{17,9},{25,1},{2,26},{10... | collective-permute-start | bytes 393224 | tf_op jit(solution)/shard_map/ppermute | solution.py:198
  5.5 9.2 %collective-permute-start = (bf16[32,2048]{1,0:T(8,128)(2,1)S(1)}, bf16[32,2048]{1,0:T(8,128)(2,1)S(1)}, u32[]{:S(2)}, u32[]{:S(2)}) collective-permute-start(bf16[32,2048]{1,0:T(8,128)(2,1)S(1)} %constant_dynamic-slice_fusion.4), channel_id=1, source_target_pairs={{0,8},{8,0},{16,24},{24,16},{1,9},{9,1},{17,25},{25,17},{2,10},{10... | collective-permute-start | bytes 393224 | tf_op jit(solution)/shard_map/ppermute | solution.py:198
  6.1 8.9 %collective-permute-start.2 = (bf16[32,2048]{1,0:T(8,128)(2,1)S(1)}, bf16[32,2048]{1,0:T(8,128)(2,1)S(1)}, u32[]{:S(2)}, u32[]{:S(2)}) collective-permute-start(bf16[32,2048]{1,0:T(8,128)(2,1)S(1)} %constant_dynamic-slice_fusion.4), channel_id=1, source_target_pairs={{0,16},{8,24},{16,0},{24,8},{1,17},{9,25},{17,1},{25,9},{2,18},{10... | collective-permute-start | bytes 393224 | tf_op jit(solution)/shard_map/ppermute | solution.py:198
  9.9 5.4 %collective-permute-start.5 = (bf16[32,2048]{1,0:T(8,128)(2,1)S(1)}, bf16[32,2048]{1,0:T(8,128)(2,1)S(1)}, u32[]{:S(2)}, u32[]{:S(2)}) collective-permute-start(bf16[32,2048]{1,0:T(8,128)(2,1)S(1)} %collective-permute-done.4), channel_id=1, source_target_pairs={{0,1},{1,0},{2,3},{3,2},{4,5},{5,4},{6,7},{7,6},{8,9},{9,8},{10,11... | collective-permute-start | bytes 393224 | tf_op jit(solution)/shard_map/ppermute | solution.py:30
  11.8 17.2 %collective-permute-start.6 = (bf16[256,1152]{1,0:T(8,128)(2,1)}, bf16[256,1152]{1,0:T(8,128)(2,1)S(1)}, u32[]{:S(2)}, u32[]{:S(2)}) collective-permute-start(bf16[256,1152]{1,0:T(8,128)(2,1)} %constant_dynamic-slice_fusion.3), channel_id=1, source_target_pairs={{0,24},{8,16},{16,8},{24,0},{1,25},{9,17},{17,9},{25,1},{2,26},{10... | collective-permute-start | bytes 1769480 | tf_op jit(solution)/shard_map/ppermute | solution.py:198
  14.8 1.3 collective-permute-start.1
  15.0 1.3 collective-permute-start.3
  16.1 1.0 copy-start.6
  17.2 1.0 copy-start.8
  17.2 1.0 copy-start.9
  18.3 0.7 copy-start.7
  19.4 10.5 %copy-start.2 = (bf16[1,128,2048]{2,1,0:T(8,128)(2,1)S(1)}, bf16[1,128,2048]{2,1,0:T(8,128)(2,1)}, u32[]{:S(2)}) copy-start(bf16[1,128,2048]{2,1,0:T(8,128)(2,1)} %param.15) | copy-start | bytes 1572868
  21.2 5.1 %collective-permute-start.8 = (bf16[16,4,128]{2,1,0:T(4,128)(2,1)S(1)}, bf16[16,4,128]{2,1,0:T(4,128)(2,1)S(1)}, u32[]{:S(2)}, u32[]{:S(2)}) collective-permute-start(bf16[16,4,128]{2,1,0:T(4,128)(2,1)S(1)} %get-tuple-element.58), channel_id=1, source_target_pairs={{1,0},{2,1},{3,2},{4,3},{5,4},{6,5},{7,6},{9,8},{10,9},{11,10},{12... | collective-permute-start | bytes 49160 | tf_op jit(solution)/shard_map/ppermute | solution.py:21
  22.5 3.9 %collective-permute-start.7 = (bf16[16,4,128]{2,1,0:T(4,128)(2,1)S(1)}, bf16[16,4,128]{2,1,0:T(4,128)(2,1)S(1)}, u32[]{:S(2)}, u32[]{:S(2)}) collective-permute-start(bf16[16,4,128]{2,1,0:T(4,128)(2,1)S(1)} %get-tuple-element.57), channel_id=1, source_target_pairs={{0,1},{1,2},{2,3},{3,4},{4,5},{5,6},{6,7},{8,9},{9,10},{10,11},{11... | collective-permute-start | bytes 49160 | tf_op jit(solution)/shard_map/ppermute | solution.py:19
  25.6 16.2 %collective-permute-start.9 = (bf16[256,1152]{1,0:T(8,128)(2,1)}, bf16[256,1152]{1,0:T(8,128)(2,1)}, u32[]{:S(2)}, u32[]{:S(2)}) collective-permute-start(bf16[256,1152]{1,0:T(8,128)(2,1)} %constant_dynamic-slice_fusion.3), channel_id=1, source_target_pairs={{0,8},{8,0},{16,24},{24,16},{1,9},{9,1},{17,25},{25,17},{2,10},{10... | collective-permute-start | bytes 1769480 | tf_op jit(solution)/shard_map/ppermute | solution.py:198
  26.2 16.3 %collective-permute-start.11 = (bf16[256,1152]{1,0:T(8,128)(2,1)}, bf16[256,1152]{1,0:T(8,128)(2,1)}, u32[]{:S(2)}, u32[]{:S(2)}) collective-permute-start(bf16[256,1152]{1,0:T(8,128)(2,1)} %constant_dynamic-slice_fusion.3), channel_id=1, source_target_pairs={{0,16},{8,24},{16,0},{24,8},{1,17},{9,25},{17,1},{25,9},{2,18},{10... | collective-permute-start | bytes 1769480 | tf_op jit(solution)/shard_map/ppermute | solution.py:198
  29.0 13.7 %collective-permute-start.13 = (bf16[256,1152]{1,0:T(8,128)(2,1)S(1)}, bf16[256,1152]{1,0:T(8,128)(2,1)}, u32[]{:S(2)}, u32[]{:S(2)}) collective-permute-start(bf16[256,1152]{1,0:T(8,128)(2,1)S(1)} %collective-permute-done.6), channel_id=1, source_target_pairs={{0,1},{1,0},{2,3},{3,2},{4,5},{5,4},{6,7},{7,6},{8,9},{9,8},{10,11... | collective-permute-start | bytes 1769480 | tf_op jit(solution)/shard_map/ppermute | solution.py:30
  31.4 30.0 %all-to-all-start.2 = ((bf16[16,128,128]{2,1,0:T(8,128)(2,1)}), bf16[16,128,128]{2,1,0:T(8,128)(2,1)S(1)}, u32[]{:S(2)}, u32[]{:S(2)}) async-start(bf16[16,128,128]{2,1,0:T(8,128)(2,1)} %bitcast.12), calls=%async_computation.2 | async-start | bytes 1048576 | tf_op jit(solution)/shard_map/all_to_all | solution.py:260
  41.7 2.4 %collective-permute-start.10 = (bf16[256,1152]{1,0:T(8,128)(2,1)}, bf16[256,1152]{1,0:T(8,128)(2,1)S(1)}, u32[]{:S(2)}, u32[]{:S(2)}) collective-permute-start(bf16[256,1152]{1,0:T(8,128)(2,1)} %collective-permute-done.9), channel_id=1, source_target_pairs={{0,1},{1,0},{2,3},{3,2},{4,5},{5,4},{6,7},{7,6},{8,9},{9,8},{10,11... | collective-permute-start | bytes 1769480 | tf_op jit(solution)/shard_map/ppermute | solution.py:30
  42.5 2.9 %collective-permute-start.12 = (bf16[256,1152]{1,0:T(8,128)(2,1)}, bf16[256,1152]{1,0:T(8,128)(2,1)S(1)}, u32[]{:S(2)}, u32[]{:S(2)}) collective-permute-start(bf16[256,1152]{1,0:T(8,128)(2,1)} %collective-permute-done.11), channel_id=1, source_target_pairs={{0,1},{1,0},{2,3},{3,2},{4,5},{5,4},{6,7},{7,6},{8,9},{9,8},{10,11... | collective-permute-start | bytes 1769480 | tf_op jit(solution)/shard_map/ppermute | solution.py:30
  46.5 1.3 copy-start.1
  56.9 11.0 %collective-permute-start.15 = (bf16[16,4,128]{2,1,0:T(4,128)(2,1)S(1)}, bf16[16,4,128]{2,1,0:T(4,128)(2,1)S(1)}, u32[]{:S(2)}, u32[]{:S(2)}) collective-permute-start(bf16[16,4,128]{2,1,0:T(4,128)(2,1)S(1)} %get-tuple-element.56), channel_id=1, source_target_pairs={{1,0},{2,1},{3,2},{4,3},{5,4},{6,5},{7,6},{9,8},{10,9},{11,10},{12... | collective-permute-start | bytes 49160 | tf_op jit(solution)/shard_map/ppermute | solution.py:21
  58.2 9.7 %collective-permute-start.14 = (bf16[16,4,128]{2,1,0:T(4,128)(2,1)S(1)}, bf16[16,4,128]{2,1,0:T(4,128)(2,1)S(1)}, u32[]{:S(2)}, u32[]{:S(2)}) collective-permute-start(bf16[16,4,128]{2,1,0:T(4,128)(2,1)S(1)} %get-tuple-element.55), channel_id=1, source_target_pairs={{0,1},{1,2},{2,3},{3,4},{4,5},{5,6},{6,7},{8,9},{9,10},{10,11},{11... | collective-permute-start | bytes 49160 | tf_op jit(solution)/shard_map/ppermute | solution.py:19
  61.5 20.7 %all-to-all-start.1 = ((bf16[16,128,128]{2,1,0:T(8,128)(2,1)}), bf16[16,128,128]{2,1,0:T(8,128)(2,1)}, u32[]{:S(2)}, u32[]{:S(2)}) async-start(bf16[16,128,128]{2,1,0:T(8,128)(2,1)} %shard_map.98), calls=%async_computation.1 | async-start | bytes 1048576 | tf_op jit(solution)/shard_map/all_to_all | solution.py:261
  66.6 1.4 copy-start
  75.0 1.0 copy-start.3
  76.4 1.6 %copy-start.5 = (bf16[128,2048]{1,0:T(8,128)(2,1)}, bf16[128,2048]{1,0:T(8,128)(2,1)S(1)}, u32[]{:S(2)}) copy-start(bf16[128,2048]{1,0:T(8,128)(2,1)S(1)} %fusion.10) | copy-start | bytes 1572868
  78.1 8.0 %copy-start.4 = (bf16[2,1024,128]{1,2,0:T(8,128)(2,1)S(1)}, bf16[2,1024,128]{1,2,0:T(8,128)(2,1)}, u32[]{:S(2)}) copy-start(bf16[2,1024,128]{1,2,0:T(8,128)(2,1)} %all_to_all.40) | copy-start | bytes 1572868
  82.2 30.2 %all-to-all-start = ((bf16[32,130,64]{1,2,0:T(8,128)(2,1)}), bf16[32,130,64]{1,2,0:T(8,128)(2,1)S(1)}, u32[]{:S(2)}, u32[]{:S(2)}) async-start(bf16[32,130,64]{1,2,0:T(8,128)(2,1)} %pad_maximum_fusion.5), calls=%async_computation | async-start | bytes 2097152 | tf_op jit(solution)/shard_map/all_to_all | solution.py:150
  90.6 23.4 %collective-permute-start.18 = (f32[64,1152]{1,0:T(8,128)}, f32[64,1152]{1,0:T(8,128)}, u32[]{:S(2)}, u32[]{:S(2)}) collective-permute-start(f32[64,1152]{1,0:T(8,128)} %get-tuple-element.43), channel_id=1, source_target_pairs={{0,24},{8,16},{16,8},{24,0},{1,25},{9,17},{17,9},{25,1},{2,26},{10... | collective-permute-start | bytes 884744 | tf_op jit(solution)/shard_map/ppermute | solution.py:175
  93.0 20.9 %collective-permute-start.17 = (f32[64,1152]{1,0:T(8,128)S(1)}, f32[64,1152]{1,0:T(8,128)}, u32[]{:S(2)}, u32[]{:S(2)}) collective-permute-start(f32[64,1152]{1,0:T(8,128)S(1)} %get-tuple-element.44), channel_id=1, source_target_pairs={{0,16},{8,24},{16,0},{24,8},{1,17},{9,25},{17,1},{25,9},{2,18},{10... | collective-permute-start | bytes 884744 | tf_op jit(solution)/shard_map/ppermute | solution.py:175
  93.6 20.4 %collective-permute-start.16 = (f32[64,1152]{1,0:T(8,128)S(1)}, f32[64,1152]{1,0:T(8,128)}, u32[]{:S(2)}, u32[]{:S(2)}) collective-permute-start(f32[64,1152]{1,0:T(8,128)S(1)} %get-tuple-element.42), channel_id=1, source_target_pairs={{0,8},{8,0},{16,24},{24,16},{1,9},{9,1},{17,25},{25,17},{2,10},{10... | collective-permute-start | bytes 884744 | tf_op jit(solution)/shard_map/ppermute | solution.py:175
  116.0 10.7 %all-to-all-start.3 = ((f32[32,1,576]{2,1,0:T(1,128)}), f32[32,1,576]{2,1,0:T(1,128)S(1)}, u32[]{:S(2)}, u32[]{:S(2)}) async-start(f32[32,1,576]{2,1,0:T(1,128)} %reshape.118), calls=%async_computation.3 | async-start | bytes 163840 | tf_op jit(solution)/shard_map/all_to_all | solution.py:161
  119.0 11.5 %collective-permute-start.21 = (f32[64,1152]{1,0:T(8,128)S(1)}, f32[64,1152]{1,0:T(8,128)S(1)}, u32[]{:S(2)}, u32[]{:S(2)}) collective-permute-start(f32[64,1152]{1,0:T(8,128)S(1)} %add_add_fusion), channel_id=1, source_target_pairs={{0,24},{8,16},{16,8},{24,0},{1,25},{9,17},{17,9},{25,1},{2,26},{10... | collective-permute-start | bytes 884744 | tf_op jit(solution)/shard_map/ppermute | solution.py:185
  121.8 14.5 %collective-permute-start.20 = (f32[64,1152]{1,0:T(8,128)S(1)}, f32[64,1152]{1,0:T(8,128)S(1)}, u32[]{:S(2)}, u32[]{:S(2)}) collective-permute-start(f32[64,1152]{1,0:T(8,128)S(1)} %add_add_fusion), channel_id=1, source_target_pairs={{0,16},{8,24},{16,0},{24,8},{1,17},{9,25},{17,1},{25,9},{2,18},{10... | collective-permute-start | bytes 884744 | tf_op jit(solution)/shard_map/ppermute | solution.py:185
  122.3 13.9 %collective-permute-start.19 = (f32[64,1152]{1,0:T(8,128)S(1)}, f32[64,1152]{1,0:T(8,128)S(1)}, u32[]{:S(2)}, u32[]{:S(2)}) collective-permute-start(f32[64,1152]{1,0:T(8,128)S(1)} %add_add_fusion), channel_id=1, source_target_pairs={{0,8},{8,0},{16,24},{24,16},{1,9},{9,1},{17,25},{25,17},{2,10},{10... | collective-permute-start | bytes 884744 | tf_op jit(solution)/shard_map/ppermute | solution.py:185

commit v21 on v20

--- a/solution.py
+++ b/solution.py
@@ -35,7 +35,7 @@
     return lax.all_to_all(jnp.tile(block, (count,) + (1,) * (block.ndim - 1)), axis, 0, 0, tiled=True)
 
 
-STEP_GROUPS = 8
+STEP_GROUPS = 16
 
 
 def forward_kernel(pad_ref, w_ref, up_ref, out_ref):

time: 139 us -> 140 us (level)
  Pallas kernels: 8.49 us -> 10.1 us
  transfers between devices with their start and end apart: 26 -> 26, of which waited for: 12 -> 12; matrix products, arithmetic and copies ran while one was open for 24% -> 24% of each run, Pallas kernels for 6% -> 7%
where the time goes in v21:
time: 140 us; the launch traced here: 138 us
  starting transfers between devices  42.9 us (31%)
  waiting for transfers between devices  42.8 us (31%)
  local copies, waits for them, and re-layouts  20.3 us (14%)
  other arithmetic  16.7 us (12%)
  Pallas kernels  10.1 us (7%)
  matrix products  4.47 us (3%)
    all_to_all x1, waiting for transfers between devices, table_and_gain(): got = lax.all_to_all(send, every, 0, 0, tiled=True)  18.4 us
    ppermute x6, waiting for transfers between devices, fetch_halves(): lax.ppermute(mine, axis, [(source, source ^ apart) for source in range(co...  9.11 us
    ppermute x6, starting transfers between devices, fetch_halves(): lax.ppermute(mine, axis, [(source, source ^ apart) for source in range(co...  8.34 us
    ppermute x3, waiting for transfers between devices, gather_by_permutes(): pieces.append(lax.ppermute(total, axis, pairs))  6.79 us
    ppermute x2, starting transfers between devices, with_halo(): lax.ppermute(tail, axis, [(i, (i + 1) % count) for i in range(ends)])  6.06 us
    all_to_all x1, starting transfers between devices, body(): group_in = lax.all_to_all(normed_g, 'seq', 0, 1, tiled=True)  5.6 us
    pallas_call x1, Pallas kernels, conv_dconv(): pl.pallas_call(forward_kernel, grid=(groups // step,), in_specs=[pl.Block...  5.21 us
    all_to_all x1, starting transfers between devices, body(): group_out = lax.all_to_all(dconv, 'seq', 0, 1, tiled=True)  5.1 us
  transfers between devices with their start and end apart: 26, of which 12 were waited for; matrix products, arithmetic and copies ran while one was open for 24% of the time, Pallas kernels for 7%

profile of v21, /device:TPU:0, one launch (start us, length us, event | category | flops | bytes accessed | tf_op | source)
XLA Modules:
  0.0 138.4 jit_solution(14430761775640267040)
XLA Ops:
  0.6 0.9 constant_dynamic-slice_fusion.4
  1.6 4.0 %collective-permute-start.4 = (bf16[32,2048]{1,0:T(8,128)(2,1)S(1)}, bf16[32,2048]{1,0:T(8,128)(2,1)S(1)}, u32[]{:S(2)}, u32[]{:S(2)}) collective-permute-start(bf16[32,2048]{1,0:T(8,128)(2,1)S(1)} %constant_dynamic-slice_fusion.4), channel_id=1, source_target_pairs={{0,24},{8,16},{16,8},{24,0},{1,25},{9,17},{17,9},{25,1},{2,26},{10... | collective-permute-start | bytes 393224 | tf_op jit(solution)/shard_map/ppermute | solution.py:198
  5.5 0.5 collective-permute-start
  6.2 3.7 %collective-permute-done.4 = bf16[32,2048]{1,0:T(8,128)(2,1)S(1)} collective-permute-done((bf16[32,2048]{1,0:T(8,128)(2,1)S(1)}, bf16[32,2048]{1,0:T(8,128)(2,1)S(1)}, u32[]{:S(2)}, u32[]{:S(2)}) %collective-permute-start.4) | collective-permute-done | bytes 131104 | tf_op jit(solution)/shard_map/ppermute | solution.py:198
  9.9 1.9 %constant_dynamic-slice_fusion.3 = bf16[256,1152]{1,0:T(8,128)(2,1)} fusion(bf16[512,1152]{1,0:T(8,128)(2,1)} %param.14, s32[]{:T(128)S(6)} %select_n.123), kind=kLoop, calls=%fused_computation.94 | loop fusion | bytes 1179652 | tf_op jit(solution)/shard_map/dynamic_slice | solution.py:196
  11.8 3.0 %collective-permute-start.6 = (bf16[256,1152]{1,0:T(8,128)(2,1)}, bf16[256,1152]{1,0:T(8,128)(2,1)S(1)}, u32[]{:S(2)}, u32[]{:S(2)}) collective-permute-start(bf16[256,1152]{1,0:T(8,128)(2,1)} %constant_dynamic-slice_fusion.3), channel_id=1, source_target_pairs={{0,24},{8,16},{16,8},{24,0},{1,25},{9,17},{17,9},{25,1},{2,26},{10... | collective-permute-start | bytes 1769480 | tf_op jit(solution)/shard_map/ppermute | solution.py:198
  15.3 0.8 collective-permute-done.1
  16.4 0.7 copy-done.6
  17.4 0.9 copy-done.8
  18.3 0.4 multiply_reduce_fusion.2
  19.4 1.0 copy.64
  20.4 0.8 fusion.40
  21.2 1.3 collective-permute-start.8
  22.5 3.0 %collective-permute-start.7 = (bf16[16,4,128]{2,1,0:T(4,128)(2,1)S(1)}, bf16[16,4,128]{2,1,0:T(4,128)(2,1)S(1)}, u32[]{:S(2)}, u32[]{:S(2)}) collective-permute-start(bf16[16,4,128]{2,1,0:T(4,128)(2,1)S(1)} %get-tuple-element.57), channel_id=1, source_target_pairs={{0,1},{1,2},{2,3},{3,4},{4,5},{5,6},{6,7},{8,9},{9,10},{10,11},{11... | collective-permute-start | bytes 49160 | tf_op jit(solution)/shard_map/ppermute | solution.py:19
  25.6 0.6 collective-permute-start.9
  26.4 2.0 %pad_maximum_fusion.6.pad_ref = bf16[16,136,128]{2,1,0:T(8,128)(2,1)} fusion(bf16[16,4,128]{2,1,0:T(4,128)(2,1)S(1)} %collective-permute-done.8, bf16[16,128,128]{2,1,0:T(8,128)(2,1)} %bitcast.12, bf16[16,4,128]{2,1,0:T(4,128)(2,1)S(1)} %collective-permute-done.7), kind=kLoop, calls=%fused_computation.47 | loop fusion | flops 1671168 | bytes 1114112 | tf_op jit(solution)/shard_map/concatenate | solution.py:17
  28.4 0.5 collective-permute-done.6
  29.0 1.0 collective-permute-start.13
  30.1 1.3 copy.66
  31.4 5.6 %all-to-all-start.2 = ((bf16[16,128,128]{2,1,0:T(8,128)(2,1)}), bf16[16,128,128]{2,1,0:T(8,128)(2,1)S(1)}, u32[]{:S(2)}, u32[]{:S(2)}) async-start(bf16[16,128,128]{2,1,0:T(8,128)(2,1)} %bitcast.12), calls=%async_computation.2 | async-start | bytes 1048576 | tf_op jit(solution)/shard_map/all_to_all | solution.py:260
  37.0 4.7 %collective-permute-done.9 = bf16[256,1152]{1,0:T(8,128)(2,1)} collective-permute-done((bf16[256,1152]{1,0:T(8,128)(2,1)}, bf16[256,1152]{1,0:T(8,128)(2,1)}, u32[]{:S(2)}, u32[]{:S(2)}) %collective-permute-start.9) | collective-permute-done | bytes 589856 | tf_op jit(solution)/shard_map/ppermute | solution.py:198
  41.7 0.5 collective-permute-start.10
  42.7 1.2 broadcast_select_fusion.1
  44.1 1.2 broadcast_select_fusion.5
  45.3 1.2 broadcast_select_fusion.3
  46.7 1.1 copy-done.1
  47.8 0.7 pad_maximum_fusion
  48.5 0.4 dynamic-slice_bitcast_fusion.3
  48.9 2.8 %pad_maximum_fusion.1 = bf16[2048,1152]{1,0:T(8,128)(2,1)} fusion(bf16[512,1152]{1,0:T(8,128)(2,1)S(1)} %get-tuple-element.35, bf16[512,1152]{1,0:T(8,128)(2,1)S(1)} %get-tuple-element.36, bf16[512,1152]{1,0:T(8,128)(2,1)S(1)} %get-tuple-element.37, bf16[512,1152]{1,0:T(8,128)(2,1)S(1)} %get-tuple-element.34), kind=kLoop, calls=%fused_computation.1 | loop fusion | flops 18874368 | bytes 9437184 | tf_op jit(solution)/shard_map/concatenate | solution.py:217
  51.7 5.2 %shard_map.98 = bf16[16,128,128]{2,1,0:T(8,128)(2,1)} custom-call(bf16[16,136,128]{2,1,0:T(8,128)(2,1)} %pad_maximum_fusion.6.pad_ref, bf16[16,128,1152]{2,1,0:T(8,128)(2,1)} %bitcast.94, f32[16,128,128]{2,1,0:T(8,128)} %bitcast.100), custom_call_target="tpu_custom_call" | custom-call | flops 603979776 | bytes 6848512 | tf_op jit(solution)/shard_map/pallas_call | solution.py:69
  57.0 0.8 fusion.39
  57.7 1.3 collective-permute-start.15
  59.0 3.0 %collective-permute-start.14 = (bf16[16,4,128]{2,1,0:T(4,128)(2,1)S(1)}, bf16[16,4,128]{2,1,0:T(4,128)(2,1)S(1)}, u32[]{:S(2)}, u32[]{:S(2)}) collective-permute-start(bf16[16,4,128]{2,1,0:T(4,128)(2,1)S(1)} %get-tuple-element.55), channel_id=1, source_target_pairs={{0,1},{1,2},{2,3},{3,4},{4,5},{5,6},{6,7},{8,9},{9,10},{10,11},{11... | collective-permute-start | bytes 49160 | tf_op jit(solution)/shard_map/ppermute | solution.py:19
  62.3 5.1 %all-to-all-start.1 = ((bf16[16,128,128]{2,1,0:T(8,128)(2,1)}), bf16[16,128,128]{2,1,0:T(8,128)(2,1)}, u32[]{:S(2)}, u32[]{:S(2)}) async-start(bf16[16,128,128]{2,1,0:T(8,128)(2,1)} %shard_map.98), calls=%async_computation.1 | async-start | bytes 1048576 | tf_op jit(solution)/shard_map/all_to_all | solution.py:261
  67.8 1.0 all_to_all.40
  68.8 1.0 pad_maximum_fusion.7.pad_ref
  69.8 4.9 %shard_map.99 = f32[16,128,128]{2,1,0:T(8,128)} custom-call(bf16[16,136,128]{2,1,0:T(8,128)(2,1)} %pad_maximum_fusion.7.pad_ref, bf16[16,128,1152]{2,1,0:T(8,128)(2,1)} %bitcast.95), custom_call_target="tpu_custom_call" | custom-call | flops 603979776 | bytes 6324224 | tf_op jit(solution)/shard_map/pallas_call | solution.py:91
  74.7 1.6 %copy.67 = f32[128,16,128]{0,2,1:T(8,128)S(1)} copy(f32[128,16,128]{2,0,1:T(8,128)} %bitcast.101) | data formatting | bytes 2097152 | tf_op jit(solution)/shard_map/transpose | solution.py:272
  77.0 0.7 copy-done.3
  77.6 0.4 fusion.10
  78.4 1.2 pad_maximum_fusion.5
  79.7 3.3 %all-to-all-done.1 = bf16[16,128,128]{2,1,0:T(8,128)(2,1)} async-done(((bf16[16,128,128]{2,1,0:T(8,128)(2,1)}), bf16[16,128,128]{2,1,0:T(8,128)(2,1)}, u32[]{:S(2)}, u32[]{:S(2)}) %all-to-all-start.1) | async-done | bytes 524320 | tf_op jit(solution)/shard_map/all_to_all | solution.py:261
  83.0 2.8 %all-to-all-start = ((bf16[32,130,64]{1,2,0:T(8,128)(2,1)}), bf16[32,130,64]{1,2,0:T(8,128)(2,1)S(1)}, u32[]{:S(2)}, u32[]{:S(2)}) async-start(bf16[32,130,64]{1,2,0:T(8,128)(2,1)} %pad_maximum_fusion.5), calls=%async_computation | async-start | bytes 2097152 | tf_op jit(solution)/shard_map/all_to_all | solution.py:150
  85.8 1.1 copy.77
  87.7 0.4 convolution_dynamic-update-slice_fusion.6
  90.6 0.8 constant_dynamic-slice_fusion.2
  91.4 2.4 %collective-permute-start.18 = (f32[64,1152]{1,0:T(8,128)}, f32[64,1152]{1,0:T(8,128)}, u32[]{:S(2)}, u32[]{:S(2)}) collective-permute-start(f32[64,1152]{1,0:T(8,128)} %get-tuple-element.43), channel_id=1, source_target_pairs={{0,24},{8,16},{16,8},{24,0},{1,25},{9,17},{17,9},{25,1},{2,26},{10... | collective-permute-start | bytes 884744 | tf_op jit(solution)/shard_map/ppermute | solution.py:175
  93.8 0.6 collective-permute-start.17
  94.4 0.5 collective-permute-start.16
  94.9 18.4 %all-to-all-done = bf16[32,130,64]{1,2,0:T(8,128)(2,1)S(1)} async-done(((bf16[32,130,64]{1,2,0:T(8,128)(2,1)}), bf16[32,130,64]{1,2,0:T(8,128)(2,1)S(1)}, u32[]{:S(2)}, u32[]{:S(2)}) %all-to-all-start) | async-done | bytes 532512 | tf_op jit(solution)/shard_map/all_to_all | solution.py:150
  113.8 0.9 fusion.2
  114.8 1.2 add_add_fusion
  116.0 0.8 reshape.118
  116.8 3.1 %all-to-all-start.3 = ((f32[32,1,576]{2,1,0:T(1,128)}), f32[32,1,576]{2,1,0:T(1,128)S(1)}, u32[]{:S(2)}, u32[]{:S(2)}) async-start(f32[32,1,576]{2,1,0:T(1,128)} %reshape.118), calls=%async_computation.3 | async-start | bytes 163840 | tf_op jit(solution)/shard_map/all_to_all | solution.py:161
  119.9 2.7 %collective-permute-start.21 = (f32[64,1152]{1,0:T(8,128)S(1)}, f32[64,1152]{1,0:T(8,128)S(1)}, u32[]{:S(2)}, u32[]{:S(2)}) collective-permute-start(f32[64,1152]{1,0:T(8,128)S(1)} %add_add_fusion), channel_id=1, source_target_pairs={{0,24},{8,16},{16,8},{24,0},{1,25},{9,17},{17,9},{25,1},{2,26},{10... | collective-permute-start | bytes 884744 | tf_op jit(solution)/shard_map/ppermute | solution.py:185
  122.6 0.6 collective-permute-start.20
  123.5 4.1 %all-to-all-done.3 = f32[32,1,576]{2,1,0:T(1,128)S(1)} async-done(((f32[32,1,576]{2,1,0:T(1,128)}), f32[32,1,576]{2,1,0:T(1,128)S(1)}, u32[]{:S(2)}, u32[]{:S(2)}) %all-to-all-start.3) | async-done | bytes 73760 | tf_op jit(solution)/shard_map/all_to_all | solution.py:161
  127.5 0.5 broadcast.56
  128.1 0.8 reduce.7
  129.0 0.7 reshape.106
  129.8 0.6 slice_reduce_fusion
  130.3 1.1 collective-permute-done.21
  131.4 5.7 %collective-permute-done.20 = f32[64,1152]{1,0:T(8,128)S(1)} collective-permute-done((f32[64,1152]{1,0:T(8,128)S(1)}, f32[64,1152]{1,0:T(8,128)S(1)}, u32[]{:S(2)}, u32[]{:S(2)}) %collective-permute-start.20) | collective-permute-done | bytes 294944 | tf_op jit(solution)/shard_map/ppermute | solution.py:185
  137.3 1.1 pad_maximum_fusion.3
  (86 shorter events, 9.2 us)
Async XLA Ops:
  1.6 8.3 %collective-permute-start.4 = (bf16[32,2048]{1,0:T(8,128)(2,1)S(1)}, bf16[32,2048]{1,0:T(8,128)(2,1)S(1)}, u32[]{:S(2)}, u32[]{:S(2)}) collective-permute-start(bf16[32,2048]{1,0:T(8,128)(2,1)S(1)} %constant_dynamic-slice_fusion.4), channel_id=1, source_target_pairs={{0,24},{8,16},{16,8},{24,0},{1,25},{9,17},{17,9},{25,1},{2,26},{10... | collective-permute-start | bytes 393224 | tf_op jit(solution)/shard_map/ppermute | solution.py:198
  5.5 9.2 %collective-permute-start = (bf16[32,2048]{1,0:T(8,128)(2,1)S(1)}, bf16[32,2048]{1,0:T(8,128)(2,1)S(1)}, u32[]{:S(2)}, u32[]{:S(2)}) collective-permute-start(bf16[32,2048]{1,0:T(8,128)(2,1)S(1)} %constant_dynamic-slice_fusion.4), channel_id=1, source_target_pairs={{0,8},{8,0},{16,24},{24,16},{1,9},{9,1},{17,25},{25,17},{2,10},{10... | collective-permute-start | bytes 393224 | tf_op jit(solution)/shard_map/ppermute | solution.py:198
  6.1 8.9 %collective-permute-start.2 = (bf16[32,2048]{1,0:T(8,128)(2,1)S(1)}, bf16[32,2048]{1,0:T(8,128)(2,1)S(1)}, u32[]{:S(2)}, u32[]{:S(2)}) collective-permute-start(bf16[32,2048]{1,0:T(8,128)(2,1)S(1)} %constant_dynamic-slice_fusion.4), channel_id=1, source_target_pairs={{0,16},{8,24},{16,0},{24,8},{1,17},{9,25},{17,1},{25,9},{2,18},{10... | collective-permute-start | bytes 393224 | tf_op jit(solution)/shard_map/ppermute | solution.py:198
  9.9 5.4 %collective-permute-start.5 = (bf16[32,2048]{1,0:T(8,128)(2,1)S(1)}, bf16[32,2048]{1,0:T(8,128)(2,1)S(1)}, u32[]{:S(2)}, u32[]{:S(2)}) collective-permute-start(bf16[32,2048]{1,0:T(8,128)(2,1)S(1)} %collective-permute-done.4), channel_id=1, source_target_pairs={{0,1},{1,0},{2,3},{3,2},{4,5},{5,4},{6,7},{7,6},{8,9},{9,8},{10,11... | collective-permute-start | bytes 393224 | tf_op jit(solution)/shard_map/ppermute | solution.py:30
  11.8 17.2 %collective-permute-start.6 = (bf16[256,1152]{1,0:T(8,128)(2,1)}, bf16[256,1152]{1,0:T(8,128)(2,1)S(1)}, u32[]{:S(2)}, u32[]{:S(2)}) collective-permute-start(bf16[256,1152]{1,0:T(8,128)(2,1)} %constant_dynamic-slice_fusion.3), channel_id=1, source_target_pairs={{0,24},{8,16},{16,8},{24,0},{1,25},{9,17},{17,9},{25,1},{2,26},{10... | collective-permute-start | bytes 1769480 | tf_op jit(solution)/shard_map/ppermute | solution.py:198
  14.8 1.3 collective-permute-start.1
  15.0 1.3 collective-permute-start.3
  16.1 1.0 copy-start.6
  17.2 1.0 copy-start.8
  17.2 1.0 copy-start.9
  18.3 0.7 copy-start.7
  19.4 10.5 %copy-start.2 = (bf16[1,128,2048]{2,1,0:T(8,128)(2,1)S(1)}, bf16[1,128,2048]{2,1,0:T(8,128)(2,1)}, u32[]{:S(2)}) copy-start(bf16[1,128,2048]{2,1,0:T(8,128)(2,1)} %param.15) | copy-start | bytes 1572868
  21.2 5.1 %collective-permute-start.8 = (bf16[16,4,128]{2,1,0:T(4,128)(2,1)S(1)}, bf16[16,4,128]{2,1,0:T(4,128)(2,1)S(1)}, u32[]{:S(2)}, u32[]{:S(2)}) collective-permute-start(bf16[16,4,128]{2,1,0:T(4,128)(2,1)S(1)} %get-tuple-element.58), channel_id=1, source_target_pairs={{1,0},{2,1},{3,2},{4,3},{5,4},{6,5},{7,6},{9,8},{10,9},{11,10},{12... | collective-permute-start | bytes 49160 | tf_op jit(solution)/shard_map/ppermute | solution.py:21
  22.5 3.9 %collective-permute-start.7 = (bf16[16,4,128]{2,1,0:T(4,128)(2,1)S(1)}, bf16[16,4,128]{2,1,0:T(4,128)(2,1)S(1)}, u32[]{:S(2)}, u32[]{:S(2)}) collective-permute-start(bf16[16,4,128]{2,1,0:T(4,128)(2,1)S(1)} %get-tuple-element.57), channel_id=1, source_target_pairs={{0,1},{1,2},{2,3},{3,4},{4,5},{5,6},{6,7},{8,9},{9,10},{10,11},{11... | collective-permute-start | bytes 49160 | tf_op jit(solution)/shard_map/ppermute | solution.py:19
  25.6 16.2 %collective-permute-start.9 = (bf16[256,1152]{1,0:T(8,128)(2,1)}, bf16[256,1152]{1,0:T(8,128)(2,1)}, u32[]{:S(2)}, u32[]{:S(2)}) collective-permute-start(bf16[256,1152]{1,0:T(8,128)(2,1)} %constant_dynamic-slice_fusion.3), channel_id=1, source_target_pairs={{0,8},{8,0},{16,24},{24,16},{1,9},{9,1},{17,25},{25,17},{2,10},{10... | collective-permute-start | bytes 1769480 | tf_op jit(solution)/shard_map/ppermute | solution.py:198
  26.2 16.3 %collective-permute-start.11 = (bf16[256,1152]{1,0:T(8,128)(2,1)}, bf16[256,1152]{1,0:T(8,128)(2,1)}, u32[]{:S(2)}, u32[]{:S(2)}) collective-permute-start(bf16[256,1152]{1,0:T(8,128)(2,1)} %constant_dynamic-slice_fusion.3), channel_id=1, source_target_pairs={{0,16},{8,24},{16,0},{24,8},{1,17},{9,25},{17,1},{25,9},{2,18},{10... | collective-permute-start | bytes 1769480 | tf_op jit(solution)/shard_map/ppermute | solution.py:198
  29.0 13.7 %collective-permute-start.13 = (bf16[256,1152]{1,0:T(8,128)(2,1)S(1)}, bf16[256,1152]{1,0:T(8,128)(2,1)}, u32[]{:S(2)}, u32[]{:S(2)}) collective-permute-start(bf16[256,1152]{1,0:T(8,128)(2,1)S(1)} %collective-permute-done.6), channel_id=1, source_target_pairs={{0,1},{1,0},{2,3},{3,2},{4,5},{5,4},{6,7},{7,6},{8,9},{9,8},{10,11... | collective-permute-start | bytes 1769480 | tf_op jit(solution)/shard_map/ppermute | solution.py:30
  31.4 30.9 %all-to-all-start.2 = ((bf16[16,128,128]{2,1,0:T(8,128)(2,1)}), bf16[16,128,128]{2,1,0:T(8,128)(2,1)S(1)}, u32[]{:S(2)}, u32[]{:S(2)}) async-start(bf16[16,128,128]{2,1,0:T(8,128)(2,1)} %bitcast.12), calls=%async_computation.2 | async-start | bytes 1048576 | tf_op jit(solution)/shard_map/all_to_all | solution.py:260
  41.7 2.4 %collective-permute-start.10 = (bf16[256,1152]{1,0:T(8,128)(2,1)}, bf16[256,1152]{1,0:T(8,128)(2,1)S(1)}, u32[]{:S(2)}, u32[]{:S(2)}) collective-permute-start(bf16[256,1152]{1,0:T(8,128)(2,1)} %collective-permute-done.9), channel_id=1, source_target_pairs={{0,1},{1,0},{2,3},{3,2},{4,5},{5,4},{6,7},{7,6},{8,9},{9,8},{10,11... | collective-permute-start | bytes 1769480 | tf_op jit(solution)/shard_map/ppermute | solution.py:30
  42.5 2.9 %collective-permute-start.12 = (bf16[256,1152]{1,0:T(8,128)(2,1)}, bf16[256,1152]{1,0:T(8,128)(2,1)S(1)}, u32[]{:S(2)}, u32[]{:S(2)}) collective-permute-start(bf16[256,1152]{1,0:T(8,128)(2,1)} %collective-permute-done.11), channel_id=1, source_target_pairs={{0,1},{1,0},{2,3},{3,2},{4,5},{5,4},{6,7},{7,6},{8,9},{9,8},{10,11... | collective-permute-start | bytes 1769480 | tf_op jit(solution)/shard_map/ppermute | solution.py:30
  46.5 1.3 copy-start.1
  57.7 11.0 %collective-permute-start.15 = (bf16[16,4,128]{2,1,0:T(4,128)(2,1)S(1)}, bf16[16,4,128]{2,1,0:T(4,128)(2,1)S(1)}, u32[]{:S(2)}, u32[]{:S(2)}) collective-permute-start(bf16[16,4,128]{2,1,0:T(4,128)(2,1)S(1)} %get-tuple-element.56), channel_id=1, source_target_pairs={{1,0},{2,1},{3,2},{4,3},{5,4},{6,5},{7,6},{9,8},{10,9},{11,10},{12... | collective-permute-start | bytes 49160 | tf_op jit(solution)/shard_map/ppermute | solution.py:21
  59.0 9.7 %collective-permute-start.14 = (bf16[16,4,128]{2,1,0:T(4,128)(2,1)S(1)}, bf16[16,4,128]{2,1,0:T(4,128)(2,1)S(1)}, u32[]{:S(2)}, u32[]{:S(2)}) collective-permute-start(bf16[16,4,128]{2,1,0:T(4,128)(2,1)S(1)} %get-tuple-element.55), channel_id=1, source_target_pairs={{0,1},{1,2},{2,3},{3,4},{4,5},{5,6},{6,7},{8,9},{9,10},{10,11},{11... | collective-permute-start | bytes 49160 | tf_op jit(solution)/shard_map/ppermute | solution.py:19
  62.3 20.7 %all-to-all-start.1 = ((bf16[16,128,128]{2,1,0:T(8,128)(2,1)}), bf16[16,128,128]{2,1,0:T(8,128)(2,1)}, u32[]{:S(2)}, u32[]{:S(2)}) async-start(bf16[16,128,128]{2,1,0:T(8,128)(2,1)} %shard_map.98), calls=%async_computation.1 | async-start | bytes 1048576 | tf_op jit(solution)/shard_map/all_to_all | solution.py:261
  67.4 1.4 copy-start
  76.6 1.0 copy-start.3
  78.0 1.6 %copy-start.5 = (bf16[128,2048]{1,0:T(8,128)(2,1)}, bf16[128,2048]{1,0:T(8,128)(2,1)S(1)}, u32[]{:S(2)}) copy-start(bf16[128,2048]{1,0:T(8,128)(2,1)S(1)} %fusion.10) | copy-start | bytes 1572868
  79.7 7.3 %copy-start.4 = (bf16[2,1024,128]{1,2,0:T(8,128)(2,1)S(1)}, bf16[2,1024,128]{1,2,0:T(8,128)(2,1)}, u32[]{:S(2)}) copy-start(bf16[2,1024,128]{1,2,0:T(8,128)(2,1)} %all_to_all.40) | copy-start | bytes 1572868
  83.0 30.2 %all-to-all-start = ((bf16[32,130,64]{1,2,0:T(8,128)(2,1)}), bf16[32,130,64]{1,2,0:T(8,128)(2,1)S(1)}, u32[]{:S(2)}, u32[]{:S(2)}) async-start(bf16[32,130,64]{1,2,0:T(8,128)(2,1)} %pad_maximum_fusion.5), calls=%async_computation | async-start | bytes 2097152 | tf_op jit(solution)/shard_map/all_to_all | solution.py:150
  91.4 23.4 %collective-permute-start.18 = (f32[64,1152]{1,0:T(8,128)}, f32[64,1152]{1,0:T(8,128)}, u32[]{:S(2)}, u32[]{:S(2)}) collective-permute-start(f32[64,1152]{1,0:T(8,128)} %get-tuple-element.43), channel_id=1, source_target_pairs={{0,24},{8,16},{16,8},{24,0},{1,25},{9,17},{17,9},{25,1},{2,26},{10... | collective-permute-start | bytes 884744 | tf_op jit(solution)/shard_map/ppermute | solution.py:175
  93.8 21.0 %collective-permute-start.17 = (f32[64,1152]{1,0:T(8,128)S(1)}, f32[64,1152]{1,0:T(8,128)}, u32[]{:S(2)}, u32[]{:S(2)}) collective-permute-start(f32[64,1152]{1,0:T(8,128)S(1)} %get-tuple-element.44), channel_id=1, source_target_pairs={{0,16},{8,24},{16,0},{24,8},{1,17},{9,25},{17,1},{25,9},{2,18},{10... | collective-permute-start | bytes 884744 | tf_op jit(solution)/shard_map/ppermute | solution.py:175
  94.4 20.4 %collective-permute-start.16 = (f32[64,1152]{1,0:T(8,128)S(1)}, f32[64,1152]{1,0:T(8,128)}, u32[]{:S(2)}, u32[]{:S(2)}) collective-permute-start(f32[64,1152]{1,0:T(8,128)S(1)} %get-tuple-element.42), channel_id=1, source_target_pairs={{0,8},{8,0},{16,24},{24,16},{1,9},{9,1},{17,25},{25,17},{2,10},{10... | collective-permute-start | bytes 884744 | tf_op jit(solution)/shard_map/ppermute | solution.py:175
  116.8 10.8 %all-to-all-start.3 = ((f32[32,1,576]{2,1,0:T(1,128)}), f32[32,1,576]{2,1,0:T(1,128)S(1)}, u32[]{:S(2)}, u32[]{:S(2)}) async-start(f32[32,1,576]{2,1,0:T(1,128)} %reshape.118), calls=%async_computation.3 | async-start | bytes 163840 | tf_op jit(solution)/shard_map/all_to_all | solution.py:161
  119.9 11.5 %collective-permute-start.21 = (f32[64,1152]{1,0:T(8,128)S(1)}, f32[64,1152]{1,0:T(8,128)S(1)}, u32[]{:S(2)}, u32[]{:S(2)}) collective-permute-start(f32[64,1152]{1,0:T(8,128)S(1)} %add_add_fusion), channel_id=1, source_target_pairs={{0,24},{8,16},{16,8},{24,0},{1,25},{9,17},{17,9},{25,1},{2,26},{10... | collective-permute-start | bytes 884744 | tf_op jit(solution)/shard_map/ppermute | solution.py:185
  122.6 14.5 %collective-permute-start.20 = (f32[64,1152]{1,0:T(8,128)S(1)}, f32[64,1152]{1,0:T(8,128)S(1)}, u32[]{:S(2)}, u32[]{:S(2)}) collective-permute-start(f32[64,1152]{1,0:T(8,128)S(1)} %add_add_fusion), channel_id=1, source_target_pairs={{0,16},{8,24},{16,0},{24,8},{1,17},{9,25},{17,1},{25,9},{2,18},{10... | collective-permute-start | bytes 884744 | tf_op jit(solution)/shard_map/ppermute | solution.py:185
  123.2 13.9 %collective-permute-start.19 = (f32[64,1152]{1,0:T(8,128)S(1)}, f32[64,1152]{1,0:T(8,128)S(1)}, u32[]{:S(2)}, u32[]{:S(2)}) collective-permute-start(f32[64,1152]{1,0:T(8,128)S(1)} %add_add_fusion), channel_id=1, source_target_pairs={{0,8},{8,0},{16,24},{24,16},{1,9},{9,1},{17,25},{25,17},{2,10},{10... | collective-permute-start | bytes 884744 | tf_op jit(solution)/shard_map/ppermute | solution.py:185

commit v22 on v20

--- a/solution.py
+++ b/solution.py
@@ -45,7 +45,7 @@
         x = jnp.concatenate([rows[k : k + length].astype(jnp.bfloat16) for k in range(KERNEL)], axis=1)
         acc = lax.dot_general(x, w_ref[g], (((1,), (1,)), ((), ())), preferred_element_type=jnp.float32)
         sig = 1.0 / (1.0 + jnp.exp(-acc))
-        out_ref[g] = (up_ref[g] * sig * (1.0 + acc * (1.0 - sig))).astype(out_ref.dtype)
+        out_ref[g] = (up_ref[g].astype(jnp.float32) * sig * (1.0 + acc * (1.0 - sig))).astype(out_ref.dtype)
 
 
 def backward_kernel(pad_ref, w_ref, out_ref):
@@ -79,7 +79,7 @@
         cost_estimate=pl.CostEstimate(
             flops=flops,
             transcendentals=up.size,
-            bytes_accessed=padded.size * 2 + weights.size * 2 + up.size * 6,
+            bytes_accessed=padded.size * 2 + weights.size * 2 + up.size * 4,
         ),
     )(padded, weights, up)
 
@@ -252,7 +252,7 @@
     kernel_swapped = {**near_swapped, **swap_halves({far: far_piece})}
     weights = assemble_shards(kernel, "fsdp", kernel_fetched, kernel_swapped).reshape(GROUPS, chans, KERNEL * chans)
     up_float = upstream[0].astype(jnp.float32)
-    up_g = up_float.reshape(length, GROUPS, chans).transpose(1, 0, 2)
+    up_g = upstream[0].reshape(length, GROUPS, chans).transpose(1, 0, 2)
     dconv = conv_dconv(padded, weights, up_g)
     dpad = with_halo(dconv, "seq", 1, half)
     dnormed = conv_transpose(dpad, weights, length)

time: 139 us -> 138 us (level)
    unnamed x23 -> x24, local copies, waits for them, and re-layouts: 4.76 us -> 5.03 us
  transfers between devices with their start and end apart: 26 -> 26, of which waited for: 12 -> 11; matrix products, arithmetic and copies ran while one was open for 24% -> 23% of each run, Pallas kernels for 6% -> 6%
where the time goes in v22:
time: 138 us; the launch traced here: 137 us
  starting transfers between devices  43.7 us (32%)
  waiting for transfers between devices  43.6 us (32%)
  local copies, waits for them, and re-layouts  20 us (14%)
  other arithmetic  15.6 us (11%)
  Pallas kernels  8.41 us (6%)
  matrix products  4.47 us (3%)
    all_to_all x1, waiting for transfers between devices, table_and_gain(): got = lax.all_to_all(send, every, 0, 0, tiled=True)  18.4 us
    ppermute x6, waiting for transfers between devices, fetch_halves(): lax.ppermute(mine, axis, [(source, source ^ apart) for source in range(co...  9.32 us
    ppermute x6, starting transfers between devices, fetch_halves(): lax.ppermute(mine, axis, [(source, source ^ apart) for source in range(co...  8.34 us
    ppermute x3, waiting for transfers between devices, gather_by_permutes(): pieces.append(lax.ppermute(total, axis, pairs))  6.79 us
    ppermute x2, starting transfers between devices, with_halo(): lax.ppermute(tail, axis, [(i, (i + 1) % count) for i in range(ends)])  6.06 us
    all_to_all x1, starting transfers between devices, body(): group_out = lax.all_to_all(dconv, 'seq', 0, 1, tiled=True)  5.87 us
    all_to_all x1, starting transfers between devices, body(): group_in = lax.all_to_all(normed_g, 'seq', 0, 1, tiled=True)  5.6 us
    unnamed x24, local copies, waits for them, and re-layouts  5.03 us
  transfers between devices with their start and end apart: 26, of which 11 were waited for; matrix products, arithmetic and copies ran while one was open for 23% of the time, Pallas kernels for 6%

profile of v22, /device:TPU:0, one launch (start us, length us, event | category | flops | bytes accessed | tf_op | source)
XLA Modules:
  0.0 137.0 jit_solution(11242825406845109341)
XLA Ops:
  0.6 0.9 constant_dynamic-slice_fusion.4
  1.6 4.0 %collective-permute-start.4 = (bf16[32,2048]{1,0:T(8,128)(2,1)S(1)}, bf16[32,2048]{1,0:T(8,128)(2,1)S(1)}, u32[]{:S(2)}, u32[]{:S(2)}) collective-permute-start(bf16[32,2048]{1,0:T(8,128)(2,1)S(1)} %constant_dynamic-slice_fusion.4), channel_id=1, source_target_pairs={{0,24},{8,16},{16,8},{24,0},{1,25},{9,17},{17,9},{25,1},{2,26},{10... | collective-permute-start | bytes 393224 | tf_op jit(solution)/shard_map/ppermute | solution.py:198
  5.5 0.5 collective-permute-start
  6.2 3.7 %collective-permute-done.4 = bf16[32,2048]{1,0:T(8,128)(2,1)S(1)} collective-permute-done((bf16[32,2048]{1,0:T(8,128)(2,1)S(1)}, bf16[32,2048]{1,0:T(8,128)(2,1)S(1)}, u32[]{:S(2)}, u32[]{:S(2)}) %collective-permute-start.4) | collective-permute-done | bytes 131104 | tf_op jit(solution)/shard_map/ppermute | solution.py:198
  9.9 1.9 %constant_dynamic-slice_fusion.3 = bf16[256,1152]{1,0:T(8,128)(2,1)} fusion(bf16[512,1152]{1,0:T(8,128)(2,1)} %param.14, s32[]{:T(128)S(6)} %select_n.123), kind=kLoop, calls=%fused_computation.94 | loop fusion | bytes 1179652 | tf_op jit(solution)/shard_map/dynamic_slice | solution.py:196
  11.8 3.0 %collective-permute-start.6 = (bf16[256,1152]{1,0:T(8,128)(2,1)}, bf16[256,1152]{1,0:T(8,128)(2,1)S(1)}, u32[]{:S(2)}, u32[]{:S(2)}) collective-permute-start(bf16[256,1152]{1,0:T(8,128)(2,1)} %constant_dynamic-slice_fusion.3), channel_id=1, source_target_pairs={{0,24},{8,16},{16,8},{24,0},{1,25},{9,17},{17,9},{25,1},{2,26},{10... | collective-permute-start | bytes 1769480 | tf_op jit(solution)/shard_map/ppermute | solution.py:198
  15.3 0.8 collective-permute-done.1
  16.4 0.7 copy-done.6
  17.3 0.9 copy-done.8
  18.3 0.4 multiply_reduce_fusion.2
  19.4 1.0 copy.64
  20.4 0.8 fusion.40
  21.2 1.3 collective-permute-start.8
  22.5 3.0 %collective-permute-start.7 = (bf16[16,4,128]{2,1,0:T(4,128)(2,1)S(1)}, bf16[16,4,128]{2,1,0:T(4,128)(2,1)S(1)}, u32[]{:S(2)}, u32[]{:S(2)}) collective-permute-start(bf16[16,4,128]{2,1,0:T(4,128)(2,1)S(1)} %get-tuple-element.57), channel_id=1, source_target_pairs={{0,1},{1,2},{2,3},{3,4},{4,5},{5,6},{6,7},{8,9},{9,10},{10,11},{11... | collective-permute-start | bytes 49160 | tf_op jit(solution)/shard_map/ppermute | solution.py:19
  25.5 0.6 collective-permute-start.9
  26.4 2.0 %pad_maximum_fusion.6.pad_ref = bf16[16,136,128]{2,1,0:T(8,128)(2,1)} fusion(bf16[16,4,128]{2,1,0:T(4,128)(2,1)S(1)} %collective-permute-done.8, bf16[16,128,128]{2,1,0:T(8,128)(2,1)} %bitcast.12, bf16[16,4,128]{2,1,0:T(4,128)(2,1)S(1)} %collective-permute-done.7), kind=kLoop, calls=%fused_computation.47 | loop fusion | flops 1671168 | bytes 1114112 | tf_op jit(solution)/shard_map/concatenate | solution.py:17
  28.4 0.5 collective-permute-done.6
  28.9 1.0 collective-permute-start.13
  30.2 1.0 copy.66
  31.2 5.6 %all-to-all-start.2 = ((bf16[16,128,128]{2,1,0:T(8,128)(2,1)}), bf16[16,128,128]{2,1,0:T(8,128)(2,1)S(1)}, u32[]{:S(2)}, u32[]{:S(2)}) async-start(bf16[16,128,128]{2,1,0:T(8,128)(2,1)} %bitcast.12), calls=%async_computation.2 | async-start | bytes 1048576 | tf_op jit(solution)/shard_map/all_to_all | solution.py:260
  36.8 4.9 %collective-permute-done.9 = bf16[256,1152]{1,0:T(8,128)(2,1)} collective-permute-done((bf16[256,1152]{1,0:T(8,128)(2,1)}, bf16[256,1152]{1,0:T(8,128)(2,1)}, u32[]{:S(2)}, u32[]{:S(2)}) %collective-permute-start.9) | collective-permute-done | bytes 589856 | tf_op jit(solution)/shard_map/ppermute | solution.py:198
  41.7 0.4 collective-permute-start.10
  42.7 1.2 broadcast_select_fusion.1
  44.0 1.2 broadcast_select_fusion.5
  45.6 1.1 copy-done.1
  46.6 0.7 pad_maximum_fusion
  47.4 0.4 dynamic-slice_bitcast_fusion.3
  47.8 2.8 %pad_maximum_fusion.1 = bf16[2048,1152]{1,0:T(8,128)(2,1)} fusion(bf16[512,1152]{1,0:T(8,128)(2,1)S(1)} %get-tuple-element.35, bf16[512,1152]{1,0:T(8,128)(2,1)S(1)} %get-tuple-element.36, bf16[512,1152]{1,0:T(8,128)(2,1)S(1)} %get-tuple-element.37, bf16[512,1152]{1,0:T(8,128)(2,1)S(1)} %get-tuple-element.34), kind=kLoop, calls=%fused_computation.1 | loop fusion | flops 18874368 | bytes 9437184 | tf_op jit(solution)/shard_map/concatenate | solution.py:217
  50.6 4.3 %shard_map.98 = bf16[16,128,128]{2,1,0:T(8,128)(2,1)} custom-call(bf16[16,136,128]{2,1,0:T(8,128)(2,1)} %pad_maximum_fusion.6.pad_ref, bf16[16,128,1152]{2,1,0:T(8,128)(2,1)} %bitcast.93, bf16[16,128,128]{2,1,0:T(8,128)(2,1)} %bitcast.100), custom_call_target="tpu_custom_call" | custom-call | flops 603979776 | bytes 6324224 | tf_op jit(solution)/shard_map/pallas_call | solution.py:69
  54.9 0.8 fusion.39
  55.7 1.3 collective-permute-start.15
  57.0 3.0 %collective-permute-start.14 = (bf16[16,4,128]{2,1,0:T(4,128)(2,1)S(1)}, bf16[16,4,128]{2,1,0:T(4,128)(2,1)S(1)}, u32[]{:S(2)}, u32[]{:S(2)}) collective-permute-start(bf16[16,4,128]{2,1,0:T(4,128)(2,1)S(1)} %get-tuple-element.55), channel_id=1, source_target_pairs={{0,1},{1,2},{2,3},{3,4},{4,5},{5,6},{6,7},{8,9},{9,10},{10,11},{11... | collective-permute-start | bytes 49160 | tf_op jit(solution)/shard_map/ppermute | solution.py:19
  60.3 5.9 %all-to-all-start.1 = ((bf16[16,128,128]{2,1,0:T(8,128)(2,1)}), bf16[16,128,128]{2,1,0:T(8,128)(2,1)}, u32[]{:S(2)}, u32[]{:S(2)}) async-start(bf16[16,128,128]{2,1,0:T(8,128)(2,1)} %shard_map.98), calls=%async_computation.1 | async-start | bytes 1048576 | tf_op jit(solution)/shard_map/all_to_all | solution.py:261
  66.4 1.0 all_to_all.40
  67.5 1.0 pad_maximum_fusion.7.pad_ref
  68.5 4.1 %shard_map.99 = f32[16,128,128]{2,1,0:T(8,128)} custom-call(bf16[16,136,128]{2,1,0:T(8,128)(2,1)} %pad_maximum_fusion.7.pad_ref, bf16[16,128,1152]{2,1,0:T(8,128)(2,1)} %bitcast.94), custom_call_target="tpu_custom_call" | custom-call | flops 603979776 | bytes 6324224 | tf_op jit(solution)/shard_map/pallas_call | solution.py:91
  72.6 1.6 %copy.67 = f32[128,16,128]{0,2,1:T(8,128)S(1)} copy(f32[128,16,128]{2,0,1:T(8,128)} %bitcast.98) | data formatting | bytes 2097152 | tf_op jit(solution)/shard_map/transpose | solution.py:272
  74.9 0.7 copy-done.4
  75.6 0.4 fusion.10
  76.4 1.2 pad_maximum_fusion.5
  77.6 4.0 %all-to-all-done.1 = bf16[16,128,128]{2,1,0:T(8,128)(2,1)} async-done(((bf16[16,128,128]{2,1,0:T(8,128)(2,1)}), bf16[16,128,128]{2,1,0:T(8,128)(2,1)}, u32[]{:S(2)}, u32[]{:S(2)}) %all-to-all-start.1) | async-done | bytes 524320 | tf_op jit(solution)/shard_map/all_to_all | solution.py:261
  81.6 2.8 %all-to-all-start = ((bf16[32,130,64]{1,2,0:T(8,128)(2,1)}), bf16[32,130,64]{1,2,0:T(8,128)(2,1)S(1)}, u32[]{:S(2)}, u32[]{:S(2)}) async-start(bf16[32,130,64]{1,2,0:T(8,128)(2,1)} %pad_maximum_fusion.5), calls=%async_computation | async-start | bytes 2097152 | tf_op jit(solution)/shard_map/all_to_all | solution.py:150
  84.4 1.1 copy.77
  86.2 0.4 convolution_dynamic-update-slice_fusion.6
  86.6 0.4 convolution_dynamic-update-slice_fusion.5
  89.2 0.8 constant_dynamic-slice_fusion.2
  90.0 2.4 %collective-permute-start.18 = (f32[64,1152]{1,0:T(8,128)}, f32[64,1152]{1,0:T(8,128)}, u32[]{:S(2)}, u32[]{:S(2)}) collective-permute-start(f32[64,1152]{1,0:T(8,128)} %get-tuple-element.43), channel_id=1, source_target_pairs={{0,24},{8,16},{16,8},{24,0},{1,25},{9,17},{17,9},{25,1},{2,26},{10... | collective-permute-start | bytes 884744 | tf_op jit(solution)/shard_map/ppermute | solution.py:175
  92.4 0.5 collective-permute-start.17
  92.9 0.6 collective-permute-start.16
  93.5 18.4 %all-to-all-done = bf16[32,130,64]{1,2,0:T(8,128)(2,1)S(1)} async-done(((bf16[32,130,64]{1,2,0:T(8,128)(2,1)}), bf16[32,130,64]{1,2,0:T(8,128)(2,1)S(1)}, u32[]{:S(2)}, u32[]{:S(2)}) %all-to-all-start) | async-done | bytes 532512 | tf_op jit(solution)/shard_map/all_to_all | solution.py:150
  112.4 0.9 fusion.2
  113.4 1.2 add_add_fusion
  114.6 0.8 reshape.113
  115.4 3.1 %all-to-all-start.3 = ((f32[32,1,576]{2,1,0:T(1,128)}), f32[32,1,576]{2,1,0:T(1,128)S(1)}, u32[]{:S(2)}, u32[]{:S(2)}) async-start(f32[32,1,576]{2,1,0:T(1,128)} %reshape.113), calls=%async_computation.3 | async-start | bytes 163840 | tf_op jit(solution)/shard_map/all_to_all | solution.py:161
  118.5 2.7 %collective-permute-start.21 = (f32[64,1152]{1,0:T(8,128)S(1)}, f32[64,1152]{1,0:T(8,128)S(1)}, u32[]{:S(2)}, u32[]{:S(2)}) collective-permute-start(f32[64,1152]{1,0:T(8,128)S(1)} %add_add_fusion), channel_id=1, source_target_pairs={{0,24},{8,16},{16,8},{24,0},{1,25},{9,17},{17,9},{25,1},{2,26},{10... | collective-permute-start | bytes 884744 | tf_op jit(solution)/shard_map/ppermute | solution.py:185
  121.2 0.6 collective-permute-start.20
  122.1 4.1 %all-to-all-done.3 = f32[32,1,576]{2,1,0:T(1,128)S(1)} async-done(((f32[32,1,576]{2,1,0:T(1,128)}), f32[32,1,576]{2,1,0:T(1,128)S(1)}, u32[]{:S(2)}, u32[]{:S(2)}) %all-to-all-start.3) | async-done | bytes 73760 | tf_op jit(solution)/shard_map/all_to_all | solution.py:161
  126.1 0.5 broadcast.56
  126.6 0.8 reduce.7
  127.6 0.7 reshape.102
  128.4 0.6 slice_reduce_fusion
  128.9 1.1 collective-permute-done.21
  130.0 5.7 %collective-permute-done.20 = f32[64,1152]{1,0:T(8,128)S(1)} collective-permute-done((f32[64,1152]{1,0:T(8,128)S(1)}, f32[64,1152]{1,0:T(8,128)S(1)}, u32[]{:S(2)}, u32[]{:S(2)}) %collective-permute-start.20) | collective-permute-done | bytes 294944 | tf_op jit(solution)/shard_map/ppermute | solution.py:185
  135.9 1.1 pad_maximum_fusion.3
  (86 shorter events, 9.1 us)
Async XLA Ops:
  1.6 8.3 %collective-permute-start.4 = (bf16[32,2048]{1,0:T(8,128)(2,1)S(1)}, bf16[32,2048]{1,0:T(8,128)(2,1)S(1)}, u32[]{:S(2)}, u32[]{:S(2)}) collective-permute-start(bf16[32,2048]{1,0:T(8,128)(2,1)S(1)} %constant_dynamic-slice_fusion.4), channel_id=1, source_target_pairs={{0,24},{8,16},{16,8},{24,0},{1,25},{9,17},{17,9},{25,1},{2,26},{10... | collective-permute-start | bytes 393224 | tf_op jit(solution)/shard_map/ppermute | solution.py:198
  5.5 9.2 %collective-permute-start = (bf16[32,2048]{1,0:T(8,128)(2,1)S(1)}, bf16[32,2048]{1,0:T(8,128)(2,1)S(1)}, u32[]{:S(2)}, u32[]{:S(2)}) collective-permute-start(bf16[32,2048]{1,0:T(8,128)(2,1)S(1)} %constant_dynamic-slice_fusion.4), channel_id=1, source_target_pairs={{0,8},{8,0},{16,24},{24,16},{1,9},{9,1},{17,25},{25,17},{2,10},{10... | collective-permute-start | bytes 393224 | tf_op jit(solution)/shard_map/ppermute | solution.py:198
  6.1 8.9 %collective-permute-start.2 = (bf16[32,2048]{1,0:T(8,128)(2,1)S(1)}, bf16[32,2048]{1,0:T(8,128)(2,1)S(1)}, u32[]{:S(2)}, u32[]{:S(2)}) collective-permute-start(bf16[32,2048]{1,0:T(8,128)(2,1)S(1)} %constant_dynamic-slice_fusion.4), channel_id=1, source_target_pairs={{0,16},{8,24},{16,0},{24,8},{1,17},{9,25},{17,1},{25,9},{2,18},{10... | collective-permute-start | bytes 393224 | tf_op jit(solution)/shard_map/ppermute | solution.py:198
  9.9 5.4 %collective-permute-start.5 = (bf16[32,2048]{1,0:T(8,128)(2,1)S(1)}, bf16[32,2048]{1,0:T(8,128)(2,1)S(1)}, u32[]{:S(2)}, u32[]{:S(2)}) collective-permute-start(bf16[32,2048]{1,0:T(8,128)(2,1)S(1)} %collective-permute-done.4), channel_id=1, source_target_pairs={{0,1},{1,0},{2,3},{3,2},{4,5},{5,4},{6,7},{7,6},{8,9},{9,8},{10,11... | collective-permute-start | bytes 393224 | tf_op jit(solution)/shard_map/ppermute | solution.py:30
  11.8 17.2 %collective-permute-start.6 = (bf16[256,1152]{1,0:T(8,128)(2,1)}, bf16[256,1152]{1,0:T(8,128)(2,1)S(1)}, u32[]{:S(2)}, u32[]{:S(2)}) collective-permute-start(bf16[256,1152]{1,0:T(8,128)(2,1)} %constant_dynamic-slice_fusion.3), channel_id=1, source_target_pairs={{0,24},{8,16},{16,8},{24,0},{1,25},{9,17},{17,9},{25,1},{2,26},{10... | collective-permute-start | bytes 1769480 | tf_op jit(solution)/shard_map/ppermute | solution.py:198
  14.7 1.3 collective-permute-start.1
  15.0 1.3 collective-permute-start.3
  16.1 1.0 copy-start.6
  17.2 1.0 copy-start.8
  17.2 1.0 copy-start.9
  18.3 0.7 copy-start.7
  19.4 10.5 %copy-start.3 = (bf16[1,128,2048]{2,1,0:T(8,128)(2,1)S(1)}, bf16[1,128,2048]{2,1,0:T(8,128)(2,1)}, u32[]{:S(2)}) copy-start(bf16[1,128,2048]{2,1,0:T(8,128)(2,1)} %param.15) | copy-start | bytes 1572868
  21.2 5.1 %collective-permute-start.8 = (bf16[16,4,128]{2,1,0:T(4,128)(2,1)S(1)}, bf16[16,4,128]{2,1,0:T(4,128)(2,1)S(1)}, u32[]{:S(2)}, u32[]{:S(2)}) collective-permute-start(bf16[16,4,128]{2,1,0:T(4,128)(2,1)S(1)} %get-tuple-element.58), channel_id=1, source_target_pairs={{1,0},{2,1},{3,2},{4,3},{5,4},{6,5},{7,6},{9,8},{10,9},{11,10},{12... | collective-permute-start | bytes 49160 | tf_op jit(solution)/shard_map/ppermute | solution.py:21
  22.5 3.9 %collective-permute-start.7 = (bf16[16,4,128]{2,1,0:T(4,128)(2,1)S(1)}, bf16[16,4,128]{2,1,0:T(4,128)(2,1)S(1)}, u32[]{:S(2)}, u32[]{:S(2)}) collective-permute-start(bf16[16,4,128]{2,1,0:T(4,128)(2,1)S(1)} %get-tuple-element.57), channel_id=1, source_target_pairs={{0,1},{1,2},{2,3},{3,4},{4,5},{5,6},{6,7},{8,9},{9,10},{10,11},{11... | collective-permute-start | bytes 49160 | tf_op jit(solution)/shard_map/ppermute | solution.py:19
  25.5 16.2 %collective-permute-start.9 = (bf16[256,1152]{1,0:T(8,128)(2,1)}, bf16[256,1152]{1,0:T(8,128)(2,1)}, u32[]{:S(2)}, u32[]{:S(2)}) collective-permute-start(bf16[256,1152]{1,0:T(8,128)(2,1)} %constant_dynamic-slice_fusion.3), channel_id=1, source_target_pairs={{0,8},{8,0},{16,24},{24,16},{1,9},{9,1},{17,25},{25,17},{2,10},{10... | collective-permute-start | bytes 1769480 | tf_op jit(solution)/shard_map/ppermute | solution.py:198
  26.1 16.2 %collective-permute-start.11 = (bf16[256,1152]{1,0:T(8,128)(2,1)}, bf16[256,1152]{1,0:T(8,128)(2,1)S(1)}, u32[]{:S(2)}, u32[]{:S(2)}) collective-permute-start(bf16[256,1152]{1,0:T(8,128)(2,1)} %constant_dynamic-slice_fusion.3), channel_id=1, source_target_pairs={{0,16},{8,24},{16,0},{24,8},{1,17},{9,25},{17,1},{25,9},{2,18},{10... | collective-permute-start | bytes 1769480 | tf_op jit(solution)/shard_map/ppermute | solution.py:198
  28.9 13.7 %collective-permute-start.13 = (bf16[256,1152]{1,0:T(8,128)(2,1)S(1)}, bf16[256,1152]{1,0:T(8,128)(2,1)}, u32[]{:S(2)}, u32[]{:S(2)}) collective-permute-start(bf16[256,1152]{1,0:T(8,128)(2,1)S(1)} %collective-permute-done.6), channel_id=1, source_target_pairs={{0,1},{1,0},{2,3},{3,2},{4,5},{5,4},{6,7},{7,6},{8,9},{9,8},{10,11... | collective-permute-start | bytes 1769480 | tf_op jit(solution)/shard_map/ppermute | solution.py:30
  31.2 29.0 %all-to-all-start.2 = ((bf16[16,128,128]{2,1,0:T(8,128)(2,1)}), bf16[16,128,128]{2,1,0:T(8,128)(2,1)S(1)}, u32[]{:S(2)}, u32[]{:S(2)}) async-start(bf16[16,128,128]{2,1,0:T(8,128)(2,1)} %bitcast.12), calls=%async_computation.2 | async-start | bytes 1048576 | tf_op jit(solution)/shard_map/all_to_all | solution.py:260
  41.7 2.3 %collective-permute-start.10 = (bf16[256,1152]{1,0:T(8,128)(2,1)}, bf16[256,1152]{1,0:T(8,128)(2,1)S(1)}, u32[]{:S(2)}, u32[]{:S(2)}) collective-permute-start(bf16[256,1152]{1,0:T(8,128)(2,1)} %collective-permute-done.9), channel_id=1, source_target_pairs={{0,1},{1,0},{2,3},{3,2},{4,5},{5,4},{6,7},{7,6},{8,9},{9,8},{10,11... | collective-permute-start | bytes 1769480 | tf_op jit(solution)/shard_map/ppermute | solution.py:30
  42.3 2.9 %collective-permute-start.12 = (bf16[256,1152]{1,0:T(8,128)(2,1)S(1)}, bf16[256,1152]{1,0:T(8,128)(2,1)S(1)}, u32[]{:S(2)}, u32[]{:S(2)}) collective-permute-start(bf16[256,1152]{1,0:T(8,128)(2,1)S(1)} %collective-permute-done.11), channel_id=1, source_target_pairs={{0,1},{1,0},{2,3},{3,2},{4,5},{5,4},{6,7},{7,6},{8,9},{9,8},{10,11... | collective-permute-start | bytes 1769480 | tf_op jit(solution)/shard_map/ppermute | solution.py:30
  45.4 1.3 copy-start.1
  55.7 11.8 %collective-permute-start.15 = (bf16[16,4,128]{2,1,0:T(4,128)(2,1)S(1)}, bf16[16,4,128]{2,1,0:T(4,128)(2,1)S(1)}, u32[]{:S(2)}, u32[]{:S(2)}) collective-permute-start(bf16[16,4,128]{2,1,0:T(4,128)(2,1)S(1)} %get-tuple-element.56), channel_id=1, source_target_pairs={{1,0},{2,1},{3,2},{4,3},{5,4},{6,5},{7,6},{9,8},{10,9},{11,10},{12... | collective-permute-start | bytes 49160 | tf_op jit(solution)/shard_map/ppermute | solution.py:21
  57.0 10.5 %collective-permute-start.14 = (bf16[16,4,128]{2,1,0:T(4,128)(2,1)S(1)}, bf16[16,4,128]{2,1,0:T(4,128)(2,1)S(1)}, u32[]{:S(2)}, u32[]{:S(2)}) collective-permute-start(bf16[16,4,128]{2,1,0:T(4,128)(2,1)S(1)} %get-tuple-element.55), channel_id=1, source_target_pairs={{0,1},{1,2},{2,3},{3,4},{4,5},{5,6},{6,7},{8,9},{9,10},{10,11},{11... | collective-permute-start | bytes 49160 | tf_op jit(solution)/shard_map/ppermute | solution.py:19
  60.3 21.3 %all-to-all-start.1 = ((bf16[16,128,128]{2,1,0:T(8,128)(2,1)}), bf16[16,128,128]{2,1,0:T(8,128)(2,1)}, u32[]{:S(2)}, u32[]{:S(2)}) async-start(bf16[16,128,128]{2,1,0:T(8,128)(2,1)} %shard_map.98), calls=%async_computation.1 | async-start | bytes 1048576 | tf_op jit(solution)/shard_map/all_to_all | solution.py:261
  66.1 1.4 copy-start
  74.5 1.0 copy-start.4
  76.0 1.6 %copy-start.5 = (bf16[128,2048]{1,0:T(8,128)(2,1)}, bf16[128,2048]{1,0:T(8,128)(2,1)S(1)}, u32[]{:S(2)}) copy-start(bf16[128,2048]{1,0:T(8,128)(2,1)S(1)} %fusion.10) | copy-start | bytes 1572868
  77.6 7.9 %copy-start.2 = (bf16[2,1024,128]{1,2,0:T(8,128)(2,1)S(1)}, bf16[2,1024,128]{1,2,0:T(8,128)(2,1)}, u32[]{:S(2)}) copy-start(bf16[2,1024,128]{1,2,0:T(8,128)(2,1)} %all_to_all.40) | copy-start | bytes 1572868
  81.6 30.2 %all-to-all-start = ((bf16[32,130,64]{1,2,0:T(8,128)(2,1)}), bf16[32,130,64]{1,2,0:T(8,128)(2,1)S(1)}, u32[]{:S(2)}, u32[]{:S(2)}) async-start(bf16[32,130,64]{1,2,0:T(8,128)(2,1)} %pad_maximum_fusion.5), calls=%async_computation | async-start | bytes 2097152 | tf_op jit(solution)/shard_map/all_to_all | solution.py:150
  90.0 23.4 %collective-permute-start.18 = (f32[64,1152]{1,0:T(8,128)}, f32[64,1152]{1,0:T(8,128)}, u32[]{:S(2)}, u32[]{:S(2)}) collective-permute-start(f32[64,1152]{1,0:T(8,128)} %get-tuple-element.43), channel_id=1, source_target_pairs={{0,24},{8,16},{16,8},{24,0},{1,25},{9,17},{17,9},{25,1},{2,26},{10... | collective-permute-start | bytes 884744 | tf_op jit(solution)/shard_map/ppermute | solution.py:175
  92.4 21.0 %collective-permute-start.17 = (f32[64,1152]{1,0:T(8,128)S(1)}, f32[64,1152]{1,0:T(8,128)}, u32[]{:S(2)}, u32[]{:S(2)}) collective-permute-start(f32[64,1152]{1,0:T(8,128)S(1)} %get-tuple-element.44), channel_id=1, source_target_pairs={{0,16},{8,24},{16,0},{24,8},{1,17},{9,25},{17,1},{25,9},{2,18},{10... | collective-permute-start | bytes 884744 | tf_op jit(solution)/shard_map/ppermute | solution.py:175
  92.9 20.5 %collective-permute-start.16 = (f32[64,1152]{1,0:T(8,128)S(1)}, f32[64,1152]{1,0:T(8,128)}, u32[]{:S(2)}, u32[]{:S(2)}) collective-permute-start(f32[64,1152]{1,0:T(8,128)S(1)} %get-tuple-element.42), channel_id=1, source_target_pairs={{0,8},{8,0},{16,24},{24,16},{1,9},{9,1},{17,25},{25,17},{2,10},{10... | collective-permute-start | bytes 884744 | tf_op jit(solution)/shard_map/ppermute | solution.py:175
  115.4 10.7 %all-to-all-start.3 = ((f32[32,1,576]{2,1,0:T(1,128)}), f32[32,1,576]{2,1,0:T(1,128)S(1)}, u32[]{:S(2)}, u32[]{:S(2)}) async-start(f32[32,1,576]{2,1,0:T(1,128)} %reshape.113), calls=%async_computation.3 | async-start | bytes 163840 | tf_op jit(solution)/shard_map/all_to_all | solution.py:161
  118.5 11.5 %collective-permute-start.21 = (f32[64,1152]{1,0:T(8,128)S(1)}, f32[64,1152]{1,0:T(8,128)S(1)}, u32[]{:S(2)}, u32[]{:S(2)}) collective-permute-start(f32[64,1152]{1,0:T(8,128)S(1)} %add_add_fusion), channel_id=1, source_target_pairs={{0,24},{8,16},{16,8},{24,0},{1,25},{9,17},{17,9},{25,1},{2,26},{10... | collective-permute-start | bytes 884744 | tf_op jit(solution)/shard_map/ppermute | solution.py:185
  121.2 14.5 %collective-permute-start.20 = (f32[64,1152]{1,0:T(8,128)S(1)}, f32[64,1152]{1,0:T(8,128)S(1)}, u32[]{:S(2)}, u32[]{:S(2)}) collective-permute-start(f32[64,1152]{1,0:T(8,128)S(1)} %add_add_fusion), channel_id=1, source_target_pairs={{0,16},{8,24},{16,0},{24,8},{1,17},{9,25},{17,1},{25,9},{2,18},{10... | collective-permute-start | bytes 884744 | tf_op jit(solution)/shard_map/ppermute | solution.py:185
  121.8 13.9 %collective-permute-start.19 = (f32[64,1152]{1,0:T(8,128)S(1)}, f32[64,1152]{1,0:T(8,128)S(1)}, u32[]{:S(2)}, u32[]{:S(2)}) collective-permute-start(f32[64,1152]{1,0:T(8,128)S(1)} %add_add_fusion), channel_id=1, source_target_pairs={{0,8},{8,0},{16,24},{24,16},{1,9},{9,1},{17,25},{25,17},{2,10},{10... | collective-permute-start | bytes 884744 | tf_op jit(solution)/shard_map/ppermute | solution.py:185
